TPU v7x, 256 devices: a whole 4x4x8 slice. The times are simulated.
256 devices in a mesh: tm: 64 (over z, x_hi, y), chan: 4 (over x_lo, core).
Axes of the slice: x: 4 (x_hi: 2, x_lo: 2; x = x_hi * 2 + x_lo), y: 4, z: 8, core: 2. Of those that a mesh axis runs over, the one named last changes fastest.
Arguments:
- signal: float32 [256, 8192], P('chan', 'tm'), may hold values from -256 to 256
- support: int32 [32], replicated, may hold values from 1 to 4, as said below
- pair_first: int32 [4, 512], replicated, may hold values from 0 to 255
- pair_second: int32 [4, 512], replicated, may hold values from 0 to 255
- pair_count: int32 [4], replicated, may hold values from 128 to 512, as said below
Outputs:
- cross: float32 [4, 512, 2, 32], P('chan', 'tm')
- coherence: float32 [4, 512, 32], P('chan', 'tm')
Inputs may be any that keep to these rules, and one draw needn't show every extreme that they name: With b = q // 8 the band of scale q, support[q] is at most (4 * 128 / 4^(3 - b) + 127) // 128, and equals it for the last scale of every band. The live slots of an owner are its first pair_count slots; some owner has all 512 slots live.
All inputs are finite; a program needn't handle non-finite values.
Results may differ from a plain program's by a relative error of at most 0.0027.
Values may be sent and summed in bfloat16 or wider, within the bound.
No kernel may reach another device: no remote copies, remote signals or barrier semaphores. Data moves between devices by JAX's collectives and lax.ppermute only.
A program may use at most 192 MiB of HBM per device.

v0:
```python
import math

import jax
import jax.numpy as jnp
import numpy as np
from jax import lax
from jax.sharding import PartitionSpec as P

NS = 32
BLK = 128
TD = 128


power_floor = 1e-06


def from_behind(array, axis, by):
    peers = lax.axis_size(axis)
    return lax.ppermute(array, axis, [(i, (i + by) % peers) for i in range(peers)])


def morlet_parts(offset, scale_index, reach_blocks):
    scale_width = 2.0 * TD * jnp.exp2((scale_index - (NS - 1)).astype(jnp.float32) / 4.0)
    scaled_offset = offset.astype(jnp.float32) / scale_width
    amplitude = (
        math.pi ** (-0.25) * lax.rsqrt(scale_width) * jnp.exp(-0.5 * scaled_offset * scaled_offset)
    )
    inside = jnp.abs(offset) < reach_blocks * BLK
    real_part = jnp.where(inside, amplitude * jnp.cos(6.0 * scaled_offset), 0.0)
    imag_part = jnp.where(inside, amplitude * jnp.sin(6.0 * scaled_offset), 0.0)
    return (real_part.astype(jnp.bfloat16), imag_part.astype(jnp.bfloat16))


def wavelet_band(extended, scale_ids, reaches, offsets, time_span):
    channels = extended.shape[0]
    blocks = time_span // BLK
    centre = 4 * time_span // BLK
    tap_blocks = 2 * offsets + 1
    pieces = [
        extended[:, (centre + offset_step) * BLK : (centre + offset_step) * BLK + time_span]
        for offset_step in range(-offsets, offsets + 1)
    ]
    unfolded = jnp.stack(pieces, axis=1).reshape(channels, tap_blocks, blocks, BLK)
    unfolded = unfolded.transpose(0, 2, 1, 3).reshape(channels * blocks, tap_blocks * BLK)
    lag_start = (jnp.arange(tap_blocks, dtype=jnp.int32) - offsets) * BLK
    within = jnp.arange(BLK, dtype=jnp.int32)
    tap_offset = lag_start[:, None, None] + within[None, :, None] - within[None, None, :]

    def single_scale(scale_index, reach_blocks):
        return morlet_parts(tap_offset, scale_index, reach_blocks)

    real_part, imag_part = jax.vmap(single_scale)(scale_ids, reaches)
    kernel_table = jnp.stack([real_part, imag_part], axis=1)
    kernel_table = kernel_table.transpose(2, 3, 0, 1, 4).reshape(tap_blocks * BLK, -1)
    coefficients = jnp.dot(unfolded, kernel_table, preferred_element_type=jnp.float32)
    scale_count = scale_ids.shape[0]
    coefficients = coefficients.astype(jnp.bfloat16).reshape(channels, blocks, scale_count, 2, BLK)
    return coefficients.transpose(2, 3, 0, 1, 4).reshape(scale_count, 2 * channels, time_span)


def pair_spectra(coefficients, flat_index):
    channels = coefficients.shape[1] // 2
    scale_count = coefficients.shape[0]
    gram_matrix = jnp.einsum(
        "qat,qbt->qab", coefficients, coefficients, preferred_element_type=jnp.float32
    )
    real_part = gram_matrix[:, :channels, :channels] + gram_matrix[:, channels:, channels:]
    imag_part = gram_matrix[:, channels:, :channels] - gram_matrix[:, :channels, channels:]
    auto_power = jnp.diagonal(real_part, axis1=1, axis2=2)
    real_pairs = jnp.take(real_part.reshape(scale_count, -1), flat_index, axis=1)
    imag_pairs = jnp.take(imag_part.reshape(scale_count, -1), flat_index, axis=1)
    return (real_pairs, imag_pairs, auto_power)


def shards(signal, support, pair_first, pair_second, pair_count):
    groups = lax.axis_size("chan")
    cluster_number = lax.axis_index("chan")
    time_index = lax.axis_index("tm")
    time_devices = lax.axis_size("tm")
    time_span = signal.shape[1]
    ntime = time_span * time_devices
    rounded = signal.astype(jnp.bfloat16)
    gathered = lax.all_gather(rounded, "chan", axis=0, tiled=True)
    neighbours = [
        from_behind(gathered, "tm", distance) for distance in (4, 3, 2, 1, -1, -2, -3, -4)
    ]
    extended = jnp.concatenate(neighbours[:4] + [gathered] + neighbours[4:], axis=1)
    channels = extended.shape[0]
    first_flat = pair_first.reshape(-1)
    second_flat = pair_second.reshape(-1)
    flat_index = first_flat * channels + second_flat
    per_group = NS // groups
    scale_ids = cluster_number * per_group + jnp.arange(per_group, dtype=jnp.int32)
    coefficients = wavelet_band(
        extended, scale_ids, support[scale_ids], 4 * time_span // BLK, time_span
    )
    real_pairs, imag_pairs, auto_power = pair_spectra(coefficients, flat_index)
    position = np.arange(NS)
    owner_devices = pair_first.shape[0]
    slots_total = pair_first.shape[1]
    stacked = jnp.stack([real_pairs, imag_pairs], axis=0)
    columns = stacked.shape[0]
    partial_value = stacked.reshape(columns, per_group, owner_devices, slots_total).transpose(
        2, 3, 0, 1
    )
    summed = lax.psum_scatter(partial_value, "tm", scatter_dimension=1, tiled=True)
    owned = lax.all_to_all(summed, "chan", split_axis=0, concat_axis=3, tiled=True)
    owned = owned[:, :, :, position] / ntime
    slots_local = owned.shape[1]
    slot_index = time_index * slots_local + jnp.arange(slots_local, dtype=jnp.int32)
    alive_mask = slot_index < pair_count[cluster_number]
    cross_real = owned[0, :, 0, :]
    cross_imag = owned[0, :, 1, :]
    power_total = lax.psum(auto_power, "tm")
    power_groups = lax.all_gather(power_total, "chan", axis=0, tiled=True)
    power_all = power_groups[position] / ntime
    first_row = lax.dynamic_index_in_dim(pair_first, cluster_number, 0, False)
    second_row = lax.dynamic_index_in_dim(pair_second, cluster_number, 0, False)
    first_owned = lax.dynamic_slice_in_dim(first_row, time_index * slots_local, slots_local)
    second_owned = lax.dynamic_slice_in_dim(second_row, time_index * slots_local, slots_local)
    first_power = power_all[:, first_owned].T
    second_power = power_all[:, second_owned].T
    coherence = (cross_real * cross_real + cross_imag * cross_imag) / (
        (first_power + power_floor) * (second_power + power_floor)
    )
    coherence = jnp.where(alive_mask[:, None], coherence, 0.0)[None]
    cross = jnp.stack([cross_real, cross_imag], axis=1)
    cross = jnp.where(alive_mask[:, None, None], cross, 0.0)[None]
    return (cross, coherence.astype(jnp.float32))


def solution(mesh):
    in_specs = (P("chan", "tm"), P(), P(), P(), P())
    out_specs = (P("chan", "tm", None, None), P("chan", "tm", None))
    return jax.shard_map(shards, mesh=mesh, in_specs=in_specs, out_specs=out_specs, check_vma=False)
```

profile of v0, /device:TPU:1, one launch (start us, length us, event | category | flops | bytes accessed | tf_op | source)
XLA Modules:
  0.0 1023.3 jit_solution(1796853218506428714)
XLA Ops:
  8.0 8.3 all_gather.6
  16.4 6.4 collective-permute-start.7
  24.0 5.5 collective-permute-start.5
  32.9 1.2 dynamic_slice.16
  35.2 147.0 %fusion.2 = (bf16[8,1,9,128,128]{4,1,0,3,2:T(2,128)(2,1)S(1)}, bf16[8,1,9,128,128]{4,1,0,3,2:T(2,128)(2,1)S(1)}) fusion(s32[9,128,128]{2,1,0:T(8,128)S(1)} %get-tuple-element.16, s32[8]{0:T(128)S(1)} %broadcast_multiply_fusion.1, f32[8]{0:T(128)S(1)} %get-tuple-element.20, f32[9,128,128]{2,1,0:T(8,128)S(1)} %get-tuple-element.15, f32[8]{0:T(128)S(1)} %get-tuple-element.19), kind=kLoop, calls=%fused_computation.13 | loop fusion | flops 14155776 | bytes 5898336 | tf_op jit(solution)/shard_map/vmap()/convert_element_type | solution.py:31
  182.2 11.7 %maximum_bitcast_fusion = bf16[9,128,8,2,128]{4,3,2,1,0:T(2,128)(2,1)} fusion(bf16[8,1,9,128,128]{4,1,0,3,2:T(2,128)(2,1)S(1)} %get-tuple-element.14, bf16[8,1,9,128,128]{4,1,0,3,2:T(2,128)(2,1)S(1)} %get-tuple-element.13), kind=kLoop, calls=%fused_computation.15 | loop fusion | flops 9437184 | bytes 9437184 | tf_op jit(solution)/shard_map/transpose | solution.py:54
  193.9 8.8 reshape.232
  204.2 7.6 collective-permute-done.1
  211.8 9.1 collective-permute-done.2
  221.3 8.4 collective-permute-done.3
  229.9 3.9 convolution_convert_fusion
  234.8 1.3 fusion.13
  236.0 1.9 slice_add_fusion
  237.9 17.3 %copy.84 = f32[8,256,256]{0,2,1:T(8,128)} copy(f32[8,256,256]{2,1,0:T(8,128)} %get-tuple-element.11) | data formatting | bytes 4194304 | tf_op jit(solution)/shard_map/reshape | solution.py:70
  255.2 16.2 %copy.85 = f32[8,256,256]{0,2,1:T(8,128)} copy(f32[8,256,256]{2,1,0:T(8,128)S(1)} %get-tuple-element.12) | data formatting | bytes 4194304 | tf_op jit(solution)/shard_map/reshape | solution.py:71
  271.4 16.0 %gather_fusion.6 = f32[2048,8]{1,0:T(8,128)S(1)} fusion(f32[8,65536]{0,1:T(8,128)} %bitcast.81, s32[2048]{0:T(1024)S(1)} %fusion.9), kind=kCustom, calls=%fused_computation.clone | custom fusion | bytes 139264 | tf_op jit(solution)/shard_map/jit(_take)/gather | solution.py:70
  287.4 16.0 %gather_fusion.7 = f32[2048,8]{1,0:T(8,128)S(1)} fusion(f32[8,65536]{0,1:T(8,128)} %bitcast.82, s32[2048]{0:T(1024)S(1)} %fusion.9), kind=kCustom, calls=%fused_computation.1.clone | custom fusion | bytes 139264 | tf_op jit(solution)/shard_map/jit(_take)/gather | solution.py:71
  305.1 1.9 maximum_bitcast_fusion.1
  307.8 2.3 gather_fusion.2
  310.1 299.8 %psum.7 = f32[8,256]{0,1:T(8,128)S(1)} all-reduce(f32[8,256]{0,1:T(8,128)S(1)} %bitcast.88), channel_id=1, replica_groups=mesh['tm'=64,'chan'=4] {'tm'}, use_global_device_ids=true, to_apply=%region_1.3 | all-reduce | flops 2048 | bytes 16384 | tf_op jit(solution)/shard_map/psum | solution.py:114
  609.9 61.3 %all_gather.7 = f32[32,256]{1,0:T(8,128)S(1)} all-gather(f32[8,256]{1,0:T(8,128)S(1)} %copy.77), channel_id=1, replica_groups=mesh['tm'=64,'chan'=4] {'chan'}, dimensions={0}, use_global_device_ids=true | all-gather | bytes 40960 | tf_op jit(solution)/shard_map/all_gather | solution.py:115
  671.8 287.3 %all-reduce.3.cloned.1.call-done = f32[4,512,2,8]{3,0,1,2:T(4,128)} async-done(((f32[4,512,2,8]{3,0,1,2:T(4,128)}), f32[4,512,2,8]{3,0,1,2:T(4,128)}) %all-reduce.3.cloned.1.call-update) | async-done | bytes 131088
  960.5 49.6 %all-to-all-start = ((f32[4,1,128]{2,1,0:T(1,128)}), f32[4,1,128]{2,1,0:T(1,128)S(1)}, u32[]{:S(2)}, u32[]{:S(2)}) async-start(f32[4,1,128]{2,1,0:T(1,128)} %reshape.313), calls=%async_computation | async-start | bytes 4096 | tf_op jit(solution)/shard_map/all_to_all | solution.py:107
  1011.4 1.6 all-to-all-done
  (78 shorter events, 17.9 us)
Async XLA Ops:
  7.2 27.0 %copy-start = (s32[32]{0:T(128)S(1)}, s32[32]{0:T(128)}, u32[]{:S(2)}) copy-start(s32[32]{0:T(128)} %param.11) | copy-start | bytes 388
  7.2 951.8 %all-reduce.3.cloned.1.call-start = ((), (), s32[]{:S(2)}) async-start(), calls=%async_computation.1 | async-start | bytes 4194304
  16.4 213.4 %collective-permute-start.7 = (bf16[256,128]{0,1:T(8,128)(2,1)S(1)}, bf16[256,128]{0,1:T(8,128)(2,1)S(1)}, u32[]{:S(2)}, u32[]{:S(2)}) collective-permute-start(bf16[256,128]{0,1:T(8,128)(2,1)S(1)} %copy.59), channel_id=1, source_target_pairs={{0,240},{4,244},{8,248},{12,252},{16,0},{20,4},{24,8},{28,12},{32,... | collective-permute-start | bytes 196616 | tf_op jit(solution)/shard_map/ppermute | solution.py:19
  22.8 207.0 %collective-permute-start.6 = (bf16[256,128]{0,1:T(8,128)(2,1)S(1)}, bf16[256,128]{0,1:T(8,128)(2,1)S(1)}, u32[]{:S(2)}, u32[]{:S(2)}) collective-permute-start(bf16[256,128]{0,1:T(8,128)(2,1)S(1)} %copy.59), channel_id=1, source_target_pairs={{0,244},{4,248},{8,252},{12,0},{16,4},{20,8},{24,12},{28,16},{32,2... | collective-permute-start | bytes 196616 | tf_op jit(solution)/shard_map/ppermute | solution.py:19
  24.0 205.8 %collective-permute-start.5 = (bf16[256,128]{0,1:T(8,128)(2,1)S(1)}, bf16[256,128]{0,1:T(8,128)(2,1)S(1)}, u32[]{:S(2)}, u32[]{:S(2)}) collective-permute-start(bf16[256,128]{0,1:T(8,128)(2,1)S(1)} %copy.59), channel_id=1, source_target_pairs={{0,248},{4,252},{8,0},{12,4},{16,8},{20,12},{24,16},{28,20},{32,24... | collective-permute-start | bytes 196616 | tf_op jit(solution)/shard_map/ppermute | solution.py:19
  29.5 200.2 %collective-permute-start.4 = (bf16[256,128]{0,1:T(8,128)(2,1)S(1)}, bf16[256,128]{0,1:T(8,128)(2,1)S(1)}, u32[]{:S(2)}, u32[]{:S(2)}) collective-permute-start(bf16[256,128]{0,1:T(8,128)(2,1)S(1)} %copy.59), channel_id=1, source_target_pairs={{0,252},{4,0},{8,4},{12,8},{16,12},{20,16},{24,20},{28,24},{32,28}... | collective-permute-start | bytes 196616 | tf_op jit(solution)/shard_map/ppermute | solution.py:19
  30.6 173.4 %collective-permute-start = (bf16[256,128]{0,1:T(8,128)(2,1)S(1)}, bf16[256,128]{0,1:T(8,128)(2,1)S(1)}, u32[]{:S(2)}, u32[]{:S(2)}) collective-permute-start(bf16[256,128]{0,1:T(8,128)(2,1)S(1)} %copy.59), channel_id=1, source_target_pairs={{0,16},{4,20},{8,24},{12,28},{16,32},{20,36},{24,40},{28,44},{32,4... | collective-permute-start | bytes 196616 | tf_op jit(solution)/shard_map/ppermute | solution.py:19
  193.9 8.9 copy-start.2
  204.1 7.7 collective-permute-start.1
  211.8 9.1 collective-permute-start.2
  220.9 8.8 collective-permute-start.3
  304.4 712.0 %copy-start.1 = (s32[32]{0:T(128)S(1)}, s32[32]{0:T(128)}, u32[]{:S(2)}) copy-start(s32[32]{0:T(128)} %param.11) | copy-start | bytes 388
  960.5 52.6 %all-to-all-start = ((f32[4,1,128]{2,1,0:T(1,128)}), f32[4,1,128]{2,1,0:T(1,128)S(1)}, u32[]{:S(2)}, u32[]{:S(2)}) async-start(f32[4,1,128]{2,1,0:T(1,128)} %reshape.313), calls=%async_computation | async-start | bytes 4096 | tf_op jit(solution)/shard_map/all_to_all | solution.py:107
Sparse Core Ops, SparseCore 0:
  307.2 651.7 all-reduce.2
where the time goes:
time: 1020 us
  blocking collectives  369 us (36%)
  waiting for transfers between devices  314 us (31%)
  other arithmetic  168 us (16%)
  local copies, waits for them, and re-layouts  87.8 us (9%)
  starting transfers between devices  64.3 us (6%)
  between operations  15 us (1%)
    psum x1, blocking collectives, shards(): power_total = lax.psum(auto_power, 'tm')  300 us
    unnamed x2, waiting for transfers between devices  287 us
    convert_element_type x1, other arithmetic, morlet_parts(): return (real_part.astype(jnp.bfloat16), imag_part.astype(jnp.bfloat16))  147 us
    all_gather x1, blocking collectives, shards(): power_groups = lax.all_gather(power_total, 'chan', axis=0, tiled=True)  61.3 us
    all_to_all x1, starting transfers between devices, shards(): lax.all_to_all(summed, 'chan', split_axis=0, concat_axis=3, tiled=True)  49.6 us
    ppermute x8, waiting for transfers between devices, from_behind(): lax.ppermute(array, axis, [(i, (i + by) % peers) for i in range(peers)])  25.2 us
  transfers between devices with their start and end apart: 10, of which 5 were waited for; matrix products, arithmetic and copies ran while one was open for 17% of the time, Pallas kernels for 0%

commit v1 on v0

--- a/solution.py
+++ b/solution.py
@@ -58,18 +58,26 @@
     return coefficients.transpose(2, 3, 0, 1, 4).reshape(scale_count, 2 * channels, time_span)
 
 
-def pair_spectra(coefficients, flat_index):
+def pair_sums(coefficients, first_flat, second_flat):
+    scale_count = coefficients.shape[0]
     channels = coefficients.shape[1] // 2
-    scale_count = coefficients.shape[0]
-    gram_matrix = jnp.einsum(
-        "qat,qbt->qab", coefficients, coefficients, preferred_element_type=jnp.float32
-    )
-    real_part = gram_matrix[:, :channels, :channels] + gram_matrix[:, channels:, channels:]
-    imag_part = gram_matrix[:, channels:, :channels] - gram_matrix[:, :channels, channels:]
-    auto_power = jnp.diagonal(real_part, axis1=1, axis2=2)
-    real_pairs = jnp.take(real_part.reshape(scale_count, -1), flat_index, axis=1)
-    imag_pairs = jnp.take(imag_part.reshape(scale_count, -1), flat_index, axis=1)
-    return (real_pairs, imag_pairs, auto_power)
+    time_span = coefficients.shape[2]
+    chan_iota = jnp.arange(channels, dtype=jnp.int32)
+    both = jnp.concatenate([first_flat, second_flat])
+    pick = (both[:, None] == chan_iota[None, :]).astype(jnp.bfloat16)
+    parts = coefficients.reshape(scale_count, 2, channels, time_span)
+    picked = jnp.einsum("pc,qrct->qrpt", pick, parts, preferred_element_type=jnp.float32)
+    picked = picked.astype(jnp.bfloat16).astype(jnp.float32)
+    pairs = first_flat.shape[0]
+    first_real = picked[:, 0, :pairs]
+    first_imag = picked[:, 1, :pairs]
+    second_real = picked[:, 0, pairs:]
+    second_imag = picked[:, 1, pairs:]
+    cross_real = jnp.sum(first_real * second_real + first_imag * second_imag, axis=-1)
+    cross_imag = jnp.sum(first_imag * second_real - first_real * second_imag, axis=-1)
+    power_first = jnp.sum(first_real * first_real + first_imag * first_imag, axis=-1)
+    power_second = jnp.sum(second_real * second_real + second_imag * second_imag, axis=-1)
+    return jnp.stack([cross_real, cross_imag, power_first, power_second], axis=1)
 
 
 def shards(signal, support, pair_first, pair_second, pair_count):
@@ -85,41 +93,26 @@
         from_behind(gathered, "tm", distance) for distance in (4, 3, 2, 1, -1, -2, -3, -4)
     ]
     extended = jnp.concatenate(neighbours[:4] + [gathered] + neighbours[4:], axis=1)
-    channels = extended.shape[0]
-    first_flat = pair_first.reshape(-1)
-    second_flat = pair_second.reshape(-1)
-    flat_index = first_flat * channels + second_flat
     per_group = NS // groups
     scale_ids = cluster_number * per_group + jnp.arange(per_group, dtype=jnp.int32)
     coefficients = wavelet_band(
         extended, scale_ids, support[scale_ids], 4 * time_span // BLK, time_span
     )
-    real_pairs, imag_pairs, auto_power = pair_spectra(coefficients, flat_index)
-    position = np.arange(NS)
-    owner_devices = pair_first.shape[0]
-    slots_total = pair_first.shape[1]
-    stacked = jnp.stack([real_pairs, imag_pairs], axis=0)
-    columns = stacked.shape[0]
-    partial_value = stacked.reshape(columns, per_group, owner_devices, slots_total).transpose(
-        2, 3, 0, 1
-    )
-    summed = lax.psum_scatter(partial_value, "tm", scatter_dimension=1, tiled=True)
-    owned = lax.all_to_all(summed, "chan", split_axis=0, concat_axis=3, tiled=True)
-    owned = owned[:, :, :, position] / ntime
-    slots_local = owned.shape[1]
+    owner_devices, slots_total = pair_first.shape
+    sums = pair_sums(coefficients, pair_first.reshape(-1), pair_second.reshape(-1))
+    slots_local = slots_total // time_devices
+    values = sums.shape[1]
+    partial_value = sums.reshape(per_group, values, owner_devices, time_devices, slots_local)
+    partial_value = partial_value.transpose(3, 2, 4, 1, 0)
+    exchanged = lax.all_to_all(partial_value, "tm", 0, 0, tiled=True)
+    summed = jnp.sum(exchanged, axis=0)
+    owned = lax.all_to_all(summed, "chan", 0, 3, tiled=True)[0] / ntime
     slot_index = time_index * slots_local + jnp.arange(slots_local, dtype=jnp.int32)
     alive_mask = slot_index < pair_count[cluster_number]
-    cross_real = owned[0, :, 0, :]
-    cross_imag = owned[0, :, 1, :]
-    power_total = lax.psum(auto_power, "tm")
-    power_groups = lax.all_gather(power_total, "chan", axis=0, tiled=True)
-    power_all = power_groups[position] / ntime
-    first_row = lax.dynamic_index_in_dim(pair_first, cluster_number, 0, False)
-    second_row = lax.dynamic_index_in_dim(pair_second, cluster_number, 0, False)
-    first_owned = lax.dynamic_slice_in_dim(first_row, time_index * slots_local, slots_local)
-    second_owned = lax.dynamic_slice_in_dim(second_row, time_index * slots_local, slots_local)
-    first_power = power_all[:, first_owned].T
-    second_power = power_all[:, second_owned].T
+    cross_real = owned[:, 0, :]
+    cross_imag = owned[:, 1, :]
+    first_power = owned[:, 2, :]
+    second_power = owned[:, 3, :]
     coherence = (cross_real * cross_real + cross_imag * cross_imag) / (
         (first_power + power_floor) * (second_power + power_floor)
     )

time: 1020 us -> 320 us (0.31)
  blocking collectives: 369 us -> 8.3 us
  waiting for transfers between devices: 314 us -> 39 us
  local copies, waits for them, and re-layouts: 87.8 us -> 35.5 us
  starting transfers between devices: 64.3 us -> 28.6 us
  other arithmetic: 168 us -> 192 us
  between operations: 15 us -> 1.15 us
  matrix products: 5.13 us -> 17.1 us
    psum x1 -> x0, blocking collectives: 300 us -> none  [shards(): power_total = lax.psum(auto_power, 'tm')]
    unnamed x2 -> x0, waiting for transfers between devices: 287 us -> none
    all_gather x1 -> x0, blocking collectives: 61.3 us -> none  [shards(): power_groups = lax.all_gather(power_total, 'chan', axis=0, tiled=True)]
    gather x9 -> x0, local copies, waits for them, and re-layouts: 36.8 us -> none  [the longest x1 16 us: pair_spectra(): jnp.take(imag_part.reshape(scale_count, -1), flat_index, axis=1)]
    all_to_all x1 -> x2, starting transfers between devices: 49.6 us -> 14 us  [the longest x1 9.34 us: shards(): owned = lax.all_to_all(summed, 'chan', 0, 3, tiled=True)[0] / ntime]
    reshape x2 -> x0, local copies, waits for them, and re-layouts: 33.5 us -> none  [the longest x1 17.3 us: pair_spectra(): real_part.reshape(scale_count, -1)]
    reduce_sum x0 -> x2, other arithmetic: none -> 16.3 us  [the longest x1 13.1 us: pair_sums(): jnp.sum(first_real * second_real + first_imag * second_imag, axis=-1)]
    unnamed x21, local copies, waits for them, and re-layouts: 3.51 us -> 16 us
  transfers between devices with their start and end apart: 10 -> 10, of which waited for: 5 -> 5; matrix products, arithmetic and copies ran while one was open for 17% -> 57% of each run, Pallas kernels for 0% -> 0%
where the time goes in v1:
time: 320 us; the launch traced here: 321 us
  other arithmetic  192 us (60%)
  waiting for transfers between devices  39 us (12%)
  local copies, waits for them, and re-layouts  35.5 us (11%)
  starting transfers between devices  28.6 us (9%)
  matrix products  17.1 us (5%)
  blocking collectives  8.3 us (3%)
    convert_element_type x1, other arithmetic, morlet_parts(): return (real_part.astype(jnp.bfloat16), imag_part.astype(jnp.bfloat16))  158 us
    ppermute x8, waiting for transfers between devices, from_behind(): lax.ppermute(array, axis, [(i, (i + by) % peers) for i in range(peers)])  25.2 us
    unnamed x21, local copies, waits for them, and re-layouts  16 us
    ppermute x8, starting transfers between devices, from_behind(): lax.ppermute(array, axis, [(i, (i + by) % peers) for i in range(peers)])  14.6 us
    dot_general x1, matrix products, pair_sums(): jnp.einsum('pc,qrct->qrpt', pick, parts, preferred_element_type=jnp.float32)  13.2 us
    reduce_sum x1, other arithmetic, pair_sums(): jnp.sum(first_real * second_real + first_imag * second_imag, axis=-1)  13.1 us
    transpose x1, other arithmetic, wavelet_band(): kernel_table.transpose(2, 3, 0, 1, 4).reshape(tap_blocks * BLK, -1)  11.7 us
    all_to_all x1, waiting for transfers between devices, shards(): exchanged = lax.all_to_all(partial_value, 'tm', 0, 0, tiled=True)  11.3 us
  transfers between devices with their start and end apart: 10, of which 5 were waited for; matrix products, arithmetic and copies ran while one was open for 57% of the time, Pallas kernels for 0%

profile of v1, /device:TPU:1, one launch (start us, length us, event | category | flops | bytes accessed | tf_op | source)
XLA Modules:
  0.0 321.2 jit_solution(1249760158313348984)
XLA Ops:
  1.4 8.3 %all_gather.3 = bf16[256,128]{1,0:T(8,128)(2,1)S(1)} all-gather(bf16[64,128]{1,0:T(8,128)(2,1)S(1)} %convert_element_type.54), channel_id=1, replica_groups=mesh['tm'=64,'chan'=4] {'chan'}, dimensions={0}, use_global_device_ids=true | all-gather | bytes 81920 | tf_op jit(solution)/shard_map/all_gather | solution.py:91
  9.8 6.4 %collective-permute-start.7 = (bf16[256,128]{0,1:T(8,128)(2,1)S(1)}, bf16[256,128]{0,1:T(8,128)(2,1)S(1)}, u32[]{:S(2)}, u32[]{:S(2)}) collective-permute-start(bf16[256,128]{0,1:T(8,128)(2,1)S(1)} %copy.30), channel_id=1, source_target_pairs={{0,240},{4,244},{8,248},{12,252},{16,0},{20,4},{24,8},{28,12},{32,... | collective-permute-start | bytes 196616 | tf_op jit(solution)/shard_map/ppermute | solution.py:19
  16.2 1.2 collective-permute-start.6
  17.4 5.5 %collective-permute-start.5 = (bf16[256,128]{0,1:T(8,128)(2,1)S(1)}, bf16[256,128]{0,1:T(8,128)(2,1)S(1)}, u32[]{:S(2)}, u32[]{:S(2)}) collective-permute-start(bf16[256,128]{0,1:T(8,128)(2,1)S(1)} %copy.30), channel_id=1, source_target_pairs={{0,248},{4,252},{8,0},{12,4},{16,8},{20,12},{24,16},{28,20},{32,24... | collective-permute-start | bytes 196616 | tf_op jit(solution)/shard_map/ppermute | solution.py:19
  26.5 157.5 %fusion.2 = (bf16[8,1,9,128,128]{4,1,0,3,2:T(2,128)(2,1)S(1)}, bf16[8,1,9,128,128]{4,1,0,3,2:T(2,128)(2,1)S(1)}) fusion(s32[9,128,128]{2,1,0:T(8,128)S(1)} %get-tuple-element.15, s32[8]{0:T(128)S(1)} %broadcast_multiply_fusion, f32[8]{0:T(128)S(1)} %get-tuple-element.17, f32[9,128,128]{2,1,0:T(8,128)S(1)} %get-tuple-element.14, f32[8]{0:T(128)S(1)} %get-tuple-element.16), kind=kLoop, calls=%fused_computation.11 | loop fusion | flops 14155776 | bytes 5898336 | tf_op jit(solution)/shard_map/vmap()/convert_element_type | solution.py:31
  184.0 11.7 %maximum_bitcast_fusion = bf16[9,128,8,2,128]{4,3,2,1,0:T(2,128)(2,1)} fusion(bf16[8,1,9,128,128]{4,1,0,3,2:T(2,128)(2,1)S(1)} %get-tuple-element.13, bf16[8,1,9,128,128]{4,1,0,3,2:T(2,128)(2,1)S(1)} %get-tuple-element.12), kind=kLoop, calls=%fused_computation.13 | loop fusion | flops 9437184 | bytes 9437184 | tf_op jit(solution)/shard_map/transpose | solution.py:54
  195.7 8.9 %reshape.245 = bf16[1152,2048]{1,0:T(8,128)(2,1)} reshape(bf16[9,128,8,2,128]{4,3,2,1,0:T(2,128)(2,1)} %maximum_bitcast_fusion) | data formatting | bytes 9437184 | tf_op jit(solution)/shard_map/reshape | solution.py:54
  204.6 7.6 %collective-permute-done.1 = bf16[256,128]{0,1:T(8,128)(2,1)S(1)} collective-permute-done((bf16[256,128]{0,1:T(8,128)(2,1)S(1)}, bf16[256,128]{0,1:T(8,128)(2,1)S(1)}, u32[]{:S(2)}, u32[]{:S(2)}) %collective-permute-start.1) | collective-permute-done | bytes 65568 | tf_op jit(solution)/shard_map/ppermute | solution.py:19
  212.2 9.1 %collective-permute-done.2 = bf16[256,128]{0,1:T(8,128)(2,1)S(1)} collective-permute-done((bf16[256,128]{0,1:T(8,128)(2,1)S(1)}, bf16[256,128]{0,1:T(8,128)(2,1)S(1)}, u32[]{:S(2)}, u32[]{:S(2)}) %collective-permute-start.2) | collective-permute-done | bytes 65568 | tf_op jit(solution)/shard_map/ppermute | solution.py:19
  221.8 8.4 %collective-permute-done.3 = bf16[256,128]{0,1:T(8,128)(2,1)S(1)} collective-permute-done((bf16[256,128]{0,1:T(8,128)(2,1)S(1)}, bf16[256,128]{0,1:T(8,128)(2,1)S(1)}, u32[]{:S(2)}, u32[]{:S(2)}) %collective-permute-start.3) | collective-permute-done | bytes 65568 | tf_op jit(solution)/shard_map/ppermute | solution.py:19
  230.3 3.9 %convolution_convert_fusion = bf16[256,2048]{1,0:T(8,128)(2,1)S(1)} fusion(bf16[256,1152]{0,1:T(8,128)(2,1)S(1)} %bitcast.72, bf16[1152,2048]{1,0:T(8,128)(2,1)} %reshape.245), kind=kOutput, calls=%fused_computation.17 | convolution fusion | flops 1208483840 | bytes 6356992 | tf_op jit(solution)/shard_map/dot_general | solution.py:55
  234.7 13.2 %convert_bitcast_fusion = f32[8,2,4096,128]{2,3,1,0:T(8,128)} fusion(bf16[8,2,256,128]{2,3,1,0:T(8,128)(2,1)S(1)} %bitcast.66, s32[4096]{0:T(1024)S(1)} %pad_add_fusion), kind=kOutput, calls=%fused_computation.1 | convolution fusion | flops 4312793088 | bytes 34619392 | tf_op jit(solution)/shard_map/pc,qrct->qrpt/dot_general | solution.py:69
  247.9 13.1 %add_reduce_fusion.2 = (f32[8,2048]{1,0:T(8,128)S(1)}, f32[8,2048]{1,0:T(8,128)S(1)}, f32[8,2048]{1,0:T(8,128)S(1)}, f32[8,2048]{1,0:T(8,128)S(1)}) fusion(f32[8,2,4096,128]{2,3,1,0:T(8,128)} %convert_bitcast_fusion), kind=kLoop, calls=%fused_computation.7 | loop fusion | flops 33488896 | bytes 33816576 | tf_op jit(solution)/shard_map/reduce_sum | solution.py:76
  262.8 1.6 stack.67
  264.4 1.7 maximum_bitcast_fusion.1
  266.1 4.6 %copy.51 = f32[64,4,8,4,8]{2,1,4,3,0:T(4,128)} copy(f32[64,4,8,4,8]{2,0,1,4,3:T(8,128)S(1)} %maximum_bitcast_fusion.1) | data formatting | bytes 524288 | tf_op jit(solution)/shard_map/transpose | solution.py:106
  270.7 6.9 %reshape.258 = f32[64,1,1024]{2,1,0:T(1,128)} reshape(f32[64,4,8,4,8]{4,3,2,1,0:T(4,128)} %bitcast.65) | data formatting | bytes 524288
  277.6 4.6 %all-to-all-start = ((f32[64,1,1024]{2,1,0:T(1,128)}), f32[64,1,1024]{2,1,0:T(1,128)S(1)}, u32[]{:S(2)}, u32[]{:S(2)}) async-start(f32[64,1,1024]{2,1,0:T(1,128)} %reshape.258), calls=%async_computation | async-start | bytes 524288 | tf_op jit(solution)/shard_map/all_to_all | solution.py:107
  282.9 11.3 %all-to-all-done = f32[64,1,1024]{2,1,0:T(1,128)S(1)} async-done(((f32[64,1,1024]{2,1,0:T(1,128)}), f32[64,1,1024]{2,1,0:T(1,128)S(1)}, u32[]{:S(2)}, u32[]{:S(2)}) %all-to-all-start) | async-done | bytes 262176 | tf_op jit(solution)/shard_map/all_to_all | solution.py:107
  294.6 1.3 reduce.4
  295.9 6.3 %reshape.259 = f32[64,4,8,4,8]{4,3,2,1,0:T(4,128)} reshape(f32[64,1024]{1,0:T(8,128)S(1)} %reduce.4) | data formatting | bytes 524288
  302.2 3.2 %bitcast_reduce_fusion = f32[4,8,4,8]{1,0,3,2:T(4,128)S(1)} fusion(f32[64,4,8,4,8]{4,3,2,1,0:T(4,128)} %reshape.259), kind=kLoop, calls=%fused_computation.54 | loop fusion | flops 64512 | bytes 266240 | tf_op jit(solution)/shard_map/reduce_sum | solution.py:108
  306.2 9.3 %all-to-all-start.1 = ((f32[4,1,256]{2,1,0:T(1,128)}), f32[4,1,256]{2,1,0:T(1,128)S(1)}, u32[]{:S(2)}, u32[]{:S(2)}) async-start(f32[4,1,256]{2,1,0:T(1,128)} %reshape.260), calls=%async_computation.1 | async-start | bytes 8192 | tf_op jit(solution)/shard_map/all_to_all | solution.py:109
  316.2 2.5 all-to-all-done.1
  (55 shorter events, 11.8 us)
Async XLA Ops:
  0.6 23.5 %copy-start = (s32[32]{0:T(128)S(1)}, s32[32]{0:T(128)}, u32[]{:S(2)}) copy-start(s32[32]{0:T(128)} %param.6) | copy-start | bytes 388
  9.8 220.5 %collective-permute-start.7 = (bf16[256,128]{0,1:T(8,128)(2,1)S(1)}, bf16[256,128]{0,1:T(8,128)(2,1)S(1)}, u32[]{:S(2)}, u32[]{:S(2)}) collective-permute-start(bf16[256,128]{0,1:T(8,128)(2,1)S(1)} %copy.30), channel_id=1, source_target_pairs={{0,240},{4,244},{8,248},{12,252},{16,0},{20,4},{24,8},{28,12},{32,... | collective-permute-start | bytes 196616 | tf_op jit(solution)/shard_map/ppermute | solution.py:19
  16.2 214.1 %collective-permute-start.6 = (bf16[256,128]{0,1:T(8,128)(2,1)S(1)}, bf16[256,128]{0,1:T(8,128)(2,1)S(1)}, u32[]{:S(2)}, u32[]{:S(2)}) collective-permute-start(bf16[256,128]{0,1:T(8,128)(2,1)S(1)} %copy.30), channel_id=1, source_target_pairs={{0,244},{4,248},{8,252},{12,0},{16,4},{20,8},{24,12},{28,16},{32,2... | collective-permute-start | bytes 196616 | tf_op jit(solution)/shard_map/ppermute | solution.py:19
  17.4 212.8 %collective-permute-start.5 = (bf16[256,128]{0,1:T(8,128)(2,1)S(1)}, bf16[256,128]{0,1:T(8,128)(2,1)S(1)}, u32[]{:S(2)}, u32[]{:S(2)}) collective-permute-start(bf16[256,128]{0,1:T(8,128)(2,1)S(1)} %copy.30), channel_id=1, source_target_pairs={{0,248},{4,252},{8,0},{12,4},{16,8},{20,12},{24,16},{28,20},{32,24... | collective-permute-start | bytes 196616 | tf_op jit(solution)/shard_map/ppermute | solution.py:19
  23.0 207.2 %collective-permute-start.4 = (bf16[256,128]{0,1:T(8,128)(2,1)S(1)}, bf16[256,128]{0,1:T(8,128)(2,1)S(1)}, u32[]{:S(2)}, u32[]{:S(2)}) collective-permute-start(bf16[256,128]{0,1:T(8,128)(2,1)S(1)} %copy.30), channel_id=1, source_target_pairs={{0,252},{4,0},{8,4},{12,8},{16,12},{20,16},{24,20},{28,24},{32,28}... | collective-permute-start | bytes 196616 | tf_op jit(solution)/shard_map/ppermute | solution.py:19
  24.0 180.6 %collective-permute-start = (bf16[256,128]{0,1:T(8,128)(2,1)S(1)}, bf16[256,128]{0,1:T(8,128)(2,1)S(1)}, u32[]{:S(2)}, u32[]{:S(2)}) collective-permute-start(bf16[256,128]{0,1:T(8,128)(2,1)S(1)} %copy.30), channel_id=1, source_target_pairs={{0,16},{4,20},{8,24},{12,28},{16,32},{20,36},{24,40},{28,44},{32,4... | collective-permute-start | bytes 196616 | tf_op jit(solution)/shard_map/ppermute | solution.py:19
  204.6 7.6 %collective-permute-start.1 = (bf16[256,128]{0,1:T(8,128)(2,1)S(1)}, bf16[256,128]{0,1:T(8,128)(2,1)S(1)}, u32[]{:S(2)}, u32[]{:S(2)}) collective-permute-start(bf16[256,128]{0,1:T(8,128)(2,1)S(1)} %copy.30), channel_id=1, source_target_pairs={{0,12},{4,16},{8,20},{12,24},{16,28},{20,32},{24,36},{28,40},{32,4... | collective-permute-start | bytes 196616 | tf_op jit(solution)/shard_map/ppermute | solution.py:19
  212.2 9.1 %collective-permute-start.2 = (bf16[256,128]{0,1:T(8,128)(2,1)S(1)}, bf16[256,128]{0,1:T(8,128)(2,1)S(1)}, u32[]{:S(2)}, u32[]{:S(2)}) collective-permute-start(bf16[256,128]{0,1:T(8,128)(2,1)S(1)} %copy.30), channel_id=1, source_target_pairs={{0,8},{4,12},{8,16},{12,20},{16,24},{20,28},{24,32},{28,36},{32,40... | collective-permute-start | bytes 196616 | tf_op jit(solution)/shard_map/ppermute | solution.py:19
  221.4 8.8 %collective-permute-start.3 = (bf16[256,128]{0,1:T(8,128)(2,1)S(1)}, bf16[256,128]{0,1:T(8,128)(2,1)S(1)}, u32[]{:S(2)}, u32[]{:S(2)}) collective-permute-start(bf16[256,128]{0,1:T(8,128)(2,1)S(1)} %copy.30), channel_id=1, source_target_pairs={{0,4},{4,8},{8,12},{12,16},{16,20},{20,24},{24,28},{28,32},{32,36}... | collective-permute-start | bytes 196616 | tf_op jit(solution)/shard_map/ppermute | solution.py:19
  266.1 16.2 %copy-start.2 = (s32[4]{0:T(128)S(1)}, s32[4]{0:T(128)}, u32[]{:S(2)}) copy-start(s32[4]{0:T(128)} %param.9) | copy-start | bytes 52
  277.6 16.5 %all-to-all-start = ((f32[64,1,1024]{2,1,0:T(1,128)}), f32[64,1,1024]{2,1,0:T(1,128)S(1)}, u32[]{:S(2)}, u32[]{:S(2)}) async-start(f32[64,1,1024]{2,1,0:T(1,128)} %reshape.258), calls=%async_computation | async-start | bytes 524288 | tf_op jit(solution)/shard_map/all_to_all | solution.py:107
  294.6 26.3 %copy-start.1 = (s32[32]{0:T(128)S(1)}, s32[32]{0:T(128)}, u32[]{:S(2)}) copy-start(s32[32]{0:T(128)} %param.6) | copy-start | bytes 388
  306.2 12.4 %all-to-all-start.1 = ((f32[4,1,256]{2,1,0:T(1,128)}), f32[4,1,256]{2,1,0:T(1,128)S(1)}, u32[]{:S(2)}, u32[]{:S(2)}) async-start(f32[4,1,256]{2,1,0:T(1,128)} %reshape.260), calls=%async_computation.1 | async-start | bytes 8192 | tf_op jit(solution)/shard_map/all_to_all | solution.py:109

commit v2 on v1

--- a/solution.py
+++ b/solution.py
@@ -19,16 +19,31 @@
     return lax.ppermute(array, axis, [(i, (i + by) % peers) for i in range(peers)])
 
 
-def morlet_parts(offset, scale_index, reach_blocks):
-    scale_width = 2.0 * TD * jnp.exp2((scale_index - (NS - 1)).astype(jnp.float32) / 4.0)
-    scaled_offset = offset.astype(jnp.float32) / scale_width
+def kernel_table(scale_ids, reaches, offsets):
+    taps = (2 * offsets + 1) * BLK
+    lag = jnp.arange(taps, dtype=jnp.int32) - offsets * BLK
+    within = jnp.arange(BLK, dtype=jnp.int32)
+    scale_width = 2.0 * TD * jnp.exp2((scale_ids - (NS - 1)).astype(jnp.float32) / 4.0)
+    offset = lag[:, None, None] - within[None, None, :]
+    scaled_offset = offset.astype(jnp.float32) / scale_width[None, :, None]
     amplitude = (
-        math.pi ** (-0.25) * lax.rsqrt(scale_width) * jnp.exp(-0.5 * scaled_offset * scaled_offset)
+        math.pi ** (-0.25)
+        * lax.rsqrt(scale_width)[None, :, None]
+        * jnp.exp(-0.5 * scaled_offset * scaled_offset)
     )
-    inside = jnp.abs(offset) < reach_blocks * BLK
-    real_part = jnp.where(inside, amplitude * jnp.cos(6.0 * scaled_offset), 0.0)
-    imag_part = jnp.where(inside, amplitude * jnp.sin(6.0 * scaled_offset), 0.0)
-    return (real_part.astype(jnp.bfloat16), imag_part.astype(jnp.bfloat16))
+    inside = jnp.abs(offset) < (reaches * BLK)[None, :, None]
+    lag_phase = 6.0 * (lag.astype(jnp.float32)[:, None] / scale_width[None, :])
+    time_phase = 6.0 * (within.astype(jnp.float32)[None, :] / scale_width[:, None])
+    lag_cos = jnp.cos(lag_phase)[:, :, None]
+    lag_sin = jnp.sin(lag_phase)[:, :, None]
+    time_cos = jnp.cos(time_phase)[None]
+    time_sin = jnp.sin(time_phase)[None]
+    cos_part = lag_cos * time_cos + lag_sin * time_sin
+    sin_part = lag_sin * time_cos - lag_cos * time_sin
+    real_part = jnp.where(inside, amplitude * cos_part, 0.0).astype(jnp.bfloat16)
+    imag_part = jnp.where(inside, amplitude * sin_part, 0.0).astype(jnp.bfloat16)
+    table = jnp.stack([real_part, imag_part], axis=2)
+    return table.reshape(taps, -1)
 
 
 def wavelet_band(extended, scale_ids, reaches, offsets, time_span):
@@ -42,17 +57,8 @@
     ]
     unfolded = jnp.stack(pieces, axis=1).reshape(channels, tap_blocks, blocks, BLK)
     unfolded = unfolded.transpose(0, 2, 1, 3).reshape(channels * blocks, tap_blocks * BLK)
-    lag_start = (jnp.arange(tap_blocks, dtype=jnp.int32) - offsets) * BLK
-    within = jnp.arange(BLK, dtype=jnp.int32)
-    tap_offset = lag_start[:, None, None] + within[None, :, None] - within[None, None, :]
-
-    def single_scale(scale_index, reach_blocks):
-        return morlet_parts(tap_offset, scale_index, reach_blocks)
-
-    real_part, imag_part = jax.vmap(single_scale)(scale_ids, reaches)
-    kernel_table = jnp.stack([real_part, imag_part], axis=1)
-    kernel_table = kernel_table.transpose(2, 3, 0, 1, 4).reshape(tap_blocks * BLK, -1)
-    coefficients = jnp.dot(unfolded, kernel_table, preferred_element_type=jnp.float32)
+    table = kernel_table(scale_ids, reaches, offsets)
+    coefficients = jnp.dot(unfolded, table, preferred_element_type=jnp.float32)
     scale_count = scale_ids.shape[0]
     coefficients = coefficients.astype(jnp.bfloat16).reshape(channels, blocks, scale_count, 2, BLK)
     return coefficients.transpose(2, 3, 0, 1, 4).reshape(scale_count, 2 * channels, time_span)

time: 320 us -> 148 us (0.46)
  other arithmetic: 192 us -> 27.3 us
  local copies, waits for them, and re-layouts: 35.5 us -> 29 us
    convert_element_type x2 -> x4, other arithmetic: 158 us -> 3.47 us  [the longest x1 3.35 us: kernel_table(): jnp.where(inside, amplitude * cos_part, 0.0).astype(jnp.bfloat16)]
    transpose x1 -> x0, other arithmetic: 11.7 us -> none  [wavelet_band(): kernel_table.transpose(2, 3, 0, 1, 4).reshape(tap_blocks * BLK, -1)]
    reshape x1 -> x0, local copies, waits for them, and re-layouts: 8.88 us -> none  [wavelet_band(): kernel_table.transpose(2, 3, 0, 1, 4).reshape(tap_blocks * BLK, -1)]
  transfers between devices with their start and end apart: 10 -> 10, of which waited for: 5 -> 5; matrix products, arithmetic and copies ran while one was open for 57% -> 7% of each run, Pallas kernels for 0% -> 0%
where the time goes in v2:
time: 148 us
  waiting for transfers between devices  38.8 us (26%)
  local copies, waits for them, and re-layouts  29 us (20%)
  starting transfers between devices  28.6 us (19%)
  other arithmetic  27.3 us (18%)
  matrix products  14.9 us (10%)
  blocking collectives  8.3 us (6%)
    ppermute x8, waiting for transfers between devices, from_behind(): lax.ppermute(array, axis, [(i, (i + by) % peers) for i in range(peers)])  25.2 us
    unnamed x21, local copies, waits for them, and re-layouts  16 us
    ppermute x8, starting transfers between devices, from_behind(): lax.ppermute(array, axis, [(i, (i + by) % peers) for i in range(peers)])  14.7 us
    dot_general x1, matrix products, pair_sums(): jnp.einsum('pc,qrct->qrpt', pick, parts, preferred_element_type=jnp.float32)  13.3 us
    reduce_sum x1, other arithmetic, pair_sums(): jnp.sum(first_real * second_real + first_imag * second_imag, axis=-1)  13.1 us
    all_to_all x1, waiting for transfers between devices, shards(): exchanged = lax.all_to_all(partial_value, 'tm', 0, 0, tiled=True)  11.2 us
    all_to_all x1, starting transfers between devices, shards(): owned = lax.all_to_all(summed, 'chan', 0, 3, tiled=True)[0] / ntime  9.34 us
    all_gather x1, blocking collectives, shards(): gathered = lax.all_gather(rounded, 'chan', axis=0, tiled=True)  8.3 us
  transfers between devices with their start and end apart: 10, of which 5 were waited for; matrix products, arithmetic and copies ran while one was open for 7% of the time, Pallas kernels for 0%

profile of v2, /device:TPU:1, one launch (start us, length us, event | category | flops | bytes accessed | tf_op | source)
XLA Modules:
  0.0 147.9 jit_solution(1848543269090394793)
XLA Ops:
  1.4 8.3 %all_gather.3 = bf16[256,128]{1,0:T(8,128)(2,1)S(1)} all-gather(bf16[64,128]{1,0:T(8,128)(2,1)S(1)} %convert_element_type.77), channel_id=1, replica_groups=mesh['tm'=64,'chan'=4] {'chan'}, dimensions={0}, use_global_device_ids=true | all-gather | bytes 81920 | tf_op jit(solution)/shard_map/all_gather | solution.py:97
  9.8 6.4 %collective-permute-start.7 = (bf16[256,128]{0,1:T(8,128)(2,1)S(1)}, bf16[256,128]{0,1:T(8,128)(2,1)S(1)}, u32[]{:S(2)}, u32[]{:S(2)}) collective-permute-start(bf16[256,128]{0,1:T(8,128)(2,1)S(1)} %copy.45), channel_id=1, source_target_pairs={{0,240},{4,244},{8,248},{12,252},{16,0},{20,4},{24,8},{28,12},{32,... | collective-permute-start | bytes 196616 | tf_op jit(solution)/shard_map/ppermute | solution.py:19
  16.2 1.2 collective-permute-start.6
  17.4 5.5 %collective-permute-start.5 = (bf16[256,128]{0,1:T(8,128)(2,1)S(1)}, bf16[256,128]{0,1:T(8,128)(2,1)S(1)}, u32[]{:S(2)}, u32[]{:S(2)}) collective-permute-start(bf16[256,128]{0,1:T(8,128)(2,1)S(1)} %copy.45), channel_id=1, source_target_pairs={{0,248},{4,252},{8,0},{12,4},{16,8},{20,12},{24,16},{28,20},{32,24... | collective-permute-start | bytes 196616 | tf_op jit(solution)/shard_map/ppermute | solution.py:19
  23.0 1.1 collective-permute-start.4
  27.7 2.1 %copy.55 = pred[1152,8,1,128]{0,3,2,1:T(8,128)(4,1)S(1)} copy(pred[1152,8,1,128]{3,1,2,0:T(8,128)(4,1)S(1)} %broadcast_compare_fusion) | data formatting | bytes 2359296 | tf_op jit(solution)/shard_map/lt | solution.py:34
  29.8 3.4 %select_convert_fusion.1 = (bf16[1152,8,1,128]{0,3,2,1:T(8,128)(2,1)S(1)}, bf16[1152,8,1,128]{0,3,2,1:T(8,128)(2,1)S(1)}) fusion(pred[1152,8,1,128]{0,3,2,1:T(8,128)(4,1)S(1)} %copy.55, f32[8,128]{1,0:T(8,128)S(1)} %get-tuple-element.21, f32[1152,8]{0,1:T(8,128)S(1)} %get-tuple-element.17, f32[8,128]{1,0:T(8,128)S(1)} %get-tuple-element.20, ...), kind=kLoop, calls=%fused_computation.11 | loop fusion | flops 18874368 | bytes 6570048 | tf_op jit(solution)/shard_map/convert_element_type | solution.py:43
  33.7 7.6 %collective-permute-done.1 = bf16[256,128]{0,1:T(8,128)(2,1)S(1)} collective-permute-done((bf16[256,128]{0,1:T(8,128)(2,1)S(1)}, bf16[256,128]{0,1:T(8,128)(2,1)S(1)}, u32[]{:S(2)}, u32[]{:S(2)}) %collective-permute-start.1) | collective-permute-done | bytes 65568 | tf_op jit(solution)/shard_map/ppermute | solution.py:19
  41.4 9.1 %collective-permute-done.2 = bf16[256,128]{0,1:T(8,128)(2,1)S(1)} collective-permute-done((bf16[256,128]{0,1:T(8,128)(2,1)S(1)}, bf16[256,128]{0,1:T(8,128)(2,1)S(1)}, u32[]{:S(2)}, u32[]{:S(2)}) %collective-permute-start.2) | collective-permute-done | bytes 65568 | tf_op jit(solution)/shard_map/ppermute | solution.py:19
  50.9 8.4 %collective-permute-done.3 = bf16[256,128]{0,1:T(8,128)(2,1)S(1)} collective-permute-done((bf16[256,128]{0,1:T(8,128)(2,1)S(1)}, bf16[256,128]{0,1:T(8,128)(2,1)S(1)}, u32[]{:S(2)}, u32[]{:S(2)}) %collective-permute-start.3) | collective-permute-done | bytes 65568 | tf_op jit(solution)/shard_map/ppermute | solution.py:19
  59.4 1.6 %convolution_convert_fusion = bf16[256,2048]{1,0:T(8,128)(2,1)S(1)} fusion(bf16[256,1152]{0,1:T(8,128)(2,1)S(1)} %bitcast.72, bf16[1152,2048]{0,1:T(8,128)(2,1)S(1)} %bitcast.65), kind=kOutput, calls=%fused_computation.15 | convolution fusion | flops 1208483840 | bytes 6356992 | tf_op jit(solution)/shard_map/dot_general | solution.py:61
  61.6 13.3 %convert_bitcast_fusion = f32[8,2,4096,128]{2,3,1,0:T(8,128)} fusion(bf16[8,2,256,128]{2,3,1,0:T(8,128)(2,1)S(1)} %bitcast.66, s32[4096]{0:T(1024)S(1)} %pad_add_fusion), kind=kOutput, calls=%fused_computation.1 | convolution fusion | flops 4312793088 | bytes 34619392 | tf_op jit(solution)/shard_map/pc,qrct->qrpt/dot_general | solution.py:75
  74.9 13.1 %add_reduce_fusion.2 = (f32[8,2048]{1,0:T(8,128)S(1)}, f32[8,2048]{1,0:T(8,128)S(1)}, f32[8,2048]{1,0:T(8,128)S(1)}, f32[8,2048]{1,0:T(8,128)S(1)}) fusion(f32[8,2,4096,128]{2,3,1,0:T(8,128)} %convert_bitcast_fusion), kind=kLoop, calls=%fused_computation.5 | loop fusion | flops 33488896 | bytes 33816576 | tf_op jit(solution)/shard_map/reduce_sum | solution.py:82
  89.7 1.6 %stack.67 = f32[8,1,4,64,8]{4,3,2,0,1:T(8,128)} reshape(f32[8,2048]{1,0:T(8,128)S(1)} %get-tuple-element.13) | data formatting | bytes 131072 | tf_op jit(solution)/shard_map/stack | solution.py:86
  91.3 1.7 %maximum_bitcast_fusion = f32[64,4,8,4,8]{2,0,1,4,3:T(8,128)S(1)} fusion(f32[8,1,4,64,8]{4,3,2,0,1:T(8,128)} %stack.67, f32[8,1,4,64,8]{4,3,2,0,1:T(8,128)S(1)} %stack.66, f32[8,1,4,64,8]{4,3,2,0,1:T(8,128)S(1)} %stack.65, f32[8,1,4,64,8]{4,3,2,0,1:T(8,128)S(1)} %stack.64), kind=kLoop, calls=%fused_computation.12 | loop fusion | flops 196608 | bytes 524288 | tf_op jit(solution)/shard_map/transpose | solution.py:112
  93.0 4.6 %copy.69 = f32[64,4,8,4,8]{2,1,4,3,0:T(4,128)} copy(f32[64,4,8,4,8]{2,0,1,4,3:T(8,128)S(1)} %maximum_bitcast_fusion) | data formatting | bytes 524288 | tf_op jit(solution)/shard_map/transpose | solution.py:112
  97.7 6.9 %reshape.416 = f32[64,1,1024]{2,1,0:T(1,128)} reshape(f32[64,4,8,4,8]{4,3,2,1,0:T(4,128)} %bitcast.64) | data formatting | bytes 524288
  104.6 4.6 %all-to-all-start = ((f32[64,1,1024]{2,1,0:T(1,128)}), f32[64,1,1024]{2,1,0:T(1,128)S(1)}, u32[]{:S(2)}, u32[]{:S(2)}) async-start(f32[64,1,1024]{2,1,0:T(1,128)} %reshape.416), calls=%async_computation | async-start | bytes 524288 | tf_op jit(solution)/shard_map/all_to_all | solution.py:113
  109.9 11.2 %all-to-all-done = f32[64,1,1024]{2,1,0:T(1,128)S(1)} async-done(((f32[64,1,1024]{2,1,0:T(1,128)}), f32[64,1,1024]{2,1,0:T(1,128)S(1)}, u32[]{:S(2)}, u32[]{:S(2)}) %all-to-all-start) | async-done | bytes 262176 | tf_op jit(solution)/shard_map/all_to_all | solution.py:113
  121.6 1.3 reduce.4
  122.8 6.3 %reshape.417 = f32[64,4,8,4,8]{4,3,2,1,0:T(4,128)} reshape(f32[64,1024]{1,0:T(8,128)S(1)} %reduce.4) | data formatting | bytes 524288
  129.1 3.2 %bitcast_reduce_fusion = f32[4,8,4,8]{1,0,3,2:T(4,128)S(1)} fusion(f32[64,4,8,4,8]{4,3,2,1,0:T(4,128)} %reshape.417), kind=kLoop, calls=%fused_computation.59 | loop fusion | flops 64512 | bytes 266240 | tf_op jit(solution)/shard_map/reduce_sum | solution.py:114
  133.2 9.3 %all-to-all-start.1 = ((f32[4,1,256]{2,1,0:T(1,128)}), f32[4,1,256]{2,1,0:T(1,128)S(1)}, u32[]{:S(2)}, u32[]{:S(2)}) async-start(f32[4,1,256]{2,1,0:T(1,128)} %reshape.418), calls=%async_computation.1 | async-start | bytes 8192 | tf_op jit(solution)/shard_map/all_to_all | solution.py:115
  143.2 2.4 %all-to-all-done.1 = f32[4,1,256]{2,1,0:T(1,128)S(1)} async-done(((f32[4,1,256]{2,1,0:T(1,128)}), f32[4,1,256]{2,1,0:T(1,128)S(1)}, u32[]{:S(2)}, u32[]{:S(2)}) %all-to-all-start.1) | async-done | bytes 4128 | tf_op jit(solution)/shard_map/all_to_all | solution.py:115
  (60 shorter events, 12.7 us)
Async XLA Ops:
  0.6 23.5 %copy-start = (s32[32]{0:T(128)S(1)}, s32[32]{0:T(128)}, u32[]{:S(2)}) copy-start(s32[32]{0:T(128)} %param.6) | copy-start | bytes 388
  9.8 49.6 %collective-permute-start.7 = (bf16[256,128]{0,1:T(8,128)(2,1)S(1)}, bf16[256,128]{0,1:T(8,128)(2,1)S(1)}, u32[]{:S(2)}, u32[]{:S(2)}) collective-permute-start(bf16[256,128]{0,1:T(8,128)(2,1)S(1)} %copy.45), channel_id=1, source_target_pairs={{0,240},{4,244},{8,248},{12,252},{16,0},{20,4},{24,8},{28,12},{32,... | collective-permute-start | bytes 196616 | tf_op jit(solution)/shard_map/ppermute | solution.py:19
  16.2 43.2 %collective-permute-start.6 = (bf16[256,128]{0,1:T(8,128)(2,1)S(1)}, bf16[256,128]{0,1:T(8,128)(2,1)S(1)}, u32[]{:S(2)}, u32[]{:S(2)}) collective-permute-start(bf16[256,128]{0,1:T(8,128)(2,1)S(1)} %copy.45), channel_id=1, source_target_pairs={{0,244},{4,248},{8,252},{12,0},{16,4},{20,8},{24,12},{28,16},{32,2... | collective-permute-start | bytes 196616 | tf_op jit(solution)/shard_map/ppermute | solution.py:19
  17.4 41.9 %collective-permute-start.5 = (bf16[256,128]{0,1:T(8,128)(2,1)S(1)}, bf16[256,128]{0,1:T(8,128)(2,1)S(1)}, u32[]{:S(2)}, u32[]{:S(2)}) collective-permute-start(bf16[256,128]{0,1:T(8,128)(2,1)S(1)} %copy.45), channel_id=1, source_target_pairs={{0,248},{4,252},{8,0},{12,4},{16,8},{20,12},{24,16},{28,20},{32,24... | collective-permute-start | bytes 196616 | tf_op jit(solution)/shard_map/ppermute | solution.py:19
  23.0 36.4 %collective-permute-start.4 = (bf16[256,128]{0,1:T(8,128)(2,1)S(1)}, bf16[256,128]{0,1:T(8,128)(2,1)S(1)}, u32[]{:S(2)}, u32[]{:S(2)}) collective-permute-start(bf16[256,128]{0,1:T(8,128)(2,1)S(1)} %copy.45), channel_id=1, source_target_pairs={{0,252},{4,0},{8,4},{12,8},{16,12},{20,16},{24,20},{28,24},{32,28}... | collective-permute-start | bytes 196616 | tf_op jit(solution)/shard_map/ppermute | solution.py:19
  24.0 9.6 %collective-permute-start = (bf16[256,128]{0,1:T(8,128)(2,1)S(1)}, bf16[256,128]{0,1:T(8,128)(2,1)S(1)}, u32[]{:S(2)}, u32[]{:S(2)}) collective-permute-start(bf16[256,128]{0,1:T(8,128)(2,1)S(1)} %copy.45), channel_id=1, source_target_pairs={{0,16},{4,20},{8,24},{12,28},{16,32},{20,36},{24,40},{28,44},{32,4... | collective-permute-start | bytes 196616 | tf_op jit(solution)/shard_map/ppermute | solution.py:19
  33.6 7.7 %collective-permute-start.1 = (bf16[256,128]{0,1:T(8,128)(2,1)S(1)}, bf16[256,128]{0,1:T(8,128)(2,1)S(1)}, u32[]{:S(2)}, u32[]{:S(2)}) collective-permute-start(bf16[256,128]{0,1:T(8,128)(2,1)S(1)} %copy.45), channel_id=1, source_target_pairs={{0,12},{4,16},{8,20},{12,24},{16,28},{20,32},{24,36},{28,40},{32,4... | collective-permute-start | bytes 196616 | tf_op jit(solution)/shard_map/ppermute | solution.py:19
  41.4 9.1 %collective-permute-start.2 = (bf16[256,128]{0,1:T(8,128)(2,1)S(1)}, bf16[256,128]{0,1:T(8,128)(2,1)S(1)}, u32[]{:S(2)}, u32[]{:S(2)}) collective-permute-start(bf16[256,128]{0,1:T(8,128)(2,1)S(1)} %copy.45), channel_id=1, source_target_pairs={{0,8},{4,12},{8,16},{12,20},{16,24},{20,28},{24,32},{28,36},{32,40... | collective-permute-start | bytes 196616 | tf_op jit(solution)/shard_map/ppermute | solution.py:19
  50.5 8.8 %collective-permute-start.3 = (bf16[256,128]{0,1:T(8,128)(2,1)S(1)}, bf16[256,128]{0,1:T(8,128)(2,1)S(1)}, u32[]{:S(2)}, u32[]{:S(2)}) collective-permute-start(bf16[256,128]{0,1:T(8,128)(2,1)S(1)} %copy.45), channel_id=1, source_target_pairs={{0,4},{4,8},{8,12},{12,16},{16,20},{20,24},{24,28},{28,32},{32,36}... | collective-permute-start | bytes 196616 | tf_op jit(solution)/shard_map/ppermute | solution.py:19
  93.0 16.2 %copy-start.2 = (s32[4]{0:T(128)S(1)}, s32[4]{0:T(128)}, u32[]{:S(2)}) copy-start(s32[4]{0:T(128)} %param.9) | copy-start | bytes 52
  104.6 16.5 %all-to-all-start = ((f32[64,1,1024]{2,1,0:T(1,128)}), f32[64,1,1024]{2,1,0:T(1,128)S(1)}, u32[]{:S(2)}, u32[]{:S(2)}) async-start(f32[64,1,1024]{2,1,0:T(1,128)} %reshape.416), calls=%async_computation | async-start | bytes 524288 | tf_op jit(solution)/shard_map/all_to_all | solution.py:113
  121.6 26.3 %copy-start.1 = (s32[32]{0:T(128)S(1)}, s32[32]{0:T(128)}, u32[]{:S(2)}) copy-start(s32[32]{0:T(128)} %param.6) | copy-start | bytes 388
  133.2 12.4 %all-to-all-start.1 = ((f32[4,1,256]{2,1,0:T(1,128)}), f32[4,1,256]{2,1,0:T(1,128)S(1)}, u32[]{:S(2)}, u32[]{:S(2)}) async-start(f32[4,1,256]{2,1,0:T(1,128)} %reshape.418), calls=%async_computation.1 | async-start | bytes 8192 | tf_op jit(solution)/shard_map/all_to_all | solution.py:115

commit v3 on v2

--- a/solution.py
+++ b/solution.py
@@ -94,25 +94,28 @@
     time_span = signal.shape[1]
     ntime = time_span * time_devices
     rounded = signal.astype(jnp.bfloat16)
-    gathered = lax.all_gather(rounded, "chan", axis=0, tiled=True)
-    neighbours = [
-        from_behind(gathered, "tm", distance) for distance in (4, 3, 2, 1, -1, -2, -3, -4)
-    ]
-    extended = jnp.concatenate(neighbours[:4] + [gathered] + neighbours[4:], axis=1)
+    near = jnp.concatenate(
+        [from_behind(rounded, "tm", 1), rounded, from_behind(rounded, "tm", -1)], axis=1
+    )
+    wide = jnp.concatenate([from_behind(near, "tm", 3), near, from_behind(near, "tm", -3)], axis=1)
+    extended = lax.all_gather(wide, "chan", axis=0, tiled=True)
     per_group = NS // groups
     scale_ids = cluster_number * per_group + jnp.arange(per_group, dtype=jnp.int32)
     coefficients = wavelet_band(
         extended, scale_ids, support[scale_ids], 4 * time_span // BLK, time_span
     )
     owner_devices, slots_total = pair_first.shape
-    sums = pair_sums(coefficients, pair_first.reshape(-1), pair_second.reshape(-1))
     slots_local = slots_total // time_devices
+
+    def by_block(pairs):
+        return pairs.reshape(owner_devices, time_devices, slots_local).transpose(1, 0, 2).reshape(-1)
+
+    sums = pair_sums(coefficients, by_block(pair_first), by_block(pair_second))
     values = sums.shape[1]
-    partial_value = sums.reshape(per_group, values, owner_devices, time_devices, slots_local)
-    partial_value = partial_value.transpose(3, 2, 4, 1, 0)
+    partial_value = sums.transpose(2, 0, 1).reshape(time_devices, -1)
     exchanged = lax.all_to_all(partial_value, "tm", 0, 0, tiled=True)
-    summed = jnp.sum(exchanged, axis=0)
-    owned = lax.all_to_all(summed, "chan", 0, 3, tiled=True)[0] / ntime
+    summed = jnp.sum(exchanged, axis=0).reshape(owner_devices, slots_local, per_group, values)
+    owned = lax.all_to_all(summed, "chan", 0, 2, tiled=True)[0].transpose(0, 2, 1) / ntime
     slot_index = time_index * slots_local + jnp.arange(slots_local, dtype=jnp.int32)
     alive_mask = slot_index < pair_count[cluster_number]
     cross_real = owned[:, 0, :]

time: 148 us -> 122 us (0.82)
  waiting for transfers between devices: 38.8 us -> 15.7 us
  local copies, waits for them, and re-layouts: 29 us -> 22.3 us
  starting transfers between devices: 28.6 us -> 33.2 us
  other arithmetic: 27.3 us -> 23.4 us
  matrix products: 14.9 us -> 17.2 us
    ppermute x8 -> x4, waiting for transfers between devices: 25.2 us -> 1.48 us  [from_behind(): lax.ppermute(array, axis, [(i, (i + by) % peers) for i in range(peers)])]
    unnamed x21 -> x33, local copies, waits for them, and re-layouts: 16 us -> 2.49 us
    all_to_all x1, local copies, waits for them, and re-layouts: 0.51 us -> 9.09 us  [shards(): exchanged = lax.all_to_all(partial_value, 'tm', 0, 0, tiled=True)]
    all_to_all x1, starting transfers between devices: 4.61 us -> 10.4 us  [shards(): exchanged = lax.all_to_all(partial_value, 'tm', 0, 0, tiled=True)]
    all_to_all x1, starting transfers between devices: 9.34 us -> 5.38 us  [shards(): lax.all_to_all(summed, 'chan', 0, 2, tiled=True)[0].transpose(0, 2, 1)]
    another operation x4 -> x0, local copies, waits for them, and re-layouts: 3.33 us -> none  [pair_sums(): jnp.stack([cross_real, cross_imag, power_first, power_second], axis=1)]
    reduce_sum x1, other arithmetic: 3.25 us -> 0.18 us  [shards(): jnp.sum(exchanged, axis=0)]
    ppermute x8 -> x4, starting transfers between devices: 14.7 us -> 17.4 us  [from_behind(): lax.ppermute(array, axis, [(i, (i + by) % peers) for i in range(peers)])]
  transfers between devices with their start and end apart: 10 -> 6, of which waited for: 5 -> 3; matrix products, arithmetic and copies ran while one was open for 7% -> 10% of each run, Pallas kernels for 0% -> 0%
where the time goes in v3:
time: 122 us
  starting transfers between devices  33.2 us (27%)
  other arithmetic  23.4 us (19%)
  local copies, waits for them, and re-layouts  22.3 us (18%)
  matrix products  17.2 us (14%)
  waiting for transfers between devices  15.7 us (13%)
  blocking collectives  8.81 us (7%)
    ppermute x4, starting transfers between devices, from_behind(): lax.ppermute(array, axis, [(i, (i + by) % peers) for i in range(peers)])  17.4 us
    dot_general x1, matrix products, pair_sums(): jnp.einsum('pc,qrct->qrpt', pick, parts, preferred_element_type=jnp.float32)  13.3 us
    reduce_sum x1, other arithmetic, pair_sums(): jnp.sum(first_real * second_real + first_imag * second_imag, axis=-1)  13.1 us
    all_to_all x1, waiting for transfers between devices, shards(): exchanged = lax.all_to_all(partial_value, 'tm', 0, 0, tiled=True)  11.8 us
    all_to_all x1, starting transfers between devices, shards(): exchanged = lax.all_to_all(partial_value, 'tm', 0, 0, tiled=True)  10.4 us
    all_to_all x1, local copies, waits for them, and re-layouts, shards(): exchanged = lax.all_to_all(partial_value, 'tm', 0, 0, tiled=True)  9.09 us
    all_gather x1, blocking collectives, shards(): extended = lax.all_gather(wide, 'chan', axis=0, tiled=True)  8.81 us
    all_to_all x1, starting transfers between devices, shards(): lax.all_to_all(summed, 'chan', 0, 2, tiled=True)[0].transpose(0, 2, 1)  5.38 us
  transfers between devices with their start and end apart: 6, of which 3 were waited for; matrix products, arithmetic and copies ran while one was open for 10% of the time, Pallas kernels for 0%

profile of v3, /device:TPU:1, one launch (start us, length us, event | category | flops | bytes accessed | tf_op | source)
XLA Modules:
  0.0 121.7 jit_solution(4800325938742391312)
XLA Ops:
  0.6 0.8 convert_element_type.77
  1.4 11.3 %collective-permute-start.1 = (bf16[64,128]{1,0:T(8,128)(2,1)S(1)}, bf16[64,128]{1,0:T(8,128)(2,1)S(1)}, u32[]{:S(2)}, u32[]{:S(2)}) collective-permute-start(bf16[64,128]{1,0:T(8,128)(2,1)S(1)} %convert_element_type.77), channel_id=1, source_target_pairs={{0,252},{4,0},{8,4},{12,8},{16,12},{20,16},{24,20},{28,24},{32,28}... | collective-permute-start | bytes 49160 | tf_op jit(solution)/shard_map/ppermute | solution.py:19
  12.8 0.6 gather_fusion
  14.1 0.8 broadcast_compare_fusion
  15.0 2.1 %copy.64 = pred[1152,8,1,128]{0,3,2,1:T(8,128)(4,1)S(1)} copy(pred[1152,8,1,128]{3,1,2,0:T(8,128)(4,1)S(1)} %broadcast_compare_fusion) | data formatting | bytes 2359296 | tf_op jit(solution)/shard_map/lt | solution.py:34
  17.1 3.4 %select_convert_fusion.1 = (bf16[1152,8,1,128]{0,3,2,1:T(8,128)(2,1)S(1)}, bf16[1152,8,1,128]{0,3,2,1:T(8,128)(2,1)S(1)}) fusion(pred[1152,8,1,128]{0,3,2,1:T(8,128)(4,1)S(1)} %copy.64, f32[8,128]{1,0:T(8,128)S(1)} %get-tuple-element.32, f32[1152,8]{0,1:T(8,128)S(1)} %get-tuple-element.28, f32[8,128]{1,0:T(8,128)S(1)} %get-tuple-element.31, ...), kind=kLoop, calls=%fused_computation.11 | loop fusion | flops 18874368 | bytes 6570048 | tf_op jit(solution)/shard_map/convert_element_type | solution.py:43
  20.5 2.6 %pad_maximum_fusion = bf16[1152,8,2,128]{0,3,2,1:T(8,128)(2,1)} fusion(bf16[1152,8,1,128]{0,3,2,1:T(8,128)(2,1)S(1)} %get-tuple-element.17, bf16[1152,8,1,128]{0,3,2,1:T(8,128)(2,1)S(1)} %get-tuple-element.16), kind=kLoop, calls=%fused_computation.9 | loop fusion | flops 2359296 | bytes 9437184 | tf_op jit(solution)/shard_map/stack | solution.py:45
  23.9 6.0 %collective-permute-start.3 = (bf16[64,384]{1,0:T(8,128)(2,1)S(1)}, bf16[64,384]{1,0:T(8,128)(2,1)S(1)}, u32[]{:S(2)}, u32[]{:S(2)}) collective-permute-start(bf16[64,384]{1,0:T(8,128)(2,1)S(1)} %pad_maximum_fusion.1), channel_id=1, source_target_pairs={{0,244},{4,248},{8,252},{12,0},{16,4},{20,8},{24,12},{28,16},{32,2... | collective-permute-start | bytes 147464 | tf_op jit(solution)/shard_map/ppermute | solution.py:19
  29.9 1.5 %collective-permute-done.2 = bf16[64,384]{1,0:T(8,128)(2,1)S(1)} collective-permute-done((bf16[64,384]{1,0:T(8,128)(2,1)S(1)}, bf16[64,384]{1,0:T(8,128)(2,1)S(1)}, u32[]{:S(2)}, u32[]{:S(2)}) %collective-permute-start.2) | collective-permute-done | bytes 49184 | tf_op jit(solution)/shard_map/ppermute | solution.py:19
  31.4 8.8 %all_gather.3 = bf16[256,1152]{1,0:T(8,128)(2,1)S(1)} all-gather(bf16[64,1152]{1,0:T(8,128)(2,1)S(1)} %constant_dynamic-update-slice_fusion), channel_id=1, replica_groups=mesh['tm'=64,'chan'=4] {'chan'}, dimensions={0}, use_global_device_ids=true | all-gather | bytes 737280 | tf_op jit(solution)/shard_map/all_gather | solution.py:101
  41.5 3.9 %convolution_convert_fusion = bf16[256,2048]{1,0:T(8,128)(2,1)S(1)} fusion(bf16[256,1152]{0,1:T(8,128)(2,1)S(1)} %bitcast.73, bf16[1152,2048]{0,1:T(8,128)(2,1)} %bitcast.62), kind=kOutput, calls=%fused_computation.14 | convolution fusion | flops 1208483840 | bytes 6356992 | tf_op jit(solution)/shard_map/dot_general | solution.py:61
  46.0 13.3 %convert_bitcast_fusion = f32[8,2,4096,128]{2,3,1,0:T(8,128)} fusion(bf16[8,2,256,128]{2,3,1,0:T(8,128)(2,1)S(1)} %bitcast.63, s32[4096]{0:T(1024)S(1)} %pad_add_fusion), kind=kOutput, calls=%fused_computation.1 | convolution fusion | flops 4312793088 | bytes 34619392 | tf_op jit(solution)/shard_map/pc,qrct->qrpt/dot_general | solution.py:75
  59.3 13.1 %add_reduce_fusion.2 = (f32[8,2048]{1,0:T(8,128)S(1)}, f32[8,2048]{1,0:T(8,128)S(1)}, f32[8,2048]{1,0:T(8,128)S(1)}, f32[8,2048]{1,0:T(8,128)S(1)}) fusion(f32[8,2,4096,128]{2,3,1,0:T(8,128)} %convert_bitcast_fusion), kind=kLoop, calls=%fused_computation.5 | loop fusion | flops 33488896 | bytes 33816576 | tf_op jit(solution)/shard_map/reduce_sum | solution.py:82
  72.4 4.8 %copy.69 = f32[2048,8,4]{2,1,0:T(8,128)} copy(f32[2048,8,4]{0,1,2:T(8,128)S(1)} %maximum_bitcast_fusion) | data formatting | bytes 524288 | tf_op jit(solution)/shard_map/transpose | solution.py:115
  77.2 9.1 %all_to_all.16 = f32[64,1,1024]{2,1,0:T(1,128)} reshape(f32[2048,8,4]{2,1,0:T(8,128)} %copy.69) | data formatting | bytes 524288 | tf_op jit(solution)/shard_map/all_to_all | solution.py:116
  86.3 10.4 %all-to-all-start = ((f32[64,1,1024]{2,1,0:T(1,128)}), f32[64,1,1024]{2,1,0:T(1,128)S(1)}, u32[]{:S(2)}, u32[]{:S(2)}) async-start(f32[64,1,1024]{2,1,0:T(1,128)} %all_to_all.16), calls=%async_computation | async-start | bytes 524288 | tf_op jit(solution)/shard_map/all_to_all | solution.py:116
  97.3 11.8 %all-to-all-done = f32[64,1,1024]{2,1,0:T(1,128)S(1)} async-done(((f32[64,1,1024]{2,1,0:T(1,128)}), f32[64,1,1024]{2,1,0:T(1,128)S(1)}, u32[]{:S(2)}, u32[]{:S(2)}) %all-to-all-start) | async-done | bytes 262176 | tf_op jit(solution)/shard_map/all_to_all | solution.py:116
  109.7 0.7 reshape.423
  110.4 5.4 %all-to-all-start.1 = ((f32[4,1,256]{2,1,0:T(1,128)}), f32[4,1,256]{2,1,0:T(1,128)S(1)}, u32[]{:S(2)}, u32[]{:S(2)}) async-start(f32[4,1,256]{2,1,0:T(1,128)} %reshape.423), calls=%async_computation.1 | async-start | bytes 8192 | tf_op jit(solution)/shard_map/all_to_all | solution.py:118
  115.8 0.7 add_compare_fusion
  116.4 2.4 %all-to-all-done.1 = f32[4,1,256]{2,1,0:T(1,128)S(1)} async-done(((f32[4,1,256]{2,1,0:T(1,128)}), f32[4,1,256]{2,1,0:T(1,128)S(1)}, u32[]{:S(2)}, u32[]{:S(2)}) %all-to-all-start.1) | async-done | bytes 4128 | tf_op jit(solution)/shard_map/all_to_all | solution.py:118
  119.4 0.7 reduce.5
  120.3 0.7 fusion.13
  121.0 0.6 copy.73
  (70 shorter events, 5.2 us)
Async XLA Ops:
  0.6 12.2 %copy-start = (s32[32]{0:T(128)S(1)}, s32[32]{0:T(128)}, u32[]{:S(2)}) copy-start(s32[32]{0:T(128)} %param.6) | copy-start | bytes 388
  1.4 22.4 %collective-permute-start.1 = (bf16[64,128]{1,0:T(8,128)(2,1)S(1)}, bf16[64,128]{1,0:T(8,128)(2,1)S(1)}, u32[]{:S(2)}, u32[]{:S(2)}) collective-permute-start(bf16[64,128]{1,0:T(8,128)(2,1)S(1)} %convert_element_type.77), channel_id=1, source_target_pairs={{0,252},{4,0},{8,4},{12,8},{16,12},{20,16},{24,20},{28,24},{32,28}... | collective-permute-start | bytes 49160 | tf_op jit(solution)/shard_map/ppermute | solution.py:19
  12.7 11.1 %collective-permute-start = (bf16[64,128]{1,0:T(8,128)(2,1)S(1)}, bf16[64,128]{1,0:T(8,128)(2,1)S(1)}, u32[]{:S(2)}, u32[]{:S(2)}) collective-permute-start(bf16[64,128]{1,0:T(8,128)(2,1)S(1)} %convert_element_type.77), channel_id=1, source_target_pairs={{0,4},{4,8},{8,12},{12,16},{16,20},{20,24},{24,28},{28,32},{32,36}... | collective-permute-start | bytes 49160 | tf_op jit(solution)/shard_map/ppermute | solution.py:19
  20.4 2.6 %copy-start.2 = (s32[4,512]{1,0:T(4,128)S(1)}, s32[4,512]{1,0:T(4,128)}, u32[]{:S(2)}) copy-start(s32[4,512]{1,0:T(4,128)} %param.7) | copy-start | bytes 24580
  20.5 3.0 %copy-start.3 = (s32[4,512]{1,0:T(4,128)S(1)}, s32[4,512]{1,0:T(4,128)}, u32[]{:S(2)}) copy-start(s32[4,512]{1,0:T(4,128)} %param.8) | copy-start | bytes 24580
  20.5 10.9 %copy-start.1 = (f32[64,128]{1,0:T(8,128)S(1)}, f32[64,128]{1,0:T(8,128)}, u32[]{:S(2)}) copy-start(f32[64,128]{1,0:T(8,128)} %param.5) | copy-start | bytes 98308
  23.8 7.5 %collective-permute-start.2 = (bf16[64,384]{1,0:T(8,128)(2,1)S(1)}, bf16[64,384]{1,0:T(8,128)(2,1)S(1)}, u32[]{:S(2)}, u32[]{:S(2)}) collective-permute-start(bf16[64,384]{1,0:T(8,128)(2,1)S(1)} %pad_maximum_fusion.1), channel_id=1, source_target_pairs={{0,12},{4,16},{8,20},{12,24},{16,28},{20,32},{24,36},{28,40},{32,4... | collective-permute-start | bytes 147464 | tf_op jit(solution)/shard_map/ppermute | solution.py:19
  23.9 7.5 %collective-permute-start.3 = (bf16[64,384]{1,0:T(8,128)(2,1)S(1)}, bf16[64,384]{1,0:T(8,128)(2,1)S(1)}, u32[]{:S(2)}, u32[]{:S(2)}) collective-permute-start(bf16[64,384]{1,0:T(8,128)(2,1)S(1)} %pad_maximum_fusion.1), channel_id=1, source_target_pairs={{0,244},{4,248},{8,252},{12,0},{16,4},{20,8},{24,12},{28,16},{32,2... | collective-permute-start | bytes 147464 | tf_op jit(solution)/shard_map/ppermute | solution.py:19
  77.2 19.5 %copy-start.4 = (s32[4]{0:T(128)S(1)}, s32[4]{0:T(128)}, u32[]{:S(2)}) copy-start(s32[4]{0:T(128)} %param.9) | copy-start | bytes 52
  86.3 22.8 %all-to-all-start = ((f32[64,1,1024]{2,1,0:T(1,128)}), f32[64,1,1024]{2,1,0:T(1,128)S(1)}, u32[]{:S(2)}, u32[]{:S(2)}) async-start(f32[64,1,1024]{2,1,0:T(1,128)} %all_to_all.16), calls=%async_computation | async-start | bytes 524288 | tf_op jit(solution)/shard_map/all_to_all | solution.py:116
  110.4 8.5 %all-to-all-start.1 = ((f32[4,1,256]{2,1,0:T(1,128)}), f32[4,1,256]{2,1,0:T(1,128)S(1)}, u32[]{:S(2)}, u32[]{:S(2)}) async-start(f32[4,1,256]{2,1,0:T(1,128)} %reshape.423), calls=%async_computation.1 | async-start | bytes 8192 | tf_op jit(solution)/shard_map/all_to_all | solution.py:118

commit v4 on v3

v4 whole, which is shorter than its diff:
```python
import math

import jax
import jax.numpy as jnp
import numpy as np
from jax import lax
from jax.experimental import pallas as pl
from jax.sharding import PartitionSpec as P

NS = 32
BLK = 128
TD = 128


power_floor = 1e-06


def from_behind(array, axis, by):
    peers = lax.axis_size(axis)
    return lax.ppermute(array, axis, [(i, (i + by) % peers) for i in range(peers)])


def kernel_table(scale_ids, reaches, offsets):
    taps = (2 * offsets + 1) * BLK
    lag = jnp.arange(taps, dtype=jnp.int32) - offsets * BLK
    within = jnp.arange(BLK, dtype=jnp.int32)
    scale_width = 2.0 * TD * jnp.exp2((scale_ids - (NS - 1)).astype(jnp.float32) / 4.0)
    offset = lag[:, None, None] - within[None, None, :]
    scaled_offset = offset.astype(jnp.float32) / scale_width[None, :, None]
    amplitude = (
        math.pi ** (-0.25)
        * lax.rsqrt(scale_width)[None, :, None]
        * jnp.exp(-0.5 * scaled_offset * scaled_offset)
    )
    inside = jnp.abs(offset) < (reaches * BLK)[None, :, None]
    lag_phase = 6.0 * (lag.astype(jnp.float32)[:, None] / scale_width[None, :])
    time_phase = 6.0 * (within.astype(jnp.float32)[None, :] / scale_width[:, None])
    lag_cos = jnp.cos(lag_phase)[:, :, None]
    lag_sin = jnp.sin(lag_phase)[:, :, None]
    time_cos = jnp.cos(time_phase)[None]
    time_sin = jnp.sin(time_phase)[None]
    cos_part = lag_cos * time_cos + lag_sin * time_sin
    sin_part = lag_sin * time_cos - lag_cos * time_sin
    real_part = jnp.where(inside, amplitude * cos_part, 0.0).astype(jnp.bfloat16)
    imag_part = jnp.where(inside, amplitude * sin_part, 0.0).astype(jnp.bfloat16)
    table = jnp.stack([real_part, imag_part], axis=2)
    return table.reshape(taps, -1)


def pair_kernel(coef_ref, pick_ref, out_ref):
    coef = coef_ref[...]
    first = jnp.dot(pick_ref[0], coef, preferred_element_type=jnp.float32)
    second = jnp.dot(pick_ref[1], coef, preferred_element_type=jnp.float32).astype(jnp.bfloat16)
    half = first.shape[1] // 2
    turned = jnp.concatenate([first[:, half:], -first[:, :half]], axis=1).astype(jnp.bfloat16)
    first = first.astype(jnp.bfloat16)
    size = first.shape[0]
    eye = lax.broadcasted_iota(jnp.int32, (size, size), 0) == lax.broadcasted_iota(
        jnp.int32, (size, size), 1
    )

    def diagonal(left, right):
        gram = lax.dot_general(
            left, right, (((1,), (1,)), ((), ())), preferred_element_type=jnp.float32
        )
        return jnp.sum(jnp.where(eye, gram, 0.0), axis=0, keepdims=True)

    out_ref[0, 0:1, :] = diagonal(first, second)
    out_ref[0, 1:2, :] = diagonal(turned, second)
    out_ref[0, 2:3, :] = diagonal(first, first)
    out_ref[0, 3:4, :] = diagonal(second, second)


def pair_sums(coefficients, first_flat, second_flat, scale_count):
    channels = coefficients.shape[0]
    width = coefficients.shape[1] // scale_count
    pairs = first_flat.shape[0]
    chan_iota = jnp.arange(channels, dtype=jnp.int32)
    both = jnp.stack([first_flat, second_flat])
    pick = (both[:, :, None] == chan_iota[None, None, :]).astype(jnp.bfloat16)
    block = 128
    return pl.pallas_call(
        pair_kernel,
        grid=(pairs // block, scale_count),
        in_specs=[
            pl.BlockSpec((channels, width), lambda b, q: (0, q)),
            pl.BlockSpec((2, block, channels), lambda b, q: (0, b, 0)),
        ],
        out_specs=pl.BlockSpec((1, 4, block), lambda b, q: (q, 0, b)),
        out_shape=jax.ShapeDtypeStruct((scale_count, 4, pairs), jnp.float32),
    )(coefficients, pick)


def shards(signal, support, pair_first, pair_second, pair_count):
    groups = lax.axis_size("chan")
    cluster_number = lax.axis_index("chan")
    time_index = lax.axis_index("tm")
    time_devices = lax.axis_size("tm")
    time_span = signal.shape[1]
    ntime = time_span * time_devices
    rounded = signal.astype(jnp.bfloat16)
    near = jnp.concatenate(
        [from_behind(rounded, "tm", 1), rounded, from_behind(rounded, "tm", -1)], axis=1
    )
    wide = jnp.concatenate([from_behind(near, "tm", 3), near, from_behind(near, "tm", -3)], axis=1)
    extended = lax.all_gather(wide, "chan", axis=0, tiled=True)
    per_group = NS // groups
    scale_ids = cluster_number * per_group + jnp.arange(per_group, dtype=jnp.int32)
    table = kernel_table(scale_ids, support[scale_ids], 4)
    coefficients = jnp.dot(extended, table, preferred_element_type=jnp.float32)
    coefficients = coefficients.astype(jnp.bfloat16)
    owner_devices, slots_total = pair_first.shape
    slots_local = slots_total // time_devices

    def by_block(pairs):
        return pairs.reshape(owner_devices, time_devices, slots_local).transpose(1, 0, 2).reshape(-1)

    sums = pair_sums(coefficients, by_block(pair_first), by_block(pair_second), per_group)
    values = sums.shape[1]
    chunk = owner_devices * slots_local
    partial_value = sums.reshape(per_group * values, time_devices, chunk).transpose(1, 0, 2)
    exchanged = lax.all_to_all(partial_value.reshape(time_devices, -1), "tm", 0, 0, tiled=True)
    summed = jnp.sum(exchanged, axis=0).reshape(per_group, values, owner_devices, slots_local)
    owned = lax.all_to_all(summed, "chan", 2, 0, tiled=True)[:, :, 0, :] / ntime
    slot_index = time_index * slots_local + jnp.arange(slots_local, dtype=jnp.int32)
    alive_mask = slot_index < pair_count[cluster_number]
    cross_real = owned[:, 0, :].T
    cross_imag = owned[:, 1, :].T
    first_power = owned[:, 2, :].T
    second_power = owned[:, 3, :].T
    coherence = (cross_real * cross_real + cross_imag * cross_imag) / (
        (first_power + power_floor) * (second_power + power_floor)
    )
    coherence = jnp.where(alive_mask[:, None], coherence, 0.0)[None]
    cross = jnp.stack([cross_real, cross_imag], axis=1)
    cross = jnp.where(alive_mask[:, None, None], cross, 0.0)[None]
    return (cross, coherence.astype(jnp.float32))


def solution(mesh):
    in_specs = (P("chan", "tm"), P(), P(), P(), P())
    out_specs = (P("chan", "tm", None, None), P("chan", "tm", None))
    return jax.shard_map(shards, mesh=mesh, in_specs=in_specs, out_specs=out_specs, check_vma=False)
```

time: 122 us -> 171 us (1.40)
  Pallas kernels: 0 us -> 88.1 us
  matrix products: 17.2 us -> 2.54 us
  other arithmetic: 23.4 us -> 9.88 us
  local copies, waits for them, and re-layouts: 22.3 us -> 9.25 us
    pallas_call x0 -> x1, Pallas kernels: none -> 88.1 us  [pair_sums(): pl.pallas_call(pair_kernel, grid=(pairs // block, scale_count), in_specs=...]
    dot_general x2 -> x1, matrix products: 17.2 us -> 2.54 us  [shards(): coefficients = jnp.dot(extended, table, preferred_element_type=jnp.float32)]
    reduce_sum x1 -> x0, other arithmetic: 13.1 us -> none  [pair_sums(): jnp.sum(first_real * second_real + first_imag * second_imag, axis=-1)]
    all_to_all x2, local copies, waits for them, and re-layouts: 9.6 us -> 1.4 us  [the longest x1 0.89 us: shards(): lax.all_to_all(partial_value.reshape(time_devices, -1), 'tm', 0, 0, tiled...]
    transpose x1, local copies, waits for them, and re-layouts: 4.76 us -> 0.32 us  [shards(): sums.reshape(per_group * values, time_devices, chunk).transpose(1, 0, 2)]
    another operation x1, other arithmetic: 2.58 us -> 0.47 us  [kernel_table(): table = jnp.stack([real_part, imag_part], axis=2)]
  transfers between devices with their start and end apart: 6 -> 6, of which waited for: 3 -> 4; matrix products, arithmetic and copies ran while one was open for 10% -> 7% of each run, Pallas kernels for 0% -> 0%
where the time goes in v4:
time: 171 us; the launch traced here: 169 us
  Pallas kernels  88.1 us (52%)
  starting transfers between devices  34.7 us (20%)
  waiting for transfers between devices  15.4 us (9%)
  other arithmetic  9.88 us (6%)
  local copies, waits for them, and re-layouts  9.25 us (5%)
  blocking collectives  8.62 us (5%)
  matrix products  2.54 us (1%)
    pallas_call x1, Pallas kernels, pair_sums(): pl.pallas_call(pair_kernel, grid=(pairs // block, scale_count), in_specs=...  88.1 us
    ppermute x4, starting transfers between devices, from_behind(): lax.ppermute(array, axis, [(i, (i + by) % peers) for i in range(peers)])  17.4 us
    all_to_all x1, starting transfers between devices, shards(): lax.all_to_all(partial_value.reshape(time_devices, -1), 'tm', 0, 0, tiled...  11.9 us
    all_to_all x1, waiting for transfers between devices, shards(): lax.all_to_all(partial_value.reshape(time_devices, -1), 'tm', 0, 0, tiled...  11.8 us
    all_gather x1, blocking collectives, shards(): extended = lax.all_gather(wide, 'chan', axis=0, tiled=True)  8.62 us
    all_to_all x1, starting transfers between devices, shards(): owned = lax.all_to_all(summed, 'chan', 2, 0, tiled=True)[:, :, 0, :] / ntime  5.38 us
  transfers between devices with their start and end apart: 6, of which 4 were waited for; matrix products, arithmetic and copies ran while one was open for 7% of the time, Pallas kernels for 0%

profile of v4, /device:TPU:1, one launch (start us, length us, event | category | flops | bytes accessed | tf_op | source)
XLA Modules:
  0.0 169.4 jit_solution(6761043247853075893)
XLA Ops:
  0.7 0.8 convert_element_type.69
  1.4 2.1 %collective-permute-start = (bf16[64,128]{1,0:T(8,128)(2,1)S(1)}, bf16[64,128]{1,0:T(8,128)(2,1)S(1)}, u32[]{:S(2)}, u32[]{:S(2)}) collective-permute-start(bf16[64,128]{1,0:T(8,128)(2,1)S(1)} %convert_element_type.69), channel_id=1, source_target_pairs={{0,4},{4,8},{8,12},{12,16},{16,20},{20,24},{24,28},{28,32},{32,36}... | collective-permute-start | bytes 49160 | tf_op jit(solution)/shard_map/ppermute | solution.py:20
  3.6 9.2 %collective-permute-start.1 = (bf16[64,128]{1,0:T(8,128)(2,1)S(1)}, bf16[64,128]{1,0:T(8,128)(2,1)S(1)}, u32[]{:S(2)}, u32[]{:S(2)}) collective-permute-start(bf16[64,128]{1,0:T(8,128)(2,1)S(1)} %convert_element_type.69), channel_id=1, source_target_pairs={{0,252},{4,0},{8,4},{12,8},{16,12},{20,16},{24,20},{28,24},{32,28}... | collective-permute-start | bytes 49160 | tf_op jit(solution)/shard_map/ppermute | solution.py:20
  13.2 0.6 gather_fusion
  14.2 0.8 broadcast_compare_fusion
  15.0 2.1 %copy.34 = pred[1152,8,1,128]{0,3,2,1:T(8,128)(4,1)S(1)} copy(pred[1152,8,1,128]{3,1,2,0:T(8,128)(4,1)S(1)} %broadcast_compare_fusion) | data formatting | bytes 2359296 | tf_op jit(solution)/shard_map/lt | solution.py:35
  17.9 3.4 %select_convert_fusion.1 = (bf16[1152,8,1,128]{0,3,2,1:T(8,128)(2,1)S(1)}, bf16[1152,8,1,128]{0,3,2,1:T(8,128)(2,1)S(1)}) fusion(pred[1152,8,1,128]{0,3,2,1:T(8,128)(4,1)S(1)} %copy.34, f32[8,128]{1,0:T(8,128)S(1)} %get-tuple-element.25, f32[1152,8]{0,1:T(8,128)S(1)} %get-tuple-element.21, f32[8,128]{1,0:T(8,128)S(1)} %get-tuple-element.24, ...), kind=kLoop, calls=%fused_computation.6 | loop fusion | flops 18874368 | bytes 6570048 | tf_op jit(solution)/shard_map/convert_element_type | solution.py:44
  21.3 1.7 fusion.2.pick_ref
  23.5 6.0 %collective-permute-start.3 = (bf16[64,384]{1,0:T(8,128)(2,1)S(1)}, bf16[64,384]{1,0:T(8,128)(2,1)S(1)}, u32[]{:S(2)}, u32[]{:S(2)}) collective-permute-start(bf16[64,384]{1,0:T(8,128)(2,1)S(1)} %pad_maximum_fusion.1), channel_id=1, source_target_pairs={{0,244},{4,248},{8,252},{12,0},{16,4},{20,8},{24,12},{28,16},{32,2... | collective-permute-start | bytes 147464 | tf_op jit(solution)/shard_map/ppermute | solution.py:20
  29.6 0.9 collective-permute-done.2
  30.8 8.6 %all_gather.3 = bf16[256,1152]{1,0:T(8,128)(2,1)S(1)} all-gather(bf16[64,1152]{1,0:T(8,128)(2,1)S(1)} %constant_dynamic-update-slice_fusion), channel_id=1, replica_groups=mesh['tm'=64,'chan'=4] {'chan'}, dimensions={0}, use_global_device_ids=true | all-gather | bytes 737280 | tf_op jit(solution)/shard_map/all_gather | solution.py:106
  39.4 2.5 %convolution_convert_fusion.coef_ref = bf16[256,2048]{1,0:T(8,128)(2,1)} fusion(bf16[256,1152]{1,0:T(8,128)(2,1)S(1)} %all_gather.3, bf16[1152,2048]{0,1:T(8,128)(2,1)S(1)} %bitcast.48), kind=kOutput, calls=%fused_computation.9 | convolution fusion | flops 1208483840 | bytes 6356992 | tf_op jit(solution)/shard_map/dot_general | solution.py:110
  41.9 88.1 %shard_map.68 = f32[8,4,2048]{2,1,0:T(4,128)} custom-call(bf16[256,2048]{1,0:T(8,128)(2,1)} %convolution_convert_fusion.coef_ref, bf16[2,2048,256]{2,1,0:T(8,128)(2,1)} %fusion.2.pick_ref), custom_call_target="tpu_custom_call" | custom-call | tf_op jit(solution)/shard_map/pallas_call | solution.py:82
  130.1 1.3 reshape.348
  131.7 0.9 copy.39
  132.6 11.9 %all-to-all-start = ((f32[64,1,1024]{2,1,0:T(1,128)}), f32[64,1,1024]{2,1,0:T(1,128)S(1)}, u32[]{:S(2)}, u32[]{:S(2)}) async-start(f32[64,1,1024]{2,1,0:T(1,128)} %copy.39), calls=%async_computation | async-start | bytes 524288 | tf_op jit(solution)/shard_map/all_to_all | solution.py:122
  145.1 11.8 %all-to-all-done = f32[64,1,1024]{2,1,0:T(1,128)S(1)} async-done(((f32[64,1,1024]{2,1,0:T(1,128)}), f32[64,1,1024]{2,1,0:T(1,128)S(1)}, u32[]{:S(2)}, u32[]{:S(2)}) %all-to-all-start) | async-done | bytes 262176 | tf_op jit(solution)/shard_map/all_to_all | solution.py:122
  157.2 0.7 reshape.358
  157.9 5.4 %all-to-all-start.1 = ((f32[4,1,256]{2,1,0:T(1,128)}), f32[4,1,256]{2,1,0:T(1,128)S(1)}, u32[]{:S(2)}, u32[]{:S(2)}) async-start(f32[4,1,256]{2,1,0:T(1,128)} %reshape.358), calls=%async_computation.1 | async-start | bytes 8192 | tf_op jit(solution)/shard_map/all_to_all | solution.py:124
  163.3 0.7 add_compare_fusion
  164.0 2.4 %all-to-all-done.1 = f32[4,1,256]{2,1,0:T(1,128)S(1)} async-done(((f32[4,1,256]{2,1,0:T(1,128)}), f32[4,1,256]{2,1,0:T(1,128)S(1)}, u32[]{:S(2)}, u32[]{:S(2)}) %all-to-all-start.1) | async-done | bytes 4128 | tf_op jit(solution)/shard_map/all_to_all | solution.py:124
  166.9 0.7 reduce.1
  168.1 0.6 copy.42
  168.8 0.7 fusion.8
  (53 shorter events, 4.5 us)
Async XLA Ops:
  0.6 12.5 %copy-start = (s32[32]{0:T(128)S(1)}, s32[32]{0:T(128)}, u32[]{:S(2)}) copy-start(s32[32]{0:T(128)} %param.6) | copy-start | bytes 388
  0.6 16.5 %copy-start.2 = (s32[4,512]{1,0:T(4,128)S(1)}, s32[4,512]{1,0:T(4,128)}, u32[]{:S(2)}) copy-start(s32[4,512]{1,0:T(4,128)} %param.7) | copy-start | bytes 24580
  0.7 16.8 %copy-start.3 = (s32[4,512]{1,0:T(4,128)S(1)}, s32[4,512]{1,0:T(4,128)}, u32[]{:S(2)}) copy-start(s32[4,512]{1,0:T(4,128)} %param.8) | copy-start | bytes 24580
  1.4 21.5 %collective-permute-start = (bf16[64,128]{1,0:T(8,128)(2,1)S(1)}, bf16[64,128]{1,0:T(8,128)(2,1)S(1)}, u32[]{:S(2)}, u32[]{:S(2)}) collective-permute-start(bf16[64,128]{1,0:T(8,128)(2,1)S(1)} %convert_element_type.69), channel_id=1, source_target_pairs={{0,4},{4,8},{8,12},{12,16},{16,20},{20,24},{24,28},{28,32},{32,36}... | collective-permute-start | bytes 49160 | tf_op jit(solution)/shard_map/ppermute | solution.py:20
  3.6 19.4 %collective-permute-start.1 = (bf16[64,128]{1,0:T(8,128)(2,1)S(1)}, bf16[64,128]{1,0:T(8,128)(2,1)S(1)}, u32[]{:S(2)}, u32[]{:S(2)}) collective-permute-start(bf16[64,128]{1,0:T(8,128)(2,1)S(1)} %convert_element_type.69), channel_id=1, source_target_pairs={{0,252},{4,0},{8,4},{12,8},{16,12},{20,16},{24,20},{28,24},{32,28}... | collective-permute-start | bytes 49160 | tf_op jit(solution)/shard_map/ppermute | solution.py:20
  23.0 7.5 %collective-permute-start.2 = (bf16[64,384]{1,0:T(8,128)(2,1)S(1)}, bf16[64,384]{1,0:T(8,128)(2,1)S(1)}, u32[]{:S(2)}, u32[]{:S(2)}) collective-permute-start(bf16[64,384]{1,0:T(8,128)(2,1)S(1)} %pad_maximum_fusion.1), channel_id=1, source_target_pairs={{0,12},{4,16},{8,20},{12,24},{16,28},{20,32},{24,36},{28,40},{32,4... | collective-permute-start | bytes 147464 | tf_op jit(solution)/shard_map/ppermute | solution.py:20
  23.0 7.5 %copy-start.1 = (f32[64,128]{1,0:T(8,128)S(1)}, f32[64,128]{1,0:T(8,128)}, u32[]{:S(2)}) copy-start(f32[64,128]{1,0:T(8,128)} %param.5) | copy-start | bytes 98308
  23.5 7.2 %collective-permute-start.3 = (bf16[64,384]{1,0:T(8,128)(2,1)S(1)}, bf16[64,384]{1,0:T(8,128)(2,1)S(1)}, u32[]{:S(2)}, u32[]{:S(2)}) collective-permute-start(bf16[64,384]{1,0:T(8,128)(2,1)S(1)} %pad_maximum_fusion.1), channel_id=1, source_target_pairs={{0,244},{4,248},{8,252},{12,0},{16,4},{20,8},{24,12},{28,16},{32,2... | collective-permute-start | bytes 147464 | tf_op jit(solution)/shard_map/ppermute | solution.py:20
  41.9 102.6 %copy-start.4 = (s32[4]{0:T(128)S(1)}, s32[4]{0:T(128)}, u32[]{:S(2)}) copy-start(s32[4]{0:T(128)} %param.9) | copy-start | bytes 52
  132.6 24.3 %all-to-all-start = ((f32[64,1,1024]{2,1,0:T(1,128)}), f32[64,1,1024]{2,1,0:T(1,128)S(1)}, u32[]{:S(2)}, u32[]{:S(2)}) async-start(f32[64,1,1024]{2,1,0:T(1,128)} %copy.39), calls=%async_computation | async-start | bytes 524288 | tf_op jit(solution)/shard_map/all_to_all | solution.py:122
  157.9 8.5 %all-to-all-start.1 = ((f32[4,1,256]{2,1,0:T(1,128)}), f32[4,1,256]{2,1,0:T(1,128)S(1)}, u32[]{:S(2)}, u32[]{:S(2)}) async-start(f32[4,1,256]{2,1,0:T(1,128)} %reshape.358), calls=%async_computation.1 | async-start | bytes 8192 | tf_op jit(solution)/shard_map/all_to_all | solution.py:124

commit v5 on v3

--- a/solution.py
+++ b/solution.py
@@ -46,44 +46,24 @@
     return table.reshape(taps, -1)
 
 
-def wavelet_band(extended, scale_ids, reaches, offsets, time_span):
-    channels = extended.shape[0]
-    blocks = time_span // BLK
-    centre = 4 * time_span // BLK
-    tap_blocks = 2 * offsets + 1
-    pieces = [
-        extended[:, (centre + offset_step) * BLK : (centre + offset_step) * BLK + time_span]
-        for offset_step in range(-offsets, offsets + 1)
-    ]
-    unfolded = jnp.stack(pieces, axis=1).reshape(channels, tap_blocks, blocks, BLK)
-    unfolded = unfolded.transpose(0, 2, 1, 3).reshape(channels * blocks, tap_blocks * BLK)
-    table = kernel_table(scale_ids, reaches, offsets)
-    coefficients = jnp.dot(unfolded, table, preferred_element_type=jnp.float32)
-    scale_count = scale_ids.shape[0]
-    coefficients = coefficients.astype(jnp.bfloat16).reshape(channels, blocks, scale_count, 2, BLK)
-    return coefficients.transpose(2, 3, 0, 1, 4).reshape(scale_count, 2 * channels, time_span)
-
-
-def pair_sums(coefficients, first_flat, second_flat):
-    scale_count = coefficients.shape[0]
-    channels = coefficients.shape[1] // 2
-    time_span = coefficients.shape[2]
+def pair_sums(coefficients, first_flat, second_flat, scale_count):
+    channels = coefficients.shape[0]
+    width = coefficients.shape[1] // scale_count
+    pairs = first_flat.shape[0]
     chan_iota = jnp.arange(channels, dtype=jnp.int32)
     both = jnp.concatenate([first_flat, second_flat])
     pick = (both[:, None] == chan_iota[None, :]).astype(jnp.bfloat16)
-    parts = coefficients.reshape(scale_count, 2, channels, time_span)
-    picked = jnp.einsum("pc,qrct->qrpt", pick, parts, preferred_element_type=jnp.float32)
-    picked = picked.astype(jnp.bfloat16).astype(jnp.float32)
-    pairs = first_flat.shape[0]
-    first_real = picked[:, 0, :pairs]
-    first_imag = picked[:, 1, :pairs]
-    second_real = picked[:, 0, pairs:]
-    second_imag = picked[:, 1, pairs:]
+    picked = jnp.dot(pick, coefficients, preferred_element_type=jnp.bfloat16)
+    picked = picked.astype(jnp.float32).reshape(2, pairs, scale_count, 2, width // 2)
+    first_real = picked[0, :, :, 0]
+    first_imag = picked[0, :, :, 1]
+    second_real = picked[1, :, :, 0]
+    second_imag = picked[1, :, :, 1]
     cross_real = jnp.sum(first_real * second_real + first_imag * second_imag, axis=-1)
     cross_imag = jnp.sum(first_imag * second_real - first_real * second_imag, axis=-1)
     power_first = jnp.sum(first_real * first_real + first_imag * first_imag, axis=-1)
     power_second = jnp.sum(second_real * second_real + second_imag * second_imag, axis=-1)
-    return jnp.stack([cross_real, cross_imag, power_first, power_second], axis=1)
+    return jnp.stack([cross_real, cross_imag, power_first, power_second], axis=-1)
 
 
 def shards(signal, support, pair_first, pair_second, pair_count):
@@ -101,27 +81,26 @@
     extended = lax.all_gather(wide, "chan", axis=0, tiled=True)
     per_group = NS // groups
     scale_ids = cluster_number * per_group + jnp.arange(per_group, dtype=jnp.int32)
-    coefficients = wavelet_band(
-        extended, scale_ids, support[scale_ids], 4 * time_span // BLK, time_span
-    )
+    table = kernel_table(scale_ids, support[scale_ids], 4)
+    coefficients = jnp.dot(extended, table, preferred_element_type=jnp.float32)
+    coefficients = coefficients.astype(jnp.bfloat16)
     owner_devices, slots_total = pair_first.shape
     slots_local = slots_total // time_devices
 
     def by_block(pairs):
         return pairs.reshape(owner_devices, time_devices, slots_local).transpose(1, 0, 2).reshape(-1)
 
-    sums = pair_sums(coefficients, by_block(pair_first), by_block(pair_second))
-    values = sums.shape[1]
-    partial_value = sums.transpose(2, 0, 1).reshape(time_devices, -1)
-    exchanged = lax.all_to_all(partial_value, "tm", 0, 0, tiled=True)
+    sums = pair_sums(coefficients, by_block(pair_first), by_block(pair_second), per_group)
+    values = sums.shape[-1]
+    exchanged = lax.all_to_all(sums.reshape(time_devices, -1), "tm", 0, 0, tiled=True)
     summed = jnp.sum(exchanged, axis=0).reshape(owner_devices, slots_local, per_group, values)
-    owned = lax.all_to_all(summed, "chan", 0, 2, tiled=True)[0].transpose(0, 2, 1) / ntime
+    owned = lax.all_to_all(summed, "chan", 0, 2, tiled=True)[0] / ntime
     slot_index = time_index * slots_local + jnp.arange(slots_local, dtype=jnp.int32)
     alive_mask = slot_index < pair_count[cluster_number]
-    cross_real = owned[:, 0, :]
-    cross_imag = owned[:, 1, :]
-    first_power = owned[:, 2, :]
-    second_power = owned[:, 3, :]
+    cross_real = owned[:, :, 0]
+    cross_imag = owned[:, :, 1]
+    first_power = owned[:, :, 2]
+    second_power = owned[:, :, 3]
     coherence = (cross_real * cross_real + cross_imag * cross_imag) / (
         (first_power + power_floor) * (second_power + power_floor)
     )

time: 122 us -> 308 us (2.52)
  other arithmetic: 23.4 us -> 166 us
  local copies, waits for them, and re-layouts: 22.3 us -> 65.6 us
    reduce_sum x1, other arithmetic: 13.1 us -> 155 us  [pair_sums(): jnp.sum(first_real * second_real + first_imag * second_imag, axis=-1)]
    reshape x1, local copies, waits for them, and re-layouts: 0.52 us -> 42.6 us  [pair_sums(): picked.astype(jnp.float32).reshape(2, pairs, scale_count, 2, width // 2)]
    transpose x1 -> x0, local copies, waits for them, and re-layouts: 4.76 us -> none  [shards(): partial_value = sums.transpose(2, 0, 1).reshape(time_devices, -1)]
    another operation x1 -> x2, local copies, waits for them, and re-layouts: 0.01 us -> 4.75 us  [the longest x1 4.75 us: pair_sums(): jnp.stack([cross_real, cross_imag, power_first, power_second], axis=-1)]
    dot_general x2 -> x1, matrix products: 17.2 us -> 16.8 us  [pair_sums(): picked = jnp.dot(pick, coefficients, preferred_element_type=jnp.bfloat16)]
  transfers between devices with their start and end apart: 6 -> 6, of which waited for: 3 -> 3; matrix products, arithmetic and copies ran while one was open for 10% -> 4% of each run, Pallas kernels for 0% -> 0%
where the time goes in v5:
time: 308 us; the launch traced here: 307 us
  other arithmetic  166 us (54%)
  local copies, waits for them, and re-layouts  65.6 us (21%)
  starting transfers between devices  33.1 us (11%)
  matrix products  16.8 us (5%)
  waiting for transfers between devices  15.7 us (5%)
  blocking collectives  8.63 us (3%)
    reduce_sum x1, other arithmetic, pair_sums(): jnp.sum(first_real * second_real + first_imag * second_imag, axis=-1)  155 us
    reshape x1, local copies, waits for them, and re-layouts, pair_sums(): picked.astype(jnp.float32).reshape(2, pairs, scale_count, 2, width // 2)  42.6 us
    ppermute x4, starting transfers between devices, from_behind(): lax.ppermute(array, axis, [(i, (i + by) % peers) for i in range(peers)])  17.4 us
    dot_general x1, matrix products, pair_sums(): picked = jnp.dot(pick, coefficients, preferred_element_type=jnp.bfloat16)  16.8 us
    all_to_all x1, waiting for transfers between devices, shards(): lax.all_to_all(sums.reshape(time_devices, -1), 'tm', 0, 0, tiled=True)  11.8 us
    all_to_all x1, starting transfers between devices, shards(): lax.all_to_all(sums.reshape(time_devices, -1), 'tm', 0, 0, tiled=True)  10.4 us
    all_to_all x1, local copies, waits for them, and re-layouts, shards(): lax.all_to_all(sums.reshape(time_devices, -1), 'tm', 0, 0, tiled=True)  9.08 us
    all_gather x1, blocking collectives, shards(): extended = lax.all_gather(wide, 'chan', axis=0, tiled=True)  8.63 us
  transfers between devices with their start and end apart: 6, of which 3 were waited for; matrix products, arithmetic and copies ran while one was open for 4% of the time, Pallas kernels for 0%

profile of v5, /device:TPU:1, one launch (start us, length us, event | category | flops | bytes accessed | tf_op | source)
XLA Modules:
  0.0 306.6 jit_solution(3329106346723499564)
XLA Ops:
  0.6 0.8 convert_element_type.68
  1.4 11.3 %collective-permute-start.1 = (bf16[64,128]{1,0:T(8,128)(2,1)S(1)}, bf16[64,128]{1,0:T(8,128)(2,1)S(1)}, u32[]{:S(2)}, u32[]{:S(2)}) collective-permute-start(bf16[64,128]{1,0:T(8,128)(2,1)S(1)} %convert_element_type.68), channel_id=1, source_target_pairs={{0,252},{4,0},{8,4},{12,8},{16,12},{20,16},{24,20},{28,24},{32,28}... | collective-permute-start | bytes 49160 | tf_op jit(solution)/shard_map/ppermute | solution.py:19
  12.8 0.6 gather_fusion
  14.1 0.8 broadcast_compare_fusion
  15.0 2.1 copy.41
  17.1 3.4 %select_convert_fusion.1 = (bf16[1152,8,1,128]{0,3,2,1:T(8,128)(2,1)S(1)}, bf16[1152,8,1,128]{0,3,2,1:T(8,128)(2,1)S(1)}) fusion(pred[1152,8,1,128]{0,3,2,1:T(8,128)(4,1)S(1)} %copy.41, f32[8,128]{1,0:T(8,128)S(1)} %get-tuple-element.27, f32[1152,8]{0,1:T(8,128)S(1)} %get-tuple-element.23, f32[8,128]{1,0:T(8,128)S(1)} %get-tuple-element.26, ...), kind=kLoop, calls=%fused_computation.11 | loop fusion | flops 18874368 | bytes 6570048 | tf_op jit(solution)/shard_map/convert_element_type | solution.py:43
  20.5 2.7 pad_maximum_fusion
  24.0 6.0 %collective-permute-start.3 = (bf16[64,384]{1,0:T(8,128)(2,1)S(1)}, bf16[64,384]{1,0:T(8,128)(2,1)S(1)}, u32[]{:S(2)}, u32[]{:S(2)}) collective-permute-start(bf16[64,384]{1,0:T(8,128)(2,1)S(1)} %pad_maximum_fusion.2), channel_id=1, source_target_pairs={{0,244},{4,248},{8,252},{12,0},{16,4},{20,8},{24,12},{28,16},{32,2... | collective-permute-start | bytes 147464 | tf_op jit(solution)/shard_map/ppermute | solution.py:19
  30.0 1.5 collective-permute-done.2
  31.5 8.6 %all_gather.3 = bf16[256,1152]{1,0:T(8,128)(2,1)S(1)} all-gather(bf16[64,1152]{1,0:T(8,128)(2,1)S(1)} %constant_dynamic-update-slice_fusion), channel_id=1, replica_groups=mesh['tm'=64,'chan'=4] {'chan'}, dimensions={0}, use_global_device_ids=true | all-gather | bytes 737280 | tf_op jit(solution)/shard_map/all_gather | solution.py:81
  40.2 16.8 %convolution_convert_fusion = f32[4096,2048]{1,0:T(8,128)} fusion(bf16[256,1152]{1,0:T(8,128)(2,1)S(1)} %all_gather.3, bf16[1152,2048]{0,1:T(8,128)(2,1)} %bitcast.29, s32[4096]{0:T(1024)S(1)} %pad_add_fusion), kind=kOutput, calls=%fused_computation.1 | convolution fusion | flops 5512888320 | bytes 38879232 | tf_op jit(solution)/shard_map/dot_general | solution.py:56
  57.0 42.6 %reshape.450 = f32[2,2048,8,2,128]{4,3,2,1,0:T(2,128)} reshape(f32[4096,2048]{1,0:T(8,128)} %convolution_convert_fusion) | data formatting | bytes 67108864 | tf_op jit(solution)/shard_map/reshape | solution.py:57
  99.6 155.3 %add_reduce_fusion.2 = (f32[2048,8]{1,0:T(8,128)}, f32[2048,8]{1,0:T(8,128)S(1)}, f32[2048,8]{1,0:T(8,128)S(1)}, f32[2048,8]{1,0:T(8,128)S(1)}) fusion(f32[2,2048,8,2,128]{4,3,2,1,0:T(2,128)} %reshape.450), kind=kLoop, calls=%fused_computation.5 | loop fusion | flops 33488896 | bytes 33816576 | tf_op jit(solution)/shard_map/reduce_sum | solution.py:62
  254.9 1.5 copy.43
  257.4 4.8 %copy.47 = f32[2048,8,4]{2,1,0:T(8,128)} copy(f32[2048,8,4]{0,1,2:T(8,128)S(1)} %pad_maximum_fusion.1) | data formatting | bytes 524288 | tf_op jit(solution)/shard_map/stack | solution.py:66
  262.1 9.1 %all_to_all.16 = f32[64,1,1024]{2,1,0:T(1,128)} reshape(f32[2048,8,4]{2,1,0:T(8,128)} %copy.47) | data formatting | bytes 524288 | tf_op jit(solution)/shard_map/all_to_all | solution.py:95
  271.2 10.4 %all-to-all-start = ((f32[64,1,1024]{2,1,0:T(1,128)}), f32[64,1,1024]{2,1,0:T(1,128)S(1)}, u32[]{:S(2)}, u32[]{:S(2)}) async-start(f32[64,1,1024]{2,1,0:T(1,128)} %all_to_all.16), calls=%async_computation | async-start | bytes 524288 | tf_op jit(solution)/shard_map/all_to_all | solution.py:95
  282.2 11.8 %all-to-all-done = f32[64,1,1024]{2,1,0:T(1,128)S(1)} async-done(((f32[64,1,1024]{2,1,0:T(1,128)}), f32[64,1,1024]{2,1,0:T(1,128)S(1)}, u32[]{:S(2)}, u32[]{:S(2)}) %all-to-all-start) | async-done | bytes 262176 | tf_op jit(solution)/shard_map/all_to_all | solution.py:95
  294.6 0.7 reshape.460
  295.3 5.4 %all-to-all-start.1 = ((f32[4,1,256]{2,1,0:T(1,128)}), f32[4,1,256]{2,1,0:T(1,128)S(1)}, u32[]{:S(2)}, u32[]{:S(2)}) async-start(f32[4,1,256]{2,1,0:T(1,128)} %reshape.460), calls=%async_computation.1 | async-start | bytes 8192 | tf_op jit(solution)/shard_map/all_to_all | solution.py:97
  300.7 0.7 add_compare_fusion
  301.4 2.4 all-to-all-done.1
  304.3 0.7 reduce.5
  305.2 0.7 fusion.10
  (57 shorter events, 5.1 us)
Async XLA Ops:
  0.6 12.2 %copy-start = (s32[32]{0:T(128)S(1)}, s32[32]{0:T(128)}, u32[]{:S(2)}) copy-start(s32[32]{0:T(128)} %param.6) | copy-start | bytes 388
  1.4 22.5 %collective-permute-start.1 = (bf16[64,128]{1,0:T(8,128)(2,1)S(1)}, bf16[64,128]{1,0:T(8,128)(2,1)S(1)}, u32[]{:S(2)}, u32[]{:S(2)}) collective-permute-start(bf16[64,128]{1,0:T(8,128)(2,1)S(1)} %convert_element_type.68), channel_id=1, source_target_pairs={{0,252},{4,0},{8,4},{12,8},{16,12},{20,16},{24,20},{28,24},{32,28}... | collective-permute-start | bytes 49160 | tf_op jit(solution)/shard_map/ppermute | solution.py:19
  12.7 11.2 %collective-permute-start = (bf16[64,128]{1,0:T(8,128)(2,1)S(1)}, bf16[64,128]{1,0:T(8,128)(2,1)S(1)}, u32[]{:S(2)}, u32[]{:S(2)}) collective-permute-start(bf16[64,128]{1,0:T(8,128)(2,1)S(1)} %convert_element_type.68), channel_id=1, source_target_pairs={{0,4},{4,8},{8,12},{12,16},{16,20},{20,24},{24,28},{28,32},{32,36}... | collective-permute-start | bytes 49160 | tf_op jit(solution)/shard_map/ppermute | solution.py:19
  20.4 2.7 copy-start.3
  20.4 3.1 %copy-start.4 = (s32[4,512]{1,0:T(4,128)S(1)}, s32[4,512]{1,0:T(4,128)}, u32[]{:S(2)}) copy-start(s32[4,512]{1,0:T(4,128)} %param.8) | copy-start | bytes 24580
  20.5 11.0 %copy-start.2 = (f32[64,128]{1,0:T(8,128)S(1)}, f32[64,128]{1,0:T(8,128)}, u32[]{:S(2)}) copy-start(f32[64,128]{1,0:T(8,128)} %param.5) | copy-start | bytes 98308
  23.9 7.5 %collective-permute-start.2 = (bf16[64,384]{1,0:T(8,128)(2,1)S(1)}, bf16[64,384]{1,0:T(8,128)(2,1)S(1)}, u32[]{:S(2)}, u32[]{:S(2)}) collective-permute-start(bf16[64,384]{1,0:T(8,128)(2,1)S(1)} %pad_maximum_fusion.2), channel_id=1, source_target_pairs={{0,12},{4,16},{8,20},{12,24},{16,28},{20,32},{24,36},{28,40},{32,4... | collective-permute-start | bytes 147464 | tf_op jit(solution)/shard_map/ppermute | solution.py:19
  24.0 7.5 %collective-permute-start.3 = (bf16[64,384]{1,0:T(8,128)(2,1)S(1)}, bf16[64,384]{1,0:T(8,128)(2,1)S(1)}, u32[]{:S(2)}, u32[]{:S(2)}) collective-permute-start(bf16[64,384]{1,0:T(8,128)(2,1)S(1)} %pad_maximum_fusion.2), channel_id=1, source_target_pairs={{0,244},{4,248},{8,252},{12,0},{16,4},{20,8},{24,12},{28,16},{32,2... | collective-permute-start | bytes 147464 | tf_op jit(solution)/shard_map/ppermute | solution.py:19
  257.4 49.2 %copy-start.1 = (s32[32]{0:T(128)S(1)}, s32[32]{0:T(128)}, u32[]{:S(2)}) copy-start(s32[32]{0:T(128)} %param.6) | copy-start | bytes 388
  262.1 19.5 %copy-start.5 = (s32[4]{0:T(128)S(1)}, s32[4]{0:T(128)}, u32[]{:S(2)}) copy-start(s32[4]{0:T(128)} %param.9) | copy-start | bytes 52
  271.2 22.8 %all-to-all-start = ((f32[64,1,1024]{2,1,0:T(1,128)}), f32[64,1,1024]{2,1,0:T(1,128)S(1)}, u32[]{:S(2)}, u32[]{:S(2)}) async-start(f32[64,1,1024]{2,1,0:T(1,128)} %all_to_all.16), calls=%async_computation | async-start | bytes 524288 | tf_op jit(solution)/shard_map/all_to_all | solution.py:95
  295.3 8.4 %all-to-all-start.1 = ((f32[4,1,256]{2,1,0:T(1,128)}), f32[4,1,256]{2,1,0:T(1,128)S(1)}, u32[]{:S(2)}, u32[]{:S(2)}) async-start(f32[4,1,256]{2,1,0:T(1,128)} %reshape.460), calls=%async_computation.1 | async-start | bytes 8192 | tf_op jit(solution)/shard_map/all_to_all | solution.py:97

commit v6 on v3

--- a/solution.py
+++ b/solution.py
@@ -72,17 +72,20 @@
     both = jnp.concatenate([first_flat, second_flat])
     pick = (both[:, None] == chan_iota[None, :]).astype(jnp.bfloat16)
     parts = coefficients.reshape(scale_count, 2, channels, time_span)
-    picked = jnp.einsum("pc,qrct->qrpt", pick, parts, preferred_element_type=jnp.float32)
-    picked = picked.astype(jnp.bfloat16).astype(jnp.float32)
+    picked = jnp.einsum("pc,qrct->qrpt", pick, parts, preferred_element_type=jnp.bfloat16)
     pairs = first_flat.shape[0]
     first_real = picked[:, 0, :pairs]
     first_imag = picked[:, 1, :pairs]
     second_real = picked[:, 0, pairs:]
     second_imag = picked[:, 1, pairs:]
-    cross_real = jnp.sum(first_real * second_real + first_imag * second_imag, axis=-1)
-    cross_imag = jnp.sum(first_imag * second_real - first_real * second_imag, axis=-1)
-    power_first = jnp.sum(first_real * first_real + first_imag * first_imag, axis=-1)
-    power_second = jnp.sum(second_real * second_real + second_imag * second_imag, axis=-1)
+
+    def time_sum(left, right):
+        return jnp.einsum("qpt,qpt->qp", left, right, preferred_element_type=jnp.float32)
+
+    cross_real = time_sum(first_real, second_real) + time_sum(first_imag, second_imag)
+    cross_imag = time_sum(first_imag, second_real) - time_sum(first_real, second_imag)
+    power_first = time_sum(first_real, first_real) + time_sum(first_imag, first_imag)
+    power_second = time_sum(second_real, second_real) + time_sum(second_imag, second_imag)
     return jnp.stack([cross_real, cross_imag, power_first, power_second], axis=1)
 
 
@@ -112,16 +115,17 @@
 
     sums = pair_sums(coefficients, by_block(pair_first), by_block(pair_second))
     values = sums.shape[1]
-    partial_value = sums.transpose(2, 0, 1).reshape(time_devices, -1)
-    exchanged = lax.all_to_all(partial_value, "tm", 0, 0, tiled=True)
-    summed = jnp.sum(exchanged, axis=0).reshape(owner_devices, slots_local, per_group, values)
-    owned = lax.all_to_all(summed, "chan", 0, 2, tiled=True)[0].transpose(0, 2, 1) / ntime
+    chunk = owner_devices * slots_local
+    partial_value = sums.reshape(per_group * values, time_devices, chunk).transpose(1, 0, 2)
+    exchanged = lax.all_to_all(partial_value.reshape(time_devices, -1), "tm", 0, 0, tiled=True)
+    summed = jnp.sum(exchanged, axis=0).reshape(per_group, values, owner_devices, slots_local)
+    owned = lax.all_to_all(summed, "chan", 2, 0, tiled=True)[:, :, 0, :] / ntime
     slot_index = time_index * slots_local + jnp.arange(slots_local, dtype=jnp.int32)
     alive_mask = slot_index < pair_count[cluster_number]
-    cross_real = owned[:, 0, :]
-    cross_imag = owned[:, 1, :]
-    first_power = owned[:, 2, :]
-    second_power = owned[:, 3, :]
+    cross_real = owned[:, 0, :].T
+    cross_imag = owned[:, 1, :].T
+    first_power = owned[:, 2, :].T
+    second_power = owned[:, 3, :].T
     coherence = (cross_real * cross_real + cross_imag * cross_imag) / (
         (first_power + power_floor) * (second_power + power_floor)
     )

time: 122 us -> 95.2 us (0.78)
  local copies, waits for them, and re-layouts: 22.3 us -> 10.1 us
  matrix products: 17.2 us -> 8.91 us
  other arithmetic: 23.4 us -> 17 us
    reduce_sum x1 -> x0, other arithmetic: 13.1 us -> none  [pair_sums(): jnp.sum(first_real * second_real + first_imag * second_imag, axis=-1)]
    dot_general x1, matrix products: 13.3 us -> 4.98 us  [pair_sums(): jnp.einsum('pc,qrct->qrpt', pick, parts, preferred_element_type=jnp.bfloa...]
    all_to_all x2, local copies, waits for them, and re-layouts: 9.6 us -> 1.4 us  [the longest x1 0.88 us: shards(): lax.all_to_all(partial_value.reshape(time_devices, -1), 'tm', 0, 0, tiled...]
    dot_general x0 -> x1, other arithmetic: none -> 6.37 us  [time_sum(): jnp.einsum('qpt,qpt->qp', left, right, preferred_element_type=jnp.float32)]
    transpose x1, local copies, waits for them, and re-layouts: 4.76 us -> 0.33 us  [shards(): sums.reshape(per_group * values, time_devices, chunk).transpose(1, 0, 2)]
    unnamed x33 -> x37, local copies, waits for them, and re-layouts: 2.49 us -> 2.8 us
  transfers between devices with their start and end apart: 6 -> 6, of which waited for: 3 -> 3; matrix products, arithmetic and copies ran while one was open for 10% -> 13% of each run, Pallas kernels for 0% -> 0%
where the time goes in v6:
time: 95.2 us; the launch traced here: 94.9 us
  starting transfers between devices  33.2 us (35%)
  other arithmetic  17 us (18%)
  waiting for transfers between devices  15.7 us (16%)
  local copies, waits for them, and re-layouts  10.1 us (11%)
  matrix products  8.91 us (9%)
  blocking collectives  8.81 us (9%)
  between operations  1.18 us (1%)
    ppermute x4, starting transfers between devices, from_behind(): lax.ppermute(array, axis, [(i, (i + by) % peers) for i in range(peers)])  17.4 us
    all_to_all x1, waiting for transfers between devices, shards(): lax.all_to_all(partial_value.reshape(time_devices, -1), 'tm', 0, 0, tiled...  11.8 us
    all_to_all x1, starting transfers between devices, shards(): lax.all_to_all(partial_value.reshape(time_devices, -1), 'tm', 0, 0, tiled...  10.4 us
    all_gather x1, blocking collectives, shards(): extended = lax.all_gather(wide, 'chan', axis=0, tiled=True)  8.81 us
    dot_general x1, other arithmetic, time_sum(): jnp.einsum('qpt,qpt->qp', left, right, preferred_element_type=jnp.float32)  6.37 us
    all_to_all x1, starting transfers between devices, shards(): owned = lax.all_to_all(summed, 'chan', 2, 0, tiled=True)[:, :, 0, :] / ntime  5.38 us
    dot_general x1, matrix products, pair_sums(): jnp.einsum('pc,qrct->qrpt', pick, parts, preferred_element_type=jnp.bfloa...  4.98 us
    dot_general x1, matrix products, wavelet_band(): coefficients = jnp.dot(unfolded, table, preferred_element_type=jnp.float32)  3.92 us
  transfers between devices with their start and end apart: 6, of which 3 were waited for; matrix products, arithmetic and copies ran while one was open for 13% of the time, Pallas kernels for 0%

profile of v6, /device:TPU:1, one launch (start us, length us, event | category | flops | bytes accessed | tf_op | source)
XLA Modules:
  0.0 94.9 jit_solution(8276963354605251969)
XLA Ops:
  0.6 0.8 convert_element_type.67
  1.4 11.3 %collective-permute-start.1 = (bf16[64,128]{1,0:T(8,128)(2,1)S(1)}, bf16[64,128]{1,0:T(8,128)(2,1)S(1)}, u32[]{:S(2)}, u32[]{:S(2)}) collective-permute-start(bf16[64,128]{1,0:T(8,128)(2,1)S(1)} %convert_element_type.67), channel_id=1, source_target_pairs={{0,252},{4,0},{8,4},{12,8},{16,12},{20,16},{24,20},{28,24},{32,28}... | collective-permute-start | bytes 49160 | tf_op jit(solution)/shard_map/ppermute | solution.py:19
  12.8 0.6 gather_fusion
  14.1 0.8 broadcast_compare_fusion
  15.0 2.1 %copy.66 = pred[1152,8,1,128]{0,3,2,1:T(8,128)(4,1)S(1)} copy(pred[1152,8,1,128]{3,1,2,0:T(8,128)(4,1)S(1)} %broadcast_compare_fusion) | data formatting | bytes 2359296 | tf_op jit(solution)/shard_map/lt | solution.py:34
  17.1 3.4 %select_convert_fusion.1 = (bf16[1152,8,1,128]{0,3,2,1:T(8,128)(2,1)S(1)}, bf16[1152,8,1,128]{0,3,2,1:T(8,128)(2,1)S(1)}) fusion(pred[1152,8,1,128]{0,3,2,1:T(8,128)(4,1)S(1)} %copy.66, f32[8,128]{1,0:T(8,128)S(1)} %get-tuple-element.42, f32[1152,8]{0,1:T(8,128)S(1)} %get-tuple-element.38, f32[8,128]{1,0:T(8,128)S(1)} %get-tuple-element.41, ...), kind=kLoop, calls=%fused_computation.23 | loop fusion | flops 18874368 | bytes 6570048 | tf_op jit(solution)/shard_map/convert_element_type | solution.py:43
  20.5 2.6 %pad_maximum_fusion = bf16[1152,8,2,128]{0,3,2,1:T(8,128)(2,1)} fusion(bf16[1152,8,1,128]{0,3,2,1:T(8,128)(2,1)S(1)} %get-tuple-element.23, bf16[1152,8,1,128]{0,3,2,1:T(8,128)(2,1)S(1)} %get-tuple-element.22), kind=kLoop, calls=%fused_computation.21 | loop fusion | flops 2359296 | bytes 9437184 | tf_op jit(solution)/shard_map/stack | solution.py:45
  23.9 6.0 %collective-permute-start.3 = (bf16[64,384]{1,0:T(8,128)(2,1)S(1)}, bf16[64,384]{1,0:T(8,128)(2,1)S(1)}, u32[]{:S(2)}, u32[]{:S(2)}) collective-permute-start(bf16[64,384]{1,0:T(8,128)(2,1)S(1)} %pad_maximum_fusion.2), channel_id=1, source_target_pairs={{0,244},{4,248},{8,252},{12,0},{16,4},{20,8},{24,12},{28,16},{32,2... | collective-permute-start | bytes 147464 | tf_op jit(solution)/shard_map/ppermute | solution.py:19
  29.9 1.5 %collective-permute-done.2 = bf16[64,384]{1,0:T(8,128)(2,1)S(1)} collective-permute-done((bf16[64,384]{1,0:T(8,128)(2,1)S(1)}, bf16[64,384]{1,0:T(8,128)(2,1)S(1)}, u32[]{:S(2)}, u32[]{:S(2)}) %collective-permute-start.2) | collective-permute-done | bytes 49184 | tf_op jit(solution)/shard_map/ppermute | solution.py:19
  31.4 8.8 %all_gather.3 = bf16[256,1152]{1,0:T(8,128)(2,1)S(1)} all-gather(bf16[64,1152]{1,0:T(8,128)(2,1)S(1)} %constant_dynamic-update-slice_fusion), channel_id=1, replica_groups=mesh['tm'=64,'chan'=4] {'chan'}, dimensions={0}, use_global_device_ids=true | all-gather | bytes 737280 | tf_op jit(solution)/shard_map/all_gather | solution.py:104
  41.5 3.9 %convolution_convert_fusion = bf16[256,2048]{1,0:T(8,128)(2,1)S(1)} fusion(bf16[256,1152]{0,1:T(8,128)(2,1)S(1)} %bitcast.122, bf16[1152,2048]{0,1:T(8,128)(2,1)} %bitcast.112), kind=kOutput, calls=%fused_computation.30 | convolution fusion | flops 1208483840 | bytes 6356992 | tf_op jit(solution)/shard_map/dot_general | solution.py:61
  46.0 5.0 %convolution_bitcast_fusion = bf16[8,2,4096,128]{2,3,1,0:T(8,128)(2,1)S(1)} fusion(bf16[8,2,256,128]{2,3,1,0:T(8,128)(2,1)S(1)} %bitcast.113, s32[4096]{0:T(1024)S(1)} %pad_add_fusion), kind=kOutput, calls=%fused_computation.9 | convolution fusion | flops 4296015872 | bytes 17842176 | tf_op jit(solution)/shard_map/pc,qrct->qrpt/dot_general | solution.py:75
  51.0 6.4 %fusion.5 = (f32[8,2048]{1,0:T(8,128)S(1)}, f32[8,2048]{1,0:T(8,128)S(1)}, f32[8,2048]{1,0:T(8,128)S(1)}, f32[8,2048]{1,0:T(8,128)S(1)}, f32[8,2048]{1,0:T(8,128...) fusion(bf16[8,2,4096,128]{2,3,1,0:T(8,128)(2,1)S(1)} %convolution_bitcast_fusion), kind=kLoop, calls=%fused_computation.15 | loop fusion | flops 41811968 | bytes 17301504 | tf_op jit(solution)/shard_map/qpt,qpt->qp/dot_general | solution.py:83
  58.6 0.9 copy.72
  59.5 10.4 %all-to-all-start = ((f32[64,1,1024]{2,1,0:T(1,128)}), f32[64,1,1024]{2,1,0:T(1,128)S(1)}, u32[]{:S(2)}, u32[]{:S(2)}) async-start(f32[64,1,1024]{2,1,0:T(1,128)} %copy.72), calls=%async_computation | async-start | bytes 524288 | tf_op jit(solution)/shard_map/all_to_all | solution.py:120
  70.0 0.6 dynamic_slice.3
  70.5 11.8 %all-to-all-done = f32[64,1,1024]{2,1,0:T(1,128)S(1)} async-done(((f32[64,1,1024]{2,1,0:T(1,128)}), f32[64,1,1024]{2,1,0:T(1,128)S(1)}, u32[]{:S(2)}, u32[]{:S(2)}) %all-to-all-start) | async-done | bytes 262176 | tf_op jit(solution)/shard_map/all_to_all | solution.py:120
  82.7 0.7 reshape.391
  83.4 5.4 %all-to-all-start.1 = ((f32[4,1,256]{2,1,0:T(1,128)}), f32[4,1,256]{2,1,0:T(1,128)S(1)}, u32[]{:S(2)}, u32[]{:S(2)}) async-start(f32[4,1,256]{2,1,0:T(1,128)} %reshape.391), calls=%async_computation.1 | async-start | bytes 8192 | tf_op jit(solution)/shard_map/all_to_all | solution.py:122
  88.8 0.7 add_compare_fusion
  89.4 2.4 %all-to-all-done.1 = f32[4,1,256]{2,1,0:T(1,128)S(1)} async-done(((f32[4,1,256]{2,1,0:T(1,128)}), f32[4,1,256]{2,1,0:T(1,128)S(1)}, u32[]{:S(2)}, u32[]{:S(2)}) %all-to-all-start.1) | async-done | bytes 4128 | tf_op jit(solution)/shard_map/all_to_all | solution.py:122
  92.4 0.7 reduce.17
  93.6 0.6 copy.75
  94.2 0.7 fusion.18
  (82 shorter events, 5.8 us)
Async XLA Ops:
  0.6 12.2 %copy-start = (s32[32]{0:T(128)S(1)}, s32[32]{0:T(128)}, u32[]{:S(2)}) copy-start(s32[32]{0:T(128)} %param.6) | copy-start | bytes 388
  1.4 22.4 %collective-permute-start.1 = (bf16[64,128]{1,0:T(8,128)(2,1)S(1)}, bf16[64,128]{1,0:T(8,128)(2,1)S(1)}, u32[]{:S(2)}, u32[]{:S(2)}) collective-permute-start(bf16[64,128]{1,0:T(8,128)(2,1)S(1)} %convert_element_type.67), channel_id=1, source_target_pairs={{0,252},{4,0},{8,4},{12,8},{16,12},{20,16},{24,20},{28,24},{32,28}... | collective-permute-start | bytes 49160 | tf_op jit(solution)/shard_map/ppermute | solution.py:19
  12.7 11.1 %collective-permute-start = (bf16[64,128]{1,0:T(8,128)(2,1)S(1)}, bf16[64,128]{1,0:T(8,128)(2,1)S(1)}, u32[]{:S(2)}, u32[]{:S(2)}) collective-permute-start(bf16[64,128]{1,0:T(8,128)(2,1)S(1)} %convert_element_type.67), channel_id=1, source_target_pairs={{0,4},{4,8},{8,12},{12,16},{16,20},{20,24},{24,28},{28,32},{32,36}... | collective-permute-start | bytes 49160 | tf_op jit(solution)/shard_map/ppermute | solution.py:19
  20.4 2.6 %copy-start.2 = (s32[4,512]{1,0:T(4,128)S(1)}, s32[4,512]{1,0:T(4,128)}, u32[]{:S(2)}) copy-start(s32[4,512]{1,0:T(4,128)} %param.7) | copy-start | bytes 24580
  20.5 3.0 %copy-start.3 = (s32[4,512]{1,0:T(4,128)S(1)}, s32[4,512]{1,0:T(4,128)}, u32[]{:S(2)}) copy-start(s32[4,512]{1,0:T(4,128)} %param.8) | copy-start | bytes 24580
  20.5 10.9 %copy-start.1 = (f32[64,128]{1,0:T(8,128)S(1)}, f32[64,128]{1,0:T(8,128)}, u32[]{:S(2)}) copy-start(f32[64,128]{1,0:T(8,128)} %param.5) | copy-start | bytes 98308
  23.8 7.5 %collective-permute-start.2 = (bf16[64,384]{1,0:T(8,128)(2,1)S(1)}, bf16[64,384]{1,0:T(8,128)(2,1)S(1)}, u32[]{:S(2)}, u32[]{:S(2)}) collective-permute-start(bf16[64,384]{1,0:T(8,128)(2,1)S(1)} %pad_maximum_fusion.2), channel_id=1, source_target_pairs={{0,12},{4,16},{8,20},{12,24},{16,28},{20,32},{24,36},{28,40},{32,4... | collective-permute-start | bytes 147464 | tf_op jit(solution)/shard_map/ppermute | solution.py:19
  23.9 7.5 %collective-permute-start.3 = (bf16[64,384]{1,0:T(8,128)(2,1)S(1)}, bf16[64,384]{1,0:T(8,128)(2,1)S(1)}, u32[]{:S(2)}, u32[]{:S(2)}) collective-permute-start(bf16[64,384]{1,0:T(8,128)(2,1)S(1)} %pad_maximum_fusion.2), channel_id=1, source_target_pairs={{0,244},{4,248},{8,252},{12,0},{16,4},{20,8},{24,12},{28,16},{32,2... | collective-permute-start | bytes 147464 | tf_op jit(solution)/shard_map/ppermute | solution.py:19
  57.4 12.6 %copy-start.4 = (s32[4]{0:T(128)S(1)}, s32[4]{0:T(128)}, u32[]{:S(2)}) copy-start(s32[4]{0:T(128)} %param.9) | copy-start | bytes 52
  59.5 22.8 %all-to-all-start = ((f32[64,1,1024]{2,1,0:T(1,128)}), f32[64,1,1024]{2,1,0:T(1,128)S(1)}, u32[]{:S(2)}, u32[]{:S(2)}) async-start(f32[64,1,1024]{2,1,0:T(1,128)} %copy.72), calls=%async_computation | async-start | bytes 524288 | tf_op jit(solution)/shard_map/all_to_all | solution.py:120
  83.4 8.5 %all-to-all-start.1 = ((f32[4,1,256]{2,1,0:T(1,128)}), f32[4,1,256]{2,1,0:T(1,128)S(1)}, u32[]{:S(2)}, u32[]{:S(2)}) async-start(f32[4,1,256]{2,1,0:T(1,128)} %reshape.391), calls=%async_computation.1 | async-start | bytes 8192 | tf_op jit(solution)/shard_map/all_to_all | solution.py:122

commit v7 on v6

--- a/solution.py
+++ b/solution.py
@@ -117,7 +117,14 @@
     values = sums.shape[1]
     chunk = owner_devices * slots_local
     partial_value = sums.reshape(per_group * values, time_devices, chunk).transpose(1, 0, 2)
-    exchanged = lax.all_to_all(partial_value.reshape(time_devices, -1), "tm", 0, 0, tiled=True)
+    inner = 8
+    outer = time_devices // inner
+    near_groups = [[o * inner + i for i in range(inner)] for o in range(outer)]
+    far_groups = [[o * inner + i for o in range(outer)] for i in range(inner)]
+    staged = partial_value.reshape(outer, inner, -1).transpose(1, 0, 2)
+    staged = lax.all_to_all(staged, "tm", 0, 0, axis_index_groups=near_groups, tiled=True)
+    staged = jnp.sum(staged.reshape(inner, outer, -1), axis=0)
+    exchanged = lax.all_to_all(staged, "tm", 0, 0, axis_index_groups=far_groups, tiled=True)
     summed = jnp.sum(exchanged, axis=0).reshape(per_group, values, owner_devices, slots_local)
     owned = lax.all_to_all(summed, "chan", 2, 0, tiled=True)[:, :, 0, :] / ntime
     slot_index = time_index * slots_local + jnp.arange(slots_local, dtype=jnp.int32)

time: 95.2 us -> 99.5 us (1.045)
  blocking collectives: 8.81 us -> 19.9 us
  waiting for transfers between devices: 15.7 us -> 10.2 us
  starting transfers between devices: 33.2 us -> 31.3 us
    all_to_all x0 -> x1, blocking collectives: none -> 11 us  [shards(): lax.all_to_all(staged, 'tm', 0, 0, axis_index_groups=near_groups, tiled=T...]
    all_to_all x1, waiting for transfers between devices: 11.8 us -> 6.28 us  [shards(): lax.all_to_all(staged, 'tm', 0, 0, axis_index_groups=far_groups, tiled=True)]
    all_to_all x1, starting transfers between devices: 10.4 us -> 7.31 us  [shards(): lax.all_to_all(staged, 'tm', 0, 0, axis_index_groups=far_groups, tiled=True)]
    all_to_all x1, starting transfers between devices: 5.38 us -> 6.68 us  [shards(): owned = lax.all_to_all(summed, 'chan', 2, 0, tiled=True)[:, :, 0, :] / ntime]
  transfers between devices with their start and end apart: 6 -> 6, of which waited for: 3 -> 3; matrix products, arithmetic and copies ran while one was open for 13% -> 12% of each run, Pallas kernels for 0% -> 0%
where the time goes in v7:
time: 99.5 us; the launch traced here: 99.1 us
  starting transfers between devices  31.3 us (31%)
  blocking collectives  19.9 us (20%)
  other arithmetic  16.8 us (17%)
  local copies, waits for them, and re-layouts  10.8 us (11%)
  waiting for transfers between devices  10.2 us (10%)
  matrix products  8.91 us (9%)
  between operations  1.17 us (1%)
    ppermute x4, starting transfers between devices, from_behind(): lax.ppermute(array, axis, [(i, (i + by) % peers) for i in range(peers)])  17.4 us
    all_to_all x1, blocking collectives, shards(): lax.all_to_all(staged, 'tm', 0, 0, axis_index_groups=near_groups, tiled=T...  11 us
    all_gather x1, blocking collectives, shards(): extended = lax.all_gather(wide, 'chan', axis=0, tiled=True)  8.81 us
    all_to_all x1, starting transfers between devices, shards(): lax.all_to_all(staged, 'tm', 0, 0, axis_index_groups=far_groups, tiled=True)  7.31 us
    all_to_all x1, starting transfers between devices, shards(): owned = lax.all_to_all(summed, 'chan', 2, 0, tiled=True)[:, :, 0, :] / ntime  6.68 us
    dot_general x1, other arithmetic, time_sum(): jnp.einsum('qpt,qpt->qp', left, right, preferred_element_type=jnp.float32)  6.37 us
    all_to_all x1, waiting for transfers between devices, shards(): lax.all_to_all(staged, 'tm', 0, 0, axis_index_groups=far_groups, tiled=True)  6.28 us
    dot_general x1, matrix products, pair_sums(): jnp.einsum('pc,qrct->qrpt', pick, parts, preferred_element_type=jnp.bfloa...  4.98 us
  transfers between devices with their start and end apart: 6, of which 3 were waited for; matrix products, arithmetic and copies ran while one was open for 12% of the time, Pallas kernels for 0%

profile of v7, /device:TPU:1, one launch (start us, length us, event | category | flops | bytes accessed | tf_op | source)
XLA Modules:
  0.0 99.1 jit_solution(13675755597468790339)
XLA Ops:
  0.6 0.8 convert_element_type.67
  1.4 11.3 %collective-permute-start.1 = (bf16[64,128]{1,0:T(8,128)(2,1)S(1)}, bf16[64,128]{1,0:T(8,128)(2,1)S(1)}, u32[]{:S(2)}, u32[]{:S(2)}) collective-permute-start(bf16[64,128]{1,0:T(8,128)(2,1)S(1)} %convert_element_type.67), channel_id=1, source_target_pairs={{0,252},{4,0},{8,4},{12,8},{16,12},{20,16},{24,20},{28,24},{32,28}... | collective-permute-start | bytes 49160 | tf_op jit(solution)/shard_map/ppermute | solution.py:19
  12.8 0.6 gather_fusion
  14.1 0.8 broadcast_compare_fusion
  15.0 2.1 %copy.66 = pred[1152,8,1,128]{0,3,2,1:T(8,128)(4,1)S(1)} copy(pred[1152,8,1,128]{3,1,2,0:T(8,128)(4,1)S(1)} %broadcast_compare_fusion) | data formatting | bytes 2359296 | tf_op jit(solution)/shard_map/lt | solution.py:34
  17.1 3.4 %select_convert_fusion.1 = (bf16[1152,8,1,128]{0,3,2,1:T(8,128)(2,1)S(1)}, bf16[1152,8,1,128]{0,3,2,1:T(8,128)(2,1)S(1)}) fusion(pred[1152,8,1,128]{0,3,2,1:T(8,128)(4,1)S(1)} %copy.66, f32[8,128]{1,0:T(8,128)S(1)} %get-tuple-element.42, f32[1152,8]{0,1:T(8,128)S(1)} %get-tuple-element.38, f32[8,128]{1,0:T(8,128)S(1)} %get-tuple-element.41, ...), kind=kLoop, calls=%fused_computation.23 | loop fusion | flops 18874368 | bytes 6570048 | tf_op jit(solution)/shard_map/convert_element_type | solution.py:43
  20.5 2.6 %pad_maximum_fusion = bf16[1152,8,2,128]{0,3,2,1:T(8,128)(2,1)} fusion(bf16[1152,8,1,128]{0,3,2,1:T(8,128)(2,1)S(1)} %get-tuple-element.23, bf16[1152,8,1,128]{0,3,2,1:T(8,128)(2,1)S(1)} %get-tuple-element.22), kind=kLoop, calls=%fused_computation.21 | loop fusion | flops 2359296 | bytes 9437184 | tf_op jit(solution)/shard_map/stack | solution.py:45
  23.9 6.0 %collective-permute-start.3 = (bf16[64,384]{1,0:T(8,128)(2,1)S(1)}, bf16[64,384]{1,0:T(8,128)(2,1)S(1)}, u32[]{:S(2)}, u32[]{:S(2)}) collective-permute-start(bf16[64,384]{1,0:T(8,128)(2,1)S(1)} %pad_maximum_fusion.2), channel_id=1, source_target_pairs={{0,244},{4,248},{8,252},{12,0},{16,4},{20,8},{24,12},{28,16},{32,2... | collective-permute-start | bytes 147464 | tf_op jit(solution)/shard_map/ppermute | solution.py:19
  29.9 1.5 %collective-permute-done.2 = bf16[64,384]{1,0:T(8,128)(2,1)S(1)} collective-permute-done((bf16[64,384]{1,0:T(8,128)(2,1)S(1)}, bf16[64,384]{1,0:T(8,128)(2,1)S(1)}, u32[]{:S(2)}, u32[]{:S(2)}) %collective-permute-start.2) | collective-permute-done | bytes 49184 | tf_op jit(solution)/shard_map/ppermute | solution.py:19
  31.4 8.8 %all_gather.3 = bf16[256,1152]{1,0:T(8,128)(2,1)S(1)} all-gather(bf16[64,1152]{1,0:T(8,128)(2,1)S(1)} %constant_dynamic-update-slice_fusion), channel_id=1, replica_groups=mesh['tm'=64,'chan'=4] {'chan'}, dimensions={0}, use_global_device_ids=true | all-gather | bytes 737280 | tf_op jit(solution)/shard_map/all_gather | solution.py:104
  41.5 3.9 %convolution_convert_fusion = bf16[256,2048]{1,0:T(8,128)(2,1)S(1)} fusion(bf16[256,1152]{0,1:T(8,128)(2,1)S(1)} %bitcast.122, bf16[1152,2048]{0,1:T(8,128)(2,1)} %bitcast.112), kind=kOutput, calls=%fused_computation.30 | convolution fusion | flops 1208483840 | bytes 6356992 | tf_op jit(solution)/shard_map/dot_general | solution.py:61
  46.0 5.0 %convolution_bitcast_fusion = bf16[8,2,4096,128]{2,3,1,0:T(8,128)(2,1)S(1)} fusion(bf16[8,2,256,128]{2,3,1,0:T(8,128)(2,1)S(1)} %bitcast.113, s32[4096]{0:T(1024)S(1)} %pad_add_fusion), kind=kOutput, calls=%fused_computation.9 | convolution fusion | flops 4296015872 | bytes 17842176 | tf_op jit(solution)/shard_map/pc,qrct->qrpt/dot_general | solution.py:75
  51.0 6.4 %fusion.5 = (f32[8,2048]{1,0:T(8,128)S(1)}, f32[8,2048]{1,0:T(8,128)S(1)}, f32[8,2048]{1,0:T(8,128)S(1)}, f32[8,2048]{1,0:T(8,128)S(1)}, f32[8,2048]{1,0:T(8,128...) fusion(bf16[8,2,4096,128]{2,3,1,0:T(8,128)(2,1)S(1)} %convolution_bitcast_fusion), kind=kLoop, calls=%fused_computation.15 | loop fusion | flops 41811968 | bytes 17301504 | tf_op jit(solution)/shard_map/qpt,qpt->qp/dot_general | solution.py:83
  59.6 11.0 %all_to_all.23 = f32[8,8,1024]{2,1,0:T(8,128)S(1)} all-to-all(f32[8,8,1024]{2,1,0:T(8,128)S(1)} %copy.72), channel_id=1, replica_groups={{0,4,8,12,16,20,24,28},{32,36,40,44,48,52,56,60},{64,68,72,76,80,84,88,..., dimensions={0} | all-to-all | bytes 524288 | tf_op jit(solution)/shard_map/all_to_all | solution.py:125
  70.6 0.6 all_to_all.17
  71.3 7.3 %all-to-all-start.1 = ((f32[8,1,1024]{2,1,0:T(1,128)}), f32[8,1,1024]{2,1,0:T(1,128)S(1)}, u32[]{:S(2)}, u32[]{:S(2)}) async-start(f32[8,1,1024]{2,1,0:T(1,128)} %all_to_all.17), calls=%async_computation.1 | async-start | bytes 65536 | tf_op jit(solution)/shard_map/all_to_all | solution.py:127
  79.2 6.3 %all-to-all-done.1 = f32[8,1,1024]{2,1,0:T(1,128)S(1)} async-done(((f32[8,1,1024]{2,1,0:T(1,128)}), f32[8,1,1024]{2,1,0:T(1,128)S(1)}, u32[]{:S(2)}, u32[]{:S(2)}) %all-to-all-start.1) | async-done | bytes 32800 | tf_op jit(solution)/shard_map/all_to_all | solution.py:127
  85.6 0.7 reshape.393
  86.3 6.7 %all-to-all-start.2 = ((f32[4,1,256]{2,1,0:T(1,128)}), f32[4,1,256]{2,1,0:T(1,128)S(1)}, u32[]{:S(2)}, u32[]{:S(2)}) async-start(f32[4,1,256]{2,1,0:T(1,128)} %reshape.393), calls=%async_computation.2 | async-start | bytes 8192 | tf_op jit(solution)/shard_map/all_to_all | solution.py:129
  93.0 0.7 add_compare_fusion
  93.7 2.4 %all-to-all-done.2 = f32[4,1,256]{2,1,0:T(1,128)S(1)} async-done(((f32[4,1,256]{2,1,0:T(1,128)}), f32[4,1,256]{2,1,0:T(1,128)S(1)}, u32[]{:S(2)}, u32[]{:S(2)}) %all-to-all-start.2) | async-done | bytes 4128 | tf_op jit(solution)/shard_map/all_to_all | solution.py:129
  96.6 0.7 reduce.17
  97.8 0.6 copy.75
  98.5 0.7 fusion.18
  (86 shorter events, 7.2 us)
Async XLA Ops:
  0.6 12.2 %copy-start = (s32[32]{0:T(128)S(1)}, s32[32]{0:T(128)}, u32[]{:S(2)}) copy-start(s32[32]{0:T(128)} %param.6) | copy-start | bytes 388
  1.4 22.4 %collective-permute-start.1 = (bf16[64,128]{1,0:T(8,128)(2,1)S(1)}, bf16[64,128]{1,0:T(8,128)(2,1)S(1)}, u32[]{:S(2)}, u32[]{:S(2)}) collective-permute-start(bf16[64,128]{1,0:T(8,128)(2,1)S(1)} %convert_element_type.67), channel_id=1, source_target_pairs={{0,252},{4,0},{8,4},{12,8},{16,12},{20,16},{24,20},{28,24},{32,28}... | collective-permute-start | bytes 49160 | tf_op jit(solution)/shard_map/ppermute | solution.py:19
  12.7 11.1 %collective-permute-start = (bf16[64,128]{1,0:T(8,128)(2,1)S(1)}, bf16[64,128]{1,0:T(8,128)(2,1)S(1)}, u32[]{:S(2)}, u32[]{:S(2)}) collective-permute-start(bf16[64,128]{1,0:T(8,128)(2,1)S(1)} %convert_element_type.67), channel_id=1, source_target_pairs={{0,4},{4,8},{8,12},{12,16},{16,20},{20,24},{24,28},{28,32},{32,36}... | collective-permute-start | bytes 49160 | tf_op jit(solution)/shard_map/ppermute | solution.py:19
  20.4 2.6 %copy-start.2 = (s32[4,512]{1,0:T(4,128)S(1)}, s32[4,512]{1,0:T(4,128)}, u32[]{:S(2)}) copy-start(s32[4,512]{1,0:T(4,128)} %param.7) | copy-start | bytes 24580
  20.5 3.0 %copy-start.3 = (s32[4,512]{1,0:T(4,128)S(1)}, s32[4,512]{1,0:T(4,128)}, u32[]{:S(2)}) copy-start(s32[4,512]{1,0:T(4,128)} %param.8) | copy-start | bytes 24580
  20.5 10.9 %copy-start.1 = (f32[64,128]{1,0:T(8,128)S(1)}, f32[64,128]{1,0:T(8,128)}, u32[]{:S(2)}) copy-start(f32[64,128]{1,0:T(8,128)} %param.5) | copy-start | bytes 98308
  23.8 7.5 %collective-permute-start.2 = (bf16[64,384]{1,0:T(8,128)(2,1)S(1)}, bf16[64,384]{1,0:T(8,128)(2,1)S(1)}, u32[]{:S(2)}, u32[]{:S(2)}) collective-permute-start(bf16[64,384]{1,0:T(8,128)(2,1)S(1)} %pad_maximum_fusion.2), channel_id=1, source_target_pairs={{0,12},{4,16},{8,20},{12,24},{16,28},{20,32},{24,36},{28,40},{32,4... | collective-permute-start | bytes 147464 | tf_op jit(solution)/shard_map/ppermute | solution.py:19
  23.9 7.5 %collective-permute-start.3 = (bf16[64,384]{1,0:T(8,128)(2,1)S(1)}, bf16[64,384]{1,0:T(8,128)(2,1)S(1)}, u32[]{:S(2)}, u32[]{:S(2)}) collective-permute-start(bf16[64,384]{1,0:T(8,128)(2,1)S(1)} %pad_maximum_fusion.2), channel_id=1, source_target_pairs={{0,244},{4,248},{8,252},{12,0},{16,4},{20,8},{24,12},{28,16},{32,2... | collective-permute-start | bytes 147464 | tf_op jit(solution)/shard_map/ppermute | solution.py:19
  57.4 21.2 %copy-start.4 = (s32[4]{0:T(128)S(1)}, s32[4]{0:T(128)}, u32[]{:S(2)}) copy-start(s32[4]{0:T(128)} %param.9) | copy-start | bytes 52
  71.3 14.2 %all-to-all-start.1 = ((f32[8,1,1024]{2,1,0:T(1,128)}), f32[8,1,1024]{2,1,0:T(1,128)S(1)}, u32[]{:S(2)}, u32[]{:S(2)}) async-start(f32[8,1,1024]{2,1,0:T(1,128)} %all_to_all.17), calls=%async_computation.1 | async-start | bytes 65536 | tf_op jit(solution)/shard_map/all_to_all | solution.py:127
  86.3 9.8 %all-to-all-start.2 = ((f32[4,1,256]{2,1,0:T(1,128)}), f32[4,1,256]{2,1,0:T(1,128)S(1)}, u32[]{:S(2)}, u32[]{:S(2)}) async-start(f32[4,1,256]{2,1,0:T(1,128)} %reshape.393), calls=%async_computation.2 | async-start | bytes 8192 | tf_op jit(solution)/shard_map/all_to_all | solution.py:129

commit v8 on v6

--- a/solution.py
+++ b/solution.py
@@ -46,22 +46,13 @@
     return table.reshape(taps, -1)
 
 
-def wavelet_band(extended, scale_ids, reaches, offsets, time_span):
+def band_coefficients(extended, scale_ids, reaches, offsets):
     channels = extended.shape[0]
-    blocks = time_span // BLK
-    centre = 4 * time_span // BLK
-    tap_blocks = 2 * offsets + 1
-    pieces = [
-        extended[:, (centre + offset_step) * BLK : (centre + offset_step) * BLK + time_span]
-        for offset_step in range(-offsets, offsets + 1)
-    ]
-    unfolded = jnp.stack(pieces, axis=1).reshape(channels, tap_blocks, blocks, BLK)
-    unfolded = unfolded.transpose(0, 2, 1, 3).reshape(channels * blocks, tap_blocks * BLK)
     table = kernel_table(scale_ids, reaches, offsets)
-    coefficients = jnp.dot(unfolded, table, preferred_element_type=jnp.float32)
+    coefficients = jnp.dot(extended, table, preferred_element_type=jnp.float32)
     scale_count = scale_ids.shape[0]
-    coefficients = coefficients.astype(jnp.bfloat16).reshape(channels, blocks, scale_count, 2, BLK)
-    return coefficients.transpose(2, 3, 0, 1, 4).reshape(scale_count, 2 * channels, time_span)
+    coefficients = coefficients.astype(jnp.bfloat16).reshape(channels, scale_count, 2, BLK)
+    return coefficients.transpose(1, 2, 0, 3).reshape(scale_count, 2 * channels, BLK)
 
 
 def pair_sums(coefficients, first_flat, second_flat):
@@ -97,29 +88,48 @@
     time_span = signal.shape[1]
     ntime = time_span * time_devices
     rounded = signal.astype(jnp.bfloat16)
+    gathered = lax.all_gather(rounded, "chan", axis=0, tiled=True)
     near = jnp.concatenate(
-        [from_behind(rounded, "tm", 1), rounded, from_behind(rounded, "tm", -1)], axis=1
+        [from_behind(gathered, "tm", 1), gathered, from_behind(gathered, "tm", -1)], axis=1
     )
     wide = jnp.concatenate([from_behind(near, "tm", 3), near, from_behind(near, "tm", -3)], axis=1)
-    extended = lax.all_gather(wide, "chan", axis=0, tiled=True)
     per_group = NS // groups
-    scale_ids = cluster_number * per_group + jnp.arange(per_group, dtype=jnp.int32)
-    coefficients = wavelet_band(
-        extended, scale_ids, support[scale_ids], 4 * time_span // BLK, time_span
-    )
+    band = NS // 4
+    narrow_count = (NS - band) // groups
+    wide_count = band // groups
+    narrow_ids = cluster_number * narrow_count + jnp.arange(narrow_count, dtype=jnp.int32)
+    wide_ids = NS - band + cluster_number * wide_count + jnp.arange(wide_count, dtype=jnp.int32)
+    narrow_coefficients = band_coefficients(near, narrow_ids, support[narrow_ids], 1)
+    wide_coefficients = band_coefficients(wide, wide_ids, support[wide_ids], 4)
     owner_devices, slots_total = pair_first.shape
     slots_local = slots_total // time_devices
 
     def by_block(pairs):
         return pairs.reshape(owner_devices, time_devices, slots_local).transpose(1, 0, 2).reshape(-1)
 
-    sums = pair_sums(coefficients, by_block(pair_first), by_block(pair_second))
+    first_flat = by_block(pair_first)
+    second_flat = by_block(pair_second)
+    sums = jnp.concatenate(
+        [
+            pair_sums(narrow_coefficients, first_flat, second_flat),
+            pair_sums(wide_coefficients, first_flat, second_flat),
+        ],
+        axis=0,
+    )
     values = sums.shape[1]
     chunk = owner_devices * slots_local
     partial_value = sums.reshape(per_group * values, time_devices, chunk).transpose(1, 0, 2)
     exchanged = lax.all_to_all(partial_value.reshape(time_devices, -1), "tm", 0, 0, tiled=True)
     summed = jnp.sum(exchanged, axis=0).reshape(per_group, values, owner_devices, slots_local)
     owned = lax.all_to_all(summed, "chan", 2, 0, tiled=True)[:, :, 0, :] / ntime
+    owned = owned.reshape(groups, per_group, values, slots_local)
+    owned = jnp.concatenate(
+        [
+            owned[:, :narrow_count].reshape(groups * narrow_count, values, slots_local),
+            owned[:, narrow_count:].reshape(groups * wide_count, values, slots_local),
+        ],
+        axis=0,
+    )
     slot_index = time_index * slots_local + jnp.arange(slots_local, dtype=jnp.int32)
     alive_mask = slot_index < pair_count[cluster_number]
     cross_real = owned[:, 0, :].T

time: 95.2 us -> 102 us (1.071)
  other arithmetic: 17 us -> 29.6 us
  matrix products: 8.91 us -> 6.66 us
  starting transfers between devices: 33.2 us -> 31 us
  waiting for transfers between devices: 15.7 us -> 13.7 us
    convert_element_type x1 -> x2, other arithmetic: 3.35 us -> 13.2 us  [kernel_table(): jnp.where(inside, amplitude * cos_part, 0.0).astype(jnp.bfloat16)]
    ppermute x4, starting transfers between devices: 17.4 us -> 11.5 us  [from_behind(): lax.ppermute(array, axis, [(i, (i + by) % peers) for i in range(peers)])]
    dot_general x1 -> x2, matrix products: 3.92 us -> 1.06 us  [band_coefficients(): coefficients = jnp.dot(extended, table, preferred_element_type=jnp.float32)]
    another operation x1 -> x2, other arithmetic: 2.59 us -> 5.4 us  [kernel_table(): table = jnp.stack([real_part, imag_part], axis=2)]
    all_to_all x1, starting transfers between devices: 10.4 us -> 12.8 us  [shards(): lax.all_to_all(partial_value.reshape(time_devices, -1), 'tm', 0, 0, tiled...]
    lt x1 -> x0, local copies, waits for them, and re-layouts: 2.08 us -> none  [kernel_table(): inside = jnp.abs(offset) < (reaches * BLK)[None, :, None]]
    reshape x1 -> x6, local copies, waits for them, and re-layouts: 0.52 us -> 2.33 us  [the longest x2 1.78 us: kernel_table(): return table.reshape(taps, -1)]
    ppermute x4, waiting for transfers between devices: 1.48 us -> 0.01 us  [from_behind(): lax.ppermute(array, axis, [(i, (i + by) % peers) for i in range(peers)])]
  transfers between devices with their start and end apart: 6 -> 6, of which waited for: 3 -> 2; matrix products, arithmetic and copies ran while one was open for 13% -> 36% of each run, Pallas kernels for 0% -> 0%
where the time goes in v8:
time: 102 us; the launch traced here: 101 us
  starting transfers between devices  31 us (30%)
  other arithmetic  29.6 us (29%)
  waiting for transfers between devices  13.7 us (13%)
  local copies, waits for them, and re-layouts  10.7 us (10%)
  blocking collectives  8.3 us (8%)
  matrix products  6.66 us (7%)
  between operations  1.27 us (1%)
    convert_element_type x2, other arithmetic, kernel_table(): jnp.where(inside, amplitude * cos_part, 0.0).astype(jnp.bfloat16)  13.2 us
    all_to_all x1, starting transfers between devices, shards(): lax.all_to_all(partial_value.reshape(time_devices, -1), 'tm', 0, 0, tiled...  12.8 us
    ppermute x4, starting transfers between devices, from_behind(): lax.ppermute(array, axis, [(i, (i + by) % peers) for i in range(peers)])  11.5 us
    all_to_all x1, waiting for transfers between devices, shards(): lax.all_to_all(partial_value.reshape(time_devices, -1), 'tm', 0, 0, tiled...  11.2 us
    all_gather x1, blocking collectives, shards(): gathered = lax.all_gather(rounded, 'chan', axis=0, tiled=True)  8.3 us
    all_to_all x1, starting transfers between devices, shards(): owned = lax.all_to_all(summed, 'chan', 2, 0, tiled=True)[:, :, 0, :] / ntime  6.73 us
    dot_general x2, other arithmetic, time_sum(): jnp.einsum('qpt,qpt->qp', left, right, preferred_element_type=jnp.float32)  6.52 us
    dot_general x2, matrix products, pair_sums(): jnp.einsum('pc,qrct->qrpt', pick, parts, preferred_element_type=jnp.bfloa...  5.6 us
  transfers between devices with their start and end apart: 6, of which 2 were waited for; matrix products, arithmetic and copies ran while one was open for 36% of the time, Pallas kernels for 0%

profile of v8, /device:TPU:1, one launch (start us, length us, event | category | flops | bytes accessed | tf_op | source)
XLA Modules:
  0.0 101.3 jit_solution(7255642394409297598)
XLA Ops:
  0.7 0.8 convert_element_type.127
  1.4 8.3 %all_gather.3 = bf16[256,128]{1,0:T(8,128)(2,1)S(1)} all-gather(bf16[64,128]{1,0:T(8,128)(2,1)S(1)} %convert_element_type.127), channel_id=1, replica_groups=mesh['tm'=64,'chan'=4] {'chan'}, dimensions={0}, use_global_device_ids=true | all-gather | bytes 81920 | tf_op jit(solution)/shard_map/all_gather | solution.py:91
  9.7 8.8 %collective-permute-start.1 = (bf16[256,128]{1,0:T(8,128)(2,1)S(1)}, bf16[256,128]{1,0:T(8,128)(2,1)S(1)}, u32[]{:S(2)}, u32[]{:S(2)}) collective-permute-start(bf16[256,128]{1,0:T(8,128)(2,1)S(1)} %all_gather.3), channel_id=1, source_target_pairs={{0,252},{4,0},{8,4},{12,8},{16,12},{20,16},{24,20},{28,24},{32,28}... | collective-permute-start | bytes 196616 | tf_op jit(solution)/shard_map/ppermute | solution.py:19
  19.3 0.6 gather_fusion
  22.4 6.7 %fusion.27 = (bf16[1152,2,1,128]{3,2,1,0:T(2,128)(2,1)S(1)}, bf16[1152,2,1,128]{3,2,1,0:T(2,128)(2,1)S(1)}) fusion(f32[2,128]{1,0:T(2,128)S(1)} %get-tuple-element.43, f32[1152,2]{1,0:T(8,128)S(1)} %copy.36, f32[2,128]{1,0:T(2,128)S(1)} %get-tuple-element.42, f32[1152,2]{1,0:T(8,128)S(1)} %copy.35, s32[1152,128]{1,0:T(8,128)S(1)} %get-tuple-element.35, ...), kind=kLoop, calls=%fused_computation.58 | loop fusion | flops 5013504 | bytes 2379800 | tf_op jit(solution)/shard_map/convert_element_type | solution.py:43
  29.2 2.7 %pad_maximum_fusion.1 = bf16[1152,2,2,128]{3,2,1,0:T(2,128)(2,1)S(1)} fusion(bf16[1152,2,1,128]{3,2,1,0:T(2,128)(2,1)S(1)} %get-tuple-element.27, bf16[1152,2,1,128]{3,2,1,0:T(2,128)(2,1)S(1)} %get-tuple-element.26), kind=kLoop, calls=%fused_computation.61 | loop fusion | flops 2359296 | bytes 2359296 | tf_op jit(solution)/shard_map/stack | solution.py:45
  31.9 1.3 %reshape.640 = bf16[1152,512]{1,0:T(8,128)(2,1)} reshape(bf16[1152,2,2,128]{3,2,1,0:T(2,128)(2,1)S(1)} %pad_maximum_fusion.1) | data formatting | bytes 2359296 | tf_op jit(solution)/shard_map/reshape | solution.py:46
  33.2 6.5 %fusion.25 = (bf16[384,6,1,128]{3,2,1,0:T(2,128)(2,1)S(1)}, bf16[384,6,1,128]{3,2,1,0:T(2,128)(2,1)S(1)}) fusion(f32[6,128]{1,0:T(8,128)S(1)} %get-tuple-element.41, f32[384,6]{1,0:T(8,128)S(1)} %copy.31, f32[6,128]{1,0:T(8,128)S(1)} %get-tuple-element.40, f32[384,6]{1,0:T(8,128)S(1)} %copy.30, s32[384,128]{1,0:T(8,128)S(1)} %get-tuple-element.39, ...), kind=kLoop, calls=%fused_computation.56 | loop fusion | flops 5013504 | bytes 1597512 | tf_op jit(solution)/shard_map/convert_element_type | solution.py:43
  39.7 2.7 %pad_maximum_fusion = bf16[384,6,2,128]{3,2,1,0:T(2,128)(2,1)S(1)} fusion(bf16[384,6,1,128]{3,2,1,0:T(2,128)(2,1)S(1)} %get-tuple-element.29, bf16[384,6,1,128]{3,2,1,0:T(2,128)(2,1)S(1)} %get-tuple-element.28), kind=kLoop, calls=%fused_computation.60 | loop fusion | flops 2359296 | bytes 2359296 | tf_op jit(solution)/shard_map/stack | solution.py:45
  43.1 2.7 %collective-permute-start.2 = (bf16[256,384]{1,0:T(8,128)(2,1)S(1)}, bf16[256,384]{1,0:T(8,128)(2,1)}, u32[]{:S(2)}, u32[]{:S(2)}) collective-permute-start(bf16[256,384]{1,0:T(8,128)(2,1)S(1)} %constant_dynamic-update-slice_fusion), channel_id=1, source_target_pairs={{0,12},{4,16},{8,20},{12,24},{16,28},{20,32},{24,36},{28,40},{32,4... | collective-permute-start | bytes 589832 | tf_op jit(solution)/shard_map/ppermute | solution.py:19
  46.6 3.9 %convolution_bitcast_fusion = bf16[6,2,4096,128]{2,3,1,0:T(8,128)(2,1)S(1)} fusion(bf16[6,2,256,128]{2,3,1,0:T(8,128)(2,1)S(1)} %bitcast.143, s32[4096]{0:T(1024)S(1)} %pad_add_fusion), kind=kOutput, calls=%fused_computation.10 | convolution fusion | flops 3222274048 | bytes 13385728 | tf_op jit(solution)/shard_map/pc,qrct->qrpt/dot_general | solution.py:66
  50.5 4.8 %fusion.5 = (f32[6,2048]{1,0:T(8,128)S(1)}, f32[6,2048]{1,0:T(8,128)S(1)}, f32[6,2048]{1,0:T(8,128)S(1)}, f32[6,2048]{1,0:T(8,128)S(1)}, f32[6,2048]{1,0:T(8,128...) fusion(bf16[6,2,4096,128]{2,3,1,0:T(8,128)(2,1)S(1)} %convolution_bitcast_fusion), kind=kLoop, calls=%fused_computation.16 | loop fusion | flops 31358976 | bytes 12976128 | tf_op jit(solution)/shard_map/qpt,qpt->qp/dot_general | solution.py:74
  55.6 1.0 %constant_dynamic-update-slice_fusion.7 = bf16[256,1152]{1,0:T(8,128)(2,1)S(1)} fusion(bf16[256,384]{1,0:T(8,128)(2,1)} %collective-permute-done.2), kind=kLoop, calls=%fused_computation.82 | loop fusion | bytes 393216
  57.4 1.7 %convolution_bitcast_fusion.1 = bf16[2,2,4096,128]{2,3,1,0:T(8,128)(2,1)S(1)} fusion(bf16[2,2,256,128]{2,3,1,0:T(8,128)(2,1)S(1)} %bitcast.145, s32[4096]{0:T(1024)S(1)} %pad_add_fusion), kind=kOutput, calls=%fused_computation.19 | convolution fusion | flops 1074790400 | bytes 4472832 | tf_op jit(solution)/shard_map/pc,qrct->qrpt/dot_general | solution.py:66
  59.2 1.7 %fusion.16 = (f32[2,2048]{1,0:T(2,128)S(1)}, f32[2,2048]{1,0:T(2,128)S(1)}, f32[2,2048]{1,0:T(2,128)S(1)}, f32[2,2048]{1,0:T(2,128)S(1)}, f32[2,2048]{1,0:T(2,12...) fusion(bf16[2,2,4096,128]{2,3,1,0:T(8,128)(2,1)S(1)} %convolution_bitcast_fusion.1), kind=kLoop, calls=%fused_computation.44 | loop fusion | flops 10452992 | bytes 4325376 | tf_op jit(solution)/shard_map/qpt,qpt->qp/dot_general | solution.py:74
  62.0 0.9 copy.39
  62.8 12.8 %all-to-all-start = ((f32[64,1,1024]{2,1,0:T(1,128)}), f32[64,1,1024]{2,1,0:T(1,128)S(1)}, u32[]{:S(2)}, u32[]{:S(2)}) async-start(f32[64,1,1024]{2,1,0:T(1,128)} %copy.39), calls=%async_computation | async-start | bytes 524288 | tf_op jit(solution)/shard_map/all_to_all | solution.py:122
  76.2 11.2 %all-to-all-done = f32[64,1,1024]{2,1,0:T(1,128)S(1)} async-done(((f32[64,1,1024]{2,1,0:T(1,128)}), f32[64,1,1024]{2,1,0:T(1,128)S(1)}, u32[]{:S(2)}, u32[]{:S(2)}) %all-to-all-start) | async-done | bytes 262176 | tf_op jit(solution)/shard_map/all_to_all | solution.py:122
  87.8 0.7 reshape.703
  88.5 6.7 %all-to-all-start.1 = ((f32[4,1,256]{2,1,0:T(1,128)}), f32[4,1,256]{2,1,0:T(1,128)S(1)}, u32[]{:S(2)}, u32[]{:S(2)}) async-start(f32[4,1,256]{2,1,0:T(1,128)} %reshape.703), calls=%async_computation.1 | async-start | bytes 8192 | tf_op jit(solution)/shard_map/all_to_all | solution.py:124
  95.2 0.7 add_compare_fusion
  95.9 2.4 %all-to-all-done.1 = f32[4,1,256]{2,1,0:T(1,128)S(1)} async-done(((f32[4,1,256]{2,1,0:T(1,128)}), f32[4,1,256]{2,1,0:T(1,128)S(1)}, u32[]{:S(2)}, u32[]{:S(2)}) %all-to-all-start.1) | async-done | bytes 4128 | tf_op jit(solution)/shard_map/all_to_all | solution.py:124
  98.8 0.7 reduce.33
  99.9 0.7 select_bitcast_fusion
  (91 shorter events, 9.0 us)
Async XLA Ops:
  0.6 18.0 %copy-start = (s32[32]{0:T(128)S(1)}, s32[32]{0:T(128)}, u32[]{:S(2)}) copy-start(s32[32]{0:T(128)} %param.6) | copy-start | bytes 388
  0.6 19.9 %copy-start.2 = (s32[4,512]{1,0:T(4,128)S(1)}, s32[4,512]{1,0:T(4,128)}, u32[]{:S(2)}) copy-start(s32[4,512]{1,0:T(4,128)} %param.7) | copy-start | bytes 24580
  0.7 20.2 %copy-start.3 = (s32[4,512]{1,0:T(4,128)S(1)}, s32[4,512]{1,0:T(4,128)}, u32[]{:S(2)}) copy-start(s32[4,512]{1,0:T(4,128)} %param.8) | copy-start | bytes 24580
  9.7 33.2 %collective-permute-start.1 = (bf16[256,128]{1,0:T(8,128)(2,1)S(1)}, bf16[256,128]{1,0:T(8,128)(2,1)S(1)}, u32[]{:S(2)}, u32[]{:S(2)}) collective-permute-start(bf16[256,128]{1,0:T(8,128)(2,1)S(1)} %all_gather.3), channel_id=1, source_target_pairs={{0,252},{4,0},{8,4},{12,8},{16,12},{20,16},{24,20},{28,24},{32,28}... | collective-permute-start | bytes 196616 | tf_op jit(solution)/shard_map/ppermute | solution.py:19
  18.5 24.4 %collective-permute-start = (bf16[256,128]{1,0:T(8,128)(2,1)S(1)}, bf16[256,128]{1,0:T(8,128)(2,1)S(1)}, u32[]{:S(2)}, u32[]{:S(2)}) collective-permute-start(bf16[256,128]{1,0:T(8,128)(2,1)S(1)} %all_gather.3), channel_id=1, source_target_pairs={{0,4},{4,8},{8,12},{12,16},{16,20},{20,24},{24,28},{28,32},{32,36}... | collective-permute-start | bytes 196616 | tf_op jit(solution)/shard_map/ppermute | solution.py:19
  43.0 13.7 %collective-permute-start.3 = (bf16[256,384]{1,0:T(8,128)(2,1)S(1)}, bf16[256,384]{1,0:T(8,128)(2,1)S(1)}, u32[]{:S(2)}, u32[]{:S(2)}) collective-permute-start(bf16[256,384]{1,0:T(8,128)(2,1)S(1)} %constant_dynamic-update-slice_fusion), channel_id=1, source_target_pairs={{0,244},{4,248},{8,252},{12,0},{16,4},{20,8},{24,12},{28,16},{32,2... | collective-permute-start | bytes 589832 | tf_op jit(solution)/shard_map/ppermute | solution.py:19
  43.1 12.5 %collective-permute-start.2 = (bf16[256,384]{1,0:T(8,128)(2,1)S(1)}, bf16[256,384]{1,0:T(8,128)(2,1)}, u32[]{:S(2)}, u32[]{:S(2)}) collective-permute-start(bf16[256,384]{1,0:T(8,128)(2,1)S(1)} %constant_dynamic-update-slice_fusion), channel_id=1, source_target_pairs={{0,12},{4,16},{8,20},{12,24},{16,28},{20,32},{24,36},{28,40},{32,4... | collective-permute-start | bytes 589832 | tf_op jit(solution)/shard_map/ppermute | solution.py:19
  55.3 1.4 %copy-start.1 = (bf16[1152,512]{1,0:T(8,128)(2,1)S(1)}, bf16[1152,512]{1,0:T(8,128)(2,1)}, u32[]{:S(2)}) copy-start(bf16[1152,512]{1,0:T(8,128)(2,1)} %reshape.640) | copy-start | bytes 3538948
  61.6 14.0 %copy-start.4 = (s32[4]{0:T(128)S(1)}, s32[4]{0:T(128)}, u32[]{:S(2)}) copy-start(s32[4]{0:T(128)} %param.9) | copy-start | bytes 52
  62.8 24.6 %all-to-all-start = ((f32[64,1,1024]{2,1,0:T(1,128)}), f32[64,1,1024]{2,1,0:T(1,128)S(1)}, u32[]{:S(2)}, u32[]{:S(2)}) async-start(f32[64,1,1024]{2,1,0:T(1,128)} %copy.39), calls=%async_computation | async-start | bytes 524288 | tf_op jit(solution)/shard_map/all_to_all | solution.py:122
  88.5 9.8 %all-to-all-start.1 = ((f32[4,1,256]{2,1,0:T(1,128)}), f32[4,1,256]{2,1,0:T(1,128)S(1)}, u32[]{:S(2)}, u32[]{:S(2)}) async-start(f32[4,1,256]{2,1,0:T(1,128)} %reshape.703), calls=%async_computation.1 | async-start | bytes 8192 | tf_op jit(solution)/shard_map/all_to_all | solution.py:124

commit v9 on v8

--- a/solution.py
+++ b/solution.py
@@ -24,35 +24,30 @@
     lag = jnp.arange(taps, dtype=jnp.int32) - offsets * BLK
     within = jnp.arange(BLK, dtype=jnp.int32)
     scale_width = 2.0 * TD * jnp.exp2((scale_ids - (NS - 1)).astype(jnp.float32) / 4.0)
-    offset = lag[:, None, None] - within[None, None, :]
-    scaled_offset = offset.astype(jnp.float32) / scale_width[None, :, None]
-    amplitude = (
-        math.pi ** (-0.25)
-        * lax.rsqrt(scale_width)[None, :, None]
-        * jnp.exp(-0.5 * scaled_offset * scaled_offset)
-    )
-    inside = jnp.abs(offset) < (reaches * BLK)[None, :, None]
-    lag_phase = 6.0 * (lag.astype(jnp.float32)[:, None] / scale_width[None, :])
+    width = scale_width[:, None, None]
+    offset = lag[None, :, None] - within[None, None, :]
+    scaled_offset = offset.astype(jnp.float32) / width
+    amplitude = math.pi ** (-0.25) * lax.rsqrt(width) * jnp.exp(-0.5 * scaled_offset * scaled_offset)
+    inside = jnp.abs(offset) < (reaches * BLK)[:, None, None]
+    lag_phase = 6.0 * (lag.astype(jnp.float32)[None, :] / scale_width[:, None])
     time_phase = 6.0 * (within.astype(jnp.float32)[None, :] / scale_width[:, None])
     lag_cos = jnp.cos(lag_phase)[:, :, None]
     lag_sin = jnp.sin(lag_phase)[:, :, None]
-    time_cos = jnp.cos(time_phase)[None]
-    time_sin = jnp.sin(time_phase)[None]
+    time_cos = jnp.cos(time_phase)[:, None, :]
+    time_sin = jnp.sin(time_phase)[:, None, :]
     cos_part = lag_cos * time_cos + lag_sin * time_sin
     sin_part = lag_sin * time_cos - lag_cos * time_sin
     real_part = jnp.where(inside, amplitude * cos_part, 0.0).astype(jnp.bfloat16)
     imag_part = jnp.where(inside, amplitude * sin_part, 0.0).astype(jnp.bfloat16)
-    table = jnp.stack([real_part, imag_part], axis=2)
-    return table.reshape(taps, -1)
+    return jnp.stack([real_part, imag_part], axis=1)
 
 
 def band_coefficients(extended, scale_ids, reaches, offsets):
     channels = extended.shape[0]
     table = kernel_table(scale_ids, reaches, offsets)
-    coefficients = jnp.dot(extended, table, preferred_element_type=jnp.float32)
+    coefficients = jnp.einsum("cm,qrmt->qrct", extended, table, preferred_element_type=jnp.float32)
     scale_count = scale_ids.shape[0]
-    coefficients = coefficients.astype(jnp.bfloat16).reshape(channels, scale_count, 2, BLK)
-    return coefficients.transpose(1, 2, 0, 3).reshape(scale_count, 2 * channels, BLK)
+    return coefficients.astype(jnp.bfloat16).reshape(scale_count, 2 * channels, BLK)
 
 
 def pair_sums(coefficients, first_flat, second_flat):

time: 102 us -> 90.8 us (0.89)
  other arithmetic: 29.6 us -> 16.8 us
  matrix products: 6.66 us -> 12.8 us
  starting transfers between devices: 31 us -> 26.9 us
  waiting for transfers between devices: 13.7 us -> 17.8 us
  local copies, waits for them, and re-layouts: 10.7 us -> 6.76 us
    convert_element_type x2, other arithmetic: 13.2 us -> 1.75 us  [kernel_table(): jnp.where(inside, amplitude * cos_part, 0.0).astype(jnp.bfloat16)]
    dot_general x2, matrix products: 5.6 us -> 12.8 us  [pair_sums(): jnp.einsum('pc,qrct->qrpt', pick, parts, preferred_element_type=jnp.bfloa...]
    another operation x2 -> x0, other arithmetic: 5.4 us -> none  [kernel_table(): table = jnp.stack([real_part, imag_part], axis=2)]
    dot_general x2, other arithmetic: 6.52 us -> 10.8 us  [time_sum(): jnp.einsum('qpt,qpt->qp', left, right, preferred_element_type=jnp.float32)]
    ppermute x4, waiting for transfers between devices: 0.01 us -> 4.14 us  [from_behind(): lax.ppermute(array, axis, [(i, (i + by) % peers) for i in range(peers)])]
    all_to_all x1, starting transfers between devices: 12.8 us -> 8.65 us  [shards(): lax.all_to_all(partial_value.reshape(time_devices, -1), 'tm', 0, 0, tiled...]
    reshape x4 -> x0, local copies, waits for them, and re-layouts: 2.18 us -> none  [the longest x2 1.78 us: kernel_table(): return table.reshape(taps, -1)]
    dot_general x2 -> x0, matrix products: 1.06 us -> none  [band_coefficients(): coefficients = jnp.dot(extended, table, preferred_element_type=jnp.float32)]
  transfers between devices with their start and end apart: 6 -> 6, of which waited for: 2 -> 3; matrix products, arithmetic and copies ran while one was open for 36% -> 24% of each run, Pallas kernels for 0% -> 0%
where the time goes in v9:
time: 90.8 us; the launch traced here: 90.5 us
  starting transfers between devices  26.9 us (30%)
  waiting for transfers between devices  17.8 us (20%)
  other arithmetic  16.8 us (19%)
  matrix products  12.8 us (14%)
  blocking collectives  8.3 us (9%)
  local copies, waits for them, and re-layouts  6.76 us (7%)
  between operations  1.16 us (1%)
    dot_general x2, matrix products, pair_sums(): jnp.einsum('pc,qrct->qrpt', pick, parts, preferred_element_type=jnp.bfloa...  12.8 us
    ppermute x4, starting transfers between devices, from_behind(): lax.ppermute(array, axis, [(i, (i + by) % peers) for i in range(peers)])  11.5 us
    all_to_all x1, waiting for transfers between devices, shards(): lax.all_to_all(partial_value.reshape(time_devices, -1), 'tm', 0, 0, tiled...  11.2 us
    dot_general x2, other arithmetic, time_sum(): jnp.einsum('qpt,qpt->qp', left, right, preferred_element_type=jnp.float32)  10.8 us
    all_to_all x1, starting transfers between devices, shards(): lax.all_to_all(partial_value.reshape(time_devices, -1), 'tm', 0, 0, tiled...  8.65 us
    all_gather x1, blocking collectives, shards(): gathered = lax.all_gather(rounded, 'chan', axis=0, tiled=True)  8.3 us
    all_to_all x1, starting transfers between devices, shards(): owned = lax.all_to_all(summed, 'chan', 2, 0, tiled=True)[:, :, 0, :] / ntime  6.74 us
    ppermute x4, waiting for transfers between devices, from_behind(): lax.ppermute(array, axis, [(i, (i + by) % peers) for i in range(peers)])  4.14 us
  transfers between devices with their start and end apart: 6, of which 3 were waited for; matrix products, arithmetic and copies ran while one was open for 24% of the time, Pallas kernels for 0%

profile of v9, /device:TPU:1, one launch (start us, length us, event | category | flops | bytes accessed | tf_op | source)
XLA Modules:
  0.0 90.5 jit_solution(12996117347685383360)
XLA Ops:
  0.7 0.8 convert_element_type.131
  1.4 8.3 %all_gather.3 = bf16[256,128]{1,0:T(8,128)(2,1)S(1)} all-gather(bf16[64,128]{1,0:T(8,128)(2,1)S(1)} %convert_element_type.131), channel_id=1, replica_groups=mesh['tm'=64,'chan'=4] {'chan'}, dimensions={0}, use_global_device_ids=true | all-gather | bytes 81920 | tf_op jit(solution)/shard_map/all_gather | solution.py:86
  9.7 8.8 %collective-permute-start.1 = (bf16[256,128]{1,0:T(8,128)(2,1)S(1)}, bf16[256,128]{1,0:T(8,128)(2,1)S(1)}, u32[]{:S(2)}, u32[]{:S(2)}) collective-permute-start(bf16[256,128]{1,0:T(8,128)(2,1)S(1)} %all_gather.3), channel_id=1, source_target_pairs={{0,252},{4,0},{8,4},{12,8},{16,12},{20,16},{24,20},{28,24},{32,28}... | collective-permute-start | bytes 196616 | tf_op jit(solution)/shard_map/ppermute | solution.py:19
  18.6 0.6 gather_fusion.1
  19.3 0.6 gather_fusion
  21.4 0.8 fusion.26
  22.2 0.9 %fusion.28 = (bf16[2,1,1152,128]{2,3,1,0:T(8,128)(2,1)S(1)}, bf16[2,1,1152,128]{2,3,1,0:T(8,128)(2,1)S(1)}) fusion(f32[2,128]{1,0:T(2,128)S(1)} %get-tuple-element.41, f32[2,1152]{1,0:T(2,128)S(1)} %get-tuple-element.31, f32[2,128]{1,0:T(2,128)S(1)} %get-tuple-element.40, f32[2,1152]{1,0:T(2,128)S(1)} %get-tuple-element.30, f32[2]{0:T(128)S(1)} %get-tuple-element.43, ...), kind=kLoop, calls=%fused_computation.59 | loop fusion | flops 5013504 | bytes 2379800 | tf_op jit(solution)/shard_map/convert_element_type | solution.py:40
  23.2 4.1 %collective-permute-done = bf16[256,128]{1,0:T(8,128)(2,1)S(1)} collective-permute-done((bf16[256,128]{1,0:T(8,128)(2,1)S(1)}, bf16[256,128]{1,0:T(8,128)(2,1)S(1)}, u32[]{:S(2)}, u32[]{:S(2)}) %collective-permute-start) | collective-permute-done | bytes 65568 | tf_op jit(solution)/shard_map/ppermute | solution.py:19
  27.5 2.7 %collective-permute-start.2 = (bf16[256,384]{1,0:T(8,128)(2,1)S(1)}, bf16[256,384]{1,0:T(8,128)(2,1)S(1)}, u32[]{:S(2)}, u32[]{:S(2)}) collective-permute-start(bf16[256,384]{1,0:T(8,128)(2,1)S(1)} %constant_dynamic-update-slice_fusion), channel_id=1, source_target_pairs={{0,12},{4,16},{8,20},{12,24},{16,28},{20,32},{24,36},{28,40},{32,4... | collective-permute-start | bytes 589832 | tf_op jit(solution)/shard_map/ppermute | solution.py:19
  30.2 8.2 %convolution_bitcast_fusion = bf16[6,2,4096,128]{2,3,1,0:T(8,128)(2,1)} fusion(s32[4096]{0:T(1024)S(1)} %pad_add_fusion, bf16[6,1,384,128]{2,3,1,0:T(8,128)(2,1)S(1)} %get-tuple-element.27, bf16[6,1,384,128]{2,3,1,0:T(8,128)(2,1)S(1)} %get-tuple-element.26, bf16[256,384]{1,0:T(8,128)(2,1)S(1)} %constant_dynamic-update-slice_fusion), kind=kOutput, calls=%fused_computation.10 | convolution fusion | flops 3525246976 | bytes 13975552 | tf_op jit(solution)/shard_map/pc,qrct->qrpt/dot_general | solution.py:61
  38.4 7.6 %fusion.5 = (f32[6,2048]{1,0:T(8,128)S(1)}, f32[6,2048]{1,0:T(8,128)S(1)}, f32[6,2048]{1,0:T(8,128)S(1)}, f32[6,2048]{1,0:T(8,128)S(1)}, f32[6,2048]{1,0:T(8,128...) fusion(bf16[6,2,4096,128]{2,3,1,0:T(8,128)(2,1)} %convolution_bitcast_fusion), kind=kLoop, calls=%fused_computation.16 | loop fusion | flops 31358976 | bytes 12976128 | tf_op jit(solution)/shard_map/qpt,qpt->qp/dot_general | solution.py:69
  46.4 4.6 %convolution_bitcast_fusion.1 = bf16[2,2,4096,128]{2,3,1,0:T(8,128)(2,1)} fusion(s32[4096]{0:T(1024)S(1)} %pad_add_fusion, bf16[2,1,1152,128]{2,3,1,0:T(8,128)(2,1)S(1)} %get-tuple-element.25, bf16[2,1,1152,128]{2,3,1,0:T(8,128)(2,1)S(1)} %get-tuple-element.24, bf16[256,1152]{1,0:T(8,128)(2,1)S(1)} %constant_dynamic-update-slice_fusion.3), kind=kOutput, calls=%fused_computation.19 | convolution fusion | flops 1377501184 | bytes 5980160 | tf_op jit(solution)/shard_map/pc,qrct->qrpt/dot_general | solution.py:61
  51.0 3.2 %fusion.16 = (f32[2,2048]{1,0:T(2,128)S(1)}, f32[2,2048]{1,0:T(2,128)S(1)}, f32[2,2048]{1,0:T(2,128)S(1)}, f32[2,2048]{1,0:T(2,128)S(1)}, f32[2,2048]{1,0:T(2,12...) fusion(bf16[2,2,4096,128]{2,3,1,0:T(8,128)(2,1)} %convolution_bitcast_fusion.1), kind=kLoop, calls=%fused_computation.39 | loop fusion | flops 10452992 | bytes 4325376 | tf_op jit(solution)/shard_map/qpt,qpt->qp/dot_general | solution.py:69
  55.3 0.9 copy.18
  56.2 8.6 %all-to-all-start = ((f32[64,1,1024]{2,1,0:T(1,128)}), f32[64,1,1024]{2,1,0:T(1,128)S(1)}, u32[]{:S(2)}, u32[]{:S(2)}) async-start(f32[64,1,1024]{2,1,0:T(1,128)} %copy.18), calls=%async_computation | async-start | bytes 524288 | tf_op jit(solution)/shard_map/all_to_all | solution.py:117
  64.8 0.6 dynamic_slice.3
  65.4 11.2 %all-to-all-done = f32[64,1,1024]{2,1,0:T(1,128)S(1)} async-done(((f32[64,1,1024]{2,1,0:T(1,128)}), f32[64,1,1024]{2,1,0:T(1,128)S(1)}, u32[]{:S(2)}, u32[]{:S(2)}) %all-to-all-start) | async-done | bytes 262176 | tf_op jit(solution)/shard_map/all_to_all | solution.py:117
  77.0 0.7 reshape.661
  77.7 6.7 %all-to-all-start.1 = ((f32[4,1,256]{2,1,0:T(1,128)}), f32[4,1,256]{2,1,0:T(1,128)S(1)}, u32[]{:S(2)}, u32[]{:S(2)}) async-start(f32[4,1,256]{2,1,0:T(1,128)} %reshape.661), calls=%async_computation.1 | async-start | bytes 8192 | tf_op jit(solution)/shard_map/all_to_all | solution.py:119
  84.5 0.7 add_compare_fusion
  85.1 2.4 %all-to-all-done.1 = f32[4,1,256]{2,1,0:T(1,128)S(1)} async-done(((f32[4,1,256]{2,1,0:T(1,128)}), f32[4,1,256]{2,1,0:T(1,128)S(1)}, u32[]{:S(2)}, u32[]{:S(2)}) %all-to-all-start.1) | async-done | bytes 4128 | tf_op jit(solution)/shard_map/all_to_all | solution.py:119
  88.1 0.7 reduce.33
  89.2 0.7 select_bitcast_fusion
  89.9 0.6 copy.23
  (77 shorter events, 4.3 us)
Async XLA Ops:
  0.6 18.0 %copy-start = (s32[32]{0:T(128)S(1)}, s32[32]{0:T(128)}, u32[]{:S(2)}) copy-start(s32[32]{0:T(128)} %param.6) | copy-start | bytes 388
  0.6 19.9 %copy-start.1 = (s32[4,512]{1,0:T(4,128)S(1)}, s32[4,512]{1,0:T(4,128)}, u32[]{:S(2)}) copy-start(s32[4,512]{1,0:T(4,128)} %param.7) | copy-start | bytes 24580
  0.7 20.2 %copy-start.2 = (s32[4,512]{1,0:T(4,128)S(1)}, s32[4,512]{1,0:T(4,128)}, u32[]{:S(2)}) copy-start(s32[4,512]{1,0:T(4,128)} %param.8) | copy-start | bytes 24580
  9.7 17.6 %collective-permute-start.1 = (bf16[256,128]{1,0:T(8,128)(2,1)S(1)}, bf16[256,128]{1,0:T(8,128)(2,1)S(1)}, u32[]{:S(2)}, u32[]{:S(2)}) collective-permute-start(bf16[256,128]{1,0:T(8,128)(2,1)S(1)} %all_gather.3), channel_id=1, source_target_pairs={{0,252},{4,0},{8,4},{12,8},{16,12},{20,16},{24,20},{28,24},{32,28}... | collective-permute-start | bytes 196616 | tf_op jit(solution)/shard_map/ppermute | solution.py:19
  18.5 8.8 %collective-permute-start = (bf16[256,128]{1,0:T(8,128)(2,1)S(1)}, bf16[256,128]{1,0:T(8,128)(2,1)S(1)}, u32[]{:S(2)}, u32[]{:S(2)}) collective-permute-start(bf16[256,128]{1,0:T(8,128)(2,1)S(1)} %all_gather.3), channel_id=1, source_target_pairs={{0,4},{4,8},{8,12},{12,16},{16,20},{20,24},{24,28},{28,32},{32,36}... | collective-permute-start | bytes 196616 | tf_op jit(solution)/shard_map/ppermute | solution.py:19
  27.4 18.9 %collective-permute-start.3 = (bf16[256,384]{1,0:T(8,128)(2,1)S(1)}, bf16[256,384]{1,0:T(8,128)(2,1)S(1)}, u32[]{:S(2)}, u32[]{:S(2)}) collective-permute-start(bf16[256,384]{1,0:T(8,128)(2,1)S(1)} %constant_dynamic-update-slice_fusion), channel_id=1, source_target_pairs={{0,244},{4,248},{8,252},{12,0},{16,4},{20,8},{24,12},{28,16},{32,2... | collective-permute-start | bytes 589832 | tf_op jit(solution)/shard_map/ppermute | solution.py:19
  27.5 18.7 %collective-permute-start.2 = (bf16[256,384]{1,0:T(8,128)(2,1)S(1)}, bf16[256,384]{1,0:T(8,128)(2,1)S(1)}, u32[]{:S(2)}, u32[]{:S(2)}) collective-permute-start(bf16[256,384]{1,0:T(8,128)(2,1)S(1)} %constant_dynamic-update-slice_fusion), channel_id=1, source_target_pairs={{0,12},{4,16},{8,20},{12,24},{16,28},{20,32},{24,36},{28,40},{32,4... | collective-permute-start | bytes 589832 | tf_op jit(solution)/shard_map/ppermute | solution.py:19
  55.0 9.9 %copy-start.3 = (s32[4]{0:T(128)S(1)}, s32[4]{0:T(128)}, u32[]{:S(2)}) copy-start(s32[4]{0:T(128)} %param.9) | copy-start | bytes 52
  56.2 20.5 %all-to-all-start = ((f32[64,1,1024]{2,1,0:T(1,128)}), f32[64,1,1024]{2,1,0:T(1,128)S(1)}, u32[]{:S(2)}, u32[]{:S(2)}) async-start(f32[64,1,1024]{2,1,0:T(1,128)} %copy.18), calls=%async_computation | async-start | bytes 524288 | tf_op jit(solution)/shard_map/all_to_all | solution.py:117
  77.7 9.8 %all-to-all-start.1 = ((f32[4,1,256]{2,1,0:T(1,128)}), f32[4,1,256]{2,1,0:T(1,128)S(1)}, u32[]{:S(2)}, u32[]{:S(2)}) async-start(f32[4,1,256]{2,1,0:T(1,128)} %reshape.661), calls=%async_computation.1 | async-start | bytes 8192 | tf_op jit(solution)/shard_map/all_to_all | solution.py:119

commit v10 on v9

--- a/solution.py
+++ b/solution.py
@@ -112,11 +112,13 @@
         axis=0,
     )
     values = sums.shape[1]
-    chunk = owner_devices * slots_local
-    partial_value = sums.reshape(per_group * values, time_devices, chunk).transpose(1, 0, 2)
-    exchanged = lax.all_to_all(partial_value.reshape(time_devices, -1), "tm", 0, 0, tiled=True)
-    summed = jnp.sum(exchanged, axis=0).reshape(per_group, values, owner_devices, slots_local)
-    owned = lax.all_to_all(summed, "chan", 2, 0, tiled=True)[:, :, 0, :] / ntime
+    destinations = time_devices * groups
+    partial_value = sums.reshape(per_group * values, destinations, slots_local).transpose(1, 0, 2)
+    exchanged = lax.all_to_all(
+        partial_value.reshape(destinations, -1), ("tm", "chan"), 0, 0, tiled=True
+    )
+    exchanged = exchanged.reshape(time_devices, groups, per_group, values, slots_local)
+    owned = jnp.sum(exchanged, axis=0) / ntime
     owned = owned.reshape(groups, per_group, values, slots_local)
     owned = jnp.concatenate(
         [

time: 90.8 us -> 98.9 us (1.089)
  local copies, waits for them, and re-layouts: 6.76 us -> 17.2 us
  starting transfers between devices: 26.9 us -> 21.3 us
  other arithmetic: 16.8 us -> 19.8 us
    reshape x3 -> x2, local copies, waits for them, and re-layouts: 0.49 us -> 9.86 us  [the longest x1 6.27 us: shards(): exchanged.reshape(time_devices, groups, per_group, values, slots_local)]
    all_to_all x2 -> x1, starting transfers between devices: 15.4 us -> 9.82 us  [shards(): lax.all_to_all(partial_value.reshape(destinations, -1), ('tm', 'chan'), 0...]
    reduce_sum x1, other arithmetic: 0.18 us -> 3.21 us  [shards(): owned = jnp.sum(exchanged, axis=0) / ntime]
    transpose x1, local copies, waits for them, and re-layouts: 0.32 us -> 2.8 us  [shards(): sums.reshape(per_group * values, destinations, slots_local)]
    all_to_all x2 -> x1, waiting for transfers between devices: 13.7 us -> 14 us  [shards(): lax.all_to_all(partial_value.reshape(destinations, -1), ('tm', 'chan'), 0...]
  transfers between devices with their start and end apart: 6 -> 5, of which waited for: 3 -> 2; matrix products, arithmetic and copies ran while one was open for 24% -> 22% of each run, Pallas kernels for 0% -> 0%
where the time goes in v10:
time: 98.9 us; the launch traced here: 98.6 us
  starting transfers between devices  21.3 us (22%)
  other arithmetic  19.8 us (20%)
  waiting for transfers between devices  18.1 us (18%)
  local copies, waits for them, and re-layouts  17.2 us (17%)
  matrix products  12.8 us (13%)
  blocking collectives  8.3 us (8%)
  between operations  1.12 us (1%)
    all_to_all x1, waiting for transfers between devices, shards(): lax.all_to_all(partial_value.reshape(destinations, -1), ('tm', 'chan'), 0...  14 us
    dot_general x2, matrix products, pair_sums(): jnp.einsum('pc,qrct->qrpt', pick, parts, preferred_element_type=jnp.bfloa...  12.8 us
    ppermute x4, starting transfers between devices, from_behind(): lax.ppermute(array, axis, [(i, (i + by) % peers) for i in range(peers)])  11.5 us
    dot_general x2, other arithmetic, time_sum(): jnp.einsum('qpt,qpt->qp', left, right, preferred_element_type=jnp.float32)  10.8 us
    all_to_all x1, starting transfers between devices, shards(): lax.all_to_all(partial_value.reshape(destinations, -1), ('tm', 'chan'), 0...  9.82 us
    all_gather x1, blocking collectives, shards(): gathered = lax.all_gather(rounded, 'chan', axis=0, tiled=True)  8.3 us
    reshape x1, local copies, waits for them, and re-layouts, shards(): exchanged.reshape(time_devices, groups, per_group, values, slots_local)  6.27 us
    ppermute x4, waiting for transfers between devices, from_behind(): lax.ppermute(array, axis, [(i, (i + by) % peers) for i in range(peers)])  4.14 us
  transfers between devices with their start and end apart: 5, of which 2 were waited for; matrix products, arithmetic and copies ran while one was open for 22% of the time, Pallas kernels for 0%

profile of v10, /device:TPU:1, one launch (start us, length us, event | category | flops | bytes accessed | tf_op | source)
XLA Modules:
  0.0 98.6 jit_solution(17687745876509681182)
XLA Ops:
  0.7 0.8 convert_element_type.131
  1.4 8.3 %all_gather.3 = bf16[256,128]{1,0:T(8,128)(2,1)S(1)} all-gather(bf16[64,128]{1,0:T(8,128)(2,1)S(1)} %convert_element_type.131), channel_id=1, replica_groups=mesh['tm'=64,'chan'=4] {'chan'}, dimensions={0}, use_global_device_ids=true | all-gather | bytes 81920 | tf_op jit(solution)/shard_map/all_gather | solution.py:86
  9.7 8.8 %collective-permute-start.1 = (bf16[256,128]{1,0:T(8,128)(2,1)S(1)}, bf16[256,128]{1,0:T(8,128)(2,1)S(1)}, u32[]{:S(2)}, u32[]{:S(2)}) collective-permute-start(bf16[256,128]{1,0:T(8,128)(2,1)S(1)} %all_gather.3), channel_id=1, source_target_pairs={{0,252},{4,0},{8,4},{12,8},{16,12},{20,16},{24,20},{28,24},{32,28}... | collective-permute-start | bytes 196616 | tf_op jit(solution)/shard_map/ppermute | solution.py:19
  18.6 0.6 gather_fusion.1
  19.3 0.6 gather_fusion
  21.4 0.8 fusion.26
  22.2 0.9 fusion.28
  23.2 4.1 %collective-permute-done = bf16[256,128]{1,0:T(8,128)(2,1)S(1)} collective-permute-done((bf16[256,128]{1,0:T(8,128)(2,1)S(1)}, bf16[256,128]{1,0:T(8,128)(2,1)S(1)}, u32[]{:S(2)}, u32[]{:S(2)}) %collective-permute-start) | collective-permute-done | bytes 65568 | tf_op jit(solution)/shard_map/ppermute | solution.py:19
  27.5 2.7 %collective-permute-start.2 = (bf16[256,384]{1,0:T(8,128)(2,1)S(1)}, bf16[256,384]{1,0:T(8,128)(2,1)S(1)}, u32[]{:S(2)}, u32[]{:S(2)}) collective-permute-start(bf16[256,384]{1,0:T(8,128)(2,1)S(1)} %constant_dynamic-update-slice_fusion), channel_id=1, source_target_pairs={{0,12},{4,16},{8,20},{12,24},{16,28},{20,32},{24,36},{28,40},{32,4... | collective-permute-start | bytes 589832 | tf_op jit(solution)/shard_map/ppermute | solution.py:19
  30.2 8.2 %convolution_bitcast_fusion = bf16[6,2,4096,128]{2,3,1,0:T(8,128)(2,1)} fusion(s32[4096]{0:T(1024)S(1)} %pad_add_fusion, bf16[6,1,384,128]{2,3,1,0:T(8,128)(2,1)S(1)} %get-tuple-element.27, bf16[6,1,384,128]{2,3,1,0:T(8,128)(2,1)S(1)} %get-tuple-element.26, bf16[256,384]{1,0:T(8,128)(2,1)S(1)} %constant_dynamic-update-slice_fusion), kind=kOutput, calls=%fused_computation.10 | convolution fusion | flops 3525246976 | bytes 13975552 | tf_op jit(solution)/shard_map/pc,qrct->qrpt/dot_general | solution.py:61
  38.4 7.6 %fusion.5 = (f32[6,2048]{1,0:T(8,128)S(1)}, f32[6,2048]{1,0:T(8,128)S(1)}, f32[6,2048]{1,0:T(8,128)S(1)}, f32[6,2048]{1,0:T(8,128)S(1)}, f32[6,2048]{1,0:T(8,128...) fusion(bf16[6,2,4096,128]{2,3,1,0:T(8,128)(2,1)} %convolution_bitcast_fusion), kind=kLoop, calls=%fused_computation.16 | loop fusion | flops 31358976 | bytes 12976128 | tf_op jit(solution)/shard_map/qpt,qpt->qp/dot_general | solution.py:69
  46.4 4.6 %convolution_bitcast_fusion.1 = bf16[2,2,4096,128]{2,3,1,0:T(8,128)(2,1)} fusion(s32[4096]{0:T(1024)S(1)} %pad_add_fusion, bf16[2,1,1152,128]{2,3,1,0:T(8,128)(2,1)S(1)} %get-tuple-element.25, bf16[2,1,1152,128]{2,3,1,0:T(8,128)(2,1)S(1)} %get-tuple-element.24, bf16[256,1152]{1,0:T(8,128)(2,1)S(1)} %constant_dynamic-update-slice_fusion.3), kind=kOutput, calls=%fused_computation.19 | convolution fusion | flops 1377501184 | bytes 5980160 | tf_op jit(solution)/shard_map/pc,qrct->qrpt/dot_general | solution.py:61
  51.0 3.2 %fusion.16 = (f32[2,2048]{1,0:T(2,128)S(1)}, f32[2,2048]{1,0:T(2,128)S(1)}, f32[2,2048]{1,0:T(2,128)S(1)}, f32[2,2048]{1,0:T(2,128)S(1)}, f32[2,2048]{1,0:T(2,12...) fusion(bf16[2,2,4096,128]{2,3,1,0:T(8,128)(2,1)} %convolution_bitcast_fusion.1), kind=kLoop, calls=%fused_computation.39 | loop fusion | flops 10452992 | bytes 4325376 | tf_op jit(solution)/shard_map/qpt,qpt->qp/dot_general | solution.py:69
  54.6 3.6 %reshape.592 = f32[32,256,8]{2,1,0:T(8,128)} reshape(f32[8,4,2048]{2,1,0:T(4,128)S(1)} %maximum_maximum_fusion) | data formatting | bytes 524288 | tf_op jit(solution)/shard_map/reshape | solution.py:116
  58.2 2.8 %copy.17 = f32[256,32,8]{0,2,1:T(8,128)S(1)} copy(f32[256,32,8]{2,0,1:T(8,128)} %bitcast.139) | data formatting | bytes 524288 | tf_op jit(solution)/shard_map/transpose | solution.py:116
  61.0 0.8 copy.18
  61.8 9.8 %all-to-all-start = ((f32[256,1,256]{2,1,0:T(1,128)}), f32[256,1,256]{2,1,0:T(1,128)S(1)}, u32[]{:S(2)}, u32[]{:S(2)}) async-start(f32[256,1,256]{2,1,0:T(1,128)} %copy.18), calls=%async_computation | async-start | bytes 524288 | tf_op jit(solution)/shard_map/all_to_all | solution.py:117
  72.3 0.7 add_compare_fusion
  72.9 14.0 %all-to-all-done = f32[256,1,256]{2,1,0:T(1,128)S(1)} async-done(((f32[256,1,256]{2,1,0:T(1,128)}), f32[256,1,256]{2,1,0:T(1,128)S(1)}, u32[]{:S(2)}, u32[]{:S(2)}) %all-to-all-start) | async-done | bytes 262176 | tf_op jit(solution)/shard_map/all_to_all | solution.py:117
  86.9 0.6 reduce.16
  87.5 6.3 %reshape.593 = f32[64,4,8,4,8]{4,3,2,1,0:T(4,128)} reshape(f32[256,256]{1,0:T(8,128)S(1)} %reduce.16) | data formatting | bytes 524288 | tf_op jit(solution)/shard_map/reshape | solution.py:120
  93.8 3.2 %reduce_sum.9 = f32[4,8,4,8]{3,2,1,0:T(4,128)S(1)} reduce(f32[64,4,8,4,8]{4,3,2,1,0:T(4,128)} %reshape.593, f32[]{:T(128)} %constant.14.clone.1), dimensions={0}, to_apply=%region_0.1 | reduce | flops 64512 | bytes 266244 | tf_op jit(solution)/shard_map/reduce_sum | solution.py:121
  97.3 0.7 select_bitcast_fusion
  98.0 0.6 copy.22
  (71 shorter events, 3.2 us)
Async XLA Ops:
  0.6 18.0 %copy-start = (s32[32]{0:T(128)S(1)}, s32[32]{0:T(128)}, u32[]{:S(2)}) copy-start(s32[32]{0:T(128)} %param.6) | copy-start | bytes 388
  0.6 19.9 %copy-start.1 = (s32[4,512]{1,0:T(4,128)S(1)}, s32[4,512]{1,0:T(4,128)}, u32[]{:S(2)}) copy-start(s32[4,512]{1,0:T(4,128)} %param.7) | copy-start | bytes 24580
  0.7 20.2 %copy-start.2 = (s32[4,512]{1,0:T(4,128)S(1)}, s32[4,512]{1,0:T(4,128)}, u32[]{:S(2)}) copy-start(s32[4,512]{1,0:T(4,128)} %param.8) | copy-start | bytes 24580
  9.7 17.6 %collective-permute-start.1 = (bf16[256,128]{1,0:T(8,128)(2,1)S(1)}, bf16[256,128]{1,0:T(8,128)(2,1)S(1)}, u32[]{:S(2)}, u32[]{:S(2)}) collective-permute-start(bf16[256,128]{1,0:T(8,128)(2,1)S(1)} %all_gather.3), channel_id=1, source_target_pairs={{0,252},{4,0},{8,4},{12,8},{16,12},{20,16},{24,20},{28,24},{32,28}... | collective-permute-start | bytes 196616 | tf_op jit(solution)/shard_map/ppermute | solution.py:19
  18.5 8.8 %collective-permute-start = (bf16[256,128]{1,0:T(8,128)(2,1)S(1)}, bf16[256,128]{1,0:T(8,128)(2,1)S(1)}, u32[]{:S(2)}, u32[]{:S(2)}) collective-permute-start(bf16[256,128]{1,0:T(8,128)(2,1)S(1)} %all_gather.3), channel_id=1, source_target_pairs={{0,4},{4,8},{8,12},{12,16},{16,20},{20,24},{24,28},{28,32},{32,36}... | collective-permute-start | bytes 196616 | tf_op jit(solution)/shard_map/ppermute | solution.py:19
  27.4 18.9 %collective-permute-start.3 = (bf16[256,384]{1,0:T(8,128)(2,1)S(1)}, bf16[256,384]{1,0:T(8,128)(2,1)S(1)}, u32[]{:S(2)}, u32[]{:S(2)}) collective-permute-start(bf16[256,384]{1,0:T(8,128)(2,1)S(1)} %constant_dynamic-update-slice_fusion), channel_id=1, source_target_pairs={{0,244},{4,248},{8,252},{12,0},{16,4},{20,8},{24,12},{28,16},{32,2... | collective-permute-start | bytes 589832 | tf_op jit(solution)/shard_map/ppermute | solution.py:19
  27.5 18.7 %collective-permute-start.2 = (bf16[256,384]{1,0:T(8,128)(2,1)S(1)}, bf16[256,384]{1,0:T(8,128)(2,1)S(1)}, u32[]{:S(2)}, u32[]{:S(2)}) collective-permute-start(bf16[256,384]{1,0:T(8,128)(2,1)S(1)} %constant_dynamic-update-slice_fusion), channel_id=1, source_target_pairs={{0,12},{4,16},{8,20},{12,24},{16,28},{20,32},{24,36},{28,40},{32,4... | collective-permute-start | bytes 589832 | tf_op jit(solution)/shard_map/ppermute | solution.py:19
  58.2 13.5 %copy-start.3 = (s32[4]{0:T(128)S(1)}, s32[4]{0:T(128)}, u32[]{:S(2)}) copy-start(s32[4]{0:T(128)} %param.9) | copy-start | bytes 52
  61.8 25.1 %all-to-all-start = ((f32[256,1,256]{2,1,0:T(1,128)}), f32[256,1,256]{2,1,0:T(1,128)S(1)}, u32[]{:S(2)}, u32[]{:S(2)}) async-start(f32[256,1,256]{2,1,0:T(1,128)} %copy.18), calls=%async_computation | async-start | bytes 524288 | tf_op jit(solution)/shard_map/all_to_all | solution.py:117

commit v11 on v10

--- a/solution.py
+++ b/solution.py
@@ -113,12 +113,10 @@
     )
     values = sums.shape[1]
     destinations = time_devices * groups
-    partial_value = sums.reshape(per_group * values, destinations, slots_local).transpose(1, 0, 2)
-    exchanged = lax.all_to_all(
-        partial_value.reshape(destinations, -1), ("tm", "chan"), 0, 0, tiled=True
-    )
-    exchanged = exchanged.reshape(time_devices, groups, per_group, values, slots_local)
-    owned = jnp.sum(exchanged, axis=0) / ntime
+    partial_value = sums.reshape(per_group * values, -1).T.reshape(destinations, -1)
+    exchanged = lax.all_to_all(partial_value, ("tm", "chan"), 0, 0, tiled=True)
+    summed = jnp.sum(exchanged.reshape(time_devices, groups, -1), axis=0)
+    owned = summed.reshape(groups, slots_local, per_group, values).transpose(0, 2, 3, 1) / ntime
     owned = owned.reshape(groups, per_group, values, slots_local)
     owned = jnp.concatenate(
         [

time: 98.9 us -> 84.5 us (0.85)
  local copies, waits for them, and re-layouts: 17.2 us -> 6 us
  other arithmetic: 19.8 us -> 16.6 us
    reshape x2, local copies, waits for them, and re-layouts: 9.86 us -> 0.17 us  [the longest x1 0.09 us: shards(): sums.reshape(per_group * values, -1).T.reshape(destinations, -1)]
    reduce_sum x1, other arithmetic: 3.21 us -> 0.09 us  [shards(): summed = jnp.sum(exchanged.reshape(time_devices, groups, -1), axis=0)]
    transpose x1, local copies, waits for them, and re-layouts: 2.8 us -> 0.33 us  [shards(): sums.reshape(per_group * values, -1).T.reshape(destinations, -1)]
  transfers between devices with their start and end apart: 5 -> 5, of which waited for: 2 -> 2; matrix products, arithmetic and copies ran while one was open for 22% -> 26% of each run, Pallas kernels for 0% -> 0%
where the time goes in v11:
time: 84.5 us; the launch traced here: 84.3 us
  starting transfers between devices  21.3 us (25%)
  waiting for transfers between devices  18.1 us (21%)
  other arithmetic  16.6 us (20%)
  matrix products  12.8 us (15%)
  blocking collectives  8.3 us (10%)
  local copies, waits for them, and re-layouts  6 us (7%)
  between operations  1.14 us (1%)
    all_to_all x1, waiting for transfers between devices, shards(): exchanged = lax.all_to_all(partial_value, ('tm', 'chan'), 0, 0, tiled=True)  14 us
    dot_general x2, matrix products, pair_sums(): jnp.einsum('pc,qrct->qrpt', pick, parts, preferred_element_type=jnp.bfloa...  12.8 us
    ppermute x4, starting transfers between devices, from_behind(): lax.ppermute(array, axis, [(i, (i + by) % peers) for i in range(peers)])  11.5 us
    dot_general x2, other arithmetic, time_sum(): jnp.einsum('qpt,qpt->qp', left, right, preferred_element_type=jnp.float32)  10.8 us
    all_to_all x1, starting transfers between devices, shards(): exchanged = lax.all_to_all(partial_value, ('tm', 'chan'), 0, 0, tiled=True)  9.81 us
    all_gather x1, blocking collectives, shards(): gathered = lax.all_gather(rounded, 'chan', axis=0, tiled=True)  8.3 us
    ppermute x4, waiting for transfers between devices, from_behind(): lax.ppermute(array, axis, [(i, (i + by) % peers) for i in range(peers)])  4.14 us
    convert_element_type x2, other arithmetic, kernel_table(): jnp.where(inside, amplitude * cos_part, 0.0).astype(jnp.bfloat16)  1.75 us
  transfers between devices with their start and end apart: 5, of which 2 were waited for; matrix products, arithmetic and copies ran while one was open for 26% of the time, Pallas kernels for 0%

profile of v11, /device:TPU:1, one launch (start us, length us, event | category | flops | bytes accessed | tf_op | source)
XLA Modules:
  0.0 84.3 jit_solution(4402259715803642357)
XLA Ops:
  0.7 0.8 convert_element_type.131
  1.4 8.3 %all_gather.3 = bf16[256,128]{1,0:T(8,128)(2,1)S(1)} all-gather(bf16[64,128]{1,0:T(8,128)(2,1)S(1)} %convert_element_type.131), channel_id=1, replica_groups=mesh['tm'=64,'chan'=4] {'chan'}, dimensions={0}, use_global_device_ids=true | all-gather | bytes 81920 | tf_op jit(solution)/shard_map/all_gather | solution.py:86
  9.7 8.8 %collective-permute-start.1 = (bf16[256,128]{1,0:T(8,128)(2,1)S(1)}, bf16[256,128]{1,0:T(8,128)(2,1)S(1)}, u32[]{:S(2)}, u32[]{:S(2)}) collective-permute-start(bf16[256,128]{1,0:T(8,128)(2,1)S(1)} %all_gather.3), channel_id=1, source_target_pairs={{0,252},{4,0},{8,4},{12,8},{16,12},{20,16},{24,20},{28,24},{32,28}... | collective-permute-start | bytes 196616 | tf_op jit(solution)/shard_map/ppermute | solution.py:19
  18.6 0.6 gather_fusion.1
  19.3 0.6 gather_fusion
  21.4 0.8 fusion.26
  22.2 0.9 %fusion.28 = (bf16[2,1,1152,128]{2,3,1,0:T(8,128)(2,1)S(1)}, bf16[2,1,1152,128]{2,3,1,0:T(8,128)(2,1)S(1)}) fusion(f32[2,128]{1,0:T(2,128)S(1)} %get-tuple-element.41, f32[2,1152]{1,0:T(2,128)S(1)} %get-tuple-element.31, f32[2,128]{1,0:T(2,128)S(1)} %get-tuple-element.40, f32[2,1152]{1,0:T(2,128)S(1)} %get-tuple-element.30, f32[2]{0:T(128)S(1)} %get-tuple-element.43, ...), kind=kLoop, calls=%fused_computation.59 | loop fusion | flops 5013504 | bytes 2379800 | tf_op jit(solution)/shard_map/convert_element_type | solution.py:40
  23.2 4.1 %collective-permute-done = bf16[256,128]{1,0:T(8,128)(2,1)S(1)} collective-permute-done((bf16[256,128]{1,0:T(8,128)(2,1)S(1)}, bf16[256,128]{1,0:T(8,128)(2,1)S(1)}, u32[]{:S(2)}, u32[]{:S(2)}) %collective-permute-start) | collective-permute-done | bytes 65568 | tf_op jit(solution)/shard_map/ppermute | solution.py:19
  27.5 2.7 %collective-permute-start.2 = (bf16[256,384]{1,0:T(8,128)(2,1)S(1)}, bf16[256,384]{1,0:T(8,128)(2,1)S(1)}, u32[]{:S(2)}, u32[]{:S(2)}) collective-permute-start(bf16[256,384]{1,0:T(8,128)(2,1)S(1)} %constant_dynamic-update-slice_fusion), channel_id=1, source_target_pairs={{0,12},{4,16},{8,20},{12,24},{16,28},{20,32},{24,36},{28,40},{32,4... | collective-permute-start | bytes 589832 | tf_op jit(solution)/shard_map/ppermute | solution.py:19
  30.2 8.2 %convolution_bitcast_fusion = bf16[6,2,4096,128]{2,3,1,0:T(8,128)(2,1)} fusion(s32[4096]{0:T(1024)S(1)} %pad_add_fusion, bf16[6,1,384,128]{2,3,1,0:T(8,128)(2,1)S(1)} %get-tuple-element.27, bf16[6,1,384,128]{2,3,1,0:T(8,128)(2,1)S(1)} %get-tuple-element.26, bf16[256,384]{1,0:T(8,128)(2,1)S(1)} %constant_dynamic-update-slice_fusion), kind=kOutput, calls=%fused_computation.10 | convolution fusion | flops 3525246976 | bytes 13975552 | tf_op jit(solution)/shard_map/pc,qrct->qrpt/dot_general | solution.py:61
  38.4 7.6 %fusion.5 = (f32[6,2048]{1,0:T(8,128)S(1)}, f32[6,2048]{1,0:T(8,128)S(1)}, f32[6,2048]{1,0:T(8,128)S(1)}, f32[6,2048]{1,0:T(8,128)S(1)}, f32[6,2048]{1,0:T(8,128...) fusion(bf16[6,2,4096,128]{2,3,1,0:T(8,128)(2,1)} %convolution_bitcast_fusion), kind=kLoop, calls=%fused_computation.16 | loop fusion | flops 31358976 | bytes 12976128 | tf_op jit(solution)/shard_map/qpt,qpt->qp/dot_general | solution.py:69
  46.4 4.6 %convolution_bitcast_fusion.1 = bf16[2,2,4096,128]{2,3,1,0:T(8,128)(2,1)} fusion(s32[4096]{0:T(1024)S(1)} %pad_add_fusion, bf16[2,1,1152,128]{2,3,1,0:T(8,128)(2,1)S(1)} %get-tuple-element.25, bf16[2,1,1152,128]{2,3,1,0:T(8,128)(2,1)S(1)} %get-tuple-element.24, bf16[256,1152]{1,0:T(8,128)(2,1)S(1)} %constant_dynamic-update-slice_fusion.3), kind=kOutput, calls=%fused_computation.19 | convolution fusion | flops 1377501184 | bytes 5980160 | tf_op jit(solution)/shard_map/pc,qrct->qrpt/dot_general | solution.py:61
  51.0 3.2 %fusion.16 = (f32[2,2048]{1,0:T(2,128)S(1)}, f32[2,2048]{1,0:T(2,128)S(1)}, f32[2,2048]{1,0:T(2,128)S(1)}, f32[2,2048]{1,0:T(2,128)S(1)}, f32[2,2048]{1,0:T(2,12...) fusion(bf16[2,2,4096,128]{2,3,1,0:T(8,128)(2,1)} %convolution_bitcast_fusion.1), kind=kLoop, calls=%fused_computation.39 | loop fusion | flops 10452992 | bytes 4325376 | tf_op jit(solution)/shard_map/qpt,qpt->qp/dot_general | solution.py:69
  54.3 0.3 maximum_maximum_fusion
  54.7 0.3 copy.17
  55.0 1.1 %all_to_all.8 = f32[256,1,256]{2,1,0:T(1,128)} reshape(f32[2048,32]{1,0:T(8,128)S(1)} %copy.17) | data formatting | bytes 524288 | tf_op jit(solution)/shard_map/all_to_all | solution.py:117
  56.2 9.8 %all-to-all-start = ((f32[256,1,256]{2,1,0:T(1,128)}), f32[256,1,256]{2,1,0:T(1,128)S(1)}, u32[]{:S(2)}, u32[]{:S(2)}) async-start(f32[256,1,256]{2,1,0:T(1,128)} %all_to_all.8), calls=%async_computation | async-start | bytes 524288 | tf_op jit(solution)/shard_map/all_to_all | solution.py:117
  66.0 0.6 dynamic_slice.3
  66.6 0.7 add_compare_fusion
  67.3 14.0 %all-to-all-done = f32[256,1,256]{2,1,0:T(1,128)S(1)} async-done(((f32[256,1,256]{2,1,0:T(1,128)}), f32[256,1,256]{2,1,0:T(1,128)S(1)}, u32[]{:S(2)}, u32[]{:S(2)}) %all-to-all-start) | async-done | bytes 262176 | tf_op jit(solution)/shard_map/all_to_all | solution.py:117
  81.3 0.6 reduce.16
  82.4 0.3 copy.19
  83.0 0.7 select_bitcast_fusion
  83.7 0.6 copy.22
  (73 shorter events, 2.9 us)
Async XLA Ops:
  0.6 18.0 %copy-start = (s32[32]{0:T(128)S(1)}, s32[32]{0:T(128)}, u32[]{:S(2)}) copy-start(s32[32]{0:T(128)} %param.6) | copy-start | bytes 388
  0.6 19.9 %copy-start.1 = (s32[4,512]{1,0:T(4,128)S(1)}, s32[4,512]{1,0:T(4,128)}, u32[]{:S(2)}) copy-start(s32[4,512]{1,0:T(4,128)} %param.7) | copy-start | bytes 24580
  0.7 20.2 %copy-start.2 = (s32[4,512]{1,0:T(4,128)S(1)}, s32[4,512]{1,0:T(4,128)}, u32[]{:S(2)}) copy-start(s32[4,512]{1,0:T(4,128)} %param.8) | copy-start | bytes 24580
  9.7 17.6 %collective-permute-start.1 = (bf16[256,128]{1,0:T(8,128)(2,1)S(1)}, bf16[256,128]{1,0:T(8,128)(2,1)S(1)}, u32[]{:S(2)}, u32[]{:S(2)}) collective-permute-start(bf16[256,128]{1,0:T(8,128)(2,1)S(1)} %all_gather.3), channel_id=1, source_target_pairs={{0,252},{4,0},{8,4},{12,8},{16,12},{20,16},{24,20},{28,24},{32,28}... | collective-permute-start | bytes 196616 | tf_op jit(solution)/shard_map/ppermute | solution.py:19
  18.5 8.8 %collective-permute-start = (bf16[256,128]{1,0:T(8,128)(2,1)S(1)}, bf16[256,128]{1,0:T(8,128)(2,1)S(1)}, u32[]{:S(2)}, u32[]{:S(2)}) collective-permute-start(bf16[256,128]{1,0:T(8,128)(2,1)S(1)} %all_gather.3), channel_id=1, source_target_pairs={{0,4},{4,8},{8,12},{12,16},{16,20},{20,24},{24,28},{28,32},{32,36}... | collective-permute-start | bytes 196616 | tf_op jit(solution)/shard_map/ppermute | solution.py:19
  27.4 18.9 %collective-permute-start.3 = (bf16[256,384]{1,0:T(8,128)(2,1)S(1)}, bf16[256,384]{1,0:T(8,128)(2,1)S(1)}, u32[]{:S(2)}, u32[]{:S(2)}) collective-permute-start(bf16[256,384]{1,0:T(8,128)(2,1)S(1)} %constant_dynamic-update-slice_fusion), channel_id=1, source_target_pairs={{0,244},{4,248},{8,252},{12,0},{16,4},{20,8},{24,12},{28,16},{32,2... | collective-permute-start | bytes 589832 | tf_op jit(solution)/shard_map/ppermute | solution.py:19
  27.5 18.7 %collective-permute-start.2 = (bf16[256,384]{1,0:T(8,128)(2,1)S(1)}, bf16[256,384]{1,0:T(8,128)(2,1)S(1)}, u32[]{:S(2)}, u32[]{:S(2)}) collective-permute-start(bf16[256,384]{1,0:T(8,128)(2,1)S(1)} %constant_dynamic-update-slice_fusion), channel_id=1, source_target_pairs={{0,12},{4,16},{8,20},{12,24},{16,28},{20,32},{24,36},{28,40},{32,4... | collective-permute-start | bytes 589832 | tf_op jit(solution)/shard_map/ppermute | solution.py:19
  55.0 11.0 %copy-start.3 = (s32[4]{0:T(128)S(1)}, s32[4]{0:T(128)}, u32[]{:S(2)}) copy-start(s32[4]{0:T(128)} %param.9) | copy-start | bytes 52
  56.2 25.1 %all-to-all-start = ((f32[256,1,256]{2,1,0:T(1,128)}), f32[256,1,256]{2,1,0:T(1,128)S(1)}, u32[]{:S(2)}, u32[]{:S(2)}) async-start(f32[256,1,256]{2,1,0:T(1,128)} %all_to_all.8), calls=%async_computation | async-start | bytes 524288 | tf_op jit(solution)/shard_map/all_to_all | solution.py:117

commit v12 on v11

--- a/solution.py
+++ b/solution.py
@@ -83,10 +83,10 @@
     time_span = signal.shape[1]
     ntime = time_span * time_devices
     rounded = signal.astype(jnp.bfloat16)
-    gathered = lax.all_gather(rounded, "chan", axis=0, tiled=True)
-    near = jnp.concatenate(
-        [from_behind(gathered, "tm", 1), gathered, from_behind(gathered, "tm", -1)], axis=1
+    triple = jnp.concatenate(
+        [from_behind(rounded, "tm", 1), rounded, from_behind(rounded, "tm", -1)], axis=1
     )
+    near = lax.all_gather(triple, "chan", axis=0, tiled=True)
     wide = jnp.concatenate([from_behind(near, "tm", 3), near, from_behind(near, "tm", -3)], axis=1)
     per_group = NS // groups
     band = NS // 4

time: 84.5 us -> 85.4 us (1.011)
  starting transfers between devices: 21.3 us -> 27.7 us
  waiting for transfers between devices: 18.1 us -> 14 us
  blocking collectives: 8.3 us -> 6.4 us
    ppermute x4, starting transfers between devices: 11.5 us -> 17.3 us  [from_behind(): lax.ppermute(array, axis, [(i, (i + by) % peers) for i in range(peers)])]
    ppermute x4, waiting for transfers between devices: 4.14 us -> 0.01 us  [from_behind(): lax.ppermute(array, axis, [(i, (i + by) % peers) for i in range(peers)])]
    all_gather x1, blocking collectives: 8.3 us -> 6.4 us  [shards(): near = lax.all_gather(triple, 'chan', axis=0, tiled=True)]
  transfers between devices with their start and end apart: 5 -> 5, of which waited for: 2 -> 1; matrix products, arithmetic and copies ran while one was open for 26% -> 26% of each run, Pallas kernels for 0% -> 0%
where the time goes in v12:
time: 85.4 us; the launch traced here: 85.1 us
  starting transfers between devices  27.7 us (32%)
  other arithmetic  16.6 us (19%)
  waiting for transfers between devices  14 us (16%)
  matrix products  12.8 us (15%)
  local copies, waits for them, and re-layouts  6.52 us (8%)
  blocking collectives  6.4 us (7%)
  between operations  1.08 us (1%)
    ppermute x4, starting transfers between devices, from_behind(): lax.ppermute(array, axis, [(i, (i + by) % peers) for i in range(peers)])  17.3 us
    all_to_all x1, waiting for transfers between devices, shards(): exchanged = lax.all_to_all(partial_value, ('tm', 'chan'), 0, 0, tiled=True)  14 us
    dot_general x2, matrix products, pair_sums(): jnp.einsum('pc,qrct->qrpt', pick, parts, preferred_element_type=jnp.bfloa...  12.8 us
    dot_general x2, other arithmetic, time_sum(): jnp.einsum('qpt,qpt->qp', left, right, preferred_element_type=jnp.float32)  10.8 us
    all_to_all x1, starting transfers between devices, shards(): exchanged = lax.all_to_all(partial_value, ('tm', 'chan'), 0, 0, tiled=True)  10.4 us
    all_gather x1, blocking collectives, shards(): near = lax.all_gather(triple, 'chan', axis=0, tiled=True)  6.4 us
    convert_element_type x2, other arithmetic, kernel_table(): jnp.where(inside, amplitude * cos_part, 0.0).astype(jnp.bfloat16)  1.74 us
  transfers between devices with their start and end apart: 5, of which 1 were waited for; matrix products, arithmetic and copies ran while one was open for 26% of the time, Pallas kernels for 0%

profile of v12, /device:TPU:1, one launch (start us, length us, event | category | flops | bytes accessed | tf_op | source)
XLA Modules:
  0.0 85.1 jit_solution(9849900905674786652)
XLA Ops:
  0.7 0.8 convert_element_type.131
  1.4 2.1 %collective-permute-start = (bf16[64,128]{1,0:T(8,128)(2,1)S(1)}, bf16[64,128]{1,0:T(8,128)(2,1)S(1)}, u32[]{:S(2)}, u32[]{:S(2)}) collective-permute-start(bf16[64,128]{1,0:T(8,128)(2,1)S(1)} %convert_element_type.131), channel_id=1, source_target_pairs={{0,4},{4,8},{8,12},{12,16},{16,20},{20,24},{24,28},{28,32},{32,36}... | collective-permute-start | bytes 49160 | tf_op jit(solution)/shard_map/ppermute | solution.py:19
  3.6 9.2 %collective-permute-start.1 = (bf16[64,128]{1,0:T(8,128)(2,1)S(1)}, bf16[64,128]{1,0:T(8,128)(2,1)S(1)}, u32[]{:S(2)}, u32[]{:S(2)}) collective-permute-start(bf16[64,128]{1,0:T(8,128)(2,1)S(1)} %convert_element_type.131), channel_id=1, source_target_pairs={{0,252},{4,0},{8,4},{12,8},{16,12},{20,16},{24,20},{28,24},{32,28}... | collective-permute-start | bytes 49160 | tf_op jit(solution)/shard_map/ppermute | solution.py:19
  13.1 0.6 gather_fusion
  13.8 0.8 reshape.591
  15.6 0.6 gather_fusion.1
  16.4 0.8 fusion.26
  17.2 0.9 %fusion.28 = (bf16[2,1,1152,128]{2,3,1,0:T(8,128)(2,1)S(1)}, bf16[2,1,1152,128]{2,3,1,0:T(8,128)(2,1)S(1)}) fusion(f32[2,128]{1,0:T(2,128)S(1)} %get-tuple-element.41, f32[2,1152]{1,0:T(2,128)S(1)} %get-tuple-element.31, f32[2,128]{1,0:T(2,128)S(1)} %get-tuple-element.40, f32[2,1152]{1,0:T(2,128)S(1)} %get-tuple-element.30, f32[2]{0:T(128)S(1)} %get-tuple-element.43, ...), kind=kLoop, calls=%fused_computation.59 | loop fusion | flops 5013504 | bytes 2379800 | tf_op jit(solution)/shard_map/convert_element_type | solution.py:40
  18.2 6.4 %all_gather.3 = bf16[256,384]{1,0:T(8,128)(2,1)S(1)} all-gather(bf16[64,384]{1,0:T(8,128)(2,1)S(1)} %pad_maximum_fusion), channel_id=1, replica_groups=mesh['tm'=64,'chan'=4] {'chan'}, dimensions={0}, use_global_device_ids=true | all-gather | bytes 245760 | tf_op jit(solution)/shard_map/all_gather | solution.py:89
  24.6 6.0 %collective-permute-start.3 = (bf16[256,384]{1,0:T(8,128)(2,1)S(1)}, bf16[256,384]{1,0:T(8,128)(2,1)S(1)}, u32[]{:S(2)}, u32[]{:S(2)}) collective-permute-start(bf16[256,384]{1,0:T(8,128)(2,1)S(1)} %all_gather.3), channel_id=1, source_target_pairs={{0,244},{4,248},{8,252},{12,0},{16,4},{20,8},{24,12},{28,16},{32,2... | collective-permute-start | bytes 589832 | tf_op jit(solution)/shard_map/ppermute | solution.py:19
  30.6 8.2 %convolution_bitcast_fusion = bf16[6,2,4096,128]{2,3,1,0:T(8,128)(2,1)} fusion(s32[4096]{0:T(1024)S(1)} %pad_add_fusion, bf16[6,1,384,128]{2,3,1,0:T(8,128)(2,1)S(1)} %get-tuple-element.27, bf16[6,1,384,128]{2,3,1,0:T(8,128)(2,1)S(1)} %get-tuple-element.26, bf16[256,384]{1,0:T(8,128)(2,1)S(1)} %all_gather.3), kind=kOutput, calls=%fused_computation.10 | convolution fusion | flops 3525246976 | bytes 13975552 | tf_op jit(solution)/shard_map/pc,qrct->qrpt/dot_general | solution.py:61
  38.8 7.6 %fusion.5 = (f32[6,2048]{1,0:T(8,128)S(1)}, f32[6,2048]{1,0:T(8,128)S(1)}, f32[6,2048]{1,0:T(8,128)S(1)}, f32[6,2048]{1,0:T(8,128)S(1)}, f32[6,2048]{1,0:T(8,128...) fusion(bf16[6,2,4096,128]{2,3,1,0:T(8,128)(2,1)} %convolution_bitcast_fusion), kind=kLoop, calls=%fused_computation.16 | loop fusion | flops 31358976 | bytes 12976128 | tf_op jit(solution)/shard_map/qpt,qpt->qp/dot_general | solution.py:69
  46.6 4.6 %convolution_bitcast_fusion.1 = bf16[2,2,4096,128]{2,3,1,0:T(8,128)(2,1)} fusion(s32[4096]{0:T(1024)S(1)} %pad_add_fusion, bf16[2,1,1152,128]{2,3,1,0:T(8,128)(2,1)S(1)} %get-tuple-element.25, bf16[2,1,1152,128]{2,3,1,0:T(8,128)(2,1)S(1)} %get-tuple-element.24, bf16[256,384]{1,0:T(8,128)(2,1)S(1)} %collective-permute-done.3, ...), kind=kOutput, calls=%fused_computation.19 | convolution fusion | flops 1379270656 | bytes 5980160 | tf_op jit(solution)/shard_map/pc,qrct->qrpt/dot_general | solution.py:61
  51.2 3.2 %fusion.16 = (f32[2,2048]{1,0:T(2,128)S(1)}, f32[2,2048]{1,0:T(2,128)S(1)}, f32[2,2048]{1,0:T(2,128)S(1)}, f32[2,2048]{1,0:T(2,128)S(1)}, f32[2,2048]{1,0:T(2,12...) fusion(bf16[2,2,4096,128]{2,3,1,0:T(8,128)(2,1)} %convolution_bitcast_fusion.1), kind=kLoop, calls=%fused_computation.39 | loop fusion | flops 10452992 | bytes 4325376 | tf_op jit(solution)/shard_map/qpt,qpt->qp/dot_general | solution.py:69
  54.9 0.3 copy.17
  55.3 1.1 %all_to_all.8 = f32[256,1,256]{2,1,0:T(1,128)} reshape(f32[2048,32]{1,0:T(8,128)S(1)} %copy.17) | data formatting | bytes 524288 | tf_op jit(solution)/shard_map/all_to_all | solution.py:117
  56.4 10.4 %all-to-all-start = ((f32[256,1,256]{2,1,0:T(1,128)}), f32[256,1,256]{2,1,0:T(1,128)S(1)}, u32[]{:S(2)}, u32[]{:S(2)}) async-start(f32[256,1,256]{2,1,0:T(1,128)} %all_to_all.8), calls=%async_computation | async-start | bytes 524288 | tf_op jit(solution)/shard_map/all_to_all | solution.py:117
  66.8 0.6 dynamic_slice.3
  67.4 0.7 add_compare_fusion
  68.1 14.0 %all-to-all-done = f32[256,1,256]{2,1,0:T(1,128)S(1)} async-done(((f32[256,1,256]{2,1,0:T(1,128)}), f32[256,1,256]{2,1,0:T(1,128)S(1)}, u32[]{:S(2)}, u32[]{:S(2)}) %all-to-all-start) | async-done | bytes 262176 | tf_op jit(solution)/shard_map/all_to_all | solution.py:117
  82.0 0.6 reduce.16
  83.0 0.3 copy.19
  83.7 0.7 select_bitcast_fusion
  84.5 0.6 copy.22
  (65 shorter events, 2.9 us)
Async XLA Ops:
  0.6 12.5 %copy-start = (s32[32]{0:T(128)S(1)}, s32[32]{0:T(128)}, u32[]{:S(2)}) copy-start(s32[32]{0:T(128)} %param.6) | copy-start | bytes 388
  0.6 14.2 %copy-start.1 = (s32[4,512]{1,0:T(4,128)S(1)}, s32[4,512]{1,0:T(4,128)}, u32[]{:S(2)}) copy-start(s32[4,512]{1,0:T(4,128)} %param.8) | copy-start | bytes 24580
  1.4 16.7 %collective-permute-start = (bf16[64,128]{1,0:T(8,128)(2,1)S(1)}, bf16[64,128]{1,0:T(8,128)(2,1)S(1)}, u32[]{:S(2)}, u32[]{:S(2)}) collective-permute-start(bf16[64,128]{1,0:T(8,128)(2,1)S(1)} %convert_element_type.131), channel_id=1, source_target_pairs={{0,4},{4,8},{8,12},{12,16},{16,20},{20,24},{24,28},{28,32},{32,36}... | collective-permute-start | bytes 49160 | tf_op jit(solution)/shard_map/ppermute | solution.py:19
  3.6 14.6 %collective-permute-start.1 = (bf16[64,128]{1,0:T(8,128)(2,1)S(1)}, bf16[64,128]{1,0:T(8,128)(2,1)S(1)}, u32[]{:S(2)}, u32[]{:S(2)}) collective-permute-start(bf16[64,128]{1,0:T(8,128)(2,1)S(1)} %convert_element_type.131), channel_id=1, source_target_pairs={{0,252},{4,0},{8,4},{12,8},{16,12},{20,16},{24,20},{28,24},{32,28}... | collective-permute-start | bytes 49160 | tf_op jit(solution)/shard_map/ppermute | solution.py:19
  24.6 22.1 %collective-permute-start.2 = (bf16[256,384]{1,0:T(8,128)(2,1)S(1)}, bf16[256,384]{1,0:T(8,128)(2,1)S(1)}, u32[]{:S(2)}, u32[]{:S(2)}) collective-permute-start(bf16[256,384]{1,0:T(8,128)(2,1)S(1)} %all_gather.3), channel_id=1, source_target_pairs={{0,12},{4,16},{8,20},{12,24},{16,28},{20,32},{24,36},{28,40},{32,4... | collective-permute-start | bytes 589832 | tf_op jit(solution)/shard_map/ppermute | solution.py:19
  24.6 22.1 %collective-permute-start.3 = (bf16[256,384]{1,0:T(8,128)(2,1)S(1)}, bf16[256,384]{1,0:T(8,128)(2,1)S(1)}, u32[]{:S(2)}, u32[]{:S(2)}) collective-permute-start(bf16[256,384]{1,0:T(8,128)(2,1)S(1)} %all_gather.3), channel_id=1, source_target_pairs={{0,244},{4,248},{8,252},{12,0},{16,4},{20,8},{24,12},{28,16},{32,2... | collective-permute-start | bytes 589832 | tf_op jit(solution)/shard_map/ppermute | solution.py:19
  55.3 11.5 %copy-start.2 = (s32[4]{0:T(128)S(1)}, s32[4]{0:T(128)}, u32[]{:S(2)}) copy-start(s32[4]{0:T(128)} %param.9) | copy-start | bytes 52
  56.4 25.6 %all-to-all-start = ((f32[256,1,256]{2,1,0:T(1,128)}), f32[256,1,256]{2,1,0:T(1,128)S(1)}, u32[]{:S(2)}, u32[]{:S(2)}) async-start(f32[256,1,256]{2,1,0:T(1,128)} %all_to_all.8), calls=%async_computation | async-start | bytes 524288 | tf_op jit(solution)/shard_map/all_to_all | solution.py:117

commit v13 on v11

--- a/solution.py
+++ b/solution.py
@@ -70,8 +70,12 @@
 
     cross_real = time_sum(first_real, second_real) + time_sum(first_imag, second_imag)
     cross_imag = time_sum(first_imag, second_real) - time_sum(first_real, second_imag)
-    power_first = time_sum(first_real, first_real) + time_sum(first_imag, first_imag)
-    power_second = time_sum(second_real, second_real) + time_sum(second_imag, second_imag)
+    power = jnp.einsum("qrct,qrct->qc", parts, parts, preferred_element_type=jnp.float32)
+    owner_power = jnp.einsum(
+        "pc,qc->qp", pick.astype(jnp.float32), power, precision=lax.Precision.HIGHEST
+    )
+    power_first = owner_power[:, :pairs]
+    power_second = owner_power[:, pairs:]
     return jnp.stack([cross_real, cross_imag, power_first, power_second], axis=1)
 
 

time: 84.5 us -> 76.1 us (0.901)
  other arithmetic: 16.6 us -> 9.67 us
  matrix products: 12.8 us -> 11.4 us
    dot_general x2, matrix products: 12.8 us -> 5.6 us  [pair_sums(): jnp.einsum('pc,qrct->qrpt', pick, parts, preferred_element_type=jnp.bfloa...]
    dot_general x2, other arithmetic: 10.8 us -> 4.04 us  [time_sum(): jnp.einsum('qpt,qpt->qp', left, right, preferred_element_type=jnp.float32)]
    dot_general x0 -> x4, matrix products: none -> 5.81 us  [the longest x2 4.63 us: pair_sums(): jnp.einsum('pc,qc->qp', pick.astype(jnp.float32), power, precision=lax.Pr...]
  transfers between devices with their start and end apart: 5 -> 5, of which waited for: 2 -> 2; matrix products, arithmetic and copies ran while one was open for 26% -> 21% of each run, Pallas kernels for 0% -> 0%
where the time goes in v13:
time: 76.1 us; the launch traced here: 75.9 us
  starting transfers between devices  21.3 us (28%)
  waiting for transfers between devices  18.1 us (24%)
  matrix products  11.4 us (15%)
  other arithmetic  9.67 us (13%)
  blocking collectives  8.3 us (11%)
  local copies, waits for them, and re-layouts  6 us (8%)
  between operations  1.09 us (1%)
    all_to_all x1, waiting for transfers between devices, shards(): exchanged = lax.all_to_all(partial_value, ('tm', 'chan'), 0, 0, tiled=True)  14 us
    ppermute x4, starting transfers between devices, from_behind(): lax.ppermute(array, axis, [(i, (i + by) % peers) for i in range(peers)])  11.5 us
    all_to_all x1, starting transfers between devices, shards(): exchanged = lax.all_to_all(partial_value, ('tm', 'chan'), 0, 0, tiled=True)  9.82 us
    all_gather x1, blocking collectives, shards(): gathered = lax.all_gather(rounded, 'chan', axis=0, tiled=True)  8.3 us
    dot_general x2, matrix products, pair_sums(): jnp.einsum('pc,qrct->qrpt', pick, parts, preferred_element_type=jnp.bfloa...  5.6 us
    dot_general x2, matrix products, pair_sums(): jnp.einsum('pc,qc->qp', pick.astype(jnp.float32), power, precision=lax.Pr...  4.63 us
    ppermute x4, waiting for transfers between devices, from_behind(): lax.ppermute(array, axis, [(i, (i + by) % peers) for i in range(peers)])  4.14 us
    dot_general x2, other arithmetic, time_sum(): jnp.einsum('qpt,qpt->qp', left, right, preferred_element_type=jnp.float32)  4.04 us
  transfers between devices with their start and end apart: 5, of which 2 were waited for; matrix products, arithmetic and copies ran while one was open for 21% of the time, Pallas kernels for 0%

profile of v13, /device:TPU:1, one launch (start us, length us, event | category | flops | bytes accessed | tf_op | source)
XLA Modules:
  0.0 75.9 jit_solution(7274665147284093133)
XLA Ops:
  0.7 0.8 %convert_element_type.133 = bf16[64,128]{1,0:T(8,128)(2,1)S(1)} convert(f32[64,128]{1,0:T(8,128)} %param.5) | non-fusion elementwise | flops 8192 | bytes 49152 | tf_op jit(solution)/shard_map/convert_element_type | solution.py:89
  1.4 8.3 %all_gather.3 = bf16[256,128]{1,0:T(8,128)(2,1)S(1)} all-gather(bf16[64,128]{1,0:T(8,128)(2,1)S(1)} %convert_element_type.133), channel_id=1, replica_groups=mesh['tm'=64,'chan'=4] {'chan'}, dimensions={0}, use_global_device_ids=true | all-gather | bytes 81920 | tf_op jit(solution)/shard_map/all_gather | solution.py:90
  9.7 8.8 %collective-permute-start.1 = (bf16[256,128]{1,0:T(8,128)(2,1)S(1)}, bf16[256,128]{1,0:T(8,128)(2,1)S(1)}, u32[]{:S(2)}, u32[]{:S(2)}) collective-permute-start(bf16[256,128]{1,0:T(8,128)(2,1)S(1)} %all_gather.3), channel_id=1, source_target_pairs={{0,252},{4,0},{8,4},{12,8},{16,12},{20,16},{24,20},{28,24},{32,28}... | collective-permute-start | bytes 196616 | tf_op jit(solution)/shard_map/ppermute | solution.py:19
  18.6 0.6 gather_fusion.1
  19.3 0.6 gather_fusion
  21.4 0.8 %fusion.22 = (bf16[6,1,384,128]{2,3,1,0:T(8,128)(2,1)S(1)}, bf16[6,1,384,128]{2,3,1,0:T(8,128)(2,1)S(1)}) fusion(f32[6,128]{1,0:T(8,128)S(1)} %get-tuple-element.35, f32[6,384]{1,0:T(8,128)S(1)} %get-tuple-element.31, f32[6,128]{1,0:T(8,128)S(1)} %get-tuple-element.34, f32[6,384]{1,0:T(8,128)S(1)} %get-tuple-element.30, f32[6]{0:T(128)S(1)} %get-tuple-element.47, ...), kind=kLoop, calls=%fused_computation.46 | loop fusion | flops 5013504 | bytes 1597512 | tf_op jit(solution)/shard_map/convert_element_type | solution.py:40
  22.2 1.0 %fusion.24 = (bf16[2,1,1152,128]{2,3,1,0:T(8,128)(2,1)S(1)}, bf16[2,1,1152,128]{2,3,1,0:T(8,128)(2,1)S(1)}) fusion(f32[2,128]{1,0:T(2,128)S(1)} %get-tuple-element.37, f32[2,1152]{1,0:T(2,128)S(1)} %get-tuple-element.27, f32[2,128]{1,0:T(2,128)S(1)} %get-tuple-element.36, f32[2,1152]{1,0:T(2,128)S(1)} %get-tuple-element.26, f32[2]{0:T(128)S(1)} %get-tuple-element.43, ...), kind=kLoop, calls=%fused_computation.48 | loop fusion | flops 5013504 | bytes 2379800 | tf_op jit(solution)/shard_map/convert_element_type | solution.py:40
  23.2 4.1 %collective-permute-done = bf16[256,128]{1,0:T(8,128)(2,1)S(1)} collective-permute-done((bf16[256,128]{1,0:T(8,128)(2,1)S(1)}, bf16[256,128]{1,0:T(8,128)(2,1)S(1)}, u32[]{:S(2)}, u32[]{:S(2)}) %collective-permute-start) | collective-permute-done | bytes 65568 | tf_op jit(solution)/shard_map/ppermute | solution.py:19
  27.5 2.7 %collective-permute-start.2 = (bf16[256,384]{1,0:T(8,128)(2,1)S(1)}, bf16[256,384]{1,0:T(8,128)(2,1)S(1)}, u32[]{:S(2)}, u32[]{:S(2)}) collective-permute-start(bf16[256,384]{1,0:T(8,128)(2,1)S(1)} %constant_dynamic-update-slice_fusion), channel_id=1, source_target_pairs={{0,12},{4,16},{8,20},{12,24},{16,28},{20,32},{24,36},{28,40},{32,4... | collective-permute-start | bytes 589832 | tf_op jit(solution)/shard_map/ppermute | solution.py:19
  30.2 0.6 fusion.17
  30.8 2.5 %fusion.5 = f32[6,4096]{1,0:T(8,128)S(1)} fusion(f32[6,256]{1,0:T(8,128)S(1)} %get-tuple-element.40, s32[4096]{0:T(1024)S(1)} %pad_add_fusion), kind=kOutput, calls=%fused_computation.14 | convolution fusion | flops 76546048 | bytes 120832 | tf_op jit(solution)/shard_map/pc,qc->qp/dot_general | solution.py:74
  33.3 3.9 %convolution_bitcast_fusion = bf16[6,2,4096,128]{2,3,1,0:T(8,128)(2,1)S(1)} fusion(s32[4096]{0:T(1024)S(1)} %pad_add_fusion, bf16[6,2,128,256]{3,2,1,0:T(8,128)(2,1)S(1)} %get-tuple-element.41), kind=kOutput, calls=%fused_computation.6 | convolution fusion | flops 3222274048 | bytes 13385728 | tf_op jit(solution)/shard_map/pc,qrct->qrpt/dot_general | solution.py:61
  37.2 3.1 %fusion.2 = (f32[6,2048]{1,0:T(8,128)S(1)}, f32[6,2048]{1,0:T(8,128)S(1)}, f32[6,2048]{1,0:T(8,128)S(1)}, f32[6,2048]{1,0:T(8,128)S(1)}) fusion(bf16[6,2,4096,128]{2,3,1,0:T(8,128)(2,1)S(1)} %convolution_bitcast_fusion), kind=kLoop, calls=%fused_computation.9 | loop fusion | flops 18825216 | bytes 12779520 | tf_op jit(solution)/shard_map/qpt,qpt->qp/dot_general | solution.py:69
  41.1 2.1 %fusion.4 = f32[2,4096]{1,0:T(2,128)S(1)} fusion(f32[2,256]{1,0:T(2,128)S(1)} %get-tuple-element.38, s32[4096]{0:T(1024)S(1)} %pad_add_fusion), kind=kOutput, calls=%fused_computation.13 | convolution fusion | flops 26214400 | bytes 51200 | tf_op jit(solution)/shard_map/pc,qc->qp/dot_general | solution.py:74
  43.2 1.7 %convolution_bitcast_fusion.1 = bf16[2,2,4096,128]{2,3,1,0:T(8,128)(2,1)S(1)} fusion(s32[4096]{0:T(1024)S(1)} %pad_add_fusion, bf16[2,2,128,256]{3,2,1,0:T(8,128)(2,1)S(1)} %get-tuple-element.39), kind=kOutput, calls=%fused_computation.11 | convolution fusion | flops 1074790400 | bytes 4472832 | tf_op jit(solution)/shard_map/pc,qrct->qrpt/dot_general | solution.py:61
  44.9 1.0 %fusion.11 = (f32[2,2048]{1,0:T(2,128)S(1)}, f32[2,2048]{1,0:T(2,128)S(1)}, f32[2,2048]{1,0:T(2,128)S(1)}, f32[2,2048]{1,0:T(2,128)S(1)}) fusion(bf16[2,2,4096,128]{2,3,1,0:T(8,128)(2,1)S(1)} %convolution_bitcast_fusion.1), kind=kLoop, calls=%fused_computation.26 | loop fusion | flops 6275072 | bytes 4259840 | tf_op jit(solution)/shard_map/qpt,qpt->qp/dot_general | solution.py:69
  46.6 1.1 %all_to_all.8 = f32[256,1,256]{2,1,0:T(1,128)} reshape(f32[2048,32]{1,0:T(8,128)S(1)} %copy.19) | data formatting | bytes 524288 | tf_op jit(solution)/shard_map/all_to_all | solution.py:121
  47.8 9.8 %all-to-all-start = ((f32[256,1,256]{2,1,0:T(1,128)}), f32[256,1,256]{2,1,0:T(1,128)S(1)}, u32[]{:S(2)}, u32[]{:S(2)}) async-start(f32[256,1,256]{2,1,0:T(1,128)} %all_to_all.8), calls=%async_computation | async-start | bytes 524288 | tf_op jit(solution)/shard_map/all_to_all | solution.py:121
  57.6 0.6 dynamic_slice.3
  58.2 0.7 add_compare_fusion
  58.9 14.0 %all-to-all-done = f32[256,1,256]{2,1,0:T(1,128)S(1)} async-done(((f32[256,1,256]{2,1,0:T(1,128)}), f32[256,1,256]{2,1,0:T(1,128)S(1)}, u32[]{:S(2)}, u32[]{:S(2)}) %all-to-all-start) | async-done | bytes 262176 | tf_op jit(solution)/shard_map/all_to_all | solution.py:121
  72.9 0.6 reduce.10
  74.6 0.7 select_bitcast_fusion
  75.3 0.6 copy.24
  (68 shorter events, 4.2 us)
Async XLA Ops:
  0.6 18.0 %copy-start = (s32[32]{0:T(128)S(1)}, s32[32]{0:T(128)}, u32[]{:S(2)}) copy-start(s32[32]{0:T(128)} %param.6) | copy-start | bytes 388
  0.6 19.9 %copy-start.1 = (s32[4,512]{1,0:T(4,128)S(1)}, s32[4,512]{1,0:T(4,128)}, u32[]{:S(2)}) copy-start(s32[4,512]{1,0:T(4,128)} %param.7) | copy-start | bytes 24580
  0.7 20.2 %copy-start.2 = (s32[4,512]{1,0:T(4,128)S(1)}, s32[4,512]{1,0:T(4,128)}, u32[]{:S(2)}) copy-start(s32[4,512]{1,0:T(4,128)} %param.8) | copy-start | bytes 24580
  9.7 17.6 %collective-permute-start.1 = (bf16[256,128]{1,0:T(8,128)(2,1)S(1)}, bf16[256,128]{1,0:T(8,128)(2,1)S(1)}, u32[]{:S(2)}, u32[]{:S(2)}) collective-permute-start(bf16[256,128]{1,0:T(8,128)(2,1)S(1)} %all_gather.3), channel_id=1, source_target_pairs={{0,252},{4,0},{8,4},{12,8},{16,12},{20,16},{24,20},{28,24},{32,28}... | collective-permute-start | bytes 196616 | tf_op jit(solution)/shard_map/ppermute | solution.py:19
  18.5 8.8 %collective-permute-start = (bf16[256,128]{1,0:T(8,128)(2,1)S(1)}, bf16[256,128]{1,0:T(8,128)(2,1)S(1)}, u32[]{:S(2)}, u32[]{:S(2)}) collective-permute-start(bf16[256,128]{1,0:T(8,128)(2,1)S(1)} %all_gather.3), channel_id=1, source_target_pairs={{0,4},{4,8},{8,12},{12,16},{16,20},{20,24},{24,28},{28,32},{32,36}... | collective-permute-start | bytes 196616 | tf_op jit(solution)/shard_map/ppermute | solution.py:19
  27.4 13.0 %collective-permute-start.3 = (bf16[256,384]{1,0:T(8,128)(2,1)S(1)}, bf16[256,384]{1,0:T(8,128)(2,1)S(1)}, u32[]{:S(2)}, u32[]{:S(2)}) collective-permute-start(bf16[256,384]{1,0:T(8,128)(2,1)S(1)} %constant_dynamic-update-slice_fusion), channel_id=1, source_target_pairs={{0,244},{4,248},{8,252},{12,0},{16,4},{20,8},{24,12},{28,16},{32,2... | collective-permute-start | bytes 589832 | tf_op jit(solution)/shard_map/ppermute | solution.py:19
  27.5 12.8 %collective-permute-start.2 = (bf16[256,384]{1,0:T(8,128)(2,1)S(1)}, bf16[256,384]{1,0:T(8,128)(2,1)S(1)}, u32[]{:S(2)}, u32[]{:S(2)}) collective-permute-start(bf16[256,384]{1,0:T(8,128)(2,1)S(1)} %constant_dynamic-update-slice_fusion), channel_id=1, source_target_pairs={{0,12},{4,16},{8,20},{12,24},{16,28},{20,32},{24,36},{28,40},{32,4... | collective-permute-start | bytes 589832 | tf_op jit(solution)/shard_map/ppermute | solution.py:19
  46.6 11.0 %copy-start.3 = (s32[4]{0:T(128)S(1)}, s32[4]{0:T(128)}, u32[]{:S(2)}) copy-start(s32[4]{0:T(128)} %param.9) | copy-start | bytes 52
  47.8 25.1 %all-to-all-start = ((f32[256,1,256]{2,1,0:T(1,128)}), f32[256,1,256]{2,1,0:T(1,128)S(1)}, u32[]{:S(2)}, u32[]{:S(2)}) async-start(f32[256,1,256]{2,1,0:T(1,128)} %all_to_all.8), calls=%async_computation | async-start | bytes 524288 | tf_op jit(solution)/shard_map/all_to_all | solution.py:121

commit v14 on v13

--- a/solution.py
+++ b/solution.py
@@ -71,9 +71,13 @@
     cross_real = time_sum(first_real, second_real) + time_sum(first_imag, second_imag)
     cross_imag = time_sum(first_imag, second_real) - time_sum(first_real, second_imag)
     power = jnp.einsum("qrct,qrct->qc", parts, parts, preferred_element_type=jnp.float32)
-    owner_power = jnp.einsum(
-        "pc,qc->qp", pick.astype(jnp.float32), power, precision=lax.Precision.HIGHEST
-    )
+    high = power.astype(jnp.bfloat16)
+    rest = power - high.astype(jnp.float32)
+    middle = rest.astype(jnp.bfloat16)
+    low = (rest - middle.astype(jnp.float32)).astype(jnp.bfloat16)
+    pieces = jnp.stack([high, middle, low])
+    picked_power = jnp.einsum("pc,kqc->kqp", pick, pieces, preferred_element_type=jnp.float32)
+    owner_power = (picked_power[0] + picked_power[1]) + picked_power[2]
     power_first = owner_power[:, :pairs]
     power_second = owner_power[:, pairs:]
     return jnp.stack([cross_real, cross_imag, power_first, power_second], axis=1)

time: 76.1 us -> 73.5 us (0.966)
  matrix products: 11.4 us -> 8.63 us
    dot_general x2, matrix products: 4.63 us -> 1.86 us  [pair_sums(): jnp.einsum('pc,kqc->kqp', pick, pieces, preferred_element_type=jnp.float32)]
  transfers between devices with their start and end apart: 5 -> 5, of which waited for: 2 -> 2; matrix products, arithmetic and copies ran while one was open for 21% -> 20% of each run, Pallas kernels for 0% -> 0%
where the time goes in v14:
time: 73.5 us; the launch traced here: 73.3 us
  starting transfers between devices  21.3 us (29%)
  waiting for transfers between devices  18.1 us (25%)
  other arithmetic  9.75 us (13%)
  matrix products  8.63 us (12%)
  blocking collectives  8.3 us (11%)
  local copies, waits for them, and re-layouts  6 us (8%)
  between operations  1.16 us (2%)
    all_to_all x1, waiting for transfers between devices, shards(): exchanged = lax.all_to_all(partial_value, ('tm', 'chan'), 0, 0, tiled=True)  14 us
    ppermute x4, starting transfers between devices, from_behind(): lax.ppermute(array, axis, [(i, (i + by) % peers) for i in range(peers)])  11.5 us
    all_to_all x1, starting transfers between devices, shards(): exchanged = lax.all_to_all(partial_value, ('tm', 'chan'), 0, 0, tiled=True)  9.8 us
    all_gather x1, blocking collectives, shards(): gathered = lax.all_gather(rounded, 'chan', axis=0, tiled=True)  8.3 us
    dot_general x2, matrix products, pair_sums(): jnp.einsum('pc,qrct->qrpt', pick, parts, preferred_element_type=jnp.bfloa...  5.6 us
    ppermute x4, waiting for transfers between devices, from_behind(): lax.ppermute(array, axis, [(i, (i + by) % peers) for i in range(peers)])  4.14 us
    dot_general x2, other arithmetic, time_sum(): jnp.einsum('qpt,qpt->qp', left, right, preferred_element_type=jnp.float32)  4.04 us
    dot_general x2, matrix products, pair_sums(): jnp.einsum('pc,kqc->kqp', pick, pieces, preferred_element_type=jnp.float32)  1.86 us
  transfers between devices with their start and end apart: 5, of which 2 were waited for; matrix products, arithmetic and copies ran while one was open for 20% of the time, Pallas kernels for 0%

profile of v14, /device:TPU:1, one launch (start us, length us, event | category | flops | bytes accessed | tf_op | source)
XLA Modules:
  0.0 73.3 jit_solution(12155675372016633947)
XLA Ops:
  0.7 0.8 %convert_element_type.161 = bf16[64,128]{1,0:T(8,128)(2,1)S(1)} convert(f32[64,128]{1,0:T(8,128)} %param.5) | non-fusion elementwise | flops 8192 | bytes 49152 | tf_op jit(solution)/shard_map/convert_element_type | solution.py:93
  1.4 8.3 %all_gather.3 = bf16[256,128]{1,0:T(8,128)(2,1)S(1)} all-gather(bf16[64,128]{1,0:T(8,128)(2,1)S(1)} %convert_element_type.161), channel_id=1, replica_groups=mesh['tm'=64,'chan'=4] {'chan'}, dimensions={0}, use_global_device_ids=true | all-gather | bytes 81920 | tf_op jit(solution)/shard_map/all_gather | solution.py:94
  9.7 8.8 %collective-permute-start.1 = (bf16[256,128]{1,0:T(8,128)(2,1)S(1)}, bf16[256,128]{1,0:T(8,128)(2,1)S(1)}, u32[]{:S(2)}, u32[]{:S(2)}) collective-permute-start(bf16[256,128]{1,0:T(8,128)(2,1)S(1)} %all_gather.3), channel_id=1, source_target_pairs={{0,252},{4,0},{8,4},{12,8},{16,12},{20,16},{24,20},{28,24},{32,28}... | collective-permute-start | bytes 196616 | tf_op jit(solution)/shard_map/ppermute | solution.py:19
  18.6 0.6 gather_fusion.1
  19.3 0.6 gather_fusion
  21.4 0.8 %fusion.25 = (bf16[6,1,384,128]{2,3,1,0:T(8,128)(2,1)S(1)}, bf16[6,1,384,128]{2,3,1,0:T(8,128)(2,1)S(1)}) fusion(f32[6,128]{1,0:T(8,128)S(1)} %get-tuple-element.45, f32[6,384]{1,0:T(8,128)S(1)} %get-tuple-element.38, f32[6,128]{1,0:T(8,128)S(1)} %get-tuple-element.44, f32[6,384]{1,0:T(8,128)S(1)} %get-tuple-element.37, f32[6]{0:T(128)S(1)} %get-tuple-element.57, ...), kind=kLoop, calls=%fused_computation.47 | loop fusion | flops 5013504 | bytes 1597512 | tf_op jit(solution)/shard_map/convert_element_type | solution.py:40
  22.2 1.0 %fusion.27 = (bf16[2,1,1152,128]{2,3,1,0:T(8,128)(2,1)S(1)}, bf16[2,1,1152,128]{2,3,1,0:T(8,128)(2,1)S(1)}) fusion(f32[2,128]{1,0:T(2,128)S(1)} %get-tuple-element.47, f32[2,1152]{1,0:T(2,128)S(1)} %get-tuple-element.31, f32[2,128]{1,0:T(2,128)S(1)} %get-tuple-element.46, f32[2,1152]{1,0:T(2,128)S(1)} %get-tuple-element.30, f32[2]{0:T(128)S(1)} %get-tuple-element.53, ...), kind=kLoop, calls=%fused_computation.49 | loop fusion | flops 5013504 | bytes 2379800 | tf_op jit(solution)/shard_map/convert_element_type | solution.py:40
  23.2 4.1 %collective-permute-done = bf16[256,128]{1,0:T(8,128)(2,1)S(1)} collective-permute-done((bf16[256,128]{1,0:T(8,128)(2,1)S(1)}, bf16[256,128]{1,0:T(8,128)(2,1)S(1)}, u32[]{:S(2)}, u32[]{:S(2)}) %collective-permute-start) | collective-permute-done | bytes 65568 | tf_op jit(solution)/shard_map/ppermute | solution.py:19
  27.5 2.7 %collective-permute-start.2 = (bf16[256,384]{1,0:T(8,128)(2,1)S(1)}, bf16[256,384]{1,0:T(8,128)(2,1)S(1)}, u32[]{:S(2)}, u32[]{:S(2)}) collective-permute-start(bf16[256,384]{1,0:T(8,128)(2,1)S(1)} %constant_dynamic-update-slice_fusion), channel_id=1, source_target_pairs={{0,12},{4,16},{8,20},{12,24},{16,28},{20,32},{24,36},{28,40},{32,4... | collective-permute-start | bytes 589832 | tf_op jit(solution)/shard_map/ppermute | solution.py:19
  30.2 0.6 fusion.20
  30.8 0.8 %fusion.10 = f32[3,6,4096]{2,1,0:T(8,128)S(1)} fusion(s32[4096]{0:T(1024)S(1)} %pad_add_fusion, bf16[1,6,256]{2,1,0:T(8,128)(2,1)S(1)} %get-tuple-element.33, bf16[1,6,256]{2,1,0:T(8,128)(2,1)S(1)} %get-tuple-element.34, bf16[1,6,256]{2,1,0:T(8,128)(2,1)S(1)} %get-tuple-element.32), kind=kOutput, calls=%fused_computation.16 | convolution fusion | flops 38806528 | bytes 320512 | tf_op jit(solution)/shard_map/pc,kqc->kqp/dot_general | solution.py:79
  31.7 3.9 %convolution_bitcast_fusion = bf16[6,2,4096,128]{2,3,1,0:T(8,128)(2,1)S(1)} fusion(s32[4096]{0:T(1024)S(1)} %pad_add_fusion, bf16[6,2,128,256]{3,2,1,0:T(8,128)(2,1)S(1)} %get-tuple-element.51), kind=kOutput, calls=%fused_computation.6 | convolution fusion | flops 3222274048 | bytes 13385728 | tf_op jit(solution)/shard_map/pc,qrct->qrpt/dot_general | solution.py:61
  35.6 3.1 %fusion.2 = (f32[6,2048]{1,0:T(8,128)S(1)}, f32[6,2048]{1,0:T(8,128)S(1)}, f32[6,2048]{1,0:T(8,128)S(1)}, f32[6,2048]{1,0:T(8,128)S(1)}) fusion(bf16[6,2,4096,128]{2,3,1,0:T(8,128)(2,1)S(1)} %convolution_bitcast_fusion), kind=kLoop, calls=%fused_computation.9 | loop fusion | flops 18825216 | bytes 12779520 | tf_op jit(solution)/shard_map/qpt,qpt->qp/dot_general | solution.py:69
  39.5 1.0 %fusion.8 = f32[3,2,4096]{2,1,0:T(2,128)S(1)} fusion(s32[4096]{0:T(1024)S(1)} %pad_add_fusion, bf16[3,2,256]{2,0,1:T(4,128)(2,1)S(1)} %pad_maximum_fusion.1), kind=kOutput, calls=%fused_computation.15 | convolution fusion | flops 13631488 | bytes 117760 | tf_op jit(solution)/shard_map/pc,kqc->kqp/dot_general | solution.py:79
  40.6 1.7 %convolution_bitcast_fusion.1 = bf16[2,2,4096,128]{2,3,1,0:T(8,128)(2,1)S(1)} fusion(s32[4096]{0:T(1024)S(1)} %pad_add_fusion, bf16[2,2,128,256]{3,2,1,0:T(8,128)(2,1)S(1)} %get-tuple-element.49), kind=kOutput, calls=%fused_computation.11 | convolution fusion | flops 1074790400 | bytes 4472832 | tf_op jit(solution)/shard_map/pc,qrct->qrpt/dot_general | solution.py:61
  42.3 1.0 %fusion.14 = (f32[2,2048]{1,0:T(2,128)S(1)}, f32[2,2048]{1,0:T(2,128)S(1)}, f32[2,2048]{1,0:T(2,128)S(1)}, f32[2,2048]{1,0:T(2,128)S(1)}) fusion(bf16[2,2,4096,128]{2,3,1,0:T(8,128)(2,1)S(1)} %convolution_bitcast_fusion.1), kind=kLoop, calls=%fused_computation.27 | loop fusion | flops 6275072 | bytes 4259840 | tf_op jit(solution)/shard_map/qpt,qpt->qp/dot_general | solution.py:69
  44.0 1.1 %all_to_all.8 = f32[256,1,256]{2,1,0:T(1,128)} reshape(f32[2048,32]{1,0:T(8,128)S(1)} %copy.62) | data formatting | bytes 524288 | tf_op jit(solution)/shard_map/all_to_all | solution.py:125
  45.2 9.8 %all-to-all-start = ((f32[256,1,256]{2,1,0:T(1,128)}), f32[256,1,256]{2,1,0:T(1,128)S(1)}, u32[]{:S(2)}, u32[]{:S(2)}) async-start(f32[256,1,256]{2,1,0:T(1,128)} %all_to_all.8), calls=%async_computation | async-start | bytes 524288 | tf_op jit(solution)/shard_map/all_to_all | solution.py:125
  55.0 0.6 dynamic_slice.3
  55.6 0.7 add_compare_fusion
  56.2 14.0 %all-to-all-done = f32[256,1,256]{2,1,0:T(1,128)S(1)} async-done(((f32[256,1,256]{2,1,0:T(1,128)}), f32[256,1,256]{2,1,0:T(1,128)S(1)}, u32[]{:S(2)}, u32[]{:S(2)}) %all-to-all-start) | async-done | bytes 262176 | tf_op jit(solution)/shard_map/all_to_all | solution.py:125
  70.2 0.6 reduce.10
  71.9 0.7 select_bitcast_fusion
  72.7 0.6 copy.67
  (76 shorter events, 4.3 us)
Async XLA Ops:
  0.6 18.0 %copy-start = (s32[32]{0:T(128)S(1)}, s32[32]{0:T(128)}, u32[]{:S(2)}) copy-start(s32[32]{0:T(128)} %param.6) | copy-start | bytes 388
  0.6 19.9 %copy-start.1 = (s32[4,512]{1,0:T(4,128)S(1)}, s32[4,512]{1,0:T(4,128)}, u32[]{:S(2)}) copy-start(s32[4,512]{1,0:T(4,128)} %param.7) | copy-start | bytes 24580
  0.7 20.2 %copy-start.2 = (s32[4,512]{1,0:T(4,128)S(1)}, s32[4,512]{1,0:T(4,128)}, u32[]{:S(2)}) copy-start(s32[4,512]{1,0:T(4,128)} %param.8) | copy-start | bytes 24580
  9.7 17.6 %collective-permute-start.1 = (bf16[256,128]{1,0:T(8,128)(2,1)S(1)}, bf16[256,128]{1,0:T(8,128)(2,1)S(1)}, u32[]{:S(2)}, u32[]{:S(2)}) collective-permute-start(bf16[256,128]{1,0:T(8,128)(2,1)S(1)} %all_gather.3), channel_id=1, source_target_pairs={{0,252},{4,0},{8,4},{12,8},{16,12},{20,16},{24,20},{28,24},{32,28}... | collective-permute-start | bytes 196616 | tf_op jit(solution)/shard_map/ppermute | solution.py:19
  18.5 8.8 %collective-permute-start = (bf16[256,128]{1,0:T(8,128)(2,1)S(1)}, bf16[256,128]{1,0:T(8,128)(2,1)S(1)}, u32[]{:S(2)}, u32[]{:S(2)}) collective-permute-start(bf16[256,128]{1,0:T(8,128)(2,1)S(1)} %all_gather.3), channel_id=1, source_target_pairs={{0,4},{4,8},{8,12},{12,16},{16,20},{20,24},{24,28},{28,32},{32,36}... | collective-permute-start | bytes 196616 | tf_op jit(solution)/shard_map/ppermute | solution.py:19
  27.4 11.4 %collective-permute-start.3 = (bf16[256,384]{1,0:T(8,128)(2,1)S(1)}, bf16[256,384]{1,0:T(8,128)(2,1)S(1)}, u32[]{:S(2)}, u32[]{:S(2)}) collective-permute-start(bf16[256,384]{1,0:T(8,128)(2,1)S(1)} %constant_dynamic-update-slice_fusion), channel_id=1, source_target_pairs={{0,244},{4,248},{8,252},{12,0},{16,4},{20,8},{24,12},{28,16},{32,2... | collective-permute-start | bytes 589832 | tf_op jit(solution)/shard_map/ppermute | solution.py:19
  27.5 11.2 %collective-permute-start.2 = (bf16[256,384]{1,0:T(8,128)(2,1)S(1)}, bf16[256,384]{1,0:T(8,128)(2,1)S(1)}, u32[]{:S(2)}, u32[]{:S(2)}) collective-permute-start(bf16[256,384]{1,0:T(8,128)(2,1)S(1)} %constant_dynamic-update-slice_fusion), channel_id=1, source_target_pairs={{0,12},{4,16},{8,20},{12,24},{16,28},{20,32},{24,36},{28,40},{32,4... | collective-permute-start | bytes 589832 | tf_op jit(solution)/shard_map/ppermute | solution.py:19
  44.0 11.0 %copy-start.3 = (s32[4]{0:T(128)S(1)}, s32[4]{0:T(128)}, u32[]{:S(2)}) copy-start(s32[4]{0:T(128)} %param.9) | copy-start | bytes 52
  45.2 25.1 %all-to-all-start = ((f32[256,1,256]{2,1,0:T(1,128)}), f32[256,1,256]{2,1,0:T(1,128)S(1)}, u32[]{:S(2)}, u32[]{:S(2)}) async-start(f32[256,1,256]{2,1,0:T(1,128)} %all_to_all.8), calls=%async_computation | async-start | bytes 524288 | tf_op jit(solution)/shard_map/all_to_all | solution.py:125

commit v15 on v14

--- a/solution.py
+++ b/solution.py
@@ -71,11 +71,11 @@
     cross_real = time_sum(first_real, second_real) + time_sum(first_imag, second_imag)
     cross_imag = time_sum(first_imag, second_real) - time_sum(first_real, second_imag)
     power = jnp.einsum("qrct,qrct->qc", parts, parts, preferred_element_type=jnp.float32)
-    high = power.astype(jnp.bfloat16)
-    rest = power - high.astype(jnp.float32)
-    middle = rest.astype(jnp.bfloat16)
-    low = (rest - middle.astype(jnp.float32)).astype(jnp.bfloat16)
-    pieces = jnp.stack([high, middle, low])
+    high = lax.reduce_precision(power, exponent_bits=8, mantissa_bits=7)
+    rest = power - high
+    middle = lax.reduce_precision(rest, exponent_bits=8, mantissa_bits=7)
+    low = rest - middle
+    pieces = jnp.stack([high, middle, low]).astype(jnp.bfloat16)
     picked_power = jnp.einsum("pc,kqc->kqp", pick, pieces, preferred_element_type=jnp.float32)
     owner_power = (picked_power[0] + picked_power[1]) + picked_power[2]
     power_first = owner_power[:, :pairs]

time: 73.5 us -> 73.5 us (level)
  no operation moved by 1% of the time
where the time goes in v15:
time: 73.5 us; the launch traced here: 73.3 us
  starting transfers between devices  21.3 us (29%)
  waiting for transfers between devices  18.1 us (25%)
  other arithmetic  9.76 us (13%)
  matrix products  8.63 us (12%)
  blocking collectives  8.3 us (11%)
  local copies, waits for them, and re-layouts  6 us (8%)
  between operations  1.15 us (2%)
    all_to_all x1, waiting for transfers between devices, shards(): exchanged = lax.all_to_all(partial_value, ('tm', 'chan'), 0, 0, tiled=True)  14 us
    ppermute x4, starting transfers between devices, from_behind(): lax.ppermute(array, axis, [(i, (i + by) % peers) for i in range(peers)])  11.5 us
    all_to_all x1, starting transfers between devices, shards(): exchanged = lax.all_to_all(partial_value, ('tm', 'chan'), 0, 0, tiled=True)  9.81 us
    all_gather x1, blocking collectives, shards(): gathered = lax.all_gather(rounded, 'chan', axis=0, tiled=True)  8.3 us
    dot_general x2, matrix products, pair_sums(): jnp.einsum('pc,qrct->qrpt', pick, parts, preferred_element_type=jnp.bfloa...  5.6 us
    ppermute x4, waiting for transfers between devices, from_behind(): lax.ppermute(array, axis, [(i, (i + by) % peers) for i in range(peers)])  4.14 us
    dot_general x2, other arithmetic, time_sum(): jnp.einsum('qpt,qpt->qp', left, right, preferred_element_type=jnp.float32)  4.04 us
    dot_general x2, matrix products, pair_sums(): jnp.einsum('pc,kqc->kqp', pick, pieces, preferred_element_type=jnp.float32)  1.86 us
  transfers between devices with their start and end apart: 5, of which 2 were waited for; matrix products, arithmetic and copies ran while one was open for 20% of the time, Pallas kernels for 0%

profile of v15, /device:TPU:1, one launch (start us, length us, event | category | flops | bytes accessed | tf_op | source)
XLA Modules:
  0.0 73.3 jit_solution(7453119186605395407)
XLA Ops:
  0.7 0.8 %convert_element_type.133 = bf16[64,128]{1,0:T(8,128)(2,1)S(1)} convert(f32[64,128]{1,0:T(8,128)} %param.5) | non-fusion elementwise | flops 8192 | bytes 49152 | tf_op jit(solution)/shard_map/convert_element_type | solution.py:93
  1.4 8.3 %all_gather.3 = bf16[256,128]{1,0:T(8,128)(2,1)S(1)} all-gather(bf16[64,128]{1,0:T(8,128)(2,1)S(1)} %convert_element_type.133), channel_id=1, replica_groups=mesh['tm'=64,'chan'=4] {'chan'}, dimensions={0}, use_global_device_ids=true | all-gather | bytes 81920 | tf_op jit(solution)/shard_map/all_gather | solution.py:94
  9.7 8.8 %collective-permute-start.1 = (bf16[256,128]{1,0:T(8,128)(2,1)S(1)}, bf16[256,128]{1,0:T(8,128)(2,1)S(1)}, u32[]{:S(2)}, u32[]{:S(2)}) collective-permute-start(bf16[256,128]{1,0:T(8,128)(2,1)S(1)} %all_gather.3), channel_id=1, source_target_pairs={{0,252},{4,0},{8,4},{12,8},{16,12},{20,16},{24,20},{28,24},{32,28}... | collective-permute-start | bytes 196616 | tf_op jit(solution)/shard_map/ppermute | solution.py:19
  18.6 0.6 gather_fusion.1
  19.3 0.6 gather_fusion
  21.4 0.8 %fusion.25 = (bf16[6,1,384,128]{2,3,1,0:T(8,128)(2,1)S(1)}, bf16[6,1,384,128]{2,3,1,0:T(8,128)(2,1)S(1)}) fusion(f32[6,128]{1,0:T(8,128)S(1)} %get-tuple-element.45, f32[6,384]{1,0:T(8,128)S(1)} %get-tuple-element.38, f32[6,128]{1,0:T(8,128)S(1)} %get-tuple-element.44, f32[6,384]{1,0:T(8,128)S(1)} %get-tuple-element.37, f32[6]{0:T(128)S(1)} %get-tuple-element.57, ...), kind=kLoop, calls=%fused_computation.47 | loop fusion | flops 5013504 | bytes 1597512 | tf_op jit(solution)/shard_map/convert_element_type | solution.py:40
  22.2 1.0 %fusion.27 = (bf16[2,1,1152,128]{2,3,1,0:T(8,128)(2,1)S(1)}, bf16[2,1,1152,128]{2,3,1,0:T(8,128)(2,1)S(1)}) fusion(f32[2,128]{1,0:T(2,128)S(1)} %get-tuple-element.47, f32[2,1152]{1,0:T(2,128)S(1)} %get-tuple-element.31, f32[2,128]{1,0:T(2,128)S(1)} %get-tuple-element.46, f32[2,1152]{1,0:T(2,128)S(1)} %get-tuple-element.30, f32[2]{0:T(128)S(1)} %get-tuple-element.53, ...), kind=kLoop, calls=%fused_computation.49 | loop fusion | flops 5013504 | bytes 2379800 | tf_op jit(solution)/shard_map/convert_element_type | solution.py:40
  23.2 4.1 %collective-permute-done = bf16[256,128]{1,0:T(8,128)(2,1)S(1)} collective-permute-done((bf16[256,128]{1,0:T(8,128)(2,1)S(1)}, bf16[256,128]{1,0:T(8,128)(2,1)S(1)}, u32[]{:S(2)}, u32[]{:S(2)}) %collective-permute-start) | collective-permute-done | bytes 65568 | tf_op jit(solution)/shard_map/ppermute | solution.py:19
  27.5 2.7 %collective-permute-start.2 = (bf16[256,384]{1,0:T(8,128)(2,1)S(1)}, bf16[256,384]{1,0:T(8,128)(2,1)S(1)}, u32[]{:S(2)}, u32[]{:S(2)}) collective-permute-start(bf16[256,384]{1,0:T(8,128)(2,1)S(1)} %constant_dynamic-update-slice_fusion), channel_id=1, source_target_pairs={{0,12},{4,16},{8,20},{12,24},{16,28},{20,32},{24,36},{28,40},{32,4... | collective-permute-start | bytes 589832 | tf_op jit(solution)/shard_map/ppermute | solution.py:19
  30.2 0.6 fusion.20
  30.8 0.8 %fusion.10 = f32[3,6,4096]{2,1,0:T(8,128)S(1)} fusion(s32[4096]{0:T(1024)S(1)} %pad_add_fusion, bf16[1,6,256]{2,1,0:T(8,128)(2,1)S(1)} %get-tuple-element.33, bf16[1,6,256]{2,1,0:T(8,128)(2,1)S(1)} %get-tuple-element.34, bf16[1,6,256]{2,1,0:T(8,128)(2,1)S(1)} %get-tuple-element.32), kind=kOutput, calls=%fused_computation.16 | convolution fusion | flops 38806528 | bytes 320512 | tf_op jit(solution)/shard_map/pc,kqc->kqp/dot_general | solution.py:79
  31.7 3.9 %convolution_bitcast_fusion = bf16[6,2,4096,128]{2,3,1,0:T(8,128)(2,1)S(1)} fusion(s32[4096]{0:T(1024)S(1)} %pad_add_fusion, bf16[6,2,128,256]{3,2,1,0:T(8,128)(2,1)S(1)} %get-tuple-element.51), kind=kOutput, calls=%fused_computation.6 | convolution fusion | flops 3222274048 | bytes 13385728 | tf_op jit(solution)/shard_map/pc,qrct->qrpt/dot_general | solution.py:61
  35.6 3.1 %fusion.2 = (f32[6,2048]{1,0:T(8,128)S(1)}, f32[6,2048]{1,0:T(8,128)S(1)}, f32[6,2048]{1,0:T(8,128)S(1)}, f32[6,2048]{1,0:T(8,128)S(1)}) fusion(bf16[6,2,4096,128]{2,3,1,0:T(8,128)(2,1)S(1)} %convolution_bitcast_fusion), kind=kLoop, calls=%fused_computation.9 | loop fusion | flops 18825216 | bytes 12779520 | tf_op jit(solution)/shard_map/qpt,qpt->qp/dot_general | solution.py:69
  39.5 1.0 %fusion.8 = f32[3,2,4096]{2,1,0:T(2,128)S(1)} fusion(s32[4096]{0:T(1024)S(1)} %pad_add_fusion, bf16[3,2,256]{2,0,1:T(4,128)(2,1)S(1)} %pad_maximum_fusion.1), kind=kOutput, calls=%fused_computation.15 | convolution fusion | flops 13631488 | bytes 117760 | tf_op jit(solution)/shard_map/pc,kqc->kqp/dot_general | solution.py:79
  40.6 1.7 %convolution_bitcast_fusion.1 = bf16[2,2,4096,128]{2,3,1,0:T(8,128)(2,1)S(1)} fusion(s32[4096]{0:T(1024)S(1)} %pad_add_fusion, bf16[2,2,128,256]{3,2,1,0:T(8,128)(2,1)S(1)} %get-tuple-element.49), kind=kOutput, calls=%fused_computation.11 | convolution fusion | flops 1074790400 | bytes 4472832 | tf_op jit(solution)/shard_map/pc,qrct->qrpt/dot_general | solution.py:61
  42.3 1.0 %fusion.14 = (f32[2,2048]{1,0:T(2,128)S(1)}, f32[2,2048]{1,0:T(2,128)S(1)}, f32[2,2048]{1,0:T(2,128)S(1)}, f32[2,2048]{1,0:T(2,128)S(1)}) fusion(bf16[2,2,4096,128]{2,3,1,0:T(8,128)(2,1)S(1)} %convolution_bitcast_fusion.1), kind=kLoop, calls=%fused_computation.27 | loop fusion | flops 6275072 | bytes 4259840 | tf_op jit(solution)/shard_map/qpt,qpt->qp/dot_general | solution.py:69
  44.0 1.1 %all_to_all.8 = f32[256,1,256]{2,1,0:T(1,128)} reshape(f32[2048,32]{1,0:T(8,128)S(1)} %copy.62) | data formatting | bytes 524288 | tf_op jit(solution)/shard_map/all_to_all | solution.py:125
  45.2 9.8 %all-to-all-start = ((f32[256,1,256]{2,1,0:T(1,128)}), f32[256,1,256]{2,1,0:T(1,128)S(1)}, u32[]{:S(2)}, u32[]{:S(2)}) async-start(f32[256,1,256]{2,1,0:T(1,128)} %all_to_all.8), calls=%async_computation | async-start | bytes 524288 | tf_op jit(solution)/shard_map/all_to_all | solution.py:125
  55.0 0.6 dynamic_slice.3
  55.6 0.7 add_compare_fusion
  56.2 14.0 %all-to-all-done = f32[256,1,256]{2,1,0:T(1,128)S(1)} async-done(((f32[256,1,256]{2,1,0:T(1,128)}), f32[256,1,256]{2,1,0:T(1,128)S(1)}, u32[]{:S(2)}, u32[]{:S(2)}) %all-to-all-start) | async-done | bytes 262176 | tf_op jit(solution)/shard_map/all_to_all | solution.py:125
  70.2 0.6 reduce.10
  71.9 0.7 select_bitcast_fusion
  72.7 0.6 copy.67
  (76 shorter events, 4.3 us)
Async XLA Ops:
  0.6 18.0 %copy-start = (s32[32]{0:T(128)S(1)}, s32[32]{0:T(128)}, u32[]{:S(2)}) copy-start(s32[32]{0:T(128)} %param.6) | copy-start | bytes 388
  0.6 19.9 %copy-start.1 = (s32[4,512]{1,0:T(4,128)S(1)}, s32[4,512]{1,0:T(4,128)}, u32[]{:S(2)}) copy-start(s32[4,512]{1,0:T(4,128)} %param.7) | copy-start | bytes 24580
  0.7 20.2 %copy-start.2 = (s32[4,512]{1,0:T(4,128)S(1)}, s32[4,512]{1,0:T(4,128)}, u32[]{:S(2)}) copy-start(s32[4,512]{1,0:T(4,128)} %param.8) | copy-start | bytes 24580
  9.7 17.6 %collective-permute-start.1 = (bf16[256,128]{1,0:T(8,128)(2,1)S(1)}, bf16[256,128]{1,0:T(8,128)(2,1)S(1)}, u32[]{:S(2)}, u32[]{:S(2)}) collective-permute-start(bf16[256,128]{1,0:T(8,128)(2,1)S(1)} %all_gather.3), channel_id=1, source_target_pairs={{0,252},{4,0},{8,4},{12,8},{16,12},{20,16},{24,20},{28,24},{32,28}... | collective-permute-start | bytes 196616 | tf_op jit(solution)/shard_map/ppermute | solution.py:19
  18.5 8.8 %collective-permute-start = (bf16[256,128]{1,0:T(8,128)(2,1)S(1)}, bf16[256,128]{1,0:T(8,128)(2,1)S(1)}, u32[]{:S(2)}, u32[]{:S(2)}) collective-permute-start(bf16[256,128]{1,0:T(8,128)(2,1)S(1)} %all_gather.3), channel_id=1, source_target_pairs={{0,4},{4,8},{8,12},{12,16},{16,20},{20,24},{24,28},{28,32},{32,36}... | collective-permute-start | bytes 196616 | tf_op jit(solution)/shard_map/ppermute | solution.py:19
  27.4 11.4 %collective-permute-start.3 = (bf16[256,384]{1,0:T(8,128)(2,1)S(1)}, bf16[256,384]{1,0:T(8,128)(2,1)S(1)}, u32[]{:S(2)}, u32[]{:S(2)}) collective-permute-start(bf16[256,384]{1,0:T(8,128)(2,1)S(1)} %constant_dynamic-update-slice_fusion), channel_id=1, source_target_pairs={{0,244},{4,248},{8,252},{12,0},{16,4},{20,8},{24,12},{28,16},{32,2... | collective-permute-start | bytes 589832 | tf_op jit(solution)/shard_map/ppermute | solution.py:19
  27.5 11.2 %collective-permute-start.2 = (bf16[256,384]{1,0:T(8,128)(2,1)S(1)}, bf16[256,384]{1,0:T(8,128)(2,1)S(1)}, u32[]{:S(2)}, u32[]{:S(2)}) collective-permute-start(bf16[256,384]{1,0:T(8,128)(2,1)S(1)} %constant_dynamic-update-slice_fusion), channel_id=1, source_target_pairs={{0,12},{4,16},{8,20},{12,24},{16,28},{20,32},{24,36},{28,40},{32,4... | collective-permute-start | bytes 589832 | tf_op jit(solution)/shard_map/ppermute | solution.py:19
  44.0 11.0 %copy-start.3 = (s32[4]{0:T(128)S(1)}, s32[4]{0:T(128)}, u32[]{:S(2)}) copy-start(s32[4]{0:T(128)} %param.9) | copy-start | bytes 52
  45.2 25.1 %all-to-all-start = ((f32[256,1,256]{2,1,0:T(1,128)}), f32[256,1,256]{2,1,0:T(1,128)S(1)}, u32[]{:S(2)}, u32[]{:S(2)}) async-start(f32[256,1,256]{2,1,0:T(1,128)} %all_to_all.8), calls=%async_computation | async-start | bytes 524288 | tf_op jit(solution)/shard_map/all_to_all | solution.py:125

commit v16 on v15

--- a/solution.py
+++ b/solution.py
@@ -91,7 +91,8 @@
     time_span = signal.shape[1]
     ntime = time_span * time_devices
     rounded = signal.astype(jnp.bfloat16)
-    gathered = lax.all_gather(rounded, "chan", axis=0, tiled=True)
+    copies = jnp.broadcast_to(rounded[None], (groups,) + rounded.shape)
+    gathered = lax.all_to_all(copies, "chan", 0, 0, tiled=True).reshape(-1, rounded.shape[1])
     near = jnp.concatenate(
         [from_behind(gathered, "tm", 1), gathered, from_behind(gathered, "tm", -1)], axis=1
     )

time: 73.5 us -> 77.8 us (1.059)
  blocking collectives: 8.3 us -> 0 us
  starting transfers between devices: 21.3 us -> 28.5 us
  waiting for transfers between devices: 18.1 us -> 23 us
    all_gather x1 -> x0, blocking collectives: 8.3 us -> none  [shards(): gathered = lax.all_gather(rounded, 'chan', axis=0, tiled=True)]
    all_to_all x0 -> x1, starting transfers between devices: none -> 6.49 us  [shards(): lax.all_to_all(copies, 'chan', 0, 0, tiled=True)]
    ppermute x4, waiting for transfers between devices: 4.14 us -> 8.84 us  [from_behind(): lax.ppermute(array, axis, [(i, (i + by) % peers) for i in range(peers)])]
    ppermute x4, starting transfers between devices: 11.5 us -> 14.9 us  [from_behind(): lax.ppermute(array, axis, [(i, (i + by) % peers) for i in range(peers)])]
    all_to_all x1, starting transfers between devices: 9.81 us -> 7.08 us  [shards(): exchanged = lax.all_to_all(partial_value, ('tm', 'chan'), 0, 0, tiled=True)]
  transfers between devices with their start and end apart: 5 -> 6, of which waited for: 2 -> 3; matrix products, arithmetic and copies ran while one was open for 20% -> 18% of each run, Pallas kernels for 0% -> 0%
where the time goes in v16:
time: 77.8 us; the launch traced here: 77.5 us
  starting transfers between devices  28.5 us (37%)
  waiting for transfers between devices  23 us (30%)
  other arithmetic  9.78 us (13%)
  matrix products  8.63 us (11%)
  local copies, waits for them, and re-layouts  6.58 us (8%)
  between operations  1.13 us (1%)
    ppermute x4, starting transfers between devices, from_behind(): lax.ppermute(array, axis, [(i, (i + by) % peers) for i in range(peers)])  14.9 us
    all_to_all x1, waiting for transfers between devices, shards(): exchanged = lax.all_to_all(partial_value, ('tm', 'chan'), 0, 0, tiled=True)  14.1 us
    ppermute x4, waiting for transfers between devices, from_behind(): lax.ppermute(array, axis, [(i, (i + by) % peers) for i in range(peers)])  8.84 us
    all_to_all x1, starting transfers between devices, shards(): exchanged = lax.all_to_all(partial_value, ('tm', 'chan'), 0, 0, tiled=True)  7.08 us
    all_to_all x1, starting transfers between devices, shards(): lax.all_to_all(copies, 'chan', 0, 0, tiled=True)  6.49 us
    dot_general x2, matrix products, pair_sums(): jnp.einsum('pc,qrct->qrpt', pick, parts, preferred_element_type=jnp.bfloa...  5.6 us
    dot_general x2, other arithmetic, time_sum(): jnp.einsum('qpt,qpt->qp', left, right, preferred_element_type=jnp.float32)  4.04 us
    dot_general x2, matrix products, pair_sums(): jnp.einsum('pc,kqc->kqp', pick, pieces, preferred_element_type=jnp.float32)  1.86 us
  transfers between devices with their start and end apart: 6, of which 3 were waited for; matrix products, arithmetic and copies ran while one was open for 18% of the time, Pallas kernels for 0%

profile of v16, /device:TPU:1, one launch (start us, length us, event | category | flops | bytes accessed | tf_op | source)
XLA Modules:
  0.0 77.5 jit_solution(10832321081606241665)
XLA Ops:
  0.6 0.8 convert_element_type.133
  1.4 0.6 broadcast_in_dim.31
  2.0 6.5 %all-to-all-start = ((bf16[4,64,128]{2,1,0:T(8,128)(2,1)}), bf16[4,64,128]{2,1,0:T(8,128)(2,1)S(1)}, u32[]{:S(2)}, u32[]{:S(2)}) async-start(bf16[4,64,128]{2,1,0:T(8,128)(2,1)} %broadcast_in_dim.31), calls=%async_computation | async-start | bytes 131072 | tf_op jit(solution)/shard_map/all_to_all | solution.py:95
  8.7 0.6 gather_fusion.1
  9.3 0.6 gather_fusion
  10.7 1.0 %fusion.27 = (bf16[2,1,1152,128]{2,3,1,0:T(8,128)(2,1)S(1)}, bf16[2,1,1152,128]{2,3,1,0:T(8,128)(2,1)S(1)}) fusion(f32[2,128]{1,0:T(2,128)S(1)} %get-tuple-element.47, f32[2,1152]{1,0:T(2,128)S(1)} %get-tuple-element.31, f32[2,128]{1,0:T(2,128)S(1)} %get-tuple-element.46, f32[2,1152]{1,0:T(2,128)S(1)} %get-tuple-element.30, f32[2]{0:T(128)S(1)} %get-tuple-element.53, ...), kind=kLoop, calls=%fused_computation.49 | loop fusion | flops 5013504 | bytes 2379800 | tf_op jit(solution)/shard_map/convert_element_type | solution.py:40
  11.7 0.8 %fusion.25 = (bf16[6,1,384,128]{2,3,1,0:T(8,128)(2,1)S(1)}, bf16[6,1,384,128]{2,3,1,0:T(8,128)(2,1)S(1)}) fusion(f32[6,128]{1,0:T(8,128)S(1)} %get-tuple-element.45, f32[6,384]{1,0:T(8,128)S(1)} %get-tuple-element.38, f32[6,128]{1,0:T(8,128)S(1)} %get-tuple-element.44, f32[6,384]{1,0:T(8,128)S(1)} %get-tuple-element.37, f32[6]{0:T(128)S(1)} %get-tuple-element.57, ...), kind=kLoop, calls=%fused_computation.47 | loop fusion | flops 5013504 | bytes 1597512 | tf_op jit(solution)/shard_map/convert_element_type | solution.py:40
  13.3 8.8 %collective-permute-start.1 = (bf16[256,128]{1,0:T(8,128)(2,1)S(1)}, bf16[256,128]{1,0:T(8,128)(2,1)S(1)}, u32[]{:S(2)}, u32[]{:S(2)}) collective-permute-start(bf16[256,128]{1,0:T(8,128)(2,1)S(1)} %bitcast.175), channel_id=1, source_target_pairs={{0,252},{4,0},{8,4},{12,8},{16,12},{20,16},{24,20},{28,24},{32,28}... | collective-permute-start | bytes 196616 | tf_op jit(solution)/shard_map/ppermute | solution.py:19
  22.1 1.3 %collective-permute-done.1 = bf16[256,128]{1,0:T(8,128)(2,1)S(1)} collective-permute-done((bf16[256,128]{1,0:T(8,128)(2,1)S(1)}, bf16[256,128]{1,0:T(8,128)(2,1)S(1)}, u32[]{:S(2)}, u32[]{:S(2)}) %collective-permute-start.1) | collective-permute-done | bytes 65568 | tf_op jit(solution)/shard_map/ppermute | solution.py:19
  23.4 7.5 %collective-permute-done = bf16[256,128]{1,0:T(8,128)(2,1)S(1)} collective-permute-done((bf16[256,128]{1,0:T(8,128)(2,1)S(1)}, bf16[256,128]{1,0:T(8,128)(2,1)S(1)}, u32[]{:S(2)}, u32[]{:S(2)}) %collective-permute-start) | collective-permute-done | bytes 65568 | tf_op jit(solution)/shard_map/ppermute | solution.py:19
  31.1 6.0 %collective-permute-start.3 = (bf16[256,384]{1,0:T(8,128)(2,1)S(1)}, bf16[256,384]{1,0:T(8,128)(2,1)S(1)}, u32[]{:S(2)}, u32[]{:S(2)}) collective-permute-start(bf16[256,384]{1,0:T(8,128)(2,1)S(1)} %pad_maximum_fusion), channel_id=1, source_target_pairs={{0,244},{4,248},{8,252},{12,0},{16,4},{20,8},{24,12},{28,16},{32,2... | collective-permute-start | bytes 589832 | tf_op jit(solution)/shard_map/ppermute | solution.py:19
  37.0 0.6 fusion.20
  37.6 0.8 %fusion.10 = f32[3,6,4096]{2,1,0:T(8,128)S(1)} fusion(s32[4096]{0:T(1024)S(1)} %pad_add_fusion, bf16[1,6,256]{2,1,0:T(8,128)(2,1)S(1)} %get-tuple-element.33, bf16[1,6,256]{2,1,0:T(8,128)(2,1)S(1)} %get-tuple-element.34, bf16[1,6,256]{2,1,0:T(8,128)(2,1)S(1)} %get-tuple-element.32), kind=kOutput, calls=%fused_computation.16 | convolution fusion | flops 38806528 | bytes 320512 | tf_op jit(solution)/shard_map/pc,kqc->kqp/dot_general | solution.py:79
  38.5 3.9 %convolution_bitcast_fusion = bf16[6,2,4096,128]{2,3,1,0:T(8,128)(2,1)S(1)} fusion(s32[4096]{0:T(1024)S(1)} %pad_add_fusion, bf16[6,2,128,256]{3,2,1,0:T(8,128)(2,1)S(1)} %get-tuple-element.51), kind=kOutput, calls=%fused_computation.6 | convolution fusion | flops 3222274048 | bytes 13385728 | tf_op jit(solution)/shard_map/pc,qrct->qrpt/dot_general | solution.py:61
  42.4 3.1 %fusion.2 = (f32[6,2048]{1,0:T(8,128)S(1)}, f32[6,2048]{1,0:T(8,128)S(1)}, f32[6,2048]{1,0:T(8,128)S(1)}, f32[6,2048]{1,0:T(8,128)S(1)}) fusion(bf16[6,2,4096,128]{2,3,1,0:T(8,128)(2,1)S(1)} %convolution_bitcast_fusion), kind=kLoop, calls=%fused_computation.9 | loop fusion | flops 18825216 | bytes 12779520 | tf_op jit(solution)/shard_map/qpt,qpt->qp/dot_general | solution.py:69
  46.4 1.0 %fusion.8 = f32[3,2,4096]{2,1,0:T(2,128)S(1)} fusion(s32[4096]{0:T(1024)S(1)} %pad_add_fusion, bf16[3,2,256]{2,0,1:T(4,128)(2,1)S(1)} %pad_maximum_fusion.2), kind=kOutput, calls=%fused_computation.15 | convolution fusion | flops 13631488 | bytes 117760 | tf_op jit(solution)/shard_map/pc,kqc->kqp/dot_general | solution.py:79
  47.4 1.7 %convolution_bitcast_fusion.1 = bf16[2,2,4096,128]{2,3,1,0:T(8,128)(2,1)S(1)} fusion(s32[4096]{0:T(1024)S(1)} %pad_add_fusion, bf16[2,2,128,256]{3,2,1,0:T(8,128)(2,1)S(1)} %get-tuple-element.49), kind=kOutput, calls=%fused_computation.11 | convolution fusion | flops 1074790400 | bytes 4472832 | tf_op jit(solution)/shard_map/pc,qrct->qrpt/dot_general | solution.py:61
  49.2 1.0 %fusion.14 = (f32[2,2048]{1,0:T(2,128)S(1)}, f32[2,2048]{1,0:T(2,128)S(1)}, f32[2,2048]{1,0:T(2,128)S(1)}, f32[2,2048]{1,0:T(2,128)S(1)}) fusion(bf16[2,2,4096,128]{2,3,1,0:T(8,128)(2,1)S(1)} %convolution_bitcast_fusion.1), kind=kLoop, calls=%fused_computation.27 | loop fusion | flops 6275072 | bytes 4259840 | tf_op jit(solution)/shard_map/qpt,qpt->qp/dot_general | solution.py:69
  50.9 1.1 %all_to_all.12 = f32[256,1,256]{2,1,0:T(1,128)} reshape(f32[2048,32]{1,0:T(8,128)S(1)} %copy.62) | data formatting | bytes 524288 | tf_op jit(solution)/shard_map/all_to_all | solution.py:126
  52.0 7.1 %all-to-all-start.1 = ((f32[256,1,256]{2,1,0:T(1,128)}), f32[256,1,256]{2,1,0:T(1,128)S(1)}, u32[]{:S(2)}, u32[]{:S(2)}) async-start(f32[256,1,256]{2,1,0:T(1,128)} %all_to_all.12), calls=%async_computation.1 | async-start | bytes 524288 | tf_op jit(solution)/shard_map/all_to_all | solution.py:126
  59.7 0.7 add_compare_fusion
  60.4 14.1 %all-to-all-done.1 = f32[256,1,256]{2,1,0:T(1,128)S(1)} async-done(((f32[256,1,256]{2,1,0:T(1,128)}), f32[256,1,256]{2,1,0:T(1,128)S(1)}, u32[]{:S(2)}, u32[]{:S(2)}) %all-to-all-start.1) | async-done | bytes 262176 | tf_op jit(solution)/shard_map/all_to_all | solution.py:126
  74.5 0.6 reduce.10
  76.2 0.7 select_bitcast_fusion
  (76 shorter events, 5.5 us)
Async XLA Ops:
  0.6 8.0 %copy-start = (s32[32]{0:T(128)S(1)}, s32[32]{0:T(128)}, u32[]{:S(2)}) copy-start(s32[32]{0:T(128)} %param.6) | copy-start | bytes 388
  2.0 11.2 %all-to-all-start = ((bf16[4,64,128]{2,1,0:T(8,128)(2,1)}), bf16[4,64,128]{2,1,0:T(8,128)(2,1)S(1)}, u32[]{:S(2)}, u32[]{:S(2)}) async-start(bf16[4,64,128]{2,1,0:T(8,128)(2,1)} %broadcast_in_dim.31), calls=%async_computation | async-start | bytes 131072 | tf_op jit(solution)/shard_map/all_to_all | solution.py:95
  11.7 0.8 %copy-start.1 = (s32[4,512]{1,0:T(4,128)S(1)}, s32[4,512]{1,0:T(4,128)}, u32[]{:S(2)}) copy-start(s32[4,512]{1,0:T(4,128)} %param.7) | copy-start | bytes 24580
  11.7 1.2 %copy-start.2 = (s32[4,512]{1,0:T(4,128)S(1)}, s32[4,512]{1,0:T(4,128)}, u32[]{:S(2)}) copy-start(s32[4,512]{1,0:T(4,128)} %param.8) | copy-start | bytes 24580
  13.3 10.2 %collective-permute-start.1 = (bf16[256,128]{1,0:T(8,128)(2,1)S(1)}, bf16[256,128]{1,0:T(8,128)(2,1)S(1)}, u32[]{:S(2)}, u32[]{:S(2)}) collective-permute-start(bf16[256,128]{1,0:T(8,128)(2,1)S(1)} %bitcast.175), channel_id=1, source_target_pairs={{0,252},{4,0},{8,4},{12,8},{16,12},{20,16},{24,20},{28,24},{32,28}... | collective-permute-start | bytes 196616 | tf_op jit(solution)/shard_map/ppermute | solution.py:19
  22.1 8.8 %collective-permute-start = (bf16[256,128]{1,0:T(8,128)(2,1)S(1)}, bf16[256,128]{1,0:T(8,128)(2,1)S(1)}, u32[]{:S(2)}, u32[]{:S(2)}) collective-permute-start(bf16[256,128]{1,0:T(8,128)(2,1)S(1)} %bitcast.176), channel_id=1, source_target_pairs={{0,4},{4,8},{8,12},{12,16},{16,20},{20,24},{24,28},{28,32},{32,36}... | collective-permute-start | bytes 196616 | tf_op jit(solution)/shard_map/ppermute | solution.py:19
  31.0 14.6 %collective-permute-start.2 = (bf16[256,384]{1,0:T(8,128)(2,1)S(1)}, bf16[256,384]{1,0:T(8,128)(2,1)S(1)}, u32[]{:S(2)}, u32[]{:S(2)}) collective-permute-start(bf16[256,384]{1,0:T(8,128)(2,1)S(1)} %pad_maximum_fusion), channel_id=1, source_target_pairs={{0,12},{4,16},{8,20},{12,24},{16,28},{20,32},{24,36},{28,40},{32,4... | collective-permute-start | bytes 589832 | tf_op jit(solution)/shard_map/ppermute | solution.py:19
  31.1 14.6 %collective-permute-start.3 = (bf16[256,384]{1,0:T(8,128)(2,1)S(1)}, bf16[256,384]{1,0:T(8,128)(2,1)S(1)}, u32[]{:S(2)}, u32[]{:S(2)}) collective-permute-start(bf16[256,384]{1,0:T(8,128)(2,1)S(1)} %pad_maximum_fusion), channel_id=1, source_target_pairs={{0,244},{4,248},{8,252},{12,0},{16,4},{20,8},{24,12},{28,16},{32,2... | collective-permute-start | bytes 589832 | tf_op jit(solution)/shard_map/ppermute | solution.py:19
  50.8 8.3 %copy-start.3 = (s32[4]{0:T(128)S(1)}, s32[4]{0:T(128)}, u32[]{:S(2)}) copy-start(s32[4]{0:T(128)} %param.9) | copy-start | bytes 52
  52.0 22.5 %all-to-all-start.1 = ((f32[256,1,256]{2,1,0:T(1,128)}), f32[256,1,256]{2,1,0:T(1,128)S(1)}, u32[]{:S(2)}, u32[]{:S(2)}) async-start(f32[256,1,256]{2,1,0:T(1,128)} %all_to_all.12), calls=%async_computation.1 | async-start | bytes 524288 | tf_op jit(solution)/shard_map/all_to_all | solution.py:126

commit v17 on v15

--- a/solution.py
+++ b/solution.py
@@ -124,27 +124,25 @@
     partial_value = sums.reshape(per_group * values, -1).T.reshape(destinations, -1)
     exchanged = lax.all_to_all(partial_value, ("tm", "chan"), 0, 0, tiled=True)
     summed = jnp.sum(exchanged.reshape(time_devices, groups, -1), axis=0)
-    owned = summed.reshape(groups, slots_local, per_group, values).transpose(0, 2, 3, 1) / ntime
-    owned = owned.reshape(groups, per_group, values, slots_local)
+    owned = summed.reshape(groups, slots_local, per_group, values).transpose(1, 3, 0, 2) / ntime
     owned = jnp.concatenate(
         [
-            owned[:, :narrow_count].reshape(groups * narrow_count, values, slots_local),
-            owned[:, narrow_count:].reshape(groups * wide_count, values, slots_local),
+            owned[:, :, :, :narrow_count].reshape(slots_local, values, groups * narrow_count),
+            owned[:, :, :, narrow_count:].reshape(slots_local, values, groups * wide_count),
         ],
-        axis=0,
+        axis=2,
     )
     slot_index = time_index * slots_local + jnp.arange(slots_local, dtype=jnp.int32)
     alive_mask = slot_index < pair_count[cluster_number]
-    cross_real = owned[:, 0, :].T
-    cross_imag = owned[:, 1, :].T
-    first_power = owned[:, 2, :].T
-    second_power = owned[:, 3, :].T
+    cross_real = owned[:, 0, :]
+    cross_imag = owned[:, 1, :]
+    first_power = owned[:, 2, :]
+    second_power = owned[:, 3, :]
     coherence = (cross_real * cross_real + cross_imag * cross_imag) / (
         (first_power + power_floor) * (second_power + power_floor)
     )
     coherence = jnp.where(alive_mask[:, None], coherence, 0.0)[None]
-    cross = jnp.stack([cross_real, cross_imag], axis=1)
-    cross = jnp.where(alive_mask[:, None, None], cross, 0.0)[None]
+    cross = jnp.where(alive_mask[:, None, None], owned[:, :2, :], 0.0)[None]
     return (cross, coherence.astype(jnp.float32))
 
 

time: 73.5 us -> 73.4 us (level)
  no operation moved by 1% of the time
where the time goes in v17:
time: 73.4 us; the launch traced here: 73.2 us
  starting transfers between devices  21.3 us (29%)
  waiting for transfers between devices  18.1 us (25%)
  other arithmetic  9.68 us (13%)
  matrix products  8.63 us (12%)
  blocking collectives  8.3 us (11%)
  local copies, waits for them, and re-layouts  6 us (8%)
  between operations  1.15 us (2%)
    all_to_all x1, waiting for transfers between devices, shards(): exchanged = lax.all_to_all(partial_value, ('tm', 'chan'), 0, 0, tiled=True)  14 us
    ppermute x4, starting transfers between devices, from_behind(): lax.ppermute(array, axis, [(i, (i + by) % peers) for i in range(peers)])  11.5 us
    all_to_all x1, starting transfers between devices, shards(): exchanged = lax.all_to_all(partial_value, ('tm', 'chan'), 0, 0, tiled=True)  9.81 us
    all_gather x1, blocking collectives, shards(): gathered = lax.all_gather(rounded, 'chan', axis=0, tiled=True)  8.3 us
    dot_general x2, matrix products, pair_sums(): jnp.einsum('pc,qrct->qrpt', pick, parts, preferred_element_type=jnp.bfloa...  5.6 us
    ppermute x4, waiting for transfers between devices, from_behind(): lax.ppermute(array, axis, [(i, (i + by) % peers) for i in range(peers)])  4.14 us
    dot_general x2, other arithmetic, time_sum(): jnp.einsum('qpt,qpt->qp', left, right, preferred_element_type=jnp.float32)  4.04 us
    dot_general x2, matrix products, pair_sums(): jnp.einsum('pc,kqc->kqp', pick, pieces, preferred_element_type=jnp.float32)  1.86 us
  transfers between devices with their start and end apart: 5, of which 2 were waited for; matrix products, arithmetic and copies ran while one was open for 20% of the time, Pallas kernels for 0%

profile of v17, /device:TPU:1, one launch (start us, length us, event | category | flops | bytes accessed | tf_op | source)
XLA Modules:
  0.0 73.2 jit_solution(12576032012574932156)
XLA Ops:
  0.7 0.8 %convert_element_type.133 = bf16[64,128]{1,0:T(8,128)(2,1)S(1)} convert(f32[64,128]{1,0:T(8,128)} %param.5) | non-fusion elementwise | flops 8192 | bytes 49152 | tf_op jit(solution)/shard_map/convert_element_type | solution.py:93
  1.4 8.3 %all_gather.3 = bf16[256,128]{1,0:T(8,128)(2,1)S(1)} all-gather(bf16[64,128]{1,0:T(8,128)(2,1)S(1)} %convert_element_type.133), channel_id=1, replica_groups=mesh['tm'=64,'chan'=4] {'chan'}, dimensions={0}, use_global_device_ids=true | all-gather | bytes 81920 | tf_op jit(solution)/shard_map/all_gather | solution.py:94
  9.7 8.8 %collective-permute-start.1 = (bf16[256,128]{1,0:T(8,128)(2,1)S(1)}, bf16[256,128]{1,0:T(8,128)(2,1)S(1)}, u32[]{:S(2)}, u32[]{:S(2)}) collective-permute-start(bf16[256,128]{1,0:T(8,128)(2,1)S(1)} %all_gather.3), channel_id=1, source_target_pairs={{0,252},{4,0},{8,4},{12,8},{16,12},{20,16},{24,20},{28,24},{32,28}... | collective-permute-start | bytes 196616 | tf_op jit(solution)/shard_map/ppermute | solution.py:19
  18.6 0.6 gather_fusion.1
  19.3 0.6 gather_fusion
  21.4 0.8 %fusion.25 = (bf16[6,1,384,128]{2,3,1,0:T(8,128)(2,1)S(1)}, bf16[6,1,384,128]{2,3,1,0:T(8,128)(2,1)S(1)}) fusion(f32[6,128]{1,0:T(8,128)S(1)} %get-tuple-element.41, f32[6,384]{1,0:T(8,128)S(1)} %get-tuple-element.34, f32[6,128]{1,0:T(8,128)S(1)} %get-tuple-element.40, f32[6,384]{1,0:T(8,128)S(1)} %get-tuple-element.33, f32[6]{0:T(128)S(1)} %get-tuple-element.53, ...), kind=kLoop, calls=%fused_computation.47 | loop fusion | flops 5013504 | bytes 1597512 | tf_op jit(solution)/shard_map/convert_element_type | solution.py:40
  22.2 1.0 %fusion.27 = (bf16[2,1,1152,128]{2,3,1,0:T(8,128)(2,1)S(1)}, bf16[2,1,1152,128]{2,3,1,0:T(8,128)(2,1)S(1)}) fusion(f32[2,128]{1,0:T(2,128)S(1)} %get-tuple-element.43, f32[2,1152]{1,0:T(2,128)S(1)} %get-tuple-element.27, f32[2,128]{1,0:T(2,128)S(1)} %get-tuple-element.42, f32[2,1152]{1,0:T(2,128)S(1)} %get-tuple-element.26, f32[2]{0:T(128)S(1)} %get-tuple-element.49, ...), kind=kLoop, calls=%fused_computation.49 | loop fusion | flops 5013504 | bytes 2379800 | tf_op jit(solution)/shard_map/convert_element_type | solution.py:40
  23.2 4.1 %collective-permute-done = bf16[256,128]{1,0:T(8,128)(2,1)S(1)} collective-permute-done((bf16[256,128]{1,0:T(8,128)(2,1)S(1)}, bf16[256,128]{1,0:T(8,128)(2,1)S(1)}, u32[]{:S(2)}, u32[]{:S(2)}) %collective-permute-start) | collective-permute-done | bytes 65568 | tf_op jit(solution)/shard_map/ppermute | solution.py:19
  27.5 2.7 %collective-permute-start.2 = (bf16[256,384]{1,0:T(8,128)(2,1)S(1)}, bf16[256,384]{1,0:T(8,128)(2,1)S(1)}, u32[]{:S(2)}, u32[]{:S(2)}) collective-permute-start(bf16[256,384]{1,0:T(8,128)(2,1)S(1)} %constant_dynamic-update-slice_fusion), channel_id=1, source_target_pairs={{0,12},{4,16},{8,20},{12,24},{16,28},{20,32},{24,36},{28,40},{32,4... | collective-permute-start | bytes 589832 | tf_op jit(solution)/shard_map/ppermute | solution.py:19
  30.2 0.6 fusion.20
  30.8 0.8 %fusion.10 = f32[3,6,4096]{2,1,0:T(8,128)S(1)} fusion(s32[4096]{0:T(1024)S(1)} %pad_add_fusion, bf16[1,6,256]{2,1,0:T(8,128)(2,1)S(1)} %get-tuple-element.29, bf16[1,6,256]{2,1,0:T(8,128)(2,1)S(1)} %get-tuple-element.30, bf16[1,6,256]{2,1,0:T(8,128)(2,1)S(1)} %get-tuple-element.28), kind=kOutput, calls=%fused_computation.16 | convolution fusion | flops 38806528 | bytes 320512 | tf_op jit(solution)/shard_map/pc,kqc->kqp/dot_general | solution.py:79
  31.7 3.9 %convolution_bitcast_fusion = bf16[6,2,4096,128]{2,3,1,0:T(8,128)(2,1)S(1)} fusion(s32[4096]{0:T(1024)S(1)} %pad_add_fusion, bf16[6,2,128,256]{3,2,1,0:T(8,128)(2,1)S(1)} %get-tuple-element.47), kind=kOutput, calls=%fused_computation.6 | convolution fusion | flops 3222274048 | bytes 13385728 | tf_op jit(solution)/shard_map/pc,qrct->qrpt/dot_general | solution.py:61
  35.6 3.1 %fusion.2 = (f32[6,2048]{1,0:T(8,128)S(1)}, f32[6,2048]{1,0:T(8,128)S(1)}, f32[6,2048]{1,0:T(8,128)S(1)}, f32[6,2048]{1,0:T(8,128)S(1)}) fusion(bf16[6,2,4096,128]{2,3,1,0:T(8,128)(2,1)S(1)} %convolution_bitcast_fusion), kind=kLoop, calls=%fused_computation.9 | loop fusion | flops 18825216 | bytes 12779520 | tf_op jit(solution)/shard_map/qpt,qpt->qp/dot_general | solution.py:69
  39.5 1.0 %fusion.8 = f32[3,2,4096]{2,1,0:T(2,128)S(1)} fusion(s32[4096]{0:T(1024)S(1)} %pad_add_fusion, bf16[3,2,256]{2,0,1:T(4,128)(2,1)S(1)} %pad_maximum_fusion.1), kind=kOutput, calls=%fused_computation.15 | convolution fusion | flops 13631488 | bytes 117760 | tf_op jit(solution)/shard_map/pc,kqc->kqp/dot_general | solution.py:79
  40.6 1.7 %convolution_bitcast_fusion.1 = bf16[2,2,4096,128]{2,3,1,0:T(8,128)(2,1)S(1)} fusion(s32[4096]{0:T(1024)S(1)} %pad_add_fusion, bf16[2,2,128,256]{3,2,1,0:T(8,128)(2,1)S(1)} %get-tuple-element.45), kind=kOutput, calls=%fused_computation.11 | convolution fusion | flops 1074790400 | bytes 4472832 | tf_op jit(solution)/shard_map/pc,qrct->qrpt/dot_general | solution.py:61
  42.3 1.0 %fusion.14 = (f32[2,2048]{1,0:T(2,128)S(1)}, f32[2,2048]{1,0:T(2,128)S(1)}, f32[2,2048]{1,0:T(2,128)S(1)}, f32[2,2048]{1,0:T(2,128)S(1)}) fusion(bf16[2,2,4096,128]{2,3,1,0:T(8,128)(2,1)S(1)} %convolution_bitcast_fusion.1), kind=kLoop, calls=%fused_computation.27 | loop fusion | flops 6275072 | bytes 4259840 | tf_op jit(solution)/shard_map/qpt,qpt->qp/dot_general | solution.py:69
  44.0 1.1 %all_to_all.8 = f32[256,1,256]{2,1,0:T(1,128)} reshape(f32[2048,32]{1,0:T(8,128)S(1)} %copy.61) | data formatting | bytes 524288 | tf_op jit(solution)/shard_map/all_to_all | solution.py:125
  45.2 9.8 %all-to-all-start = ((f32[256,1,256]{2,1,0:T(1,128)}), f32[256,1,256]{2,1,0:T(1,128)S(1)}, u32[]{:S(2)}, u32[]{:S(2)}) async-start(f32[256,1,256]{2,1,0:T(1,128)} %all_to_all.8), calls=%async_computation | async-start | bytes 524288 | tf_op jit(solution)/shard_map/all_to_all | solution.py:125
  55.0 0.6 dynamic_slice.3
  55.6 0.7 add_compare_fusion
  56.2 14.0 %all-to-all-done = f32[256,1,256]{2,1,0:T(1,128)S(1)} async-done(((f32[256,1,256]{2,1,0:T(1,128)}), f32[256,1,256]{2,1,0:T(1,128)S(1)}, u32[]{:S(2)}, u32[]{:S(2)}) %all-to-all-start) | async-done | bytes 262176 | tf_op jit(solution)/shard_map/all_to_all | solution.py:125
  70.2 0.6 reduce.10
  71.8 0.7 bitcast_select_fusion
  72.6 0.6 copy.66
  (75 shorter events, 4.2 us)
Async XLA Ops:
  0.6 18.0 %copy-start = (s32[32]{0:T(128)S(1)}, s32[32]{0:T(128)}, u32[]{:S(2)}) copy-start(s32[32]{0:T(128)} %param.6) | copy-start | bytes 388
  0.6 19.9 %copy-start.1 = (s32[4,512]{1,0:T(4,128)S(1)}, s32[4,512]{1,0:T(4,128)}, u32[]{:S(2)}) copy-start(s32[4,512]{1,0:T(4,128)} %param.7) | copy-start | bytes 24580
  0.7 20.2 %copy-start.2 = (s32[4,512]{1,0:T(4,128)S(1)}, s32[4,512]{1,0:T(4,128)}, u32[]{:S(2)}) copy-start(s32[4,512]{1,0:T(4,128)} %param.8) | copy-start | bytes 24580
  9.7 17.6 %collective-permute-start.1 = (bf16[256,128]{1,0:T(8,128)(2,1)S(1)}, bf16[256,128]{1,0:T(8,128)(2,1)S(1)}, u32[]{:S(2)}, u32[]{:S(2)}) collective-permute-start(bf16[256,128]{1,0:T(8,128)(2,1)S(1)} %all_gather.3), channel_id=1, source_target_pairs={{0,252},{4,0},{8,4},{12,8},{16,12},{20,16},{24,20},{28,24},{32,28}... | collective-permute-start | bytes 196616 | tf_op jit(solution)/shard_map/ppermute | solution.py:19
  18.5 8.8 %collective-permute-start = (bf16[256,128]{1,0:T(8,128)(2,1)S(1)}, bf16[256,128]{1,0:T(8,128)(2,1)S(1)}, u32[]{:S(2)}, u32[]{:S(2)}) collective-permute-start(bf16[256,128]{1,0:T(8,128)(2,1)S(1)} %all_gather.3), channel_id=1, source_target_pairs={{0,4},{4,8},{8,12},{12,16},{16,20},{20,24},{24,28},{28,32},{32,36}... | collective-permute-start | bytes 196616 | tf_op jit(solution)/shard_map/ppermute | solution.py:19
  27.4 11.4 %collective-permute-start.3 = (bf16[256,384]{1,0:T(8,128)(2,1)S(1)}, bf16[256,384]{1,0:T(8,128)(2,1)S(1)}, u32[]{:S(2)}, u32[]{:S(2)}) collective-permute-start(bf16[256,384]{1,0:T(8,128)(2,1)S(1)} %constant_dynamic-update-slice_fusion), channel_id=1, source_target_pairs={{0,244},{4,248},{8,252},{12,0},{16,4},{20,8},{24,12},{28,16},{32,2... | collective-permute-start | bytes 589832 | tf_op jit(solution)/shard_map/ppermute | solution.py:19
  27.5 11.2 %collective-permute-start.2 = (bf16[256,384]{1,0:T(8,128)(2,1)S(1)}, bf16[256,384]{1,0:T(8,128)(2,1)S(1)}, u32[]{:S(2)}, u32[]{:S(2)}) collective-permute-start(bf16[256,384]{1,0:T(8,128)(2,1)S(1)} %constant_dynamic-update-slice_fusion), channel_id=1, source_target_pairs={{0,12},{4,16},{8,20},{12,24},{16,28},{20,32},{24,36},{28,40},{32,4... | collective-permute-start | bytes 589832 | tf_op jit(solution)/shard_map/ppermute | solution.py:19
  44.0 11.0 %copy-start.3 = (s32[4]{0:T(128)S(1)}, s32[4]{0:T(128)}, u32[]{:S(2)}) copy-start(s32[4]{0:T(128)} %param.9) | copy-start | bytes 52
  45.2 25.1 %all-to-all-start = ((f32[256,1,256]{2,1,0:T(1,128)}), f32[256,1,256]{2,1,0:T(1,128)S(1)}, u32[]{:S(2)}, u32[]{:S(2)}) async-start(f32[256,1,256]{2,1,0:T(1,128)} %all_to_all.8), calls=%async_computation | async-start | bytes 524288 | tf_op jit(solution)/shard_map/all_to_all | solution.py:125

commit v18 on v15

--- a/solution.py
+++ b/solution.py
@@ -91,10 +91,13 @@
     time_span = signal.shape[1]
     ntime = time_span * time_devices
     rounded = signal.astype(jnp.bfloat16)
+    sides = jnp.concatenate(
+        [from_behind(rounded, "tm", 1), from_behind(rounded, "tm", -1)], axis=1
+    )
     gathered = lax.all_gather(rounded, "chan", axis=0, tiled=True)
-    near = jnp.concatenate(
-        [from_behind(gathered, "tm", 1), gathered, from_behind(gathered, "tm", -1)], axis=1
-    )
+    sides = lax.all_gather(sides, "chan", axis=0, tiled=True)
+    span = rounded.shape[1]
+    near = jnp.concatenate([sides[:, :span], gathered, sides[:, span:]], axis=1)
     wide = jnp.concatenate([from_behind(near, "tm", 3), near, from_behind(near, "tm", -3)], axis=1)
     per_group = NS // groups
     band = NS // 4

time: 73.5 us -> 75.7 us (1.030)
  waiting for transfers between devices: 18.1 us -> 14 us
  blocking collectives: 8.3 us -> 11.5 us
  starting transfers between devices: 21.3 us -> 24.5 us
    ppermute x4, starting transfers between devices: 11.5 us -> 17.4 us  [from_behind(): lax.ppermute(array, axis, [(i, (i + by) % peers) for i in range(peers)])]
    all_gather x0 -> x1, blocking collectives: none -> 5.43 us  [shards(): sides = lax.all_gather(sides, 'chan', axis=0, tiled=True)]
    ppermute x4, waiting for transfers between devices: 4.14 us -> 0.01 us  [from_behind(): lax.ppermute(array, axis, [(i, (i + by) % peers) for i in range(peers)])]
    all_to_all x1, starting transfers between devices: 9.81 us -> 7.16 us  [shards(): exchanged = lax.all_to_all(partial_value, ('tm', 'chan'), 0, 0, tiled=True)]
    all_gather x1, blocking collectives: 8.3 us -> 6.03 us  [shards(): gathered = lax.all_gather(rounded, 'chan', axis=0, tiled=True)]
  transfers between devices with their start and end apart: 5 -> 5, of which waited for: 2 -> 1; matrix products, arithmetic and copies ran while one was open for 20% -> 19% of each run, Pallas kernels for 0% -> 0%
where the time goes in v18:
time: 75.7 us; the launch traced here: 75.5 us
  starting transfers between devices  24.5 us (32%)
  waiting for transfers between devices  14 us (18%)
  blocking collectives  11.5 us (15%)
  other arithmetic  9.79 us (13%)
  matrix products  8.63 us (11%)
  local copies, waits for them, and re-layouts  5.96 us (8%)
  between operations  1.15 us (2%)
    ppermute x4, starting transfers between devices, from_behind(): lax.ppermute(array, axis, [(i, (i + by) % peers) for i in range(peers)])  17.4 us
    all_to_all x1, waiting for transfers between devices, shards(): exchanged = lax.all_to_all(partial_value, ('tm', 'chan'), 0, 0, tiled=True)  14 us
    all_to_all x1, starting transfers between devices, shards(): exchanged = lax.all_to_all(partial_value, ('tm', 'chan'), 0, 0, tiled=True)  7.16 us
    all_gather x1, blocking collectives, shards(): gathered = lax.all_gather(rounded, 'chan', axis=0, tiled=True)  6.03 us
    dot_general x2, matrix products, pair_sums(): jnp.einsum('pc,qrct->qrpt', pick, parts, preferred_element_type=jnp.bfloa...  5.6 us
    all_gather x1, blocking collectives, shards(): sides = lax.all_gather(sides, 'chan', axis=0, tiled=True)  5.43 us
    dot_general x2, other arithmetic, time_sum(): jnp.einsum('qpt,qpt->qp', left, right, preferred_element_type=jnp.float32)  4.04 us
    dot_general x2, matrix products, pair_sums(): jnp.einsum('pc,kqc->kqp', pick, pieces, preferred_element_type=jnp.float32)  1.86 us
  transfers between devices with their start and end apart: 5, of which 1 were waited for; matrix products, arithmetic and copies ran while one was open for 19% of the time, Pallas kernels for 0%

profile of v18, /device:TPU:1, one launch (start us, length us, event | category | flops | bytes accessed | tf_op | source)
XLA Modules:
  0.0 75.5 jit_solution(17741410999585214715)
XLA Ops:
  0.7 0.8 %convert_element_type.133 = bf16[64,128]{1,0:T(8,128)(2,1)S(1)} convert(f32[64,128]{1,0:T(8,128)} %param.5) | non-fusion elementwise | flops 8192 | bytes 49152 | tf_op jit(solution)/shard_map/convert_element_type | solution.py:93
  1.4 11.3 %collective-permute-start.1 = (bf16[64,128]{1,0:T(8,128)(2,1)S(1)}, bf16[64,128]{1,0:T(8,128)(2,1)S(1)}, u32[]{:S(2)}, u32[]{:S(2)}) collective-permute-start(bf16[64,128]{1,0:T(8,128)(2,1)S(1)} %convert_element_type.133), channel_id=1, source_target_pairs={{0,252},{4,0},{8,4},{12,8},{16,12},{20,16},{24,20},{28,24},{32,28}... | collective-permute-start | bytes 49160 | tf_op jit(solution)/shard_map/ppermute | solution.py:19
  12.9 0.6 gather_fusion.1
  13.5 0.6 gather_fusion
  15.7 0.8 %fusion.25 = (bf16[6,1,384,128]{2,3,1,0:T(8,128)(2,1)S(1)}, bf16[6,1,384,128]{2,3,1,0:T(8,128)(2,1)S(1)}) fusion(f32[6,128]{1,0:T(8,128)S(1)} %get-tuple-element.47, f32[6,384]{1,0:T(8,128)S(1)} %get-tuple-element.40, f32[6,128]{1,0:T(8,128)S(1)} %get-tuple-element.46, f32[6,384]{1,0:T(8,128)S(1)} %get-tuple-element.39, f32[6]{0:T(128)S(1)} %get-tuple-element.59, ...), kind=kLoop, calls=%fused_computation.47 | loop fusion | flops 5013504 | bytes 1597512 | tf_op jit(solution)/shard_map/convert_element_type | solution.py:40
  16.5 1.0 %fusion.27 = (bf16[2,1,1152,128]{2,3,1,0:T(8,128)(2,1)S(1)}, bf16[2,1,1152,128]{2,3,1,0:T(8,128)(2,1)S(1)}) fusion(f32[2,128]{1,0:T(2,128)S(1)} %get-tuple-element.49, f32[2,1152]{1,0:T(2,128)S(1)} %get-tuple-element.33, f32[2,128]{1,0:T(2,128)S(1)} %get-tuple-element.48, f32[2,1152]{1,0:T(2,128)S(1)} %get-tuple-element.32, f32[2]{0:T(128)S(1)} %get-tuple-element.55, ...), kind=kLoop, calls=%fused_computation.49 | loop fusion | flops 5013504 | bytes 2379800 | tf_op jit(solution)/shard_map/convert_element_type | solution.py:40
  17.5 6.0 %all_gather.7 = bf16[256,128]{1,0:T(8,128)(2,1)S(1)} all-gather(bf16[64,128]{1,0:T(8,128)(2,1)S(1)} %convert_element_type.133), channel_id=1, replica_groups=mesh['tm'=64,'chan'=4] {'chan'}, dimensions={0}, use_global_device_ids=true | all-gather | bytes 81920 | tf_op jit(solution)/shard_map/all_gather | solution.py:97
  23.5 5.4 %all_gather.6 = bf16[256,256]{1,0:T(8,128)(2,1)S(1)} all-gather(bf16[64,256]{1,0:T(8,128)(2,1)S(1)} %pad_maximum_fusion.1), channel_id=1, replica_groups=mesh['tm'=64,'chan'=4] {'chan'}, dimensions={0}, use_global_device_ids=true | all-gather | bytes 163840 | tf_op jit(solution)/shard_map/all_gather | solution.py:98
  29.1 6.0 %collective-permute-start.3 = (bf16[256,384]{1,0:T(8,128)(2,1)S(1)}, bf16[256,384]{1,0:T(8,128)(2,1)S(1)}, u32[]{:S(2)}, u32[]{:S(2)}) collective-permute-start(bf16[256,384]{1,0:T(8,128)(2,1)S(1)} %pad_maximum_fusion), channel_id=1, source_target_pairs={{0,244},{4,248},{8,252},{12,0},{16,4},{20,8},{24,12},{28,16},{32,2... | collective-permute-start | bytes 589832 | tf_op jit(solution)/shard_map/ppermute | solution.py:19
  35.1 0.6 fusion.20
  35.7 0.8 %fusion.10 = f32[3,6,4096]{2,1,0:T(8,128)S(1)} fusion(s32[4096]{0:T(1024)S(1)} %pad_add_fusion, bf16[1,6,256]{2,1,0:T(8,128)(2,1)S(1)} %get-tuple-element.35, bf16[1,6,256]{2,1,0:T(8,128)(2,1)S(1)} %get-tuple-element.36, bf16[1,6,256]{2,1,0:T(8,128)(2,1)S(1)} %get-tuple-element.34), kind=kOutput, calls=%fused_computation.16 | convolution fusion | flops 38806528 | bytes 320512 | tf_op jit(solution)/shard_map/pc,kqc->kqp/dot_general | solution.py:79
  36.6 3.9 %convolution_bitcast_fusion = bf16[6,2,4096,128]{2,3,1,0:T(8,128)(2,1)S(1)} fusion(s32[4096]{0:T(1024)S(1)} %pad_add_fusion, bf16[6,2,128,256]{3,2,1,0:T(8,128)(2,1)S(1)} %get-tuple-element.53), kind=kOutput, calls=%fused_computation.6 | convolution fusion | flops 3222274048 | bytes 13385728 | tf_op jit(solution)/shard_map/pc,qrct->qrpt/dot_general | solution.py:61
  40.5 3.1 %fusion.2 = (f32[6,2048]{1,0:T(8,128)S(1)}, f32[6,2048]{1,0:T(8,128)S(1)}, f32[6,2048]{1,0:T(8,128)S(1)}, f32[6,2048]{1,0:T(8,128)S(1)}) fusion(bf16[6,2,4096,128]{2,3,1,0:T(8,128)(2,1)S(1)} %convolution_bitcast_fusion), kind=kLoop, calls=%fused_computation.9 | loop fusion | flops 18825216 | bytes 12779520 | tf_op jit(solution)/shard_map/qpt,qpt->qp/dot_general | solution.py:69
  44.4 1.0 %fusion.8 = f32[3,2,4096]{2,1,0:T(2,128)S(1)} fusion(s32[4096]{0:T(1024)S(1)} %pad_add_fusion, bf16[3,2,256]{2,0,1:T(4,128)(2,1)S(1)} %pad_maximum_fusion.3), kind=kOutput, calls=%fused_computation.15 | convolution fusion | flops 13631488 | bytes 117760 | tf_op jit(solution)/shard_map/pc,kqc->kqp/dot_general | solution.py:79
  45.5 1.7 %convolution_bitcast_fusion.1 = bf16[2,2,4096,128]{2,3,1,0:T(8,128)(2,1)S(1)} fusion(s32[4096]{0:T(1024)S(1)} %pad_add_fusion, bf16[2,2,128,256]{3,2,1,0:T(8,128)(2,1)S(1)} %get-tuple-element.51), kind=kOutput, calls=%fused_computation.11 | convolution fusion | flops 1074790400 | bytes 4472832 | tf_op jit(solution)/shard_map/pc,qrct->qrpt/dot_general | solution.py:61
  47.2 1.0 %fusion.14 = (f32[2,2048]{1,0:T(2,128)S(1)}, f32[2,2048]{1,0:T(2,128)S(1)}, f32[2,2048]{1,0:T(2,128)S(1)}, f32[2,2048]{1,0:T(2,128)S(1)}) fusion(bf16[2,2,4096,128]{2,3,1,0:T(8,128)(2,1)S(1)} %convolution_bitcast_fusion.1), kind=kLoop, calls=%fused_computation.27 | loop fusion | flops 6275072 | bytes 4259840 | tf_op jit(solution)/shard_map/qpt,qpt->qp/dot_general | solution.py:69
  48.9 1.1 %all_to_all.8 = f32[256,1,256]{2,1,0:T(1,128)} reshape(f32[2048,32]{1,0:T(8,128)S(1)} %copy.62) | data formatting | bytes 524288 | tf_op jit(solution)/shard_map/all_to_all | solution.py:128
  50.0 7.2 %all-to-all-start = ((f32[256,1,256]{2,1,0:T(1,128)}), f32[256,1,256]{2,1,0:T(1,128)S(1)}, u32[]{:S(2)}, u32[]{:S(2)}) async-start(f32[256,1,256]{2,1,0:T(1,128)} %all_to_all.8), calls=%async_computation | async-start | bytes 524288 | tf_op jit(solution)/shard_map/all_to_all | solution.py:128
  57.2 0.6 dynamic_slice.3
  57.8 0.7 add_compare_fusion
  58.5 14.0 %all-to-all-done = f32[256,1,256]{2,1,0:T(1,128)S(1)} async-done(((f32[256,1,256]{2,1,0:T(1,128)}), f32[256,1,256]{2,1,0:T(1,128)S(1)}, u32[]{:S(2)}, u32[]{:S(2)}) %all-to-all-start) | async-done | bytes 262176 | tf_op jit(solution)/shard_map/all_to_all | solution.py:128
  72.5 0.6 reduce.10
  74.2 0.7 select_bitcast_fusion
  74.9 0.6 copy.67
  (77 shorter events, 4.3 us)
Async XLA Ops:
  0.6 12.3 %copy-start = (s32[32]{0:T(128)S(1)}, s32[32]{0:T(128)}, u32[]{:S(2)}) copy-start(s32[32]{0:T(128)} %param.6) | copy-start | bytes 388
  0.6 14.1 %copy-start.1 = (s32[4,512]{1,0:T(4,128)S(1)}, s32[4,512]{1,0:T(4,128)}, u32[]{:S(2)}) copy-start(s32[4,512]{1,0:T(4,128)} %param.7) | copy-start | bytes 24580
  0.7 14.5 %copy-start.2 = (s32[4,512]{1,0:T(4,128)S(1)}, s32[4,512]{1,0:T(4,128)}, u32[]{:S(2)}) copy-start(s32[4,512]{1,0:T(4,128)} %param.8) | copy-start | bytes 24580
  1.4 22.1 %collective-permute-start.1 = (bf16[64,128]{1,0:T(8,128)(2,1)S(1)}, bf16[64,128]{1,0:T(8,128)(2,1)S(1)}, u32[]{:S(2)}, u32[]{:S(2)}) collective-permute-start(bf16[64,128]{1,0:T(8,128)(2,1)S(1)} %convert_element_type.133), channel_id=1, source_target_pairs={{0,252},{4,0},{8,4},{12,8},{16,12},{20,16},{24,20},{28,24},{32,28}... | collective-permute-start | bytes 49160 | tf_op jit(solution)/shard_map/ppermute | solution.py:19
  12.8 10.7 %collective-permute-start = (bf16[64,128]{1,0:T(8,128)(2,1)S(1)}, bf16[64,128]{1,0:T(8,128)(2,1)S(1)}, u32[]{:S(2)}, u32[]{:S(2)}) collective-permute-start(bf16[64,128]{1,0:T(8,128)(2,1)S(1)} %convert_element_type.133), channel_id=1, source_target_pairs={{0,4},{4,8},{8,12},{12,16},{16,20},{20,24},{24,28},{28,32},{32,36}... | collective-permute-start | bytes 49160 | tf_op jit(solution)/shard_map/ppermute | solution.py:19
  29.0 14.6 %collective-permute-start.2 = (bf16[256,384]{1,0:T(8,128)(2,1)S(1)}, bf16[256,384]{1,0:T(8,128)(2,1)S(1)}, u32[]{:S(2)}, u32[]{:S(2)}) collective-permute-start(bf16[256,384]{1,0:T(8,128)(2,1)S(1)} %pad_maximum_fusion), channel_id=1, source_target_pairs={{0,12},{4,16},{8,20},{12,24},{16,28},{20,32},{24,36},{28,40},{32,4... | collective-permute-start | bytes 589832 | tf_op jit(solution)/shard_map/ppermute | solution.py:19
  29.1 14.6 %collective-permute-start.3 = (bf16[256,384]{1,0:T(8,128)(2,1)S(1)}, bf16[256,384]{1,0:T(8,128)(2,1)S(1)}, u32[]{:S(2)}, u32[]{:S(2)}) collective-permute-start(bf16[256,384]{1,0:T(8,128)(2,1)S(1)} %pad_maximum_fusion), channel_id=1, source_target_pairs={{0,244},{4,248},{8,252},{12,0},{16,4},{20,8},{24,12},{28,16},{32,2... | collective-permute-start | bytes 589832 | tf_op jit(solution)/shard_map/ppermute | solution.py:19
  48.9 8.3 %copy-start.3 = (s32[4]{0:T(128)S(1)}, s32[4]{0:T(128)}, u32[]{:S(2)}) copy-start(s32[4]{0:T(128)} %param.9) | copy-start | bytes 52
  50.0 22.4 %all-to-all-start = ((f32[256,1,256]{2,1,0:T(1,128)}), f32[256,1,256]{2,1,0:T(1,128)S(1)}, u32[]{:S(2)}, u32[]{:S(2)}) async-start(f32[256,1,256]{2,1,0:T(1,128)} %all_to_all.8), calls=%async_computation | async-start | bytes 524288 | tf_op jit(solution)/shard_map/all_to_all | solution.py:128

commit v19 on v15

--- a/solution.py
+++ b/solution.py
@@ -121,7 +121,7 @@
     )
     values = sums.shape[1]
     destinations = time_devices * groups
-    partial_value = sums.reshape(per_group * values, -1).T.reshape(destinations, -1)
+    partial_value = sums.reshape(per_group * values, -1).T.reshape(destinations, 2, -1)
     exchanged = lax.all_to_all(partial_value, ("tm", "chan"), 0, 0, tiled=True)
     summed = jnp.sum(exchanged.reshape(time_devices, groups, -1), axis=0)
     owned = summed.reshape(groups, slots_local, per_group, values).transpose(0, 2, 3, 1) / ntime

time: 73.5 us -> 72.9 us (level)
    all_to_all x1 -> x0, local copies, waits for them, and re-layouts: 1.15 us -> none  [shards(): exchanged = lax.all_to_all(partial_value, ('tm', 'chan'), 0, 0, tiled=True)]
    reshape x1 -> x2, local copies, waits for them, and re-layouts: 0.09 us -> 1.13 us  [shards(): sums.reshape(per_group * values, -1).T.reshape(destinations, 2, -1)]
where the time goes in v19:
time: 72.9 us; the launch traced here: 72.7 us
  starting transfers between devices  21.3 us (29%)
  waiting for transfers between devices  18.1 us (25%)
  other arithmetic  9.14 us (13%)
  matrix products  8.63 us (12%)
  blocking collectives  8.3 us (11%)
  local copies, waits for them, and re-layouts  6.07 us (8%)
  between operations  1.14 us (2%)
    all_to_all x1, waiting for transfers between devices, shards(): exchanged = lax.all_to_all(partial_value, ('tm', 'chan'), 0, 0, tiled=True)  14 us
    ppermute x4, starting transfers between devices, from_behind(): lax.ppermute(array, axis, [(i, (i + by) % peers) for i in range(peers)])  11.5 us
    all_to_all x1, starting transfers between devices, shards(): exchanged = lax.all_to_all(partial_value, ('tm', 'chan'), 0, 0, tiled=True)  9.81 us
    all_gather x1, blocking collectives, shards(): gathered = lax.all_gather(rounded, 'chan', axis=0, tiled=True)  8.3 us
    dot_general x2, matrix products, pair_sums(): jnp.einsum('pc,qrct->qrpt', pick, parts, preferred_element_type=jnp.bfloa...  5.6 us
    ppermute x4, waiting for transfers between devices, from_behind(): lax.ppermute(array, axis, [(i, (i + by) % peers) for i in range(peers)])  4.14 us
    dot_general x2, other arithmetic, time_sum(): jnp.einsum('qpt,qpt->qp', left, right, preferred_element_type=jnp.float32)  4.04 us
    dot_general x2, matrix products, pair_sums(): jnp.einsum('pc,kqc->kqp', pick, pieces, preferred_element_type=jnp.float32)  1.86 us
  transfers between devices with their start and end apart: 5, of which 2 were waited for; matrix products, arithmetic and copies ran while one was open for 20% of the time, Pallas kernels for 0%

profile of v19, /device:TPU:1, one launch (start us, length us, event | category | flops | bytes accessed | tf_op | source)
XLA Modules:
  0.0 72.7 jit_solution(5216623961551149893)
XLA Ops:
  0.7 0.8 %convert_element_type.133 = bf16[64,128]{1,0:T(8,128)(2,1)S(1)} convert(f32[64,128]{1,0:T(8,128)} %param.5) | non-fusion elementwise | flops 8192 | bytes 49152 | tf_op jit(solution)/shard_map/convert_element_type | solution.py:93
  1.4 8.3 %all_gather.3 = bf16[256,128]{1,0:T(8,128)(2,1)S(1)} all-gather(bf16[64,128]{1,0:T(8,128)(2,1)S(1)} %convert_element_type.133), channel_id=1, replica_groups=mesh['tm'=64,'chan'=4] {'chan'}, dimensions={0}, use_global_device_ids=true | all-gather | bytes 81920 | tf_op jit(solution)/shard_map/all_gather | solution.py:94
  9.7 8.8 %collective-permute-start.1 = (bf16[256,128]{1,0:T(8,128)(2,1)S(1)}, bf16[256,128]{1,0:T(8,128)(2,1)S(1)}, u32[]{:S(2)}, u32[]{:S(2)}) collective-permute-start(bf16[256,128]{1,0:T(8,128)(2,1)S(1)} %all_gather.3), channel_id=1, source_target_pairs={{0,252},{4,0},{8,4},{12,8},{16,12},{20,16},{24,20},{28,24},{32,28}... | collective-permute-start | bytes 196616 | tf_op jit(solution)/shard_map/ppermute | solution.py:19
  18.6 0.6 gather_fusion.1
  19.3 0.6 gather_fusion
  21.4 0.8 %fusion.25 = (bf16[6,1,384,128]{2,3,1,0:T(8,128)(2,1)S(1)}, bf16[6,1,384,128]{2,3,1,0:T(8,128)(2,1)S(1)}) fusion(f32[6,128]{1,0:T(8,128)S(1)} %get-tuple-element.43, f32[6,384]{1,0:T(8,128)S(1)} %get-tuple-element.36, f32[6,128]{1,0:T(8,128)S(1)} %get-tuple-element.42, f32[6,384]{1,0:T(8,128)S(1)} %get-tuple-element.35, f32[6]{0:T(128)S(1)} %get-tuple-element.55, ...), kind=kLoop, calls=%fused_computation.47 | loop fusion | flops 5013504 | bytes 1597512 | tf_op jit(solution)/shard_map/convert_element_type | solution.py:40
  22.2 1.0 %fusion.27 = (bf16[2,1,1152,128]{2,3,1,0:T(8,128)(2,1)S(1)}, bf16[2,1,1152,128]{2,3,1,0:T(8,128)(2,1)S(1)}) fusion(f32[2,128]{1,0:T(2,128)S(1)} %get-tuple-element.45, f32[2,1152]{1,0:T(2,128)S(1)} %get-tuple-element.29, f32[2,128]{1,0:T(2,128)S(1)} %get-tuple-element.44, f32[2,1152]{1,0:T(2,128)S(1)} %get-tuple-element.28, f32[2]{0:T(128)S(1)} %get-tuple-element.51, ...), kind=kLoop, calls=%fused_computation.49 | loop fusion | flops 5013504 | bytes 2379800 | tf_op jit(solution)/shard_map/convert_element_type | solution.py:40
  23.2 4.1 %collective-permute-done = bf16[256,128]{1,0:T(8,128)(2,1)S(1)} collective-permute-done((bf16[256,128]{1,0:T(8,128)(2,1)S(1)}, bf16[256,128]{1,0:T(8,128)(2,1)S(1)}, u32[]{:S(2)}, u32[]{:S(2)}) %collective-permute-start) | collective-permute-done | bytes 65568 | tf_op jit(solution)/shard_map/ppermute | solution.py:19
  27.5 2.7 %collective-permute-start.2 = (bf16[256,384]{1,0:T(8,128)(2,1)S(1)}, bf16[256,384]{1,0:T(8,128)(2,1)S(1)}, u32[]{:S(2)}, u32[]{:S(2)}) collective-permute-start(bf16[256,384]{1,0:T(8,128)(2,1)S(1)} %constant_dynamic-update-slice_fusion), channel_id=1, source_target_pairs={{0,12},{4,16},{8,20},{12,24},{16,28},{20,32},{24,36},{28,40},{32,4... | collective-permute-start | bytes 589832 | tf_op jit(solution)/shard_map/ppermute | solution.py:19
  30.2 0.6 fusion.20
  30.8 0.8 %fusion.10 = f32[3,6,4096]{2,1,0:T(8,128)S(1)} fusion(s32[4096]{0:T(1024)S(1)} %pad_add_fusion, bf16[1,6,256]{2,1,0:T(8,128)(2,1)S(1)} %get-tuple-element.31, bf16[1,6,256]{2,1,0:T(8,128)(2,1)S(1)} %get-tuple-element.32, bf16[1,6,256]{2,1,0:T(8,128)(2,1)S(1)} %get-tuple-element.30), kind=kOutput, calls=%fused_computation.16 | convolution fusion | flops 38806528 | bytes 320512 | tf_op jit(solution)/shard_map/pc,kqc->kqp/dot_general | solution.py:79
  31.7 3.9 %convolution_bitcast_fusion = bf16[6,2,4096,128]{2,3,1,0:T(8,128)(2,1)S(1)} fusion(s32[4096]{0:T(1024)S(1)} %pad_add_fusion, bf16[6,2,128,256]{3,2,1,0:T(8,128)(2,1)S(1)} %get-tuple-element.49), kind=kOutput, calls=%fused_computation.6 | convolution fusion | flops 3222274048 | bytes 13385728 | tf_op jit(solution)/shard_map/pc,qrct->qrpt/dot_general | solution.py:61
  35.6 3.1 %fusion.2 = (f32[6,2048]{1,0:T(8,128)S(1)}, f32[6,2048]{1,0:T(8,128)S(1)}, f32[6,2048]{1,0:T(8,128)S(1)}, f32[6,2048]{1,0:T(8,128)S(1)}) fusion(bf16[6,2,4096,128]{2,3,1,0:T(8,128)(2,1)S(1)} %convolution_bitcast_fusion), kind=kLoop, calls=%fused_computation.9 | loop fusion | flops 18825216 | bytes 12779520 | tf_op jit(solution)/shard_map/qpt,qpt->qp/dot_general | solution.py:69
  38.9 0.6 fusion.39
  39.5 1.0 %fusion.8 = f32[3,2,4096]{2,1,0:T(2,128)S(1)} fusion(s32[4096]{0:T(1024)S(1)} %pad_add_fusion, bf16[3,2,256]{2,0,1:T(4,128)(2,1)S(1)} %pad_maximum_fusion.1), kind=kOutput, calls=%fused_computation.15 | convolution fusion | flops 13631488 | bytes 117760 | tf_op jit(solution)/shard_map/pc,kqc->kqp/dot_general | solution.py:79
  40.6 1.7 %convolution_bitcast_fusion.1 = bf16[2,2,4096,128]{2,3,1,0:T(8,128)(2,1)S(1)} fusion(s32[4096]{0:T(1024)S(1)} %pad_add_fusion, bf16[2,2,128,256]{3,2,1,0:T(8,128)(2,1)S(1)} %get-tuple-element.47), kind=kOutput, calls=%fused_computation.11 | convolution fusion | flops 1074790400 | bytes 4472832 | tf_op jit(solution)/shard_map/pc,qrct->qrpt/dot_general | solution.py:61
  42.3 1.0 %fusion.14 = (f32[2,2048]{1,0:T(2,128)S(1)}, f32[2,2048]{1,0:T(2,128)S(1)}, f32[2,2048]{1,0:T(2,128)S(1)}, f32[2,2048]{1,0:T(2,128)S(1)}) fusion(bf16[2,2,4096,128]{2,3,1,0:T(8,128)(2,1)S(1)} %convolution_bitcast_fusion.1), kind=kLoop, calls=%fused_computation.27 | loop fusion | flops 6275072 | bytes 4259840 | tf_op jit(solution)/shard_map/qpt,qpt->qp/dot_general | solution.py:69
  44.0 1.0 %reshape.598 = f32[256,2,128]{2,1,0:T(2,128)} reshape(f32[2048,32]{1,0:T(8,128)S(1)} %copy.48) | data formatting | bytes 524288 | tf_op jit(solution)/shard_map/reshape | solution.py:124
  45.0 9.8 %all-to-all-start = ((f32[256,2,128]{2,1,0:T(2,128)}), f32[256,2,128]{2,1,0:T(2,128)S(1)}, u32[]{:S(2)}, u32[]{:S(2)}) async-start(f32[256,2,128]{2,1,0:T(2,128)} %reshape.598), calls=%async_computation | async-start | bytes 524288 | tf_op jit(solution)/shard_map/all_to_all | solution.py:125
  54.9 0.6 dynamic_slice.3
  55.5 0.7 add_compare_fusion
  56.1 14.0 %all-to-all-done = f32[256,2,128]{2,1,0:T(2,128)S(1)} async-done(((f32[256,2,128]{2,1,0:T(2,128)}), f32[256,2,128]{2,1,0:T(2,128)S(1)}, u32[]{:S(2)}, u32[]{:S(2)}) %all-to-all-start) | async-done | bytes 262176 | tf_op jit(solution)/shard_map/all_to_all | solution.py:125
  71.4 0.7 select_bitcast_fusion
  72.1 0.6 copy.52
  (75 shorter events, 3.9 us)
Async XLA Ops:
  0.6 18.0 %copy-start = (s32[32]{0:T(128)S(1)}, s32[32]{0:T(128)}, u32[]{:S(2)}) copy-start(s32[32]{0:T(128)} %param.6) | copy-start | bytes 388
  0.6 19.9 %copy-start.1 = (s32[4,512]{1,0:T(4,128)S(1)}, s32[4,512]{1,0:T(4,128)}, u32[]{:S(2)}) copy-start(s32[4,512]{1,0:T(4,128)} %param.7) | copy-start | bytes 24580
  0.7 20.2 %copy-start.2 = (s32[4,512]{1,0:T(4,128)S(1)}, s32[4,512]{1,0:T(4,128)}, u32[]{:S(2)}) copy-start(s32[4,512]{1,0:T(4,128)} %param.8) | copy-start | bytes 24580
  9.7 17.6 %collective-permute-start.1 = (bf16[256,128]{1,0:T(8,128)(2,1)S(1)}, bf16[256,128]{1,0:T(8,128)(2,1)S(1)}, u32[]{:S(2)}, u32[]{:S(2)}) collective-permute-start(bf16[256,128]{1,0:T(8,128)(2,1)S(1)} %all_gather.3), channel_id=1, source_target_pairs={{0,252},{4,0},{8,4},{12,8},{16,12},{20,16},{24,20},{28,24},{32,28}... | collective-permute-start | bytes 196616 | tf_op jit(solution)/shard_map/ppermute | solution.py:19
  18.5 8.8 %collective-permute-start = (bf16[256,128]{1,0:T(8,128)(2,1)S(1)}, bf16[256,128]{1,0:T(8,128)(2,1)S(1)}, u32[]{:S(2)}, u32[]{:S(2)}) collective-permute-start(bf16[256,128]{1,0:T(8,128)(2,1)S(1)} %all_gather.3), channel_id=1, source_target_pairs={{0,4},{4,8},{8,12},{12,16},{16,20},{20,24},{24,28},{28,32},{32,36}... | collective-permute-start | bytes 196616 | tf_op jit(solution)/shard_map/ppermute | solution.py:19
  27.4 11.4 %collective-permute-start.3 = (bf16[256,384]{1,0:T(8,128)(2,1)S(1)}, bf16[256,384]{1,0:T(8,128)(2,1)S(1)}, u32[]{:S(2)}, u32[]{:S(2)}) collective-permute-start(bf16[256,384]{1,0:T(8,128)(2,1)S(1)} %constant_dynamic-update-slice_fusion), channel_id=1, source_target_pairs={{0,244},{4,248},{8,252},{12,0},{16,4},{20,8},{24,12},{28,16},{32,2... | collective-permute-start | bytes 589832 | tf_op jit(solution)/shard_map/ppermute | solution.py:19
  27.5 11.2 %collective-permute-start.2 = (bf16[256,384]{1,0:T(8,128)(2,1)S(1)}, bf16[256,384]{1,0:T(8,128)(2,1)S(1)}, u32[]{:S(2)}, u32[]{:S(2)}) collective-permute-start(bf16[256,384]{1,0:T(8,128)(2,1)S(1)} %constant_dynamic-update-slice_fusion), channel_id=1, source_target_pairs={{0,12},{4,16},{8,20},{12,24},{16,28},{20,32},{24,36},{28,40},{32,4... | collective-permute-start | bytes 589832 | tf_op jit(solution)/shard_map/ppermute | solution.py:19
  44.0 10.9 %copy-start.3 = (s32[4]{0:T(128)S(1)}, s32[4]{0:T(128)}, u32[]{:S(2)}) copy-start(s32[4]{0:T(128)} %param.9) | copy-start | bytes 52
  45.0 25.1 %all-to-all-start = ((f32[256,2,128]{2,1,0:T(2,128)}), f32[256,2,128]{2,1,0:T(2,128)S(1)}, u32[]{:S(2)}, u32[]{:S(2)}) async-start(f32[256,2,128]{2,1,0:T(2,128)} %reshape.598), calls=%async_computation | async-start | bytes 524288 | tf_op jit(solution)/shard_map/all_to_all | solution.py:125

commit v20 on v19

--- a/solution.py
+++ b/solution.py
@@ -108,7 +108,7 @@
     slots_local = slots_total // time_devices
 
     def by_block(pairs):
-        return pairs.reshape(owner_devices, time_devices, slots_local).transpose(1, 0, 2).reshape(-1)
+        return pairs.reshape(owner_devices, time_devices, slots_local).transpose(2, 1, 0).reshape(-1)
 
     first_flat = by_block(pair_first)
     second_flat = by_block(pair_second)
@@ -121,10 +121,11 @@
     )
     values = sums.shape[1]
     destinations = time_devices * groups
-    partial_value = sums.reshape(per_group * values, -1).T.reshape(destinations, 2, -1)
+    partial_value = sums.reshape(per_group * values * slots_local, destinations).T
+    partial_value = partial_value.reshape(destinations, 2, -1)
     exchanged = lax.all_to_all(partial_value, ("tm", "chan"), 0, 0, tiled=True)
     summed = jnp.sum(exchanged.reshape(time_devices, groups, -1), axis=0)
-    owned = summed.reshape(groups, slots_local, per_group, values).transpose(0, 2, 3, 1) / ntime
+    owned = summed.reshape(groups, per_group, values, slots_local) / ntime
     owned = owned.reshape(groups, per_group, values, slots_local)
     owned = jnp.concatenate(
         [

time: 72.9 us -> 72.8 us (level)
  starting transfers between devices: 21.3 us -> 22.2 us
  waiting for transfers between devices: 18.1 us -> 17.3 us
    all_to_all x1, starting transfers between devices: 9.81 us -> 10.6 us  [shards(): exchanged = lax.all_to_all(partial_value, ('tm', 'chan'), 0, 0, tiled=True)]
    ppermute x4, waiting for transfers between devices: 4.14 us -> 3.3 us  [from_behind(): lax.ppermute(array, axis, [(i, (i + by) % peers) for i in range(peers)])]
  transfers between devices with their start and end apart: 5 -> 5, of which waited for: 2 -> 2; matrix products, arithmetic and copies ran while one was open for 20% -> 21% of each run, Pallas kernels for 0% -> 0%
where the time goes in v20:
time: 72.8 us; the launch traced here: 72.6 us
  starting transfers between devices  22.2 us (30%)
  waiting for transfers between devices  17.3 us (24%)
  other arithmetic  9.15 us (13%)
  matrix products  8.63 us (12%)
  blocking collectives  8.3 us (11%)
  local copies, waits for them, and re-layouts  5.9 us (8%)
  between operations  1.14 us (2%)
    all_to_all x1, waiting for transfers between devices, shards(): exchanged = lax.all_to_all(partial_value, ('tm', 'chan'), 0, 0, tiled=True)  14 us
    ppermute x4, starting transfers between devices, from_behind(): lax.ppermute(array, axis, [(i, (i + by) % peers) for i in range(peers)])  11.5 us
    all_to_all x1, starting transfers between devices, shards(): exchanged = lax.all_to_all(partial_value, ('tm', 'chan'), 0, 0, tiled=True)  10.6 us
    all_gather x1, blocking collectives, shards(): gathered = lax.all_gather(rounded, 'chan', axis=0, tiled=True)  8.3 us
    dot_general x2, matrix products, pair_sums(): jnp.einsum('pc,qrct->qrpt', pick, parts, preferred_element_type=jnp.bfloa...  5.6 us
    dot_general x2, other arithmetic, time_sum(): jnp.einsum('qpt,qpt->qp', left, right, preferred_element_type=jnp.float32)  4.04 us
    ppermute x4, waiting for transfers between devices, from_behind(): lax.ppermute(array, axis, [(i, (i + by) % peers) for i in range(peers)])  3.3 us
    dot_general x2, matrix products, pair_sums(): jnp.einsum('pc,kqc->kqp', pick, pieces, preferred_element_type=jnp.float32)  1.86 us
  transfers between devices with their start and end apart: 5, of which 2 were waited for; matrix products, arithmetic and copies ran while one was open for 21% of the time, Pallas kernels for 0%

profile of v20, /device:TPU:1, one launch (start us, length us, event | category | flops | bytes accessed | tf_op | source)
XLA Modules:
  0.0 72.6 jit_solution(3698254476402934474)
XLA Ops:
  0.7 0.8 %convert_element_type.133 = bf16[64,128]{1,0:T(8,128)(2,1)S(1)} convert(f32[64,128]{1,0:T(8,128)} %param.5) | non-fusion elementwise | flops 8192 | bytes 49152 | tf_op jit(solution)/shard_map/convert_element_type | solution.py:93
  1.4 8.3 %all_gather.3 = bf16[256,128]{1,0:T(8,128)(2,1)S(1)} all-gather(bf16[64,128]{1,0:T(8,128)(2,1)S(1)} %convert_element_type.133), channel_id=1, replica_groups=mesh['tm'=64,'chan'=4] {'chan'}, dimensions={0}, use_global_device_ids=true | all-gather | bytes 81920 | tf_op jit(solution)/shard_map/all_gather | solution.py:94
  9.7 8.8 %collective-permute-start.1 = (bf16[256,128]{1,0:T(8,128)(2,1)S(1)}, bf16[256,128]{1,0:T(8,128)(2,1)S(1)}, u32[]{:S(2)}, u32[]{:S(2)}) collective-permute-start(bf16[256,128]{1,0:T(8,128)(2,1)S(1)} %all_gather.3), channel_id=1, source_target_pairs={{0,252},{4,0},{8,4},{12,8},{16,12},{20,16},{24,20},{28,24},{32,28}... | collective-permute-start | bytes 196616 | tf_op jit(solution)/shard_map/ppermute | solution.py:19
  18.6 0.6 gather_fusion.1
  19.3 0.6 gather_fusion
  22.3 0.8 %fusion.25 = (bf16[6,1,384,128]{2,3,1,0:T(8,128)(2,1)S(1)}, bf16[6,1,384,128]{2,3,1,0:T(8,128)(2,1)S(1)}) fusion(f32[6,128]{1,0:T(8,128)S(1)} %get-tuple-element.43, f32[6,384]{1,0:T(8,128)S(1)} %get-tuple-element.36, f32[6,128]{1,0:T(8,128)S(1)} %get-tuple-element.42, f32[6,384]{1,0:T(8,128)S(1)} %get-tuple-element.35, f32[6]{0:T(128)S(1)} %get-tuple-element.55, ...), kind=kLoop, calls=%fused_computation.47 | loop fusion | flops 5013504 | bytes 1597512 | tf_op jit(solution)/shard_map/convert_element_type | solution.py:40
  23.1 1.0 %fusion.27 = (bf16[2,1,1152,128]{2,3,1,0:T(8,128)(2,1)S(1)}, bf16[2,1,1152,128]{2,3,1,0:T(8,128)(2,1)S(1)}) fusion(f32[2,128]{1,0:T(2,128)S(1)} %get-tuple-element.45, f32[2,1152]{1,0:T(2,128)S(1)} %get-tuple-element.29, f32[2,128]{1,0:T(2,128)S(1)} %get-tuple-element.44, f32[2,1152]{1,0:T(2,128)S(1)} %get-tuple-element.28, f32[2]{0:T(128)S(1)} %get-tuple-element.51, ...), kind=kLoop, calls=%fused_computation.49 | loop fusion | flops 5013504 | bytes 2379800 | tf_op jit(solution)/shard_map/convert_element_type | solution.py:40
  24.0 3.3 %collective-permute-done = bf16[256,128]{1,0:T(8,128)(2,1)S(1)} collective-permute-done((bf16[256,128]{1,0:T(8,128)(2,1)S(1)}, bf16[256,128]{1,0:T(8,128)(2,1)S(1)}, u32[]{:S(2)}, u32[]{:S(2)}) %collective-permute-start) | collective-permute-done | bytes 65568 | tf_op jit(solution)/shard_map/ppermute | solution.py:19
  27.5 2.7 %collective-permute-start.2 = (bf16[256,384]{1,0:T(8,128)(2,1)S(1)}, bf16[256,384]{1,0:T(8,128)(2,1)S(1)}, u32[]{:S(2)}, u32[]{:S(2)}) collective-permute-start(bf16[256,384]{1,0:T(8,128)(2,1)S(1)} %constant_dynamic-update-slice_fusion), channel_id=1, source_target_pairs={{0,12},{4,16},{8,20},{12,24},{16,28},{20,32},{24,36},{28,40},{32,4... | collective-permute-start | bytes 589832 | tf_op jit(solution)/shard_map/ppermute | solution.py:19
  30.2 0.6 fusion.20
  30.8 0.8 %fusion.10 = f32[3,6,4096]{2,1,0:T(8,128)S(1)} fusion(s32[4096]{0:T(1024)S(1)} %pad_add_fusion, bf16[1,6,256]{2,1,0:T(8,128)(2,1)S(1)} %get-tuple-element.31, bf16[1,6,256]{2,1,0:T(8,128)(2,1)S(1)} %get-tuple-element.32, bf16[1,6,256]{2,1,0:T(8,128)(2,1)S(1)} %get-tuple-element.30), kind=kOutput, calls=%fused_computation.16 | convolution fusion | flops 38806528 | bytes 320512 | tf_op jit(solution)/shard_map/pc,kqc->kqp/dot_general | solution.py:79
  31.7 3.9 %convolution_bitcast_fusion = bf16[6,2,4096,128]{2,3,1,0:T(8,128)(2,1)S(1)} fusion(s32[4096]{0:T(1024)S(1)} %pad_add_fusion, bf16[6,2,128,256]{3,2,1,0:T(8,128)(2,1)S(1)} %get-tuple-element.49), kind=kOutput, calls=%fused_computation.6 | convolution fusion | flops 3222274048 | bytes 13385728 | tf_op jit(solution)/shard_map/pc,qrct->qrpt/dot_general | solution.py:61
  35.6 3.1 %fusion.2 = (f32[6,2048]{1,0:T(8,128)S(1)}, f32[6,2048]{1,0:T(8,128)S(1)}, f32[6,2048]{1,0:T(8,128)S(1)}, f32[6,2048]{1,0:T(8,128)S(1)}) fusion(bf16[6,2,4096,128]{2,3,1,0:T(8,128)(2,1)S(1)} %convolution_bitcast_fusion), kind=kLoop, calls=%fused_computation.9 | loop fusion | flops 18825216 | bytes 12779520 | tf_op jit(solution)/shard_map/qpt,qpt->qp/dot_general | solution.py:69
  38.9 0.6 fusion.39
  39.5 1.0 %fusion.8 = f32[3,2,4096]{2,1,0:T(2,128)S(1)} fusion(s32[4096]{0:T(1024)S(1)} %pad_add_fusion, bf16[3,2,256]{2,0,1:T(4,128)(2,1)S(1)} %pad_maximum_fusion.1), kind=kOutput, calls=%fused_computation.15 | convolution fusion | flops 13631488 | bytes 117760 | tf_op jit(solution)/shard_map/pc,kqc->kqp/dot_general | solution.py:79
  40.6 1.7 %convolution_bitcast_fusion.1 = bf16[2,2,4096,128]{2,3,1,0:T(8,128)(2,1)S(1)} fusion(s32[4096]{0:T(1024)S(1)} %pad_add_fusion, bf16[2,2,128,256]{3,2,1,0:T(8,128)(2,1)S(1)} %get-tuple-element.47), kind=kOutput, calls=%fused_computation.11 | convolution fusion | flops 1074790400 | bytes 4472832 | tf_op jit(solution)/shard_map/pc,qrct->qrpt/dot_general | solution.py:61
  42.3 1.0 %fusion.14 = (f32[2,2048]{1,0:T(2,128)S(1)}, f32[2,2048]{1,0:T(2,128)S(1)}, f32[2,2048]{1,0:T(2,128)S(1)}, f32[2,2048]{1,0:T(2,128)S(1)}) fusion(bf16[2,2,4096,128]{2,3,1,0:T(8,128)(2,1)S(1)} %convolution_bitcast_fusion.1), kind=kLoop, calls=%fused_computation.27 | loop fusion | flops 6275072 | bytes 4259840 | tf_op jit(solution)/shard_map/qpt,qpt->qp/dot_general | solution.py:69
  43.7 0.8 %copy.48 = f32[256,2,128]{2,1,0:T(2,128)} copy(f32[256,2,128]{0,2,1:T(8,128)S(1)} %bitcast.170) | data formatting | bytes 524288 | tf_op jit(solution)/shard_map/reshape | solution.py:125
  44.5 10.6 %all-to-all-start = ((f32[256,2,128]{2,1,0:T(2,128)}), f32[256,2,128]{2,1,0:T(2,128)S(1)}, u32[]{:S(2)}, u32[]{:S(2)}) async-start(f32[256,2,128]{2,1,0:T(2,128)} %copy.48), calls=%async_computation | async-start | bytes 524288 | tf_op jit(solution)/shard_map/all_to_all | solution.py:126
  55.2 0.6 dynamic_slice.3
  55.8 0.7 add_compare_fusion
  56.5 14.0 %all-to-all-done = f32[256,2,128]{2,1,0:T(2,128)S(1)} async-done(((f32[256,2,128]{2,1,0:T(2,128)}), f32[256,2,128]{2,1,0:T(2,128)S(1)}, u32[]{:S(2)}, u32[]{:S(2)}) %all-to-all-start) | async-done | bytes 262176 | tf_op jit(solution)/shard_map/all_to_all | solution.py:126
  71.2 0.7 select_bitcast_fusion
  72.0 0.6 copy.52
  (73 shorter events, 3.9 us)
Async XLA Ops:
  0.6 18.0 %copy-start = (s32[32]{0:T(128)S(1)}, s32[32]{0:T(128)}, u32[]{:S(2)}) copy-start(s32[32]{0:T(128)} %param.6) | copy-start | bytes 388
  0.6 19.9 %copy-start.1 = (s32[4,512]{1,0:T(4,128)S(1)}, s32[4,512]{1,0:T(4,128)}, u32[]{:S(2)}) copy-start(s32[4,512]{1,0:T(4,128)} %param.7) | copy-start | bytes 24580
  0.7 20.7 %copy-start.2 = (s32[4,512]{1,0:T(4,128)S(1)}, s32[4,512]{1,0:T(4,128)}, u32[]{:S(2)}) copy-start(s32[4,512]{1,0:T(4,128)} %param.8) | copy-start | bytes 24580
  9.7 17.6 %collective-permute-start.1 = (bf16[256,128]{1,0:T(8,128)(2,1)S(1)}, bf16[256,128]{1,0:T(8,128)(2,1)S(1)}, u32[]{:S(2)}, u32[]{:S(2)}) collective-permute-start(bf16[256,128]{1,0:T(8,128)(2,1)S(1)} %all_gather.3), channel_id=1, source_target_pairs={{0,252},{4,0},{8,4},{12,8},{16,12},{20,16},{24,20},{28,24},{32,28}... | collective-permute-start | bytes 196616 | tf_op jit(solution)/shard_map/ppermute | solution.py:19
  18.5 8.8 %collective-permute-start = (bf16[256,128]{1,0:T(8,128)(2,1)S(1)}, bf16[256,128]{1,0:T(8,128)(2,1)S(1)}, u32[]{:S(2)}, u32[]{:S(2)}) collective-permute-start(bf16[256,128]{1,0:T(8,128)(2,1)S(1)} %all_gather.3), channel_id=1, source_target_pairs={{0,4},{4,8},{8,12},{12,16},{16,20},{20,24},{24,28},{28,32},{32,36}... | collective-permute-start | bytes 196616 | tf_op jit(solution)/shard_map/ppermute | solution.py:19
  27.4 11.4 %collective-permute-start.3 = (bf16[256,384]{1,0:T(8,128)(2,1)S(1)}, bf16[256,384]{1,0:T(8,128)(2,1)S(1)}, u32[]{:S(2)}, u32[]{:S(2)}) collective-permute-start(bf16[256,384]{1,0:T(8,128)(2,1)S(1)} %constant_dynamic-update-slice_fusion), channel_id=1, source_target_pairs={{0,244},{4,248},{8,252},{12,0},{16,4},{20,8},{24,12},{28,16},{32,2... | collective-permute-start | bytes 589832 | tf_op jit(solution)/shard_map/ppermute | solution.py:19
  27.5 11.2 %collective-permute-start.2 = (bf16[256,384]{1,0:T(8,128)(2,1)S(1)}, bf16[256,384]{1,0:T(8,128)(2,1)S(1)}, u32[]{:S(2)}, u32[]{:S(2)}) collective-permute-start(bf16[256,384]{1,0:T(8,128)(2,1)S(1)} %constant_dynamic-update-slice_fusion), channel_id=1, source_target_pairs={{0,12},{4,16},{8,20},{12,24},{16,28},{20,32},{24,36},{28,40},{32,4... | collective-permute-start | bytes 589832 | tf_op jit(solution)/shard_map/ppermute | solution.py:19
  43.4 11.8 %copy-start.3 = (s32[4]{0:T(128)S(1)}, s32[4]{0:T(128)}, u32[]{:S(2)}) copy-start(s32[4]{0:T(128)} %param.9) | copy-start | bytes 52
  44.5 25.9 %all-to-all-start = ((f32[256,2,128]{2,1,0:T(2,128)}), f32[256,2,128]{2,1,0:T(2,128)S(1)}, u32[]{:S(2)}, u32[]{:S(2)}) async-start(f32[256,2,128]{2,1,0:T(2,128)} %copy.48), calls=%async_computation | async-start | bytes 524288 | tf_op jit(solution)/shard_map/all_to_all | solution.py:126

commit v21 on v17

--- a/solution.py
+++ b/solution.py
@@ -121,7 +121,7 @@
     )
     values = sums.shape[1]
     destinations = time_devices * groups
-    partial_value = sums.reshape(per_group * values, -1).T.reshape(destinations, -1)
+    partial_value = sums.reshape(per_group * values, -1).T.reshape(destinations, 2, -1)
     exchanged = lax.all_to_all(partial_value, ("tm", "chan"), 0, 0, tiled=True)
     summed = jnp.sum(exchanged.reshape(time_devices, groups, -1), axis=0)
     owned = summed.reshape(groups, slots_local, per_group, values).transpose(1, 3, 0, 2) / ntime

time: 73.4 us -> 72.9 us (level)
    all_to_all x1 -> x0, local copies, waits for them, and re-layouts: 1.15 us -> none  [shards(): exchanged = lax.all_to_all(partial_value, ('tm', 'chan'), 0, 0, tiled=True)]
    reshape x1 -> x2, local copies, waits for them, and re-layouts: 0.09 us -> 1.13 us  [shards(): sums.reshape(per_group * values, -1).T.reshape(destinations, 2, -1)]
where the time goes in v21:
time: 72.9 us; the launch traced here: 72.7 us
  starting transfers between devices  21.3 us (29%)
  waiting for transfers between devices  18.1 us (25%)
  other arithmetic  9.07 us (12%)
  matrix products  8.63 us (12%)
  blocking collectives  8.3 us (11%)
  local copies, waits for them, and re-layouts  6.07 us (8%)
  between operations  1.14 us (2%)
    all_to_all x1, waiting for transfers between devices, shards(): exchanged = lax.all_to_all(partial_value, ('tm', 'chan'), 0, 0, tiled=True)  14 us
    ppermute x4, starting transfers between devices, from_behind(): lax.ppermute(array, axis, [(i, (i + by) % peers) for i in range(peers)])  11.5 us
    all_to_all x1, starting transfers between devices, shards(): exchanged = lax.all_to_all(partial_value, ('tm', 'chan'), 0, 0, tiled=True)  9.81 us
    all_gather x1, blocking collectives, shards(): gathered = lax.all_gather(rounded, 'chan', axis=0, tiled=True)  8.3 us
    dot_general x2, matrix products, pair_sums(): jnp.einsum('pc,qrct->qrpt', pick, parts, preferred_element_type=jnp.bfloa...  5.6 us
    ppermute x4, waiting for transfers between devices, from_behind(): lax.ppermute(array, axis, [(i, (i + by) % peers) for i in range(peers)])  4.14 us
    dot_general x2, other arithmetic, time_sum(): jnp.einsum('qpt,qpt->qp', left, right, preferred_element_type=jnp.float32)  4.04 us
    dot_general x2, matrix products, pair_sums(): jnp.einsum('pc,kqc->kqp', pick, pieces, preferred_element_type=jnp.float32)  1.86 us
  transfers between devices with their start and end apart: 5, of which 2 were waited for; matrix products, arithmetic and copies ran while one was open for 20% of the time, Pallas kernels for 0%

profile of v21, /device:TPU:1, one launch (start us, length us, event | category | flops | bytes accessed | tf_op | source)
XLA Modules:
  0.0 72.7 jit_solution(14290526557123109863)
XLA Ops:
  0.7 0.8 %convert_element_type.133 = bf16[64,128]{1,0:T(8,128)(2,1)S(1)} convert(f32[64,128]{1,0:T(8,128)} %param.5) | non-fusion elementwise | flops 8192 | bytes 49152 | tf_op jit(solution)/shard_map/convert_element_type | solution.py:93
  1.4 8.3 %all_gather.3 = bf16[256,128]{1,0:T(8,128)(2,1)S(1)} all-gather(bf16[64,128]{1,0:T(8,128)(2,1)S(1)} %convert_element_type.133), channel_id=1, replica_groups=mesh['tm'=64,'chan'=4] {'chan'}, dimensions={0}, use_global_device_ids=true | all-gather | bytes 81920 | tf_op jit(solution)/shard_map/all_gather | solution.py:94
  9.7 8.8 %collective-permute-start.1 = (bf16[256,128]{1,0:T(8,128)(2,1)S(1)}, bf16[256,128]{1,0:T(8,128)(2,1)S(1)}, u32[]{:S(2)}, u32[]{:S(2)}) collective-permute-start(bf16[256,128]{1,0:T(8,128)(2,1)S(1)} %all_gather.3), channel_id=1, source_target_pairs={{0,252},{4,0},{8,4},{12,8},{16,12},{20,16},{24,20},{28,24},{32,28}... | collective-permute-start | bytes 196616 | tf_op jit(solution)/shard_map/ppermute | solution.py:19
  18.6 0.6 gather_fusion.1
  19.3 0.6 gather_fusion
  21.4 0.8 %fusion.25 = (bf16[6,1,384,128]{2,3,1,0:T(8,128)(2,1)S(1)}, bf16[6,1,384,128]{2,3,1,0:T(8,128)(2,1)S(1)}) fusion(f32[6,128]{1,0:T(8,128)S(1)} %get-tuple-element.39, f32[6,384]{1,0:T(8,128)S(1)} %get-tuple-element.32, f32[6,128]{1,0:T(8,128)S(1)} %get-tuple-element.38, f32[6,384]{1,0:T(8,128)S(1)} %get-tuple-element.31, f32[6]{0:T(128)S(1)} %get-tuple-element.51, ...), kind=kLoop, calls=%fused_computation.47 | loop fusion | flops 5013504 | bytes 1597512 | tf_op jit(solution)/shard_map/convert_element_type | solution.py:40
  22.2 1.0 %fusion.27 = (bf16[2,1,1152,128]{2,3,1,0:T(8,128)(2,1)S(1)}, bf16[2,1,1152,128]{2,3,1,0:T(8,128)(2,1)S(1)}) fusion(f32[2,128]{1,0:T(2,128)S(1)} %get-tuple-element.41, f32[2,1152]{1,0:T(2,128)S(1)} %get-tuple-element.25, f32[2,128]{1,0:T(2,128)S(1)} %get-tuple-element.40, f32[2,1152]{1,0:T(2,128)S(1)} %get-tuple-element.24, f32[2]{0:T(128)S(1)} %get-tuple-element.47, ...), kind=kLoop, calls=%fused_computation.49 | loop fusion | flops 5013504 | bytes 2379800 | tf_op jit(solution)/shard_map/convert_element_type | solution.py:40
  23.2 4.1 %collective-permute-done = bf16[256,128]{1,0:T(8,128)(2,1)S(1)} collective-permute-done((bf16[256,128]{1,0:T(8,128)(2,1)S(1)}, bf16[256,128]{1,0:T(8,128)(2,1)S(1)}, u32[]{:S(2)}, u32[]{:S(2)}) %collective-permute-start) | collective-permute-done | bytes 65568 | tf_op jit(solution)/shard_map/ppermute | solution.py:19
  27.5 2.7 %collective-permute-start.2 = (bf16[256,384]{1,0:T(8,128)(2,1)S(1)}, bf16[256,384]{1,0:T(8,128)(2,1)S(1)}, u32[]{:S(2)}, u32[]{:S(2)}) collective-permute-start(bf16[256,384]{1,0:T(8,128)(2,1)S(1)} %constant_dynamic-update-slice_fusion), channel_id=1, source_target_pairs={{0,12},{4,16},{8,20},{12,24},{16,28},{20,32},{24,36},{28,40},{32,4... | collective-permute-start | bytes 589832 | tf_op jit(solution)/shard_map/ppermute | solution.py:19
  30.2 0.6 fusion.20
  30.8 0.8 %fusion.10 = f32[3,6,4096]{2,1,0:T(8,128)S(1)} fusion(s32[4096]{0:T(1024)S(1)} %pad_add_fusion, bf16[1,6,256]{2,1,0:T(8,128)(2,1)S(1)} %get-tuple-element.27, bf16[1,6,256]{2,1,0:T(8,128)(2,1)S(1)} %get-tuple-element.28, bf16[1,6,256]{2,1,0:T(8,128)(2,1)S(1)} %get-tuple-element.26), kind=kOutput, calls=%fused_computation.16 | convolution fusion | flops 38806528 | bytes 320512 | tf_op jit(solution)/shard_map/pc,kqc->kqp/dot_general | solution.py:79
  31.7 3.9 %convolution_bitcast_fusion = bf16[6,2,4096,128]{2,3,1,0:T(8,128)(2,1)S(1)} fusion(s32[4096]{0:T(1024)S(1)} %pad_add_fusion, bf16[6,2,128,256]{3,2,1,0:T(8,128)(2,1)S(1)} %get-tuple-element.45), kind=kOutput, calls=%fused_computation.6 | convolution fusion | flops 3222274048 | bytes 13385728 | tf_op jit(solution)/shard_map/pc,qrct->qrpt/dot_general | solution.py:61
  35.6 3.1 %fusion.2 = (f32[6,2048]{1,0:T(8,128)S(1)}, f32[6,2048]{1,0:T(8,128)S(1)}, f32[6,2048]{1,0:T(8,128)S(1)}, f32[6,2048]{1,0:T(8,128)S(1)}) fusion(bf16[6,2,4096,128]{2,3,1,0:T(8,128)(2,1)S(1)} %convolution_bitcast_fusion), kind=kLoop, calls=%fused_computation.9 | loop fusion | flops 18825216 | bytes 12779520 | tf_op jit(solution)/shard_map/qpt,qpt->qp/dot_general | solution.py:69
  38.9 0.6 fusion.39
  39.5 1.0 %fusion.8 = f32[3,2,4096]{2,1,0:T(2,128)S(1)} fusion(s32[4096]{0:T(1024)S(1)} %pad_add_fusion, bf16[3,2,256]{2,0,1:T(4,128)(2,1)S(1)} %pad_maximum_fusion.1), kind=kOutput, calls=%fused_computation.15 | convolution fusion | flops 13631488 | bytes 117760 | tf_op jit(solution)/shard_map/pc,kqc->kqp/dot_general | solution.py:79
  40.6 1.7 %convolution_bitcast_fusion.1 = bf16[2,2,4096,128]{2,3,1,0:T(8,128)(2,1)S(1)} fusion(s32[4096]{0:T(1024)S(1)} %pad_add_fusion, bf16[2,2,128,256]{3,2,1,0:T(8,128)(2,1)S(1)} %get-tuple-element.43), kind=kOutput, calls=%fused_computation.11 | convolution fusion | flops 1074790400 | bytes 4472832 | tf_op jit(solution)/shard_map/pc,qrct->qrpt/dot_general | solution.py:61
  42.3 1.0 %fusion.14 = (f32[2,2048]{1,0:T(2,128)S(1)}, f32[2,2048]{1,0:T(2,128)S(1)}, f32[2,2048]{1,0:T(2,128)S(1)}, f32[2,2048]{1,0:T(2,128)S(1)}) fusion(bf16[2,2,4096,128]{2,3,1,0:T(8,128)(2,1)S(1)} %convolution_bitcast_fusion.1), kind=kLoop, calls=%fused_computation.27 | loop fusion | flops 6275072 | bytes 4259840 | tf_op jit(solution)/shard_map/qpt,qpt->qp/dot_general | solution.py:69
  44.0 1.0 %reshape.642 = f32[256,2,128]{2,1,0:T(2,128)} reshape(f32[2048,32]{1,0:T(8,128)S(1)} %copy.47) | data formatting | bytes 524288 | tf_op jit(solution)/shard_map/reshape | solution.py:124
  45.0 9.8 %all-to-all-start = ((f32[256,2,128]{2,1,0:T(2,128)}), f32[256,2,128]{2,1,0:T(2,128)S(1)}, u32[]{:S(2)}, u32[]{:S(2)}) async-start(f32[256,2,128]{2,1,0:T(2,128)} %reshape.642), calls=%async_computation | async-start | bytes 524288 | tf_op jit(solution)/shard_map/all_to_all | solution.py:125
  54.9 0.6 dynamic_slice.3
  55.5 0.7 add_compare_fusion
  56.1 14.0 %all-to-all-done = f32[256,2,128]{2,1,0:T(2,128)S(1)} async-done(((f32[256,2,128]{2,1,0:T(2,128)}), f32[256,2,128]{2,1,0:T(2,128)S(1)}, u32[]{:S(2)}, u32[]{:S(2)}) %all-to-all-start) | async-done | bytes 262176 | tf_op jit(solution)/shard_map/all_to_all | solution.py:125
  71.3 0.7 bitcast_select_fusion
  72.0 0.6 copy.51
  (74 shorter events, 3.8 us)
Async XLA Ops:
  0.6 18.0 %copy-start = (s32[32]{0:T(128)S(1)}, s32[32]{0:T(128)}, u32[]{:S(2)}) copy-start(s32[32]{0:T(128)} %param.6) | copy-start | bytes 388
  0.6 19.9 %copy-start.1 = (s32[4,512]{1,0:T(4,128)S(1)}, s32[4,512]{1,0:T(4,128)}, u32[]{:S(2)}) copy-start(s32[4,512]{1,0:T(4,128)} %param.7) | copy-start | bytes 24580
  0.7 20.2 %copy-start.2 = (s32[4,512]{1,0:T(4,128)S(1)}, s32[4,512]{1,0:T(4,128)}, u32[]{:S(2)}) copy-start(s32[4,512]{1,0:T(4,128)} %param.8) | copy-start | bytes 24580
  9.7 17.6 %collective-permute-start.1 = (bf16[256,128]{1,0:T(8,128)(2,1)S(1)}, bf16[256,128]{1,0:T(8,128)(2,1)S(1)}, u32[]{:S(2)}, u32[]{:S(2)}) collective-permute-start(bf16[256,128]{1,0:T(8,128)(2,1)S(1)} %all_gather.3), channel_id=1, source_target_pairs={{0,252},{4,0},{8,4},{12,8},{16,12},{20,16},{24,20},{28,24},{32,28}... | collective-permute-start | bytes 196616 | tf_op jit(solution)/shard_map/ppermute | solution.py:19
  18.5 8.8 %collective-permute-start = (bf16[256,128]{1,0:T(8,128)(2,1)S(1)}, bf16[256,128]{1,0:T(8,128)(2,1)S(1)}, u32[]{:S(2)}, u32[]{:S(2)}) collective-permute-start(bf16[256,128]{1,0:T(8,128)(2,1)S(1)} %all_gather.3), channel_id=1, source_target_pairs={{0,4},{4,8},{8,12},{12,16},{16,20},{20,24},{24,28},{28,32},{32,36}... | collective-permute-start | bytes 196616 | tf_op jit(solution)/shard_map/ppermute | solution.py:19
  27.4 11.4 %collective-permute-start.3 = (bf16[256,384]{1,0:T(8,128)(2,1)S(1)}, bf16[256,384]{1,0:T(8,128)(2,1)S(1)}, u32[]{:S(2)}, u32[]{:S(2)}) collective-permute-start(bf16[256,384]{1,0:T(8,128)(2,1)S(1)} %constant_dynamic-update-slice_fusion), channel_id=1, source_target_pairs={{0,244},{4,248},{8,252},{12,0},{16,4},{20,8},{24,12},{28,16},{32,2... | collective-permute-start | bytes 589832 | tf_op jit(solution)/shard_map/ppermute | solution.py:19
  27.5 11.2 %collective-permute-start.2 = (bf16[256,384]{1,0:T(8,128)(2,1)S(1)}, bf16[256,384]{1,0:T(8,128)(2,1)S(1)}, u32[]{:S(2)}, u32[]{:S(2)}) collective-permute-start(bf16[256,384]{1,0:T(8,128)(2,1)S(1)} %constant_dynamic-update-slice_fusion), channel_id=1, source_target_pairs={{0,12},{4,16},{8,20},{12,24},{16,28},{20,32},{24,36},{28,40},{32,4... | collective-permute-start | bytes 589832 | tf_op jit(solution)/shard_map/ppermute | solution.py:19
  44.0 10.9 %copy-start.3 = (s32[4]{0:T(128)S(1)}, s32[4]{0:T(128)}, u32[]{:S(2)}) copy-start(s32[4]{0:T(128)} %param.9) | copy-start | bytes 52
  45.0 25.1 %all-to-all-start = ((f32[256,2,128]{2,1,0:T(2,128)}), f32[256,2,128]{2,1,0:T(2,128)S(1)}, u32[]{:S(2)}, u32[]{:S(2)}) async-start(f32[256,2,128]{2,1,0:T(2,128)} %reshape.642), calls=%async_computation | async-start | bytes 524288 | tf_op jit(solution)/shard_map/all_to_all | solution.py:125
